TPU v7x, 32 devices: a whole 2x2x4 slice. The times are simulated.
32 devices in a mesh: grp: 2 (over x), seq: 16 (over z, y, core).
Axes of the slice: x: 2, y: 2, z: 4, core: 2. Of those that a mesh axis runs over, the one named last changes fastest.
Arguments:
- tokens: int32 [4, 2048], P('grp', 'seq'), parts along dimension 0, may hold values from 0 to 3
- emb_half: bfloat16 [2, 512], replicated, may hold values from -6 to 6
- norm_gain: float32 [512], replicated, may hold values from 0.1 to 1.9
- w_xbc: bfloat16 [512, 1152], replicated, may hold values from -0.25 to 0.25
- w_z: bfloat16 [512, 1024], replicated, may hold values from -0.25 to 0.25
- w_dt: bfloat16 [512, 16], replicated, may hold values from -0.25 to 0.25
- conv_w: float32 [4, 1152], replicated, may hold values from -3 to 3
- conv_bias: float32 [1152], replicated, may hold values from -3 to 3
- dt_bias: float32 [16], replicated, may hold values from -1 to 1
- a_log: float32 [16], replicated
- d_skip: float32 [16], replicated, may hold values from 0.5 to 1.5
- inner_gain: float32 [1024], replicated, may hold values from 0.1 to 1.9
- w_out: bfloat16 [1024, 512], replicated, may hold values from -0.1875 to 0.1875
- final_gain: float32 [512], replicated, may hold values from 0.1 to 1.9
- w_head_half: bfloat16 [512, 2], replicated, may hold values from -0.25 to 0.25
- teacher_top: int32 [4, 2, 2048], P('grp', None, 'seq'), parts along dimension 0, may hold values from 0 to 3, as said below
- teacher_vals: float32 [4, 2, 2048], P('grp', None, 'seq'), parts along dimension 0, may hold values from -8 to 405
Outputs:
- hidden_out: bfloat16 [4, 2048, 512], P('grp', 'seq'), parts along dimension 0
- divergence: float32 [4, 2048], P('grp', 'seq'), parts along dimension 0
There are 2 independent parts, one for each index of `grp`. A program takes and returns all parts, laid end to end along the dimension named above; an argument that names none is the same for every part. Nothing has to cross between parts.
Inputs may be any that keep to these rules, and one draw needn't show every extreme that they name: `teacher_top`: the 2 bases kept at a position are distinct.
All inputs are finite; a program needn't handle non-finite values.
Results may differ from a plain program's by a relative error of at most 0.012.
Values may be sent and summed in bfloat16 or wider, within the bound.
No kernel may reach another device: no remote copies, remote signals or barrier semaphores. Data moves between devices by JAX's collectives and lax.ppermute only.
A program may use at most 320 MiB of HBM per device.

v0:
```python
import jax
import jax.numpy as jnp
import numpy as np
from jax import lax
from jax.sharding import PartitionSpec as P

INNER = 1024
HD = 64
NS = 64
KW = 4
BLK = 128
HEADS = 16
CONVW = 1152
BASES = 4
GRAMS = 344


EPS = 1e-05
HIGH = lax.Precision.HIGHEST


def rms_gain(values, gain_row):
    return values * lax.rsqrt(jnp.mean(values * values, axis=-1, keepdims=True) + EPS) * gain_row


def to_blocks(values, block_width):
    streams, count = (values.shape[0], values.shape[1])
    return jnp.moveaxis(
        values.reshape((streams, count // block_width, block_width) + values.shape[2:]), 1, 0
    )


def ssd_block(carry_state, block_in):
    x_blk, b_blk, c_blk, decay_blk, dt_blk = block_in
    cumulated = jnp.cumsum(decay_blk, axis=2)
    block_len = decay_blk.shape[2]
    scores = jnp.einsum("gtn,gsn->gts", c_blk, b_blk, precision=HIGH)
    seg_diff = cumulated[:, :, :, None] - cumulated[:, :, None, :]
    lower_mask = jnp.arange(block_len)[:, None] >= jnp.arange(block_len)[None, :]
    decays = jnp.where(lower_mask, jnp.exp(jnp.where(lower_mask, seg_diff, 0.0)), 0.0)
    weights = (scores[:, None] * decays * dt_blk[:, :, None, :]).astype(jnp.bfloat16)
    y_intra = jnp.einsum("ghts,gshp->gthp", weights, x_blk, preferred_element_type=jnp.float32)
    y_inter = (
        jnp.einsum("gtn,ghpn->gthp", c_blk, carry_state, precision=HIGH)
        * jnp.swapaxes(jnp.exp(cumulated), 1, 2)[..., None]
    )
    last_cum = cumulated[:, :, -1:]
    scaled = jnp.exp(last_cum - cumulated) * dt_blk
    x_weighted = x_blk.astype(jnp.float32) * jnp.swapaxes(scaled, 1, 2)[..., None]
    new_state = jnp.exp(last_cum)[..., None] * carry_state + jnp.einsum(
        "gshp,gsn->ghpn", x_weighted, b_blk, precision=HIGH
    )
    return (new_state, y_intra + y_inter)


def gram_layout():
    rows = []
    for real in range(1, KW + 1):
        for code in range(BASES**real):
            taps = [None] * (KW - real) + [
                (code // BASES ** (real - 1 - k)) % BASES for k in range(real)
            ]
            rows.append(taps)
    picks = np.zeros((GRAMS, KW * BASES), np.float32)
    for row, taps in enumerate(rows):
        for offset, base in enumerate(taps):
            if base is not None:
                picks[row, offset * BASES + base] = 1.0
    return picks


def gram_tables(emb_full, norm_gain, w_xbc, w_z, w_dt, conv_w, conv_bias):
    row_norm = rms_gain(emb_full.astype(jnp.float32), norm_gain).astype(jnp.bfloat16)
    xbc_rows = jnp.dot(row_norm, w_xbc, preferred_element_type=jnp.float32).astype(jnp.bfloat16)
    z_rows = jnp.dot(row_norm, w_z, preferred_element_type=jnp.float32).astype(jnp.bfloat16)
    dt_rows = jnp.dot(row_norm, w_dt, preferred_element_type=jnp.float32)
    taps = (conv_w[:, None, :] * xbc_rows.astype(jnp.float32)[None]).reshape(KW * BASES, CONVW)
    conv_sum = conv_bias + jnp.dot(jnp.asarray(gram_layout()), taps, precision=HIGH)
    return jax.nn.silu(conv_sum), z_rows, dt_rows


def gram_ids(seq_tok):
    streams, total = seq_tok.shape
    padded = jnp.concatenate([jnp.zeros((streams, KW - 1), seq_tok.dtype), seq_tok], axis=1)
    where_in = jnp.arange(total)[None, :]
    code = jnp.zeros_like(seq_tok)
    ids = jnp.zeros_like(seq_tok)
    offset_of = 0
    for real in range(1, KW + 1):
        code = code + padded[:, KW - real : KW - real + total] * BASES ** (real - 1)
        chosen = (where_in >= real - 1) if real == KW else (where_in == real - 1)
        ids = jnp.where(chosen, offset_of + code, ids)
        offset_of += BASES**real
    return ids


def gather_all(tokens, axis):
    count = lax.axis_size(axis)
    place = lax.axis_index(axis)
    held = tokens
    bit = 0
    while 2**bit < count:
        mask = 2**bit
        other = lax.ppermute(held, axis, [(src, src ^ mask) for src in range(count)])
        upper = (place // mask) % 2 == 1
        held = jnp.where(
            upper,
            jnp.concatenate([other, held], axis=1),
            jnp.concatenate([held, other], axis=1),
        )
        bit += 1
    return held


def base_lookup(rows, bases):
    picked = jnp.zeros(bases.shape + rows.shape[1:], jnp.float32)
    for base in range(BASES):
        picked = picked + jnp.where(
            (bases == base)[..., None], rows[base].astype(jnp.float32), 0.0
        )
    return picked


def local(
    tokens,
    emb_half,
    norm_gain,
    w_xbc,
    w_z,
    w_dt,
    conv_w,
    conv_bias,
    dt_bias,
    a_log,
    d_skip,
    inner_gain,
    w_out,
    final_gain,
    w_head_half,
    teacher_top,
    teacher_vals,
):
    windows, count = tokens.shape
    nseq = lax.axis_size("seq")
    place = lax.axis_index("seq")
    total = count * nseq
    nblk = total // BLK
    streams = 2 * windows

    emb_full = jnp.concatenate([emb_half, emb_half[::-1, ::-1]], axis=0)
    activated_tab, z_rows, dt_rows = gram_tables(
        emb_full, norm_gain, w_xbc, w_z, w_dt, conv_w, conv_bias
    )
    x_tab = activated_tab[:, :INNER].astype(jnp.bfloat16)
    b_tab = activated_tab[:, INNER : INNER + NS]

    every = gather_all(tokens, "seq")
    seq_tok = jnp.concatenate([every, (BASES - 1) - every[:, ::-1]], axis=0)
    gram = gram_ids(seq_tok)

    step_dt = jax.nn.softplus(base_lookup(dt_rows, seq_tok) + dt_bias)
    log_decay = -jnp.exp(a_log) * step_dt

    fwd_start = place * count
    rc_start = (nseq - 1 - place) * count
    start = jnp.concatenate(
        [jnp.full((windows,), fwd_start), jnp.full((windows,), rc_start)]
    )
    first_blk = start // BLK

    cum = jnp.cumsum(log_decay.reshape(streams, nblk, BLK, HEADS), axis=2)
    blk_total = cum[:, :, -1, :]
    within = jnp.exp(blk_total[:, :, None, :] - cum) * step_dt.reshape(
        streams, nblk, BLK, HEADS
    )
    blk_idx = jnp.arange(nblk)
    between = (blk_idx[None, :, None] < blk_idx[None, None, :]) & (
        blk_idx[None, None, :] < first_blk[:, None, None]
    )
    span = jnp.sum(
        jnp.where(between[..., None], blk_total[:, None, :, :], 0.0), axis=2
    )
    across = jnp.where(
        (blk_idx[None, :] < first_blk[:, None])[..., None], jnp.exp(span), 0.0
    )
    weight = (within * across[:, :, None, :]).reshape(streams, total, HEADS)

    onehot = (gram[..., None] == jnp.arange(GRAMS, dtype=gram.dtype)).astype(jnp.bfloat16)
    weight_hi = weight.astype(jnp.bfloat16)
    weight_lo = (weight - weight_hi.astype(jnp.float32)).astype(jnp.bfloat16)
    per_gram = jnp.einsum(
        "rpg,rph->rgh", onehot, weight_hi, preferred_element_type=jnp.float32
    ) + jnp.einsum("rpg,rph->rgh", onehot, weight_lo, preferred_element_type=jnp.float32)
    b_scaled = per_gram.transpose(0, 2, 1)[..., None] * b_tab[None, None]
    b_hi = b_scaled.astype(jnp.bfloat16)
    b_lo = (b_scaled - b_hi.astype(jnp.float32)).astype(jnp.bfloat16)
    x_heads = x_tab.reshape(GRAMS, HEADS, HD).transpose(1, 0, 2)
    start_state = jnp.einsum(
        "hgp,rhgn->rhpn", x_heads, b_hi, preferred_element_type=jnp.float32
    ) + jnp.einsum("hgp,rhgn->rhpn", x_heads, b_lo, preferred_element_type=jnp.float32)

    def mine(values):
        fwd = lax.dynamic_slice_in_dim(values[:windows], fwd_start, count, axis=1)
        rc = lax.dynamic_slice_in_dim(values[windows:], rc_start, count, axis=1)
        return jnp.concatenate([fwd, rc], axis=0)

    act = jnp.take(activated_tab, mine(gram), axis=0)
    x_act = act[..., :INNER].astype(jnp.bfloat16)
    b_all = act[..., INNER : INNER + NS]
    c_all = act[..., INNER + NS :]
    local_tok = jnp.concatenate([tokens, (BASES - 1) - tokens[:, ::-1]], axis=0)
    gate_z = jnp.take(z_rows, local_tok, axis=0)
    blocks = (
        to_blocks(x_act.reshape(streams, count, HEADS, HD), BLK),
        to_blocks(b_all, BLK),
        to_blocks(c_all, BLK),
        jnp.swapaxes(to_blocks(mine(log_decay), BLK), 2, 3),
        jnp.swapaxes(to_blocks(mine(step_dt), BLK), 2, 3),
    )
    _, y_blocks = lax.scan(ssd_block, start_state, blocks)
    y_local = jnp.moveaxis(y_blocks, 0, 1).reshape(streams, count, HEADS, HD)
    y_all = y_local + d_skip[:, None] * x_act.astype(jnp.float32).reshape(
        streams, count, HEADS, HD
    )
    gated_y = y_all * jax.nn.silu(gate_z.astype(jnp.float32)).reshape(streams, count, HEADS, HD)
    normed = (
        rms_gain(gated_y, inner_gain.reshape(HEADS, HD))
        .astype(jnp.bfloat16)
        .reshape(streams, count, INNER)
    )
    outputs = jnp.einsum("gre,ed->grd", normed, w_out, preferred_element_type=jnp.float32).astype(
        jnp.bfloat16
    )

    embedded = jnp.take(emb_full, tokens, axis=0)
    returned = outputs[windows:, ::-1, ::-1]
    hidden_out = (
        embedded.astype(jnp.float32)
        + outputs[:windows].astype(jnp.float32)
        + returned.astype(jnp.float32)
    ).astype(jnp.bfloat16)
    final_normed = rms_gain(hidden_out.astype(jnp.float32), final_gain).astype(jnp.bfloat16)
    head_full = jnp.concatenate([w_head_half, w_head_half[::-1, ::-1]], axis=1)
    logits = jnp.einsum("grd,db->grb", final_normed, head_full, preferred_element_type=jnp.float32)
    log_q = logits - jnp.log(jnp.sum(jnp.exp(logits), axis=-1, keepdims=True))
    top_value = jnp.max(teacher_vals, axis=1, keepdims=True)
    shifted = teacher_vals - top_value
    log_p = shifted - jnp.log(jnp.sum(jnp.exp(shifted), axis=1, keepdims=True))
    matches = teacher_top[..., None] == jnp.arange(4, dtype=jnp.int32)
    picked = jnp.sum(jnp.where(matches, log_q[:, None, :, :], 0.0), axis=-1)
    divergence = jnp.sum(jnp.exp(log_p) * (log_p - picked), axis=1)
    return (hidden_out, divergence)


def solution(mesh):
    placed = (
        P("grp", "seq"),
        P(),
        P(),
        P(),
        P(),
        P(),
        P(),
        P(),
        P(),
        P(),
        P(),
        P(),
        P(),
        P(),
        P(),
        P("grp", None, "seq"),
        P("grp", None, "seq"),
    )
    return jax.shard_map(
        local,
        mesh=mesh,
        in_specs=placed,
        out_specs=(P("grp", "seq", None), P("grp", "seq")),
        check_vma=False,
    )
```

profile of v0, /device:TPU:0, one launch (start us, length us, event | category | flops | bytes accessed | tf_op | source)
XLA Modules:
  0.0 97.0 jit_solution(750776242244539998)
XLA Ops:
  1.2 0.8 rev.17
  2.0 0.6 iota_compare_fusion.5
  2.6 0.7 fusion.100
  3.3 1.2 %compare_and_fusion.2 = pred[2,128]{1,0:T(4,128)(4,1)} fusion(s32[2,128]{1,0:T(2,128)} %param.18), kind=kLoop, calls=%fused_computation.180 | loop fusion | flops 1536 | bytes 1280 | tf_op jit(solution)/shard_map/jit(_take)/and | solution.py:235
  4.5 1.6 %rev.15 = bf16[2,512]{1,0:T(2,128)(2,1)S(1)} reverse(bf16[2,512]{1,0:T(2,128)(2,1)} %param.19), dimensions={0,1} | reverse | bytes 4096 | tf_op jit(solution)/shard_map/rev | solution.py:150
  6.1 0.8 fusion.89
  6.9 1.5 %convolution_convert_fusion.2 = bf16[4,1024]{1,0:T(4,128)(2,1)S(1)} fusion(bf16[512,1024]{1,0:T(8,128)(2,1)} %param.22, bf16[4,512]{1,0:T(4,128)(2,1)S(1)} %get-tuple-element.21, f32[512]{0:T(512)} %param.20, f32[4]{0:T(128)S(1)} %add_rsqrt_fusion.2), kind=kOutput, calls=%fused_computation.89 | convolution fusion | flops 4206592 | bytes 1062928 | tf_op jit(solution)/shard_map/dot_general | solution.py:75
  8.5 1.0 %fusion.32 = f32[4,1152]{1,0:T(4,128)S(1)} fusion(bf16[512,1152]{1,0:T(8,128)(2,1)S(1)} %copy-done, bf16[4,512]{1,0:T(4,128)(2,1)S(1)} %get-tuple-element.21, f32[512]{0:T(512)} %param.20, f32[4]{0:T(128)S(1)} %add_rsqrt_fusion.2), kind=kOutput, calls=%fused_computation.45 | convolution fusion | flops 4736000 | bytes 1204240 | tf_op jit(solution)/shard_map/dot_general | solution.py:74
  9.5 0.7 broadcast_multiply_fusion.1
  11.2 1.6 %divide_multiply_fusion = f32[344,1152]{1,0:T(8,128)S(1)} fusion(f32[16,1152]{1,0:T(8,128)S(1)} %mul.249, f32[344,16]{1,0:T(8,128)S(1)} %copy-done.31, f32[1152]{0:T(1024)S(1)} %copy-done.27), kind=kOutput, calls=%fused_computation.83 | convolution fusion | flops 78068736 | bytes 1685504 | tf_op jit(solution)/shard_map/dot_general | solution.py:78
  12.9 2.8 %collective-permute-start.1 = (s32[2,256]{1,0:T(2,128)S(1)}, s32[2,256]{1,0:T(2,128)S(1)}, u32[]{:S(2)}, u32[]{:S(2)}) collective-permute-start(s32[2,256]{1,0:T(2,128)S(1)} %add_select_fusion.5), channel_id=1, source_target_pairs={{0,2},{1,3},{2,0},{3,1},{4,6},{5,7},{6,4},{7,5},{8,10},{9,11},{10,... | collective-permute-start | bytes 6152 | tf_op jit(solution)/shard_map/ppermute | solution.py:104
  15.6 1.6 %collective-permute-done.1 = s32[2,256]{1,0:T(2,128)S(1)} collective-permute-done((s32[2,256]{1,0:T(2,128)S(1)}, s32[2,256]{1,0:T(2,128)S(1)}, u32[]{:S(2)}, u32[]{:S(2)}) %collective-permute-start.1) | collective-permute-done | bytes 2080 | tf_op jit(solution)/shard_map/ppermute | solution.py:104
  17.2 2.1 %collective-permute-start.2 = (s32[2,512]{1,0:T(2,128)S(1)}, s32[2,512]{1,0:T(2,128)S(1)}, u32[]{:S(2)}, u32[]{:S(2)}) collective-permute-start(s32[2,512]{1,0:T(2,128)S(1)} %add_select_fusion.4), channel_id=1, source_target_pairs={{0,4},{1,5},{2,6},{3,7},{4,0},{5,1},{6,2},{7,3},{8,12},{9,13},{10,... | collective-permute-start | bytes 12296 | tf_op jit(solution)/shard_map/ppermute | solution.py:104
  19.9 2.8 %gather_fusion.2 = bf16[512,1024]{1,0:T(8,128)(2,1)} fusion(bf16[4,1024]{1,0:T(4,128)(2,1)S(1)} %convolution_convert_fusion.2, s32[1024]{0:T(1024)S(1)} %pad_clamp_fusion), kind=kCustom, calls=%fused_computation.2 | custom fusion | bytes 2099200 | tf_op jit(solution)/shard_map/jit(_take)/gather | solution.py:212
  22.7 4.0 %reshape.544 = bf16[4,128,16,64]{3,2,1,0:T(8,128)(2,1)} reshape(bf16[512,1024]{1,0:T(8,128)(2,1)} %gather_fusion.2) | data formatting | bytes 2097152 | tf_op jit(solution)/shard_map/jit(_take)/gather | solution.py:212
  26.7 3.6 %copy.50 = bf16[4,128,16,64]{1,3,2,0:T(8,128)(2,1)} copy(bf16[4,128,16,64]{3,2,1,0:T(8,128)(2,1)} %reshape.544) | data formatting | bytes 2097152 | tf_op jit(solution)/shard_map/jit(_take)/gather | solution.py:212
  30.3 1.1 %copy.46 = bf16[344,1024]{0,1:T(8,128)(2,1)} copy(bf16[344,1024]{1,0:T(8,128)(2,1)S(1)} %slice.132) | data formatting | bytes 1409024 | tf_op jit(solution)/shard_map/slice | solution.py:154
  31.6 1.3 %copy.48 = bf16[4,128,1024]{1,2,0:T(8,128)(2,1)} copy(bf16[4,128,1024]{2,1,0:T(8,128)(2,1)S(1)} %bitcast.111) | data formatting | bytes 2097152 | tf_op jit(solution)/shard_map/jit(_take)/gather | solution.py:212
  33.0 0.7 mul.270
  33.7 1.9 %gather_fusion = bf16[256,512]{1,0:T(8,128)(2,1)} fusion(bf16[4,512]{1,0:T(4,128)(2,1)S(1)} %get-tuple-element.21, s32[1024]{0:T(1024)S(1)} %pad_clamp_fusion.2), kind=kCustom, calls=%fused_computation | custom fusion | bytes 525312 | tf_op jit(solution)/shard_map/jit(_take)/gather | solution.py:235
  35.5 1.3 %rev.19 = bf16[512,2]{0,1:T(2,128)(2,1)} reverse(bf16[512,2]{0,1:T(2,128)(2,1)S(1)} %copy-done.18), dimensions={0,1} | reverse | bytes 4096 | tf_op jit(solution)/shard_map/rev | solution.py:243
  36.9 2.7 %collective-permute-start.3 = (s32[2,1024]{1,0:T(2,128)S(1)}, s32[2,1024]{1,0:T(2,128)S(1)}, u32[]{:S(2)}, u32[]{:S(2)}) collective-permute-start(s32[2,1024]{1,0:T(2,128)S(1)} %add_select_fusion.2), channel_id=1, source_target_pairs={{0,8},{1,9},{2,10},{3,11},{4,12},{5,13},{6,14},{7,15},{8,0},{9,1},... | collective-permute-start | bytes 24584 | tf_op jit(solution)/shard_map/ppermute | solution.py:104
  39.6 1.9 %collective-permute-done.3 = s32[2,1024]{1,0:T(2,128)S(1)} collective-permute-done((s32[2,1024]{1,0:T(2,128)S(1)}, s32[2,1024]{1,0:T(2,128)S(1)}, u32[]{:S(2)}, u32[]{:S(2)}) %collective-permute-start.3) | collective-permute-done | bytes 8224 | tf_op jit(solution)/shard_map/ppermute | solution.py:104
  41.5 1.5 %rev.16 = s32[2,2048]{1,0:T(2,128)S(1)} reverse(s32[2,2048]{1,0:T(2,128)S(1)} %add_select_fusion), dimensions={1} | reverse | bytes 32768 | tf_op jit(solution)/shard_map/rev | solution.py:158
  44.1 4.9 %fusion.9 = f32[4,16,128,16]{3,1,2,0:T(8,128)S(1)} fusion(f32[16]{0:T(128)S(1)} %copy-done.17, f32[16]{0:T(128)S(1)} %get-tuple-element.49, f32[16]{0:T(128)S(1)} %get-tuple-element.50, f32[16]{0:T(128)S(1)} %get-tuple-element.51, f32[16]{0:T(128)S(1)} %get-tuple-element.48, f32[16]{0:T(128)S(1)} %exponential_negate_fusion, ...), kind=kOutput, calls=%fused_computation.16 | output fusion | flops 18612224 | bytes 557440 | tf_op jit(solution)/shard_map/jit(cumsum)/reduce_window_sum | solution.py:171
  49.0 2.5 %subtract_exponential_fusion = f32[4,16,128,16]{3,1,2,0:T(8,128)} fusion(f32[4,16,128,16]{3,1,2,0:T(8,128)S(1)} %fusion.9, f32[4,16,16]{2,1,0:T(8,128)S(1)} %slice_bitcast_fusion), kind=kLoop, calls=%fused_computation.17 | loop fusion | flops 131072 | bytes 1052672 | tf_op jit(solution)/shard_map/exp | solution.py:173
  52.2 3.4 %copy.43 = f32[4,16,128,16]{2,1,3,0:T(8,128)S(1)} copy(f32[4,16,128,16]{3,1,2,0:T(8,128)} %subtract_exponential_fusion) | data formatting | bytes 1048576 | tf_op jit(solution)/shard_map/exp | solution.py:173
  55.7 1.6 %broadcast_multiply_fusion = (f32[4,2048,16]{1,2,0:T(8,128)}, f32[4,2048,16]{1,2,0:T(8,128)}) fusion(f32[16]{0:T(128)S(1)} %exponential_negate_fusion, f32[16]{0:T(128)S(1)} %copy-done.17, f32[16]{0:T(128)S(1)} %get-tuple-element.49, pred[4,2048]{1,0:T(4,128)(4,1)S(1)} %get-tuple-element.42, f32[16]{0:T(128)S(1)} %get-tuple-element.50, ...), kind=kLoop, calls=%fused_computation.106 | loop fusion | flops 1966080 | bytes 1081728 | tf_op jit(solution)/shard_map/mul | solution.py:162
  57.3 2.6 %fusion.2 = f32[4,16,344]{2,1,0:T(8,128)S(1)} fusion(s32[4,2048]{1,0:T(4,128)S(1)} %select_select_fusion, f32[4,2048,16]{1,2,0:T(8,128)S(1)} %mul.262, f32[4,2048,16]{1,2,0:T(8,128)S(1)} %exp.69, f32[16]{0:T(128)S(1)} %copy-done.17, f32[16]{0:T(128)S(1)} %get-tuple-element.49, f32[16]{0:T(128)S(1)} %get-tuple-element.50, f32[16]{0:T(128)S(1)} %get-tuple-element.51, ...), kind=kOutput, calls=%fused_computation.7 | convolution fusion | flops 95617024 | bytes 1202496 | tf_op jit(solution)/shard_map/rpg,rph->rgh/dot_general | solution.py:193
  60.0 2.6 %fusion.69 = f32[4,16,344]{2,1,0:T(8,128)S(1)} fusion(f32[4,16,344]{2,1,0:T(8,128)S(1)} %fusion.2, s32[4,2048]{1,0:T(4,128)S(1)} %select_select_fusion, f32[4,2048,16]{1,2,0:T(8,128)S(1)} %mul.262, f32[4,2048,16]{1,2,0:T(8,128)S(1)} %exp.69, f32[16]{0:T(128)S(1)} %copy-done.17, f32[16]{0:T(128)S(1)} %get-tuple-element.49, f32[16]{0:T(128)S(1)} %get-tuple-element.50, ...), kind=kOutput, calls=%fused_computation.88 | convolution fusion | flops 95245824 | bytes 1290560 | tf_op jit(solution)/shard_map/rpg,rph->rgh/dot_general | solution.py:191
  62.6 2.4 %fusion.7 = f32[16,4,64,64]{3,2,0,1:T(8,128)} fusion(bf16[16,344,64,1]{1,2,0,3:T(8,128)(2,1)S(1)} %bitcast.115, f32[344,64]{0,1:T(8,128)S(1)} %copy.45, f32[4,16,344]{2,1,0:T(8,128)S(1)} %fusion.69), kind=kOutput, calls=%fused_computation.14 | convolution fusion | flops 183173120 | bytes 1929216 | tf_op jit(solution)/shard_map/hgp,rhgn->rhpn/dot_general | solution.py:198
  65.0 2.4 %fusion.25 = f32[16,4,64,64]{3,2,0,1:T(8,128)} fusion(bf16[16,344,64,1]{1,2,0,3:T(8,128)(2,1)S(1)} %bitcast.116, f32[344,64]{0,1:T(8,128)S(1)} %copy.45, f32[4,16,344]{2,1,0:T(8,128)S(1)} %fusion.69), kind=kOutput, calls=%fused_computation.33 | convolution fusion | flops 187400192 | bytes 1929216 | tf_op jit(solution)/shard_map/hgp,rhgn->rhpn/dot_general | solution.py:200
  67.4 2.9 %gather_fusion.1 = f32[512,1152]{1,0:T(8,128)} fusion(f32[344,1152]{1,0:T(8,128)S(1)} %copy-done.2, s32[1024]{0:T(1024)S(1)} %pad_clamp_fusion.1), kind=kCustom, calls=%fused_computation.1 | custom fusion | bytes 4720640 | tf_op jit(solution)/shard_map/jit(_take)/gather | solution.py:207
  70.2 3.1 %copy.38 = f32[4,128,1152]{1,2,0:T(8,128)} copy(f32[4,128,1152]{2,1,0:T(8,128)} %bitcast.112) | data formatting | bytes 4718592 | tf_op jit(solution)/shard_map/jit(_take)/gather | solution.py:207
  73.3 1.8 %broadcast_select_fusion = f32[4,128,1152]{1,2,0:T(8,128)S(1)} fusion(f32[4,128,1152]{1,2,0:T(8,128)} %copy.38, pred[4,128]{1,0:T(4,128)(4,1)S(1)} %compare_and_fusion.1), kind=kLoop, calls=%fused_computation.87 | loop fusion | flops 589824 | bytes 4719104 | tf_op jit(solution)/shard_map/jit(_take)/select_n | solution.py:207
  75.2 1.1 %slice.131 = bf16[4,128,1024]{1,2,0:T(8,128)(2,1)} slice(f32[4,128,1152]{1,2,0:T(8,128)S(1)} %broadcast_select_fusion), slice={[0:4], [0:128], [0:1024]} | slice | bytes 2097152 | tf_op jit(solution)/shard_map/slice | solution.py:208
  76.3 1.3 %fusion.81 = f32[4,128,128]{2,1,0:T(8,128)} fusion(f32[4,128,1152]{1,2,0:T(8,128)S(1)} %broadcast_select_fusion), kind=kOutput, calls=%fused_computation.107 | convolution fusion | flops 50331648 | bytes 524288 | tf_op jit(solution)/shard_map/while/body/eval_jaxpr/gtn,gsn->gts/dot_general | solution.py:37
  77.7 0.6 constant_dynamic-slice_fusion.1
  78.3 0.6 maximum_bitcast_fusion
  78.9 3.1 %reduce_window_sum.23 = f32[4,16,128]{2,1,0:T(8,128)} reduce-window(f32[4,16,128]{2,1,0:T(8,128)} %maximum_bitcast_fusion, f32[]{:T(128)} %constant.188.clone.1), window={size=1x1x128 pad=0_0x0_0x127_0}, to_apply=%region_1.2 | reduce-window | flops 1040384 | bytes 65540 | tf_op jit(solution)/shard_map/while/body/eval_jaxpr/jit(cumsum)/reduce_window_sum | solution.py:35
  82.1 0.8 exponential_bitcast_fusion
  82.8 0.7 maximum_bitcast_fusion.1
  83.6 4.4 %fusion.33 = f32[4,16,64,128]{3,2,1,0:T(8,128)S(1)} fusion(bf16[4,128,16,64]{1,3,2,0:T(8,128)(2,1)} %bitcast.114, f32[4,16,128]{2,1,0:T(8,128)S(1)} %maximum_bitcast_fusion.1, f32[4,16,128]{2,1,0:T(8,128)} %reduce_window_sum.23, f32[4,128,128]{2,1,0:T(8,128)} %fusion.81, pred[128,128]{1,0:T(8,128)(4,1)} %iota_compare_fusion.5), kind=kOutput, calls=%fused_computation.46 | convolution fusion | flops 140509184 | bytes 3489792 | tf_op jit(solution)/shard_map/while/body/eval_jaxpr/ghts,gshp->gthp/dot_general | solution.py:42
  88.1 4.3 %fusion.61 = (f32[4,128,16]{1,2,0:T(8,128)S(1)}, f32[4,128,16,64]{1,3,2,0:T(8,128)S(1)}) fusion(bf16[4,128,16,64]{1,3,2,0:T(8,128)(2,1)S(1)} %copy-done.7, f32[16]{0:T(128)S(1)} %copy-done.25, pred[4,128]{1,0:T(4,128)(4,1)S(1)} %copy-done.22, bf16[4,128,1024]{1,2,0:T(8,128)(2,1)S(1)} %copy-done.10, f32[4,128,16]{1,2,0:T(8,128)S(1)} %exponential_bitcast_fusion, ...), kind=kOutput, calls=%fused_computation.77 | convolution fusion | flops 410247168 | bytes 10683392 | tf_op jit(solution)/shard_map/while/body/eval_jaxpr/gtn,ghpn->gthp/dot_general | solution.py:44
  92.5 1.4 %fusion.60 = bf16[4,128,1024]{1,2,0:T(8,128)(2,1)S(1)} fusion(f32[4,128,16,64]{1,3,2,0:T(8,128)S(1)} %get-tuple-element.55, f32[1024]{0:T(1024)S(1)} %copy-done.16, f32[4,128,16]{1,2,0:T(8,128)S(1)} %add_rsqrt_fusion, bf16[4,128,1024]{1,2,0:T(8,128)(2,1)S(1)} %copy-done.4, f32[1024]{0:T(1024)S(1)} %copy-done.14, pred[4,128]{1,0:T(4,128)(4,1)S(1)} %copy-done.22, ...), kind=kLoop, calls=%fused_computation.76 | loop fusion | flops 6815744 | bytes 5284352 | tf_op jit(solution)/shard_map/convert_element_type | solution.py:228
  94.0 0.7 convolution_convert_fusion.1
  94.8 0.9 rev.18
  96.4 0.6 multiply_reduce_fusion
  (140 shorter events, 5.0 us)
Async XLA Ops:
  0.6 7.8 %copy-start = (bf16[512,1152]{1,0:T(8,128)(2,1)S(1)}, bf16[512,1152]{1,0:T(8,128)(2,1)}, u32[]{:S(2)}) copy-start(bf16[512,1152]{1,0:T(8,128)(2,1)} %param.21) | copy-start | bytes 3538948
  0.6 10.5 %copy-start.31 = (f32[344,16]{1,0:T(8,128)S(1)}, f32[344,16]{1,0:T(8,128)}, u32[]{:S(2)}) copy-start(f32[344,16]{1,0:T(8,128)} %constant.196.clone) | copy-start | bytes 66052
  0.7 10.5 %copy-start.13 = (s32[2,128]{1,0:T(2,128)S(1)}, s32[2,128]{1,0:T(2,128)}, u32[]{:S(2)}) copy-start(s32[2,128]{1,0:T(2,128)} %param.18) | copy-start | bytes 3076
  0.7 9.6 %copy-start.15 = (f32[512]{0:T(512)S(1)}, f32[512]{0:T(512)}, u32[]{:S(2)}) copy-start(f32[512]{0:T(512)} %param.20) | copy-start | bytes 6148
  0.7 9.6 %copy-start.30 = (f32[16]{0:T(128)S(1)}, f32[16]{0:T(128)}, u32[]{:S(2)}) copy-start(f32[16]{0:T(128)} %param.27) | copy-start | bytes 196
  0.7 9.6 %copy-start.26 = (bf16[512,16]{0,1:T(8,128)(2,1)S(1)}, bf16[512,16]{0,1:T(8,128)(2,1)}, u32[]{:S(2)}) copy-start(bf16[512,16]{0,1:T(8,128)(2,1)} %param.23) | copy-start | bytes 49156
  0.7 9.9 %copy-start.28 = (f32[2,2,128]{2,1,0:T(2,128)S(1)}, f32[2,2,128]{2,1,0:T(2,128)}, u32[]{:S(2)}) copy-start(f32[2,2,128]{2,1,0:T(2,128)} %param.34) | copy-start | bytes 6148
  0.7 10.5 %copy-start.27 = (f32[1152]{0:T(1024)S(1)}, f32[1152]{0:T(1024)}, u32[]{:S(2)}) copy-start(f32[1152]{0:T(1024)} %param.25) | copy-start | bytes 13828
  0.7 12.1 %collective-permute-start = (s32[2,128]{1,0:T(2,128)}, s32[2,128]{1,0:T(2,128)S(1)}, u32[]{:S(2)}, u32[]{:S(2)}) collective-permute-start(s32[2,128]{1,0:T(2,128)} %param.18), channel_id=1, source_target_pairs={{0,1},{1,0},{2,3},{3,2},{4,5},{5,4},{6,7},{7,6},{8,9},{9,8},{10,11... | collective-permute-start | bytes 3080 | tf_op jit(solution)/shard_map/ppermute | solution.py:104
  12.8 9.9 %copy-start.1 = (f32[344,1152]{1,0:T(8,128)}, f32[344,1152]{1,0:T(8,128)S(1)}, u32[]{:S(2)}) copy-start(f32[344,1152]{1,0:T(8,128)S(1)} %divide_multiply_fusion) | copy-start | bytes 4755460
  12.9 4.3 %collective-permute-start.1 = (s32[2,256]{1,0:T(2,128)S(1)}, s32[2,256]{1,0:T(2,128)S(1)}, u32[]{:S(2)}, u32[]{:S(2)}) collective-permute-start(s32[2,256]{1,0:T(2,128)S(1)} %add_select_fusion.5), channel_id=1, source_target_pairs={{0,2},{1,3},{2,0},{3,1},{4,6},{5,7},{6,4},{7,5},{8,10},{9,11},{10,... | collective-permute-start | bytes 6152 | tf_op jit(solution)/shard_map/ppermute | solution.py:104
  17.2 19.7 %collective-permute-start.2 = (s32[2,512]{1,0:T(2,128)S(1)}, s32[2,512]{1,0:T(2,128)S(1)}, u32[]{:S(2)}, u32[]{:S(2)}) collective-permute-start(s32[2,512]{1,0:T(2,128)S(1)} %add_select_fusion.4), channel_id=1, source_target_pairs={{0,4},{1,5},{2,6},{3,7},{4,0},{5,1},{6,2},{7,3},{8,12},{9,13},{10,... | collective-permute-start | bytes 12296 | tf_op jit(solution)/shard_map/ppermute | solution.py:104
  26.7 4.8 %slice-start = ((f32[344,1152]{1,0:T(8,128)}), f32[344,64]{1,0:T(8,128)S(1)}, s32[]{:S(2)}) async-start(f32[344,1152]{1,0:T(8,128)} %copy-done.1), calls=%async_computation | async-start | bytes 352256 | tf_op jit(solution)/shard_map/slice | solution.py:155
  26.7 4.9 %copy-start.3 = (bf16[512,1024]{1,0:T(8,128)(2,1)S(1)}, bf16[512,1024]{1,0:T(8,128)(2,1)}, u32[]{:S(2)}) copy-start(bf16[512,1024]{1,0:T(8,128)(2,1)} %gather_fusion.2) | copy-start | bytes 3145732
  30.3 2.6 %copy-start.24 = (f32[16]{0:T(128)S(1)}, f32[16]{0:T(128)}, u32[]{:S(2)}) copy-start(f32[16]{0:T(128)} %param.28) | copy-start | bytes 196
  31.5 4.1 %copy-start.18 = (bf16[512,2]{0,1:T(2,128)(2,1)S(1)}, bf16[512,2]{0,1:T(2,128)(2,1)}, u32[]{:S(2)}) copy-start(bf16[512,2]{0,1:T(2,128)(2,1)} %param.32) | copy-start | bytes 6148
  31.6 12.5 %copy-start.17 = (f32[16]{0:T(128)S(1)}, f32[16]{0:T(128)}, u32[]{:S(2)}) copy-start(f32[16]{0:T(128)} %param.26) | copy-start | bytes 196
  36.9 4.6 %collective-permute-start.3 = (s32[2,1024]{1,0:T(2,128)S(1)}, s32[2,1024]{1,0:T(2,128)S(1)}, u32[]{:S(2)}, u32[]{:S(2)}) collective-permute-start(s32[2,1024]{1,0:T(2,128)S(1)} %add_select_fusion.2), channel_id=1, source_target_pairs={{0,8},{1,9},{2,10},{3,11},{4,12},{5,13},{6,14},{7,15},{8,0},{9,1},... | collective-permute-start | bytes 24584 | tf_op jit(solution)/shard_map/ppermute | solution.py:104
  60.0 2.6 %copy-start.11 = (bf16[344,1024]{0,1:T(8,128)(2,1)S(1)}, bf16[344,1024]{0,1:T(8,128)(2,1)}, u32[]{:S(2)}) copy-start(bf16[344,1024]{0,1:T(8,128)(2,1)} %copy.46) | copy-start | bytes 2113540
  65.0 2.4 %copy-start.2 = (f32[344,1152]{1,0:T(8,128)S(1)}, f32[344,1152]{1,0:T(8,128)}, u32[]{:S(2)}) copy-start(f32[344,1152]{1,0:T(8,128)} %copy-done.1) | copy-start | bytes 4755460
  75.2 2.4 %copy-start.6 = (f32[4,2048,16]{1,2,0:T(8,128)S(1)}, f32[4,2048,16]{1,2,0:T(8,128)}, u32[]{:S(2)}) copy-start(f32[4,2048,16]{1,2,0:T(8,128)} %get-tuple-element.35) | copy-start | bytes 1572868
  75.2 2.4 %copy-start.5 = (f32[4,2048,16]{1,2,0:T(8,128)S(1)}, f32[4,2048,16]{1,2,0:T(8,128)}, u32[]{:S(2)}) copy-start(f32[4,2048,16]{1,2,0:T(8,128)} %get-tuple-element.34) | copy-start | bytes 1572868
  83.5 4.5 %copy-start.7 = (bf16[4,128,16,64]{1,3,2,0:T(8,128)(2,1)S(1)}, bf16[4,128,16,64]{1,3,2,0:T(8,128)(2,1)}, u32[]{:S(2)}) copy-start(bf16[4,128,16,64]{1,3,2,0:T(8,128)(2,1)} %copy.50) | copy-start | bytes 3145732
  83.6 4.5 %copy-start.10 = (bf16[4,128,1024]{1,2,0:T(8,128)(2,1)S(1)}, bf16[4,128,1024]{1,2,0:T(8,128)(2,1)}, u32[]{:S(2)}) copy-start(bf16[4,128,1024]{1,2,0:T(8,128)(2,1)} %slice.131) | copy-start | bytes 3145732
  83.6 4.5 %copy-start.22 = (pred[4,128]{1,0:T(4,128)(4,1)S(1)}, pred[4,128]{1,0:T(4,128)(4,1)}, u32[]{:S(2)}) copy-start(pred[4,128]{1,0:T(4,128)(4,1)} %compare_and_fusion) | copy-start | bytes 1540
  83.6 4.5 %copy-start.25 = (f32[16]{0:T(128)S(1)}, f32[16]{0:T(128)}, u32[]{:S(2)}) copy-start(f32[16]{0:T(128)} %param.28) | copy-start | bytes 196
  83.6 4.5 %copy-start.33 = (f32[16,4,64,64]{3,2,0,1:T(8,128)S(1)}, f32[16,4,64,64]{3,2,0,1:T(8,128)}, u32[]{:S(2)}) copy-start(f32[16,4,64,64]{3,2,0,1:T(8,128)} %fusion.7) | copy-start | bytes 3145732
  83.6 4.5 %copy-start.34 = (f32[16,4,64,64]{3,2,0,1:T(8,128)S(1)}, f32[16,4,64,64]{3,2,0,1:T(8,128)}, u32[]{:S(2)}) copy-start(f32[16,4,64,64]{3,2,0,1:T(8,128)} %fusion.25) | copy-start | bytes 3145732
  88.1 4.4 %copy-start.4 = (bf16[4,128,1024]{1,2,0:T(8,128)(2,1)S(1)}, bf16[4,128,1024]{1,2,0:T(8,128)(2,1)}, u32[]{:S(2)}) copy-start(bf16[4,128,1024]{1,2,0:T(8,128)(2,1)} %copy.48) | copy-start | bytes 3145732
  88.1 4.4 %copy-start.14 = (f32[1024]{0:T(1024)S(1)}, f32[1024]{0:T(1024)}, u32[]{:S(2)}) copy-start(f32[1024]{0:T(1024)} %mul.270) | copy-start | bytes 12292
  88.1 4.4 %copy-start.16 = (f32[1024]{0:T(1024)S(1)}, f32[1024]{0:T(1024)}, u32[]{:S(2)}) copy-start(f32[1024]{0:T(1024)} %param.29) | copy-start | bytes 12292
  92.5 1.4 %copy-start.9 = (bf16[1024,512]{1,0:T(8,128)(2,1)S(1)}, bf16[1024,512]{1,0:T(8,128)(2,1)}, u32[]{:S(2)}) copy-start(bf16[1024,512]{1,0:T(8,128)(2,1)} %param.30) | copy-start | bytes 3145732
  94.0 1.8 %copy-start.8 = (bf16[256,512]{1,0:T(8,128)(2,1)S(1)}, bf16[256,512]{1,0:T(8,128)(2,1)}, u32[]{:S(2)}) copy-start(bf16[256,512]{1,0:T(8,128)(2,1)} %gather_fusion) | copy-start | bytes 786436
  94.0 1.8 %copy-start.23 = (pred[2,128]{1,0:T(4,128)(4,1)S(1)}, pred[2,128]{1,0:T(4,128)(4,1)}, u32[]{:S(2)}) copy-start(pred[2,128]{1,0:T(4,128)(4,1)} %compare_and_fusion.2) | copy-start | bytes 772
  94.0 2.1 %copy-start.19 = (bf16[512,2]{0,1:T(2,128)(2,1)S(1)}, bf16[512,2]{0,1:T(2,128)(2,1)}, u32[]{:S(2)}) copy-start(bf16[512,2]{0,1:T(2,128)(2,1)} %param.32) | copy-start | bytes 6148
  94.0 2.1 %copy-start.20 = (bf16[512,2]{0,1:T(2,128)(2,1)S(1)}, bf16[512,2]{0,1:T(2,128)(2,1)}, u32[]{:S(2)}) copy-start(bf16[512,2]{0,1:T(2,128)(2,1)} %rev.19) | copy-start | bytes 6148
  94.0 2.1 %copy-start.29 = (f32[512]{0:T(512)S(1)}, f32[512]{0:T(512)}, u32[]{:S(2)}) copy-start(f32[512]{0:T(512)} %param.31) | copy-start | bytes 6148
  94.0 2.4 %copy-start.21 = (s32[2,2,128]{2,1,0:T(2,128)S(1)}, s32[2,2,128]{2,1,0:T(2,128)}, u32[]{:S(2)}) copy-start(s32[2,2,128]{2,1,0:T(2,128)} %param.33) | copy-start | bytes 6148
  94.0 2.4 %copy-start.32 = (f32[2,2,128]{2,1,0:T(2,128)S(1)}, f32[2,2,128]{2,1,0:T(2,128)}, u32[]{:S(2)}) copy-start(f32[2,2,128]{2,1,0:T(2,128)} %fusion.70) | copy-start | bytes 6148
  96.0 1.0 %copy-start.12 = (bf16[2,128,512]{2,1,0:T(8,128)(2,1)}, bf16[2,128,512]{2,1,0:T(8,128)(2,1)S(1)}, u32[]{:S(2)}) copy-start(bf16[2,128,512]{2,1,0:T(8,128)(2,1)S(1)} %get-tuple-element.19) | copy-start | bytes 786436
where the time goes:
time: 97.7 us; the launch traced here: 97 us
  local copies, waits for them, and re-layouts  35.1 us (36%)
  matrix products  25.3 us (26%)
  other arithmetic  23.6 us (24%)
  starting transfers between devices  8 us (8%)
  waiting for transfers between devices  3.5 us (4%)
  between operations  1.48 us (2%)
    gather x4, local copies, waits for them, and re-layouts, local(): gate_z = jnp.take(z_rows, local_tok, axis=0)  11.8 us
    ppermute x4, starting transfers between devices, gather_all(): lax.ppermute(held, axis, [(src, src ^ mask) for src in range(count)])  8 us
    gather x2, local copies, waits for them, and re-layouts, local(): act = jnp.take(activated_tab, mine(gram), axis=0)  5.94 us
    another operation x1, other arithmetic, local(): cum = jnp.cumsum(log_decay.reshape(streams, nblk, BLK, HEADS), axis=2)  4.93 us
    dot_general x1, matrix products, ssd_block(): jnp.einsum('ghts,gshp->gthp', weights, x_blk, preferred_element_type=jnp....  4.43 us
    dot_general x1, matrix products, ssd_block(): jnp.einsum('gtn,ghpn->gthp', c_blk, carry_state, precision=HIGH)  4.35 us
    ppermute x4, waiting for transfers between devices, gather_all(): lax.ppermute(held, axis, [(src, src ^ mask) for src in range(count)])  3.5 us
    exp x2, local copies, waits for them, and re-layouts, local(): jnp.exp(blk_total[:, :, None, :] - cum)  3.48 us
  transfers between devices with their start and end apart: 4, of which 2 were waited for; matrix products, arithmetic and copies ran while one was open for 30% of the time, Pallas kernels for 0%

commit v1 on v0

--- a/solution.py
+++ b/solution.py
@@ -79,15 +79,13 @@
     return jax.nn.silu(conv_sum), z_rows, dt_rows
 
 
-def gram_ids(seq_tok):
-    streams, total = seq_tok.shape
-    padded = jnp.concatenate([jnp.zeros((streams, KW - 1), seq_tok.dtype), seq_tok], axis=1)
-    where_in = jnp.arange(total)[None, :]
-    code = jnp.zeros_like(seq_tok)
-    ids = jnp.zeros_like(seq_tok)
+def gram_ids(ext, where_in):
+    count = where_in.shape[1]
+    code = jnp.zeros_like(where_in)
+    ids = jnp.zeros_like(where_in)
     offset_of = 0
     for real in range(1, KW + 1):
-        code = code + padded[:, KW - real : KW - real + total] * BASES ** (real - 1)
+        code = code + ext[:, KW - real : KW - real + count] * BASES ** (real - 1)
         chosen = (where_in >= real - 1) if real == KW else (where_in == real - 1)
         ids = jnp.where(chosen, offset_of + code, ids)
         offset_of += BASES**real
@@ -112,13 +110,26 @@
     return held
 
 
-def base_lookup(rows, bases):
-    picked = jnp.zeros(bases.shape + rows.shape[1:], jnp.float32)
+def heads_lookup(rows, bases):
+    picked = jnp.zeros(bases.shape[:-1] + (rows.shape[1], bases.shape[-1]), jnp.float32)
     for base in range(BASES):
         picked = picked + jnp.where(
-            (bases == base)[..., None], rows[base].astype(jnp.float32), 0.0
+            (bases == base)[..., None, :], rows[base][:, None], 0.0
         )
     return picked
+
+
+def onehot(ids, size):
+    return (ids[..., None] == jnp.arange(size, dtype=ids.dtype)).astype(jnp.bfloat16)
+
+
+def split_bf16(values):
+    high = values.astype(jnp.bfloat16)
+    return high, (values - high.astype(jnp.float32)).astype(jnp.bfloat16)
+
+
+def block_cumsum(values, tri):
+    return jnp.einsum("...s,st->...t", values, tri, precision=HIGH)
 
 
 def local(
@@ -145,94 +156,115 @@
     place = lax.axis_index("seq")
     total = count * nseq
     nblk = total // BLK
+    nloc = count // BLK
     streams = 2 * windows
+    units = streams * nloc
+    tri = (jnp.arange(BLK)[:, None] <= jnp.arange(BLK)[None, :]).astype(jnp.float32)
 
     emb_full = jnp.concatenate([emb_half, emb_half[::-1, ::-1]], axis=0)
-    activated_tab, z_rows, dt_rows = gram_tables(
-        emb_full, norm_gain, w_xbc, w_z, w_dt, conv_w, conv_bias
-    )
-    x_tab = activated_tab[:, :INNER].astype(jnp.bfloat16)
-    b_tab = activated_tab[:, INNER : INNER + NS]
+    act_tab, z_rows, dt_rows = gram_tables(emb_full, norm_gain, w_xbc, w_z, w_dt, conv_w, conv_bias)
+    x_tab = act_tab[:, :INNER].astype(jnp.bfloat16)
+    b_tab = act_tab[:, INNER : INNER + NS]
+    bc_tab = act_tab[:, INNER:]
+    x_heads = x_tab.reshape(GRAMS, HEADS, HD).transpose(1, 0, 2)
+    neg_rate = -jnp.exp(a_log)[:, None]
+
+    rc_tok = (BASES - 1) - tokens[:, ::-1]
+    fwd_rim = lax.ppermute(
+        tokens[:, count - (KW - 1) :], "seq", [(src, src + 1) for src in range(nseq - 1)]
+    )
+    rc_rim = lax.ppermute(
+        rc_tok[:, count - (KW - 1) :], "seq", [(src, src - 1) for src in range(1, nseq)]
+    )
+    local_tok = jnp.concatenate([tokens, rc_tok], axis=0)
+    ext = jnp.concatenate([jnp.concatenate([fwd_rim, rc_rim], axis=0), local_tok], axis=1)
+    pos0 = jnp.concatenate(
+        [jnp.full((windows, 1), place * count), jnp.full((windows, 1), (nseq - 1 - place) * count)]
+    ).astype(jnp.int32)
+    local_gram = gram_ids(ext, pos0 + jnp.arange(count, dtype=jnp.int32)[None, :])
+
+    oh_loc = onehot(local_gram, GRAMS)
+    x_loc = jnp.einsum("rtg,gc->rtc", oh_loc, x_tab, preferred_element_type=jnp.float32).astype(
+        jnp.bfloat16
+    )
+    bc_loc = jnp.einsum("rtg,gc->rtc", oh_loc, bc_tab, precision=HIGH)
+    oh_tok = onehot(local_tok, BASES)
+    z_loc = jnp.einsum("rtk,kc->rtc", oh_tok, z_rows, preferred_element_type=jnp.float32)
+    dt_loc = jax.nn.softplus(heads_lookup(dt_rows, local_tok) + dt_bias[:, None])
+    ld_loc = neg_rate * dt_loc
+
+    def per_unit(values, axis):
+        shape = values.shape
+        split = shape[:axis] + (nloc, BLK) + shape[axis + 1 :]
+        moved = jnp.moveaxis(values.reshape(split), axis, 1)
+        return moved.reshape((units,) + moved.shape[2:])
+
+    x_u = per_unit(x_loc, 1).reshape(units, BLK, HEADS, HD)
+    b_u = per_unit(bc_loc[..., :NS], 1)
+    c_u = per_unit(bc_loc[..., NS:], 1)
+    dt_u = per_unit(dt_loc, 2)
+    cum_u = block_cumsum(per_unit(ld_loc, 2), tri)
+
+    scores = jnp.einsum("utn,usn->uts", c_u, b_u, precision=HIGH)
+    seg_diff = cum_u[:, :, :, None] - cum_u[:, :, None, :]
+    lower = tri.T > 0
+    decays = jnp.where(lower, jnp.exp(jnp.where(lower, seg_diff, 0.0)), 0.0)
+    weights = (scores[:, None] * decays * dt_u[:, :, None, :]).astype(jnp.bfloat16)
+    y_intra = jnp.einsum("uhts,ushp->uthp", weights, x_u, preferred_element_type=jnp.float32)
 
     every = gather_all(tokens, "seq")
     seq_tok = jnp.concatenate([every, (BASES - 1) - every[:, ::-1]], axis=0)
-    gram = gram_ids(seq_tok)
-
-    step_dt = jax.nn.softplus(base_lookup(dt_rows, seq_tok) + dt_bias)
-    log_decay = -jnp.exp(a_log) * step_dt
-
-    fwd_start = place * count
-    rc_start = (nseq - 1 - place) * count
-    start = jnp.concatenate(
-        [jnp.full((windows,), fwd_start), jnp.full((windows,), rc_start)]
-    )
-    first_blk = start // BLK
-
-    cum = jnp.cumsum(log_decay.reshape(streams, nblk, BLK, HEADS), axis=2)
-    blk_total = cum[:, :, -1, :]
-    within = jnp.exp(blk_total[:, :, None, :] - cum) * step_dt.reshape(
-        streams, nblk, BLK, HEADS
+    ext_all = jnp.concatenate([jnp.zeros((streams, KW - 1), seq_tok.dtype), seq_tok], axis=1)
+    gram = gram_ids(ext_all, jnp.broadcast_to(jnp.arange(total, dtype=jnp.int32), (streams, total)))
+    dt_all = jax.nn.softplus(heads_lookup(dt_rows, seq_tok) + dt_bias[:, None])
+    ld_all = neg_rate * dt_all
+    cum = block_cumsum(ld_all.reshape(streams, HEADS, nblk, BLK), tri)
+    blk_total = cum[..., -1]
+    within = jnp.exp(blk_total[..., None] - cum) * dt_all.reshape(streams, HEADS, nblk, BLK)
+
+    first_blk = (
+        jnp.repeat(pos0[:, 0] // BLK, nloc) + jnp.tile(jnp.arange(nloc, dtype=jnp.int32), streams)
     )
     blk_idx = jnp.arange(nblk)
-    between = (blk_idx[None, :, None] < blk_idx[None, None, :]) & (
+    total_u = jnp.repeat(blk_total, nloc, axis=0)
+    between = (blk_idx[:, None] < blk_idx[None, :])[None] & (
         blk_idx[None, None, :] < first_blk[:, None, None]
     )
-    span = jnp.sum(
-        jnp.where(between[..., None], blk_total[:, None, :, :], 0.0), axis=2
-    )
-    across = jnp.where(
-        (blk_idx[None, :] < first_blk[:, None])[..., None], jnp.exp(span), 0.0
-    )
-    weight = (within * across[:, :, None, :]).reshape(streams, total, HEADS)
-
-    onehot = (gram[..., None] == jnp.arange(GRAMS, dtype=gram.dtype)).astype(jnp.bfloat16)
-    weight_hi = weight.astype(jnp.bfloat16)
-    weight_lo = (weight - weight_hi.astype(jnp.float32)).astype(jnp.bfloat16)
+    span = jnp.sum(jnp.where(between[:, None], total_u[:, :, None, :], 0.0), axis=3)
+    across = jnp.where(blk_idx[None, None, :] < first_blk[:, None, None], jnp.exp(span), 0.0)
+    weight = (jnp.repeat(within, nloc, axis=0) * across[..., None]).reshape(units, HEADS, total)
+    w_hi, w_lo = split_bf16(weight)
+    oh_all = jnp.repeat(onehot(gram, GRAMS), nloc, axis=0)
     per_gram = jnp.einsum(
-        "rpg,rph->rgh", onehot, weight_hi, preferred_element_type=jnp.float32
-    ) + jnp.einsum("rpg,rph->rgh", onehot, weight_lo, preferred_element_type=jnp.float32)
-    b_scaled = per_gram.transpose(0, 2, 1)[..., None] * b_tab[None, None]
-    b_hi = b_scaled.astype(jnp.bfloat16)
-    b_lo = (b_scaled - b_hi.astype(jnp.float32)).astype(jnp.bfloat16)
-    x_heads = x_tab.reshape(GRAMS, HEADS, HD).transpose(1, 0, 2)
+        "uhp,upg->uhg",
+        jnp.concatenate([w_hi, w_lo], axis=1),
+        oh_all,
+        preferred_element_type=jnp.float32,
+    )
+    per_gram = per_gram[:, :HEADS] + per_gram[:, HEADS:]
+    b_hi, b_lo = split_bf16(per_gram[..., None] * b_tab[None, None])
     start_state = jnp.einsum(
-        "hgp,rhgn->rhpn", x_heads, b_hi, preferred_element_type=jnp.float32
-    ) + jnp.einsum("hgp,rhgn->rhpn", x_heads, b_lo, preferred_element_type=jnp.float32)
-
-    def mine(values):
-        fwd = lax.dynamic_slice_in_dim(values[:windows], fwd_start, count, axis=1)
-        rc = lax.dynamic_slice_in_dim(values[windows:], rc_start, count, axis=1)
-        return jnp.concatenate([fwd, rc], axis=0)
-
-    act = jnp.take(activated_tab, mine(gram), axis=0)
-    x_act = act[..., :INNER].astype(jnp.bfloat16)
-    b_all = act[..., INNER : INNER + NS]
-    c_all = act[..., INNER + NS :]
-    local_tok = jnp.concatenate([tokens, (BASES - 1) - tokens[:, ::-1]], axis=0)
-    gate_z = jnp.take(z_rows, local_tok, axis=0)
-    blocks = (
-        to_blocks(x_act.reshape(streams, count, HEADS, HD), BLK),
-        to_blocks(b_all, BLK),
-        to_blocks(c_all, BLK),
-        jnp.swapaxes(to_blocks(mine(log_decay), BLK), 2, 3),
-        jnp.swapaxes(to_blocks(mine(step_dt), BLK), 2, 3),
-    )
-    _, y_blocks = lax.scan(ssd_block, start_state, blocks)
-    y_local = jnp.moveaxis(y_blocks, 0, 1).reshape(streams, count, HEADS, HD)
-    y_all = y_local + d_skip[:, None] * x_act.astype(jnp.float32).reshape(
-        streams, count, HEADS, HD
-    )
-    gated_y = y_all * jax.nn.silu(gate_z.astype(jnp.float32)).reshape(streams, count, HEADS, HD)
-    normed = (
-        rms_gain(gated_y, inner_gain.reshape(HEADS, HD))
-        .astype(jnp.bfloat16)
-        .reshape(streams, count, INNER)
+        "hgp,uhgn->uhpn", x_heads, b_hi, preferred_element_type=jnp.float32
+    ) + jnp.einsum("hgp,uhgn->uhpn", x_heads, b_lo, preferred_element_type=jnp.float32)
+
+    y_inter = (
+        jnp.einsum("utn,uhpn->uthp", c_u, start_state, precision=HIGH)
+        * jnp.exp(cum_u).transpose(0, 2, 1)[..., None]
+    )
+    y_u = y_intra + y_inter + d_skip[:, None] * x_u.astype(jnp.float32)
+    z_u = per_unit(z_loc, 1).reshape(units, BLK, HEADS, HD)
+    gated_y = y_u * jax.nn.silu(z_u)
+    normed = rms_gain(gated_y, inner_gain.reshape(HEADS, HD)).astype(jnp.bfloat16)
+    normed = jnp.moveaxis(normed.reshape(streams, nloc, BLK, INNER), 1, 1).reshape(
+        streams, count, INNER
     )
     outputs = jnp.einsum("gre,ed->grd", normed, w_out, preferred_element_type=jnp.float32).astype(
         jnp.bfloat16
     )
 
-    embedded = jnp.take(emb_full, tokens, axis=0)
+    embedded = jnp.einsum(
+        "grk,kd->grd", oh_tok[:windows], emb_full, preferred_element_type=jnp.float32
+    ).astype(jnp.bfloat16)
     returned = outputs[windows:, ::-1, ::-1]
     hidden_out = (
         embedded.astype(jnp.float32)

time: 97.7 us -> 80.2 us (0.82)
  local copies, waits for them, and re-layouts: 35.1 us -> 22.5 us
  other arithmetic: 23.6 us -> 16 us
  starting transfers between devices: 8 us -> 11.8 us
  waiting for transfers between devices: 3.5 us -> 0.7 us
  matrix products: 25.3 us -> 26.4 us
    gather x7 -> x0, local copies, waits for them, and re-layouts: 19.6 us -> none  [the longest x4 11.8 us: local(): gate_z = jnp.take(z_rows, local_tok, axis=0)]
    another operation x2 -> x0, other arithmetic: 8.07 us -> none  [the longest x1 4.93 us: local(): cum = jnp.cumsum(log_decay.reshape(streams, nblk, BLK, HEADS), axis=2)]
    unnamed x72 -> x94, local copies, waits for them, and re-layouts: 0.18 us -> 4.72 us
    ppermute x0 -> x2, starting transfers between devices: none -> 4.3 us  [the longest x1 3.02 us: local(): lax.ppermute(tokens[:, count - (KW - 1):], 'seq', [(src, src + 1) for src...]
    rev x1, local copies, waits for them, and re-layouts: 1.46 us -> 5.24 us  [local(): seq_tok = jnp.concatenate([every, BASES - 1 - every[:, ::-1]], axis=0)]
    exp x3 -> x1, local copies, waits for them, and re-layouts: 4.25 us -> 0.62 us  [local(): jnp.exp(cum_u).transpose(0, 2, 1)[..., None]]
    select_n x6, other arithmetic: 0.04 us -> 2.94 us  [gather_all(): jnp.where(upper, jnp.concatenate([other, held], axis=1), jnp.concatenate(...]
    ppermute x4, waiting for transfers between devices: 3.5 us -> 0.7 us  [gather_all(): lax.ppermute(held, axis, [(src, src ^ mask) for src in range(count)])]
  transfers between devices with their start and end apart: 4 -> 6, of which waited for: 2 -> 1; matrix products, arithmetic and copies ran while one was open for 30% -> 40% of each run, Pallas kernels for 0% -> 0%
where the time goes in v1:
time: 80.2 us; the launch traced here: 78.8 us
  matrix products  26.4 us (33%)
  local copies, waits for them, and re-layouts  22.5 us (28%)
  other arithmetic  16 us (20%)
  starting transfers between devices  11.8 us (15%)
  between operations  1.48 us (2%)
    ppermute x4, starting transfers between devices, gather_all(): lax.ppermute(held, axis, [(src, src ^ mask) for src in range(count)])  7.53 us
    rev x1, local copies, waits for them, and re-layouts, local(): seq_tok = jnp.concatenate([every, BASES - 1 - every[:, ::-1]], axis=0)  5.24 us
    unnamed x94, local copies, waits for them, and re-layouts  4.72 us
    dot_general x1, matrix products, local(): jnp.einsum('uhts,ushp->uthp', weights, x_u, preferred_element_type=jnp.fl...  4.48 us
    dot_general x1, matrix products, local(): jnp.einsum('utn,uhpn->uthp', c_u, start_state, precision=HIGH)  4.32 us
    ppermute x1, starting transfers between devices, local(): lax.ppermute(tokens[:, count - (KW - 1):], 'seq', [(src, src + 1) for src...  3.02 us
    select_n x6, other arithmetic, gather_all(): jnp.where(upper, jnp.concatenate([other, held], axis=1), jnp.concatenate(...  2.94 us
    dot_general x1, matrix products, gram_tables(): jnp.dot(jnp.asarray(gram_layout()), taps, precision=HIGH)  2.54 us
  transfers between devices with their start and end apart: 6, of which 1 were waited for; matrix products, arithmetic and copies ran while one was open for 40% of the time, Pallas kernels for 0%

profile of v1, /device:TPU:0, one launch (start us, length us, event | category | flops | bytes accessed | tf_op | source)
XLA Modules:
  0.0 78.8 jit_solution(2173096947424146130)
XLA Ops:
  1.2 0.8 rev.15
  2.0 1.3 %collective-permute-start.1 = (s32[2,3]{1,0:T(2,128)S(1)}, s32[2,3]{1,0:T(2,128)S(1)}, u32[]{:S(2)}, u32[]{:S(2)}) collective-permute-start(s32[2,3]{1,0:T(2,128)S(1)} %slice.76), channel_id=1, source_target_pairs={{1,0},{2,1},{3,2},{4,3},{5,4},{6,5},{7,6},{8,7},{9,8},{10,9},{11,1... | collective-permute-start | bytes 80 | tf_op jit(solution)/shard_map/ppermute | solution.py:176
  3.3 0.8 slice.75
  4.1 3.0 %collective-permute-start = (s32[2,3]{1,0:T(2,128)S(1)}, s32[2,3]{1,0:T(2,128)S(1)}, u32[]{:S(2)}, u32[]{:S(2)}) collective-permute-start(s32[2,3]{1,0:T(2,128)S(1)} %slice.75), channel_id=1, source_target_pairs={{0,1},{1,2},{2,3},{3,4},{4,5},{5,6},{6,7},{7,8},{8,9},{9,10},{10,1... | collective-permute-start | bytes 80 | tf_op jit(solution)/shard_map/ppermute | solution.py:173
  8.4 1.6 %rev.16 = bf16[2,512]{1,0:T(2,128)(2,1)S(1)} reverse(bf16[2,512]{1,0:T(2,128)(2,1)} %param.19), dimensions={0,1} | reverse | bytes 4096 | tf_op jit(solution)/shard_map/rev | solution.py:164
  9.9 0.8 %fusion.78 = f32[4]{0:T(128)S(1)} fusion(bf16[2,512]{1,0:T(2,128)(2,1)S(1)} %rev.16, bf16[2,512]{1,0:T(2,128)(2,1)} %param.19), kind=kLoop, calls=%fused_computation.119 | loop fusion | flops 12284 | bytes 4112 | tf_op jit(solution)/shard_map/reduce_sum | solution.py:23
  10.8 1.0 %fusion.13 = f32[4,1152]{1,0:T(4,128)S(1)} fusion(bf16[512,1152]{1,0:T(8,128)(2,1)S(1)} %copy-done, f32[512]{0:T(512)} %param.20, f32[4]{0:T(128)S(1)} %add_rsqrt_fusion.2, bf16[2,512]{1,0:T(2,128)(2,1)S(1)} %rev.16, bf16[2,512]{1,0:T(2,128)(2,1)} %param.19), kind=kOutput, calls=%fused_computation.18 | convolution fusion | flops 4742144 | bytes 1204240 | tf_op jit(solution)/shard_map/dot_general | solution.py:74
  11.8 0.7 broadcast_multiply_fusion
  12.6 2.5 %divide_multiply_fusion = f32[344,1152]{1,0:T(8,128)S(1)} fusion(f32[16,1152]{1,0:T(8,128)S(1)} %mul.214, f32[344,16]{1,0:T(8,128)} %constant.138.clone, f32[1152]{0:T(1024)} %param.25), kind=kOutput, calls=%fused_computation.34 | convolution fusion | flops 78068736 | bytes 1685504 | tf_op jit(solution)/shard_map/dot_general | solution.py:78
  15.3 1.0 %copy-done.1 = f32[344,1152]{1,0:T(8,128)} copy-done((f32[344,1152]{1,0:T(8,128)}, f32[344,1152]{1,0:T(8,128)S(1)}, u32[]{:S(2)}) %copy-start.1) | copy-done | bytes 1585176
  16.4 0.6 convert_compare_fusion
  17.4 1.2 %copy.32 = bf16[344,1024]{0,1:T(8,128)(2,1)} copy(bf16[344,1024]{1,0:T(8,128)(2,1)S(1)} %slice.153) | data formatting | bytes 1409024 | tf_op jit(solution)/shard_map/slice | solution.py:166
  18.6 0.8 copy.31
  19.3 0.7 compare_select_fusion.2
  20.9 0.6 exponential_bitcast_fusion
  21.5 0.7 mul.244
  22.2 1.4 %rev.19 = bf16[512,2]{0,1:T(2,128)(2,1)} reverse(bf16[512,2]{0,1:T(2,128)(2,1)S(1)} %copy-done.32), dimensions={0,1} | reverse | bytes 4096 | tf_op jit(solution)/shard_map/rev | solution.py:275
  24.9 0.6 pad_add_fusion.2
  25.6 2.1 %convolution_convert_fusion.1 = bf16[4,128,1024]{2,1,0:T(8,128)(2,1)S(1)} fusion(s32[4,128]{1,0:T(4,128)S(1)} %get-tuple-element.11, f32[344,1152]{1,0:T(8,128)} %copy-done.1), kind=kOutput, calls=%fused_computation.36 | convolution fusion | flops 361410560 | bytes 1755136 | tf_op jit(solution)/shard_map/rtg,gc->rtc/dot_general | solution.py:187
  27.7 1.3 %fusion.38 = f32[4,128,128]{1,2,0:T(8,128)S(1)} fusion(s32[4,128]{1,0:T(4,128)S(1)} %get-tuple-element.11, f32[344,1152]{1,0:T(8,128)} %copy-done.1), kind=kOutput, calls=%fused_computation.52 | convolution fusion | flops 270708736 | bytes 440320 | tf_op jit(solution)/shard_map/rtg,gc->rtc/dot_general | solution.py:190
  29.0 1.3 %fusion.65 = f32[4,128,128]{2,1,0:T(8,128)} fusion(f32[4,128,128]{1,2,0:T(8,128)S(1)} %fusion.38), kind=kOutput, calls=%fused_computation.85 | convolution fusion | flops 50331648 | bytes 524288 | tf_op jit(solution)/shard_map/utn,usn->uts/dot_general | solution.py:208
  30.3 0.7 copy.30
  31.0 2.7 %collective-permute-start.3 = (s32[2,256]{1,0:T(2,128)S(1)}, s32[2,256]{1,0:T(2,128)S(1)}, u32[]{:S(2)}, u32[]{:S(2)}) collective-permute-start(s32[2,256]{1,0:T(2,128)S(1)} %add_select_fusion.5), channel_id=1, source_target_pairs={{0,2},{1,3},{2,0},{3,1},{4,6},{5,7},{6,4},{7,5},{8,10},{9,11},{10,... | collective-permute-start | bytes 6152 | tf_op jit(solution)/shard_map/ppermute | solution.py:102
  33.7 4.5 %fusion.14 = f32[4,16,64,128]{3,2,1,0:T(8,128)} fusion(bf16[4,128,16,64]{1,3,2,0:T(8,128)(2,1)S(1)} %bitcast.94, f32[4,16,128]{2,1,0:T(8,128)} %compare_select_fusion.2, f32[4,16,128]{2,1,0:T(8,128)} %copy-done.11, f32[4,128,128]{2,1,0:T(8,128)} %fusion.65, pred[128,128]{1,0:T(8,128)(4,1)} %convert_compare_fusion), kind=kOutput, calls=%fused_computation.19 | convolution fusion | flops 140509184 | bytes 3489792 | tf_op jit(solution)/shard_map/uhts,ushp->uthp/dot_general | solution.py:213
  38.2 1.7 %collective-permute-start.4 = (s32[2,512]{1,0:T(2,128)S(1)}, s32[2,512]{1,0:T(2,128)S(1)}, u32[]{:S(2)}, u32[]{:S(2)}) collective-permute-start(s32[2,512]{1,0:T(2,128)S(1)} %add_select_fusion.4), channel_id=1, source_target_pairs={{0,4},{1,5},{2,6},{3,7},{4,0},{5,1},{6,2},{7,3},{8,12},{9,13},{10,... | collective-permute-start | bytes 12296 | tf_op jit(solution)/shard_map/ppermute | solution.py:102
  39.9 2.0 %fusion.39 = f32[4,128,1024]{1,2,0:T(8,128)S(1)} fusion(bf16[512,1024]{1,0:T(8,128)(2,1)} %param.22, s32[4,128]{1,0:T(4,128)} %get-tuple-element.10, f32[512]{0:T(512)} %param.20, f32[4]{0:T(128)} %copy-done.36, bf16[2,512]{1,0:T(2,128)(2,1)S(1)} %rev.16, bf16[2,512]{1,0:T(2,128)(2,1)S(1)} %copy-done.13), kind=kOutput, calls=%fused_computation.55 | convolution fusion | flops 8409088 | bytes 3153936 | tf_op jit(solution)/shard_map/rtk,kc->rtc/dot_general | solution.py:192
  42.5 2.7 %collective-permute-start.5 = (s32[2,1024]{1,0:T(2,128)S(1)}, s32[2,1024]{1,0:T(2,128)}, u32[]{:S(2)}, u32[]{:S(2)}) collective-permute-start(s32[2,1024]{1,0:T(2,128)S(1)} %add_select_fusion.2), channel_id=1, source_target_pairs={{0,8},{1,9},{2,10},{3,11},{4,12},{5,13},{6,14},{7,15},{8,0},{9,1},... | collective-permute-start | bytes 24584 | tf_op jit(solution)/shard_map/ppermute | solution.py:102
  45.1 1.4 %add_select_fusion.3 = s32[2,8,128]{2,1,0:T(8,128)} fusion(s32[2,4,128]{2,1,0:T(4,128)} %concatenate.128, s32[2,4,128]{2,1,0:T(4,128)S(1)} %concatenate.127, pred[]{:T(512)S(6)} %eq.160), kind=kLoop, calls=%fused_computation.124 | loop fusion | flops 6144 | bytes 16385 | tf_op jit(solution)/shard_map/jit(_where)/select_n | solution.py:104
  46.5 0.7 collective-permute-done.5
  47.2 1.3 %copy.46 = s32[1,2,8,128]{3,2,1,0:T(8,128)} copy(s32[1,2,8,128]{3,1,2,0:T(2,128)} %bitcast.29) | data formatting | bytes 16384
  48.5 0.8 %add_select_fusion.1 = s32[2,2048]{1,0:T(2,128)S(1)} fusion(s32[2,1024]{1,0:T(2,128)} %copy-done.12, s32[2,1024]{1,0:T(2,128)} %collective-permute-done.5, pred[]{:T(512)S(6)} %eq.159), kind=kLoop, calls=%fused_computation.110 | loop fusion | flops 12288 | bytes 32769 | tf_op jit(solution)/shard_map/jit(_where)/select_n | solution.py:104
  49.3 5.2 %rev.17 = s32[2,2048]{1,0:T(2,128)} reverse(s32[2,2048]{1,0:T(2,128)S(1)} %add_select_fusion.1), dimensions={1} | reverse | bytes 32768 | tf_op jit(solution)/shard_map/rev | solution.py:216
  54.6 1.3 %fusion.107 = (s32[1,2,16,128]{3,1,2,0:T(2,128)S(1)}, s32[2,2048]{1,0:T(2,128)}) fusion(s32[2,2048]{1,0:T(2,128)} %rev.17), kind=kLoop, calls=%fused_computation.190 | loop fusion | flops 4096 | bytes 49152
  55.9 0.8 add_select_fusion
  56.7 1.6 %fusion.46 = f32[4,16,16,128]{3,2,1,0:T(8,128)S(1)} fusion(f32[16]{0:T(128)} %param.26, f32[16]{0:T(128)} %copy-done.21, f32[16]{0:T(128)} %copy-done.23, f32[16]{0:T(128)} %copy-done.25, f32[16]{0:T(128)} %copy-done.19, f32[16]{0:T(128)} %copy-done.43, pred[4,16,128]{2,1,0:T(8,128)(4,1)S(1)} %get-tuple-element.7, ...), kind=kOutput, calls=%fused_computation.66 | convolution fusion | flops 203309056 | bytes 557440 | tf_op jit(solution)/shard_map/...s,st->...t/dot_general | solution.py:132
  59.0 1.4 %multiply_multiply_fusion = f32[4,16,16,128]{3,2,1,0:T(8,128)} fusion(f32[4,16,16,128]{3,2,1,0:T(8,128)S(1)} %fusion.46, f32[4,16,16]{2,1,0:T(8,128)S(1)} %exponential_select_fusion, f32[4,16,16]{2,1,0:T(8,128)S(1)} %slice_reduce_fusion, f32[16]{0:T(128)S(1)} %copy-done.29, f32[16]{0:T(128)S(1)} %copy-done.22, f32[16]{0:T(128)S(1)} %copy-done.24, ...), kind=kLoop, calls=%fused_computation.65 | loop fusion | flops 2228224 | bytes 1089856 | tf_op jit(solution)/shard_map/mul | solution.py:235
  60.4 1.9 %reshape.308 = f32[4,16,2048]{2,1,0:T(8,128)} reshape(f32[4,16,16,128]{3,2,1,0:T(8,128)} %multiply_multiply_fusion) | data formatting | bytes 1048576 | tf_op jit(solution)/shard_map/reshape | solution.py:235
  62.3 1.3 %subtract_convert_fusion = (bf16[4,16,2048]{2,1,0:T(8,128)(2,1)S(1)}, bf16[4,16,2048]{2,1,0:T(8,128)(2,1)S(1)}) fusion(f32[4,16,2048]{2,1,0:T(8,128)} %reshape.308), kind=kLoop, calls=%fused_computation.63 | loop fusion | flops 524288 | bytes 1048576 | tf_op jit(solution)/shard_map/convert_element_type | solution.py:128
  63.6 0.7 pad_add_fusion.1
  64.3 0.8 %select_select_fusion = s32[4,2048]{1,0:T(4,128)S(1)} fusion(s32[4,2048]{1,0:T(4,128)S(1)} %pad_add_fusion.1, pred[2048]{0:T(1024)(128)(4,1)} %get-tuple-element.26, pred[2048]{0:T(1024)(128)(4,1)} %get-tuple-element.27, pred[2048]{0:T(1024)(128)(4,1)} %get-tuple-element.28, pred[2048]{0:T(1024)(128)(4,1)} %get-tuple-element.29), kind=kLoop, calls=%fused_computation.103 | loop fusion | flops 106496 | bytes 73728 | tf_op jit(solution)/shard_map/jit(_where)/select_n | solution.py:90
  65.1 2.0 %fusion.2 = f32[4,32,344]{2,1,0:T(8,128)S(1)} fusion(s32[4,2048]{1,0:T(4,128)S(1)} %select_select_fusion, bf16[4,16,2048]{2,1,0:T(8,128)(2,1)S(1)} %get-tuple-element.2, bf16[4,16,2048]{2,1,0:T(8,128)(2,1)S(1)} %get-tuple-element.3), kind=kOutput, calls=%fused_computation.3 | convolution fusion | flops 184221696 | bytes 733184 | tf_op jit(solution)/shard_map/uhp,upg->uhg/dot_general | solution.py:238
  67.2 1.0 %fusion.6 = f32[16,4,64,64]{3,2,0,1:T(8,128)S(1)} fusion(bf16[16,344,64,1]{1,2,0,3:T(8,128)(2,1)S(1)} %bitcast.96, f32[344,64]{0,1:T(8,128)S(1)} %copy-done.6, f32[4,16,344]{2,1,0:T(8,128)S(1)} %slice_add_fusion), kind=kOutput, calls=%fused_computation.10 | convolution fusion | flops 187400192 | bytes 1929216 | tf_op jit(solution)/shard_map/hgp,uhgn->uhpn/dot_general | solution.py:248
  68.2 1.0 %fusion.5 = f32[16,4,64,64]{3,2,0,1:T(8,128)S(1)} fusion(bf16[16,344,64,1]{1,2,0,3:T(8,128)(2,1)S(1)} %bitcast.97, f32[344,64]{0,1:T(8,128)S(1)} %copy-done.6, f32[4,16,344]{2,1,0:T(8,128)S(1)} %slice_add_fusion), kind=kOutput, calls=%fused_computation.8 | convolution fusion | flops 183173120 | bytes 1929216 | tf_op jit(solution)/shard_map/hgp,uhgn->uhpn/dot_general | solution.py:246
  69.4 0.7 copy-done.45
  70.1 4.3 %multiply_reduce_fusion = (f32[4,128,16]{1,2,0:T(8,128)S(1)}, f32[4,128,16,64]{1,3,2,0:T(8,128)S(1)}) fusion(f32[4,128,16,64]{1,3,2,0:T(8,128)S(1)} %bitcast.93, bf16[4,128,16,64]{1,3,2,0:T(8,128)(2,1)S(1)} %bitcast.95, f32[16]{0:T(128)S(1)} %copy-done.41, f32[4,128,16]{1,2,0:T(8,128)S(1)} %copy-done.10, f32[16,4,64,64]{3,2,0,1:T(8,128)S(1)} %fusion.5, ...), kind=kOutput, calls=%fused_computation.26 | convolution fusion | flops 409198592 | bytes 11731456 | tf_op jit(solution)/shard_map/utn,uhpn->uthp/dot_general | solution.py:251
  75.0 0.7 copy-done.2
  75.7 0.7 convolution_convert_fusion.2
  76.5 0.9 %rev.18 = bf16[2,128,512]{2,1,0:T(8,128)(2,1)S(1)} reverse(bf16[2,128,512]{2,1,0:T(8,128)(2,1)S(1)} %slice.109), dimensions={1,2} | reverse | bytes 524288 | tf_op jit(solution)/shard_map/rev | solution.py:268
  (135 shorter events, 7.9 us)
Async XLA Ops:
  0.6 10.1 %copy-start = (bf16[512,1152]{1,0:T(8,128)(2,1)S(1)}, bf16[512,1152]{1,0:T(8,128)(2,1)}, u32[]{:S(2)}) copy-start(bf16[512,1152]{1,0:T(8,128)(2,1)} %param.21) | copy-start | bytes 3538948
  0.6 30.4 %collective-permute-start.2 = (s32[2,128]{1,0:T(2,128)}, s32[2,128]{1,0:T(2,128)S(1)}, u32[]{:S(2)}, u32[]{:S(2)}) collective-permute-start(s32[2,128]{1,0:T(2,128)} %param.18), channel_id=1, source_target_pairs={{0,1},{1,0},{2,3},{3,2},{4,5},{5,4},{6,7},{7,6},{8,9},{9,8},{10,11... | collective-permute-start | bytes 3080 | tf_op jit(solution)/shard_map/ppermute | solution.py:102
  2.0 22.8 %collective-permute-start.1 = (s32[2,3]{1,0:T(2,128)S(1)}, s32[2,3]{1,0:T(2,128)S(1)}, u32[]{:S(2)}, u32[]{:S(2)}) collective-permute-start(s32[2,3]{1,0:T(2,128)S(1)} %slice.76), channel_id=1, source_target_pairs={{1,0},{2,1},{3,2},{4,3},{5,4},{6,5},{7,6},{8,7},{9,8},{10,9},{11,1... | collective-permute-start | bytes 80 | tf_op jit(solution)/shard_map/ppermute | solution.py:176
  4.1 20.8 %collective-permute-start = (s32[2,3]{1,0:T(2,128)S(1)}, s32[2,3]{1,0:T(2,128)S(1)}, u32[]{:S(2)}, u32[]{:S(2)}) collective-permute-start(s32[2,3]{1,0:T(2,128)S(1)} %slice.75), channel_id=1, source_target_pairs={{0,1},{1,2},{2,3},{3,4},{4,5},{5,6},{6,7},{7,8},{8,9},{9,10},{10,1... | collective-permute-start | bytes 80 | tf_op jit(solution)/shard_map/ppermute | solution.py:173
  9.9 29.9 %copy-start.15 = (bf16[2,512]{1,0:T(2,128)(2,1)}, bf16[2,512]{1,0:T(2,128)(2,1)S(1)}, u32[]{:S(2)}) copy-start(bf16[2,512]{1,0:T(2,128)(2,1)S(1)} %rev.16) | copy-start | bytes 6148
  10.8 6.3 %copy-start.36 = (f32[4]{0:T(128)}, f32[4]{0:T(128)S(1)}, u32[]{:S(2)}) copy-start(f32[4]{0:T(128)S(1)} %add_rsqrt_fusion.2) | copy-start | bytes 52
  12.6 3.8 %copy-start.7 = (s32[2,128]{1,0:T(2,128)S(1)}, s32[2,128]{1,0:T(2,128)}, u32[]{:S(2)}) copy-start(s32[2,128]{1,0:T(2,128)} %param.18) | copy-start | bytes 3076
  12.6 4.5 %copy-start.13 = (bf16[2,512]{1,0:T(2,128)(2,1)S(1)}, bf16[2,512]{1,0:T(2,128)(2,1)}, u32[]{:S(2)}) copy-start(bf16[2,512]{1,0:T(2,128)(2,1)} %param.19) | copy-start | bytes 6148
  12.6 4.4 %copy-start.17 = (f32[512]{0:T(512)S(1)}, f32[512]{0:T(512)}, u32[]{:S(2)}) copy-start(f32[512]{0:T(512)} %param.20) | copy-start | bytes 6148
  12.6 4.4 %copy-start.37 = (bf16[512,16]{0,1:T(8,128)(2,1)S(1)}, bf16[512,16]{0,1:T(8,128)(2,1)}, u32[]{:S(2)}) copy-start(bf16[512,16]{0,1:T(8,128)(2,1)} %param.23) | copy-start | bytes 49156
  12.6 4.6 %copy-start.40 = (f32[16]{0:T(128)S(1)}, f32[16]{0:T(128)}, u32[]{:S(2)}) copy-start(f32[16]{0:T(128)} %param.27) | copy-start | bytes 196
  15.2 4.2 %copy-start.28 = (f32[16]{0:T(128)S(1)}, f32[16]{0:T(128)}, u32[]{:S(2)}) copy-start(f32[16]{0:T(128)} %param.26) | copy-start | bytes 196
  15.2 6.3 %copy-start.27 = (f32[1024]{0:T(1024)S(1)}, f32[1024]{0:T(1024)}, u32[]{:S(2)}) copy-start(f32[1024]{0:T(1024)} %param.29) | copy-start | bytes 12292
  15.2 7.0 %copy-start.32 = (bf16[512,2]{0,1:T(2,128)(2,1)S(1)}, bf16[512,2]{0,1:T(2,128)(2,1)}, u32[]{:S(2)}) copy-start(bf16[512,2]{0,1:T(2,128)(2,1)} %param.32) | copy-start | bytes 6148
  15.2 8.4 %copy-start.38 = (f32[2,2,128]{2,1,0:T(2,128)S(1)}, f32[2,2,128]{2,1,0:T(2,128)}, u32[]{:S(2)}) copy-start(f32[2,2,128]{2,1,0:T(2,128)} %param.34) | copy-start | bytes 6148
  17.2 8.3 %copy-start.19 = (f32[16]{0:T(128)}, f32[16]{0:T(128)S(1)}, u32[]{:S(2)}) copy-start(f32[16]{0:T(128)S(1)} %get-tuple-element.16) | copy-start | bytes 196
  17.2 8.3 %copy-start.21 = (f32[16]{0:T(128)}, f32[16]{0:T(128)S(1)}, u32[]{:S(2)}) copy-start(f32[16]{0:T(128)S(1)} %get-tuple-element.17) | copy-start | bytes 196
  17.2 8.3 %copy-start.23 = (f32[16]{0:T(128)}, f32[16]{0:T(128)S(1)}, u32[]{:S(2)}) copy-start(f32[16]{0:T(128)S(1)} %get-tuple-element.18) | copy-start | bytes 196
  17.3 8.3 %copy-start.25 = (f32[16]{0:T(128)}, f32[16]{0:T(128)S(1)}, u32[]{:S(2)}) copy-start(f32[16]{0:T(128)S(1)} %get-tuple-element.19) | copy-start | bytes 196
  17.3 8.3 %copy-start.43 = (f32[16]{0:T(128)}, f32[16]{0:T(128)S(1)}, u32[]{:S(2)}) copy-start(f32[16]{0:T(128)S(1)} %exponential_negate_fusion) | copy-start | bytes 196
  17.4 8.2 %copy-start.30 = (pred[4,16]{1,0:T(4,128)(4,1)}, pred[4,16]{1,0:T(4,128)(4,1)S(1)}, u32[]{:S(2)}) copy-start(pred[4,16]{1,0:T(4,128)(4,1)S(1)} %iota_compare_fusion.16) | copy-start | bytes 196
  31.0 7.2 %copy-start.3 = (bf16[4,128,1024]{1,2,0:T(8,128)(2,1)}, bf16[4,128,1024]{1,2,0:T(8,128)(2,1)S(1)}, u32[]{:S(2)}) copy-start(bf16[4,128,1024]{1,2,0:T(8,128)(2,1)S(1)} %copy.30) | copy-start | bytes 3145732
  31.0 7.2 %collective-permute-start.3 = (s32[2,256]{1,0:T(2,128)S(1)}, s32[2,256]{1,0:T(2,128)S(1)}, u32[]{:S(2)}, u32[]{:S(2)}) collective-permute-start(s32[2,256]{1,0:T(2,128)S(1)} %add_select_fusion.5), channel_id=1, source_target_pairs={{0,2},{1,3},{2,0},{3,1},{4,6},{5,7},{6,4},{7,5},{8,10},{9,11},{10,... | collective-permute-start | bytes 6152 | tf_op jit(solution)/shard_map/ppermute | solution.py:102
  38.2 4.2 %collective-permute-start.4 = (s32[2,512]{1,0:T(2,128)S(1)}, s32[2,512]{1,0:T(2,128)S(1)}, u32[]{:S(2)}, u32[]{:S(2)}) collective-permute-start(s32[2,512]{1,0:T(2,128)S(1)} %add_select_fusion.4), channel_id=1, source_target_pairs={{0,4},{1,5},{2,6},{3,7},{4,0},{5,1},{6,2},{7,3},{8,12},{9,13},{10,... | collective-permute-start | bytes 12296 | tf_op jit(solution)/shard_map/ppermute | solution.py:102
  42.4 4.7 %copy-start.12 = (s32[2,1024]{1,0:T(2,128)}, s32[2,1024]{1,0:T(2,128)S(1)}, u32[]{:S(2)}) copy-start(s32[2,1024]{1,0:T(2,128)S(1)} %add_select_fusion.2) | copy-start | bytes 24580
  42.5 4.7 %collective-permute-start.5 = (s32[2,1024]{1,0:T(2,128)S(1)}, s32[2,1024]{1,0:T(2,128)}, u32[]{:S(2)}, u32[]{:S(2)}) collective-permute-start(s32[2,1024]{1,0:T(2,128)S(1)} %add_select_fusion.2), channel_id=1, source_target_pairs={{0,8},{1,9},{2,10},{3,11},{4,12},{5,13},{6,14},{7,15},{8,0},{9,1},... | collective-permute-start | bytes 24584 | tf_op jit(solution)/shard_map/ppermute | solution.py:102
  54.5 4.2 %copy-start.9 = (pred[4,16,16]{2,1,0:T(8,128)(4,1)S(1)}, pred[4,16,16]{2,1,0:T(8,128)(4,1)}, u32[]{:S(2)}) copy-start(pred[4,16,16]{2,1,0:T(8,128)(4,1)} %broadcast_and_fusion) | copy-start | bytes 3076
  54.5 4.4 %copy-start.31 = (pred[4,16]{1,0:T(4,128)(4,1)S(1)}, pred[4,16]{1,0:T(4,128)(4,1)}, u32[]{:S(2)}) copy-start(pred[4,16]{1,0:T(4,128)(4,1)} %copy-done.30) | copy-start | bytes 196
  54.5 4.4 %copy-start.20 = (f32[16]{0:T(128)S(1)}, f32[16]{0:T(128)}, u32[]{:S(2)}) copy-start(f32[16]{0:T(128)} %copy-done.19) | copy-start | bytes 196
  54.5 4.4 %copy-start.22 = (f32[16]{0:T(128)S(1)}, f32[16]{0:T(128)}, u32[]{:S(2)}) copy-start(f32[16]{0:T(128)} %copy-done.21) | copy-start | bytes 196
  54.5 4.4 %copy-start.24 = (f32[16]{0:T(128)S(1)}, f32[16]{0:T(128)}, u32[]{:S(2)}) copy-start(f32[16]{0:T(128)} %copy-done.23) | copy-start | bytes 196
  54.5 4.4 %copy-start.26 = (f32[16]{0:T(128)S(1)}, f32[16]{0:T(128)}, u32[]{:S(2)}) copy-start(f32[16]{0:T(128)} %copy-done.25) | copy-start | bytes 196
  54.5 4.4 %copy-start.29 = (f32[16]{0:T(128)S(1)}, f32[16]{0:T(128)}, u32[]{:S(2)}) copy-start(f32[16]{0:T(128)} %param.26) | copy-start | bytes 196
  65.1 2.0 %copy-start.5 = (bf16[344,1024]{0,1:T(8,128)(2,1)S(1)}, bf16[344,1024]{0,1:T(8,128)(2,1)}, u32[]{:S(2)}) copy-start(bf16[344,1024]{0,1:T(8,128)(2,1)} %copy.32) | copy-start | bytes 2113540
  65.1 2.0 %copy-start.6 = (f32[344,64]{0,1:T(8,128)S(1)}, f32[344,64]{0,1:T(8,128)}, u32[]{:S(2)}) copy-start(f32[344,64]{0,1:T(8,128)} %copy.31) | copy-start | bytes 264196
  68.2 1.2 %copy-start.4 = (bf16[4,128,1024]{1,2,0:T(8,128)(2,1)S(1)}, bf16[4,128,1024]{1,2,0:T(8,128)(2,1)}, u32[]{:S(2)}) copy-start(bf16[4,128,1024]{1,2,0:T(8,128)(2,1)} %copy-done.3) | copy-start | bytes 3145732
  68.2 1.2 %copy-start.10 = (f32[4,128,16]{1,2,0:T(8,128)S(1)}, f32[4,128,16]{1,2,0:T(8,128)}, u32[]{:S(2)}) copy-start(f32[4,128,16]{1,2,0:T(8,128)} %exponential_bitcast_fusion) | copy-start | bytes 98308
  68.2 1.9 %copy-start.45 = (f32[4,16,64,128]{3,2,1,0:T(8,128)S(1)}, f32[4,16,64,128]{3,2,1,0:T(8,128)}, u32[]{:S(2)}) copy-start(f32[4,16,64,128]{3,2,1,0:T(8,128)} %fusion.14) | copy-start | bytes 6291460
  70.1 4.4 %copy-start.8 = (f32[16,64]{1,0:T(8,128)S(1)}, f32[16,64]{1,0:T(8,128)}, u32[]{:S(2)}) copy-start(f32[16,64]{1,0:T(8,128)} %mul.244) | copy-start | bytes 12292
  74.5 1.2 %copy-start.2 = (bf16[1024,512]{1,0:T(8,128)(2,1)S(1)}, bf16[1024,512]{1,0:T(8,128)(2,1)}, u32[]{:S(2)}) copy-start(bf16[1024,512]{1,0:T(8,128)(2,1)} %param.30) | copy-start | bytes 3145732
  75.0 2.4 %copy-start.14 = (bf16[2,512]{1,0:T(2,128)(2,1)S(1)}, bf16[2,512]{1,0:T(2,128)(2,1)}, u32[]{:S(2)}) copy-start(bf16[2,512]{1,0:T(2,128)(2,1)} %param.19) | copy-start | bytes 6148
  75.0 2.4 %copy-start.16 = (bf16[2,512]{1,0:T(2,128)(2,1)S(1)}, bf16[2,512]{1,0:T(2,128)(2,1)}, u32[]{:S(2)}) copy-start(bf16[2,512]{1,0:T(2,128)(2,1)} %copy-done.15) | copy-start | bytes 6148
  75.0 2.4 %copy-start.18 = (s32[4,128]{1,0:T(4,128)S(1)}, s32[4,128]{1,0:T(4,128)}, u32[]{:S(2)}) copy-start(s32[4,128]{1,0:T(4,128)} %get-tuple-element.10) | copy-start | bytes 6148
  75.7 2.1 %copy-start.33 = (bf16[512,2]{0,1:T(2,128)(2,1)S(1)}, bf16[512,2]{0,1:T(2,128)(2,1)}, u32[]{:S(2)}) copy-start(bf16[512,2]{0,1:T(2,128)(2,1)} %param.32) | copy-start | bytes 6148
  75.7 2.2 %copy-start.34 = (bf16[512,2]{0,1:T(2,128)(2,1)S(1)}, bf16[512,2]{0,1:T(2,128)(2,1)}, u32[]{:S(2)}) copy-start(bf16[512,2]{0,1:T(2,128)(2,1)} %rev.19) | copy-start | bytes 6148
  75.7 2.2 %copy-start.39 = (f32[512]{0:T(512)S(1)}, f32[512]{0:T(512)}, u32[]{:S(2)}) copy-start(f32[512]{0:T(512)} %param.31) | copy-start | bytes 6148
  75.7 2.5 %copy-start.35 = (s32[2,2,128]{2,1,0:T(2,128)S(1)}, s32[2,2,128]{2,1,0:T(2,128)}, u32[]{:S(2)}) copy-start(s32[2,2,128]{2,1,0:T(2,128)} %param.33) | copy-start | bytes 6148
  75.7 2.5 %copy-start.44 = (f32[2,2,128]{2,1,0:T(2,128)S(1)}, f32[2,2,128]{2,1,0:T(2,128)}, u32[]{:S(2)}) copy-start(f32[2,2,128]{2,1,0:T(2,128)} %fusion.33) | copy-start | bytes 6148
  (4 other events, 4.0 us)

commit v2 on v1

--- a/solution.py
+++ b/solution.py
@@ -212,8 +212,14 @@
     weights = (scores[:, None] * decays * dt_u[:, :, None, :]).astype(jnp.bfloat16)
     y_intra = jnp.einsum("uhts,ushp->uthp", weights, x_u, preferred_element_type=jnp.float32)
 
-    every = gather_all(tokens, "seq")
-    seq_tok = jnp.concatenate([every, (BASES - 1) - every[:, ::-1]], axis=0)
+    mine = jnp.concatenate([tokens, rc_tok], axis=0).astype(jnp.float32)
+    slots = jnp.where(
+        (jnp.arange(nseq) == place)[:, None, None], mine[None], 0.0
+    )
+    slots = lax.psum(slots, "seq").astype(jnp.int32)
+    fwd_all = jnp.moveaxis(slots[:, :windows], 0, 1).reshape(windows, total)
+    rc_all = jnp.moveaxis(slots[::-1, windows:], 0, 1).reshape(windows, total)
+    seq_tok = jnp.concatenate([fwd_all, rc_all], axis=0)
     ext_all = jnp.concatenate([jnp.zeros((streams, KW - 1), seq_tok.dtype), seq_tok], axis=1)
     gram = gram_ids(ext_all, jnp.broadcast_to(jnp.arange(total, dtype=jnp.int32), (streams, total)))
     dt_all = jax.nn.softplus(heads_lookup(dt_rows, seq_tok) + dt_bias[:, None])

time: 80.2 us -> 112 us (1.40)
  blocking collectives: 0 us -> 62.5 us
  local copies, waits for them, and re-layouts: 22.5 us -> 11.1 us
  other arithmetic: 16 us -> 6.6 us
  starting transfers between devices: 11.8 us -> 4.3 us
    psum x0 -> x1, blocking collectives: none -> 62.5 us  [local(): slots = lax.psum(slots, 'seq').astype(jnp.int32)]
    ppermute x4 -> x0, starting transfers between devices: 7.53 us -> none  [gather_all(): lax.ppermute(held, axis, [(src, src ^ mask) for src in range(count)])]
    rev x1, local copies, waits for them, and re-layouts: 5.24 us -> 0.01 us  [local(): rc_all = jnp.moveaxis(slots[::-1, windows:], 0, 1).reshape(windows, total)]
    select_n x6 -> x1, other arithmetic: 2.94 us -> 0.07 us  [local(): jnp.where((jnp.arange(nseq) == place)[:, None, None], mine[None], 0.0)]
    unnamed x94 -> x54, local copies, waits for them, and re-layouts: 4.72 us -> 2.43 us
    reshape x1, local copies, waits for them, and re-layouts: 1.93 us -> 0.08 us  [local(): (jnp.repeat(within, nloc, axis=0) * across[..., None]).reshape(units, HEA...]
    dot_general x1, matrix products: 2.11 us -> 0.75 us  [local(): jnp.einsum('rtg,gc->rtc', oh_loc, x_tab, preferred_element_type=jnp.float32)]
    dot_general x1, matrix products: 0.97 us -> 2.32 us  [local(): jnp.einsum('hgp,uhgn->uhpn', x_heads, b_lo, preferred_element_type=jnp.fl...]
  transfers between devices with their start and end apart: 6 -> 2, of which waited for: 1 -> 0; matrix products, arithmetic and copies ran while one was open for 40% -> 11% of each run, Pallas kernels for 0% -> 0%
where the time goes in v2:
time: 112 us
  blocking collectives  62.5 us (56%)
  matrix products  25.8 us (23%)
  local copies, waits for them, and re-layouts  11.1 us (10%)
  other arithmetic  6.6 us (6%)
  starting transfers between devices  4.3 us (4%)
  between operations  1.24 us (1%)
    psum x1, blocking collectives, local(): slots = lax.psum(slots, 'seq').astype(jnp.int32)  62.5 us
    dot_general x1, matrix products, local(): jnp.einsum('utn,uhpn->uthp', c_u, start_state, precision=HIGH)  4.39 us
    dot_general x1, matrix products, local(): jnp.einsum('uhts,ushp->uthp', weights, x_u, preferred_element_type=jnp.fl...  4.11 us
    ppermute x1, starting transfers between devices, local(): lax.ppermute(tokens[:, count - (KW - 1):], 'seq', [(src, src + 1) for src...  3.02 us
    dot_general x1, matrix products, gram_tables(): jnp.dot(jnp.asarray(gram_layout()), taps, precision=HIGH)  2.54 us
    unnamed x54, local copies, waits for them, and re-layouts  2.43 us
    dot_general x1, matrix products, local(): jnp.einsum('hgp,uhgn->uhpn', x_heads, b_lo, preferred_element_type=jnp.fl...  2.32 us
    dot_general x1, matrix products, local(): jnp.einsum('hgp,uhgn->uhpn', x_heads, b_hi, preferred_element_type=jnp.fl...  2.28 us
  transfers between devices with their start and end apart: 2, of which 0 were waited for; matrix products, arithmetic and copies ran while one was open for 11% of the time, Pallas kernels for 0%

profile of v2, /device:TPU:0, one launch (start us, length us, event | category | flops | bytes accessed | tf_op | source)
XLA Modules:
  0.0 111.5 jit_solution(16466286786566491538)
XLA Ops:
  0.6 0.9 rev.15
  1.5 0.1 slice.82
  1.6 1.3 %collective-permute-start.1 = (s32[2,3]{1,0:T(2,128)S(1)}, s32[2,3]{1,0:T(2,128)S(1)}, u32[]{:S(2)}, u32[]{:S(2)}) collective-permute-start(s32[2,3]{1,0:T(2,128)S(1)} %slice.82), channel_id=1, source_target_pairs={{1,0},{2,1},{3,2},{4,3},{5,4},{6,5},{7,6},{8,7},{9,8},{10,9},{11,1... | collective-permute-start | bytes 80 | tf_op jit(solution)/shard_map/ppermute | solution.py:176
  2.9 0.8 slice.81
  3.6 3.0 %collective-permute-start = (s32[2,3]{1,0:T(2,128)S(1)}, s32[2,3]{1,0:T(2,128)S(1)}, u32[]{:S(2)}, u32[]{:S(2)}) collective-permute-start(s32[2,3]{1,0:T(2,128)S(1)} %slice.81), channel_id=1, source_target_pairs={{0,1},{1,2},{2,3},{3,4},{4,5},{5,6},{6,7},{7,8},{8,9},{9,10},{10,1... | collective-permute-start | bytes 80 | tf_op jit(solution)/shard_map/ppermute | solution.py:173
  6.7 1.6 %rev.16 = bf16[2,512]{1,0:T(2,128)(2,1)S(1)} reverse(bf16[2,512]{1,0:T(2,128)(2,1)} %param.19), dimensions={0,1} | reverse | bytes 4096 | tf_op jit(solution)/shard_map/rev | solution.py:164
  8.3 0.8 fusion.78
  9.1 1.0 fusion.13
  10.1 0.7 broadcast_multiply_fusion
  11.0 2.5 %divide_multiply_fusion = f32[344,1152]{1,0:T(8,128)S(1)} fusion(f32[16,1152]{1,0:T(8,128)S(1)} %mul.214, f32[344,16]{1,0:T(8,128)} %constant.21.clone, f32[1152]{0:T(1024)} %param.25), kind=kOutput, calls=%fused_computation.34 | convolution fusion | flops 78068736 | bytes 1685504 | tf_op jit(solution)/shard_map/dot_general | solution.py:78
  13.6 0.1 slice.165
  13.7 1.0 copy-done.1
  14.7 0.6 convert_compare_fusion
  15.4 0.2 fusion.110
  15.7 0.4 copy.32
  16.1 0.1 copy.31
  16.2 0.7 compare_select_fusion.2
  16.9 0.2 fusion.72
  17.1 0.6 copy-done.5
  17.7 0.6 exponential_bitcast_fusion
  18.4 1.4 %rev.19 = bf16[512,2]{0,1:T(2,128)(2,1)} reverse(bf16[512,2]{0,1:T(2,128)(2,1)S(1)} %copy-done.13), dimensions={0,1} | reverse | bytes 4096 | tf_op jit(solution)/shard_map/rev | solution.py:281
  19.8 0.6 fusion.33
  20.4 0.1 add_add_fusion
  20.5 0.6 fusion.107
  21.2 62.5 %psum.7 = f32[16,4,128]{2,0,1:T(8,128)S(1)} all-reduce(f32[16,4,128]{2,0,1:T(8,128)S(1)} %broadcast_select_fusion), channel_id=1, replica_groups=mesh['grp'=2,'seq'=16] {'seq'}, use_global_device_ids=true, to_apply=%region_1.2 | all-reduce | flops 8192 | bytes 65536 | tf_op jit(solution)/shard_map/psum | solution.py:219
  83.7 0.9 fusion.46
  84.6 0.4 slice_reduce_fusion
  85.0 0.2 select_reduce_fusion
  85.3 0.6 multiply_multiply_fusion
  85.9 0.1 reshape.305
  86.1 0.1 select_select_fusion
  86.2 2.0 %fusion.2 = f32[4,32,344]{2,1,0:T(8,128)S(1)} fusion(s32[4,2048]{1,0:T(4,128)S(1)} %select_select_fusion, bf16[4,16,2048]{2,1,0:T(8,128)(2,1)S(1)} %get-tuple-element.2, bf16[4,16,2048]{2,1,0:T(8,128)(2,1)S(1)} %get-tuple-element.3), kind=kOutput, calls=%fused_computation.3 | convolution fusion | flops 184221696 | bytes 733184 | tf_op jit(solution)/shard_map/uhp,upg->uhg/dot_general | solution.py:244
  88.2 2.3 %fusion.6 = f32[16,4,64,64]{3,2,0,1:T(8,128)} fusion(bf16[16,344,64,1]{1,2,0,3:T(8,128)(2,1)S(1)} %bitcast.97, f32[344,64]{0,1:T(8,128)S(1)} %copy.31, f32[4,16,344]{2,1,0:T(8,128)S(1)} %slice_add_fusion), kind=kOutput, calls=%fused_computation.10 | convolution fusion | flops 187400192 | bytes 1929216 | tf_op jit(solution)/shard_map/hgp,uhgn->uhpn/dot_general | solution.py:254
  90.5 2.3 %fusion.5 = f32[16,4,64,64]{3,2,0,1:T(8,128)} fusion(bf16[16,344,64,1]{1,2,0,3:T(8,128)(2,1)S(1)} %bitcast.98, f32[344,64]{0,1:T(8,128)S(1)} %copy.31, f32[4,16,344]{2,1,0:T(8,128)S(1)} %slice_add_fusion), kind=kOutput, calls=%fused_computation.8 | convolution fusion | flops 183173120 | bytes 1929216 | tf_op jit(solution)/shard_map/hgp,uhgn->uhpn/dot_general | solution.py:252
  92.8 0.8 convolution_convert_fusion.1
  93.6 0.4 fusion.38
  94.0 1.3 %copy.30 = bf16[4,128,1024]{1,2,0:T(8,128)(2,1)} copy(bf16[4,128,1024]{2,1,0:T(8,128)(2,1)S(1)} %convolution_convert_fusion.1) | data formatting | bytes 2097152 | tf_op jit(solution)/shard_map/convert_element_type | solution.py:187
  95.3 1.3 %fusion.65 = f32[4,128,128]{2,1,0:T(8,128)} fusion(f32[4,128,128]{1,2,0:T(8,128)S(1)} %fusion.38), kind=kOutput, calls=%fused_computation.85 | convolution fusion | flops 50331648 | bytes 524288 | tf_op jit(solution)/shard_map/utn,usn->uts/dot_general | solution.py:208
  96.6 2.0 %fusion.39 = f32[4,128,1024]{1,2,0:T(8,128)S(1)} fusion(bf16[512,1024]{1,0:T(8,128)(2,1)} %param.22, s32[4,128]{1,0:T(4,128)} %get-tuple-element.13, f32[512]{0:T(512)} %param.20, f32[4]{0:T(128)} %copy-done.17, bf16[2,512]{1,0:T(2,128)(2,1)S(1)} %rev.16, bf16[2,512]{1,0:T(2,128)(2,1)S(1)} %copy-done.7), kind=kOutput, calls=%fused_computation.55 | convolution fusion | flops 8409088 | bytes 3153936 | tf_op jit(solution)/shard_map/rtk,kc->rtc/dot_general | solution.py:192
  98.7 4.1 %fusion.14 = f32[4,16,64,128]{3,2,1,0:T(8,128)S(1)} fusion(bf16[4,128,16,64]{1,3,2,0:T(8,128)(2,1)} %bitcast.95, f32[4,16,128]{2,1,0:T(8,128)} %compare_select_fusion.2, f32[4,16,128]{2,1,0:T(8,128)} %copy-done.5, f32[4,128,128]{2,1,0:T(8,128)} %fusion.65, pred[128,128]{1,0:T(8,128)(4,1)} %convert_compare_fusion), kind=kOutput, calls=%fused_computation.19 | convolution fusion | flops 140509184 | bytes 3489792 | tf_op jit(solution)/shard_map/uhts,ushp->uthp/dot_general | solution.py:213
  102.8 4.4 %multiply_reduce_fusion = (f32[4,128,16]{1,2,0:T(8,128)S(1)}, f32[4,128,16,64]{1,3,2,0:T(8,128)S(1)}) fusion(f32[4,128,16,64]{1,3,2,0:T(8,128)S(1)} %bitcast.94, bf16[4,128,16,64]{1,3,2,0:T(8,128)(2,1)S(1)} %bitcast.96, f32[16]{0:T(128)S(1)} %copy-done.22, f32[4,128,16]{1,2,0:T(8,128)S(1)} %copy-done.6, f32[16,4,64,64]{3,2,0,1:T(8,128)S(1)} %copy-done.25, ...), kind=kOutput, calls=%fused_computation.26 | convolution fusion | flops 409198592 | bytes 11731456 | tf_op jit(solution)/shard_map/utn,uhpn->uthp/dot_general | solution.py:257
  107.3 0.5 multiply_convert_fusion.4
  107.7 0.7 copy-done.3
  108.5 0.7 convolution_convert_fusion.2
  109.2 0.9 rev.18
  110.2 0.4 fusion.40
  110.6 0.2 fusion.50
  110.9 0.6 multiply_reduce_fusion.1
  (84 shorter events, 0.8 us)
Async XLA Ops:
  0.6 8.5 %copy-start = (bf16[512,1152]{1,0:T(8,128)(2,1)S(1)}, bf16[512,1152]{1,0:T(8,128)(2,1)}, u32[]{:S(2)}) copy-start(bf16[512,1152]{1,0:T(8,128)(2,1)} %param.21) | copy-start | bytes 3538948
  1.6 18.8 %collective-permute-start.1 = (s32[2,3]{1,0:T(2,128)S(1)}, s32[2,3]{1,0:T(2,128)S(1)}, u32[]{:S(2)}, u32[]{:S(2)}) collective-permute-start(s32[2,3]{1,0:T(2,128)S(1)} %slice.82), channel_id=1, source_target_pairs={{1,0},{2,1},{3,2},{4,3},{5,4},{6,5},{7,6},{8,7},{9,8},{10,9},{11,1... | collective-permute-start | bytes 80 | tf_op jit(solution)/shard_map/ppermute | solution.py:176
  3.6 16.8 %collective-permute-start = (s32[2,3]{1,0:T(2,128)S(1)}, s32[2,3]{1,0:T(2,128)S(1)}, u32[]{:S(2)}, u32[]{:S(2)}) collective-permute-start(s32[2,3]{1,0:T(2,128)S(1)} %slice.81), channel_id=1, source_target_pairs={{0,1},{1,2},{2,3},{3,4},{4,5},{5,6},{6,7},{7,8},{8,9},{9,10},{10,1... | collective-permute-start | bytes 80 | tf_op jit(solution)/shard_map/ppermute | solution.py:173
  9.1 6.2 %copy-start.17 = (f32[4]{0:T(128)}, f32[4]{0:T(128)S(1)}, u32[]{:S(2)}) copy-start(f32[4]{0:T(128)S(1)} %add_rsqrt_fusion.2) | copy-start | bytes 52
  10.9 3.8 %copy-start.8 = (s32[2,128]{1,0:T(2,128)S(1)}, s32[2,128]{1,0:T(2,128)}, u32[]{:S(2)}) copy-start(s32[2,128]{1,0:T(2,128)} %param.18) | copy-start | bytes 3076
  10.9 4.4 %copy-start.7 = (bf16[2,512]{1,0:T(2,128)(2,1)S(1)}, bf16[2,512]{1,0:T(2,128)(2,1)}, u32[]{:S(2)}) copy-start(bf16[2,512]{1,0:T(2,128)(2,1)} %param.19) | copy-start | bytes 6148
  10.9 4.4 %copy-start.9 = (f32[512]{0:T(512)S(1)}, f32[512]{0:T(512)}, u32[]{:S(2)}) copy-start(f32[512]{0:T(512)} %param.20) | copy-start | bytes 6148
  10.9 4.4 %copy-start.18 = (bf16[512,16]{0,1:T(8,128)(2,1)S(1)}, bf16[512,16]{0,1:T(8,128)(2,1)}, u32[]{:S(2)}) copy-start(bf16[512,16]{0,1:T(8,128)(2,1)} %param.23) | copy-start | bytes 49156
  11.0 4.6 %copy-start.21 = (f32[16]{0:T(128)S(1)}, f32[16]{0:T(128)}, u32[]{:S(2)}) copy-start(f32[16]{0:T(128)} %param.27) | copy-start | bytes 196
  13.5 1.2 %copy-start.1 = (f32[344,1152]{1,0:T(8,128)}, f32[344,1152]{1,0:T(8,128)S(1)}, u32[]{:S(2)}) copy-start(f32[344,1152]{1,0:T(8,128)S(1)} %divide_multiply_fusion) | copy-start | bytes 4755460
  13.5 2.6 %copy-start.12 = (f32[16]{0:T(128)S(1)}, f32[16]{0:T(128)}, u32[]{:S(2)}) copy-start(f32[16]{0:T(128)} %param.26) | copy-start | bytes 196
  13.5 4.8 %copy-start.11 = (f32[1024]{0:T(1024)S(1)}, f32[1024]{0:T(1024)}, u32[]{:S(2)}) copy-start(f32[1024]{0:T(1024)} %param.29) | copy-start | bytes 12292
  13.6 4.9 %copy-start.13 = (bf16[512,2]{0,1:T(2,128)(2,1)S(1)}, bf16[512,2]{0,1:T(2,128)(2,1)}, u32[]{:S(2)}) copy-start(bf16[512,2]{0,1:T(2,128)(2,1)} %param.32) | copy-start | bytes 6148
  13.6 6.2 %copy-start.19 = (f32[2,2,128]{2,1,0:T(2,128)S(1)}, f32[2,2,128]{2,1,0:T(2,128)}, u32[]{:S(2)}) copy-start(f32[2,2,128]{2,1,0:T(2,128)} %param.34) | copy-start | bytes 6148
  17.1 0.6 copy-start.5
  90.5 2.3 %copy-start.2 = (f32[344,1152]{1,0:T(8,128)S(1)}, f32[344,1152]{1,0:T(8,128)}, u32[]{:S(2)}) copy-start(f32[344,1152]{1,0:T(8,128)} %copy-done.1) | copy-start | bytes 4755460
  98.6 4.2 %copy-start.4 = (bf16[4,128,1024]{1,2,0:T(8,128)(2,1)S(1)}, bf16[4,128,1024]{1,2,0:T(8,128)(2,1)}, u32[]{:S(2)}) copy-start(bf16[4,128,1024]{1,2,0:T(8,128)(2,1)} %copy.30) | copy-start | bytes 3145732
  98.6 4.2 %copy-start.6 = (f32[4,128,16]{1,2,0:T(8,128)S(1)}, f32[4,128,16]{1,2,0:T(8,128)}, u32[]{:S(2)}) copy-start(f32[4,128,16]{1,2,0:T(8,128)} %exponential_bitcast_fusion) | copy-start | bytes 98308
  98.6 4.2 %copy-start.22 = (f32[16]{0:T(128)S(1)}, f32[16]{0:T(128)}, u32[]{:S(2)}) copy-start(f32[16]{0:T(128)} %param.28) | copy-start | bytes 196
  98.6 4.2 %copy-start.25 = (f32[16,4,64,64]{3,2,0,1:T(8,128)S(1)}, f32[16,4,64,64]{3,2,0,1:T(8,128)}, u32[]{:S(2)}) copy-start(f32[16,4,64,64]{3,2,0,1:T(8,128)} %fusion.5) | copy-start | bytes 3145732
  98.6 4.2 %copy-start.26 = (f32[16,4,64,64]{3,2,0,1:T(8,128)S(1)}, f32[16,4,64,64]{3,2,0,1:T(8,128)}, u32[]{:S(2)}) copy-start(f32[16,4,64,64]{3,2,0,1:T(8,128)} %fusion.6) | copy-start | bytes 3145732
  107.2 1.2 %copy-start.3 = (bf16[1024,512]{1,0:T(8,128)(2,1)S(1)}, bf16[1024,512]{1,0:T(8,128)(2,1)}, u32[]{:S(2)}) copy-start(bf16[1024,512]{1,0:T(8,128)(2,1)} %param.30) | copy-start | bytes 3145732
  107.7 2.4 %copy-start.10 = (s32[4,128]{1,0:T(4,128)S(1)}, s32[4,128]{1,0:T(4,128)}, u32[]{:S(2)}) copy-start(s32[4,128]{1,0:T(4,128)} %get-tuple-element.13) | copy-start | bytes 6148
  108.5 2.1 %copy-start.14 = (bf16[512,2]{0,1:T(2,128)(2,1)S(1)}, bf16[512,2]{0,1:T(2,128)(2,1)}, u32[]{:S(2)}) copy-start(bf16[512,2]{0,1:T(2,128)(2,1)} %param.32) | copy-start | bytes 6148
  108.5 2.1 %copy-start.15 = (bf16[512,2]{0,1:T(2,128)(2,1)S(1)}, bf16[512,2]{0,1:T(2,128)(2,1)}, u32[]{:S(2)}) copy-start(bf16[512,2]{0,1:T(2,128)(2,1)} %rev.19) | copy-start | bytes 6148
  108.5 2.1 %copy-start.20 = (f32[512]{0:T(512)S(1)}, f32[512]{0:T(512)}, u32[]{:S(2)}) copy-start(f32[512]{0:T(512)} %param.31) | copy-start | bytes 6148
  108.5 2.4 %copy-start.16 = (s32[2,2,128]{2,1,0:T(2,128)S(1)}, s32[2,2,128]{2,1,0:T(2,128)}, u32[]{:S(2)}) copy-start(s32[2,2,128]{2,1,0:T(2,128)} %param.33) | copy-start | bytes 6148
  108.5 2.5 %copy-start.24 = (f32[2,2,128]{2,1,0:T(2,128)S(1)}, f32[2,2,128]{2,1,0:T(2,128)}, u32[]{:S(2)}) copy-start(f32[2,2,128]{2,1,0:T(2,128)} %fusion.33) | copy-start | bytes 6148
  110.5 1.0 copy-start.23

commit v3 on v1

--- a/solution.py
+++ b/solution.py
@@ -92,19 +92,24 @@
     return ids
 
 
-def gather_all(tokens, axis):
+def gather_all(fwd, rc, axis):
     count = lax.axis_size(axis)
     place = lax.axis_index(axis)
-    held = tokens
+    rows = fwd.shape[0]
+    held = jnp.concatenate([fwd, rc], axis=0)
     bit = 0
     while 2**bit < count:
         mask = 2**bit
         other = lax.ppermute(held, axis, [(src, src ^ mask) for src in range(count)])
         upper = (place // mask) % 2 == 1
-        held = jnp.where(
-            upper,
-            jnp.concatenate([other, held], axis=1),
-            jnp.concatenate([held, other], axis=1),
+        low_first = jnp.concatenate([held, other], axis=1)
+        high_first = jnp.concatenate([other, held], axis=1)
+        held = jnp.concatenate(
+            [
+                jnp.where(upper, high_first[:rows], low_first[:rows]),
+                jnp.where(upper, low_first[rows:], high_first[rows:]),
+            ],
+            axis=0,
         )
         bit += 1
     return held
@@ -212,8 +217,7 @@
     weights = (scores[:, None] * decays * dt_u[:, :, None, :]).astype(jnp.bfloat16)
     y_intra = jnp.einsum("uhts,ushp->uthp", weights, x_u, preferred_element_type=jnp.float32)
 
-    every = gather_all(tokens, "seq")
-    seq_tok = jnp.concatenate([every, (BASES - 1) - every[:, ::-1]], axis=0)
+    seq_tok = gather_all(tokens, rc_tok, "seq")
     ext_all = jnp.concatenate([jnp.zeros((streams, KW - 1), seq_tok.dtype), seq_tok], axis=1)
     gram = gram_ids(ext_all, jnp.broadcast_to(jnp.arange(total, dtype=jnp.int32), (streams, total)))
     dt_all = jax.nn.softplus(heads_lookup(dt_rows, seq_tok) + dt_bias[:, None])

time: 80.2 us -> 71 us (0.89)
  local copies, waits for them, and re-layouts: 22.5 us -> 15.3 us
  other arithmetic: 16 us -> 12.8 us
  starting transfers between devices: 11.8 us -> 12.8 us
    rev x1 -> x0, local copies, waits for them, and re-layouts: 5.24 us -> none  [local(): seq_tok = jnp.concatenate([every, BASES - 1 - every[:, ::-1]], axis=0)]
    select_n x6 -> x4, other arithmetic: 2.94 us -> 0.05 us  [gather_all(): jnp.where(upper, high_first[:rows], low_first[:rows])]
    concatenate x1 -> x8, other arithmetic: 0.74 us -> 2.1 us  [the longest x4 1.27 us: gather_all(): jnp.concatenate([jnp.where(upper, high_first[:rows], low_first[:rows]), j...]
    unnamed x1 -> x0, other arithmetic: 1.34 us -> none
    unnamed x94 -> x101, local copies, waits for them, and re-layouts: 4.72 us -> 3.44 us
    ppermute x4, starting transfers between devices: 7.53 us -> 8.54 us  [gather_all(): lax.ppermute(held, axis, [(src, src ^ mask) for src in range(count)])]
where the time goes in v3:
time: 71 us; the launch traced here: 70.1 us
  matrix products  26.4 us (37%)
  local copies, waits for them, and re-layouts  15.3 us (22%)
  other arithmetic  12.8 us (18%)
  starting transfers between devices  12.8 us (18%)
  between operations  1.62 us (2%)
  waiting for transfers between devices  1.11 us (2%)
    ppermute x4, starting transfers between devices, gather_all(): lax.ppermute(held, axis, [(src, src ^ mask) for src in range(count)])  8.54 us
    dot_general x1, matrix products, local(): jnp.einsum('uhts,ushp->uthp', weights, x_u, preferred_element_type=jnp.fl...  4.51 us
    dot_general x1, matrix products, local(): jnp.einsum('utn,uhpn->uthp', c_u, start_state, precision=HIGH)  4.32 us
    unnamed x101, local copies, waits for them, and re-layouts  3.44 us
    ppermute x1, starting transfers between devices, local(): lax.ppermute(tokens[:, count - (KW - 1):], 'seq', [(src, src + 1) for src...  3.02 us
    dot_general x1, matrix products, gram_tables(): jnp.dot(jnp.asarray(gram_layout()), taps, precision=HIGH)  2.54 us
    dot_general x1, matrix products, local(): jnp.einsum('rtg,gc->rtc', oh_loc, x_tab, preferred_element_type=jnp.float32)  2.11 us
    dot_general x1, matrix products, local(): jnp.einsum('uhp,upg->uhg', jnp.concatenate([w_hi, w_lo], axis=1), oh_all,...  2 us
  transfers between devices with their start and end apart: 6, of which 1 were waited for; matrix products, arithmetic and copies ran while one was open for 40% of the time, Pallas kernels for 0%

profile of v3, /device:TPU:0, one launch (start us, length us, event | category | flops | bytes accessed | tf_op | source)
XLA Modules:
  0.0 70.1 jit_solution(12880941025766200230)
XLA Ops:
  0.6 0.9 %rev.12 = s32[2,128]{1,0:T(2,128)S(1)} reverse(s32[2,128]{1,0:T(2,128)} %param.18), dimensions={1} | reverse | bytes 2048 | tf_op jit(solution)/shard_map/rev | solution.py:177
  1.6 1.3 %collective-permute-start.1 = (s32[2,3]{1,0:T(2,128)S(1)}, s32[2,3]{1,0:T(2,128)S(1)}, u32[]{:S(2)}, u32[]{:S(2)}) collective-permute-start(s32[2,3]{1,0:T(2,128)S(1)} %slice.124), channel_id=1, source_target_pairs={{1,0},{2,1},{3,2},{4,3},{5,4},{6,5},{7,6},{8,7},{9,8},{10,9},{11,1... | collective-permute-start | bytes 80 | tf_op jit(solution)/shard_map/ppermute | solution.py:181
  2.9 0.8 %slice.123 = s32[2,3]{1,0:T(2,128)S(1)} slice(s32[2,128]{1,0:T(2,128)} %param.18), slice={[0:2], [125:128]} | slice | bytes 48 | tf_op jit(solution)/shard_map/slice | solution.py:179
  3.6 3.0 %collective-permute-start = (s32[2,3]{1,0:T(2,128)S(1)}, s32[2,3]{1,0:T(2,128)S(1)}, u32[]{:S(2)}, u32[]{:S(2)}) collective-permute-start(s32[2,3]{1,0:T(2,128)S(1)} %slice.123), channel_id=1, source_target_pairs={{0,1},{1,2},{2,3},{3,4},{4,5},{5,6},{6,7},{7,8},{8,9},{9,10},{10,1... | collective-permute-start | bytes 80 | tf_op jit(solution)/shard_map/ppermute | solution.py:178
  6.7 0.6 iota_compare_fusion.8
  8.0 1.6 %rev.13 = bf16[2,512]{1,0:T(2,128)(2,1)S(1)} reverse(bf16[2,512]{1,0:T(2,128)(2,1)} %param.19), dimensions={0,1} | reverse | bytes 4096 | tf_op jit(solution)/shard_map/rev | solution.py:169
  9.5 0.8 %fusion.78 = f32[4]{0:T(128)S(1)} fusion(bf16[2,512]{1,0:T(2,128)(2,1)S(1)} %rev.13, bf16[2,512]{1,0:T(2,128)(2,1)} %param.19), kind=kLoop, calls=%fused_computation.124 | loop fusion | flops 12284 | bytes 4112 | tf_op jit(solution)/shard_map/reduce_sum | solution.py:23
  10.4 1.0 %fusion.13 = f32[4,1152]{1,0:T(4,128)S(1)} fusion(bf16[512,1152]{1,0:T(8,128)(2,1)S(1)} %copy-done, f32[512]{0:T(512)} %param.20, f32[4]{0:T(128)S(1)} %add_rsqrt_fusion.2, bf16[2,512]{1,0:T(2,128)(2,1)S(1)} %rev.13, bf16[2,512]{1,0:T(2,128)(2,1)} %param.19), kind=kOutput, calls=%fused_computation.18 | convolution fusion | flops 4742144 | bytes 1204240 | tf_op jit(solution)/shard_map/dot_general | solution.py:74
  11.4 0.7 %broadcast_multiply_fusion = f32[4,4,1152]{2,1,0:T(4,128)S(1)} fusion(f32[4,1152]{1,0:T(4,128)S(1)} %fusion.13, f32[4,1152]{1,0:T(4,128)} %param.24), kind=kLoop, calls=%fused_computation.98 | loop fusion | flops 18432 | bytes 110592 | tf_op jit(solution)/shard_map/mul | solution.py:77
  12.2 2.5 %divide_multiply_fusion = f32[344,1152]{1,0:T(8,128)S(1)} fusion(f32[16,1152]{1,0:T(8,128)S(1)} %mul.214, f32[344,16]{1,0:T(8,128)} %constant.137.clone, f32[1152]{0:T(1024)} %param.25), kind=kOutput, calls=%fused_computation.34 | convolution fusion | flops 78068736 | bytes 1685504 | tf_op jit(solution)/shard_map/dot_general | solution.py:78
  14.9 1.0 %copy-done.1 = f32[344,1152]{1,0:T(8,128)} copy-done((f32[344,1152]{1,0:T(8,128)}, f32[344,1152]{1,0:T(8,128)S(1)}, u32[]{:S(2)}) %copy-start.1) | copy-done | bytes 1585176
  16.0 0.6 convert_compare_fusion
  17.0 1.1 %copy.32 = bf16[344,1024]{0,1:T(8,128)(2,1)} copy(bf16[344,1024]{1,0:T(8,128)(2,1)S(1)} %slice.249) | data formatting | bytes 1409024 | tf_op jit(solution)/shard_map/slice | solution.py:171
  18.1 0.8 %copy.31 = f32[344,64]{0,1:T(8,128)} copy(f32[344,64]{1,0:T(8,128)S(1)} %slice.187) | data formatting | bytes 176128 | tf_op jit(solution)/shard_map/slice | solution.py:172
  18.9 0.7 %compare_select_fusion.2 = f32[4,16,128]{2,1,0:T(8,128)} fusion(f32[16]{0:T(128)S(1)} %copy-done.32, f32[16]{0:T(128)S(1)} %get-tuple-element.31, f32[16]{0:T(128)S(1)} %get-tuple-element.32, f32[16]{0:T(128)S(1)} %get-tuple-element.33, f32[16]{0:T(128)S(1)} %get-tuple-element.30, pred[4,128]{1,0:T(4,128)(4,1)S(1)} %get-tuple-element.29, ...), kind=kLoop, calls=%fused_computation.91 | loop fusion | flops 114688 | bytes 35136 | tf_op jit(solution)/shard_map/jit(softplus)/select_n | solution.py:198
  20.5 0.6 exponential_bitcast_fusion
  21.1 0.7 mul.244
  21.8 1.3 %rev.15 = bf16[512,2]{0,1:T(2,128)(2,1)} reverse(bf16[512,2]{0,1:T(2,128)(2,1)S(1)} %copy-done.36), dimensions={0,1} | reverse | bytes 4096 | tf_op jit(solution)/shard_map/rev | solution.py:279
  23.1 0.6 fusion.33
  23.7 0.6 broadcast_and_fusion
  24.5 2.6 %collective-permute-start.2 = (s32[4,128]{1,0:T(4,128)S(1)}, s32[4,128]{1,0:T(4,128)S(1)}, u32[]{:S(2)}, u32[]{:S(2)}) collective-permute-start(s32[4,128]{1,0:T(4,128)S(1)} %get-tuple-element.24), channel_id=1, source_target_pairs={{0,1},{1,0},{2,3},{3,2},{4,5},{5,4},{6,7},{7,6},{8,9},{9,8},{10,11... | collective-permute-start | bytes 6152 | tf_op jit(solution)/shard_map/ppermute | solution.py:103
  27.1 2.1 %convolution_convert_fusion.1 = bf16[4,128,1024]{2,1,0:T(8,128)(2,1)S(1)} fusion(s32[4,128]{1,0:T(4,128)S(1)} %get-tuple-element.25, f32[344,1152]{1,0:T(8,128)} %copy-done.1), kind=kOutput, calls=%fused_computation.36 | convolution fusion | flops 361410560 | bytes 1755136 | tf_op jit(solution)/shard_map/rtg,gc->rtc/dot_general | solution.py:192
  29.3 1.3 %fusion.38 = f32[4,128,128]{1,2,0:T(8,128)S(1)} fusion(s32[4,128]{1,0:T(4,128)S(1)} %get-tuple-element.25, f32[344,1152]{1,0:T(8,128)} %copy-done.1), kind=kOutput, calls=%fused_computation.52 | convolution fusion | flops 270708736 | bytes 440320 | tf_op jit(solution)/shard_map/rtg,gc->rtc/dot_general | solution.py:195
  30.7 2.4 %collective-permute-start.3 = (s32[4,256]{1,0:T(4,128)S(1)}, s32[4,256]{1,0:T(4,128)S(1)}, u32[]{:S(2)}, u32[]{:S(2)}) collective-permute-start(s32[4,256]{1,0:T(4,128)S(1)} %pad_add_fusion.7), channel_id=1, source_target_pairs={{0,2},{1,3},{2,0},{3,1},{4,6},{5,7},{6,4},{7,5},{8,10},{9,11},{10,... | collective-permute-start | bytes 12296 | tf_op jit(solution)/shard_map/ppermute | solution.py:103
  33.1 1.3 %fusion.65 = f32[4,128,128]{2,1,0:T(8,128)} fusion(f32[4,128,128]{1,2,0:T(8,128)S(1)} %fusion.38), kind=kOutput, calls=%fused_computation.85 | convolution fusion | flops 50331648 | bytes 524288 | tf_op jit(solution)/shard_map/utn,usn->uts/dot_general | solution.py:213
  34.4 0.7 copy.30
  35.1 1.6 %collective-permute-start.4 = (s32[4,512]{1,0:T(4,128)S(1)}, s32[4,512]{1,0:T(4,128)S(1)}, u32[]{:S(2)}, u32[]{:S(2)}) collective-permute-start(s32[4,512]{1,0:T(4,128)S(1)} %pad_add_fusion.5), channel_id=1, source_target_pairs={{0,4},{1,5},{2,6},{3,7},{4,0},{5,1},{6,2},{7,3},{8,12},{9,13},{10,... | collective-permute-start | bytes 24584 | tf_op jit(solution)/shard_map/ppermute | solution.py:103
  36.8 4.5 %fusion.14 = f32[4,16,64,128]{3,2,1,0:T(8,128)} fusion(bf16[4,128,16,64]{1,3,2,0:T(8,128)(2,1)S(1)} %bitcast.91, f32[4,16,128]{2,1,0:T(8,128)} %compare_select_fusion.2, f32[4,16,128]{2,1,0:T(8,128)} %copy-done.11, f32[4,128,128]{2,1,0:T(8,128)} %fusion.65, pred[128,128]{1,0:T(8,128)(4,1)} %convert_compare_fusion), kind=kOutput, calls=%fused_computation.19 | convolution fusion | flops 140509184 | bytes 3489792 | tf_op jit(solution)/shard_map/uhts,ushp->uthp/dot_general | solution.py:218
  41.3 0.6 pad_add_fusion.3
  41.9 1.9 %collective-permute-start.5 = (s32[4,1024]{1,0:T(4,128)}, s32[4,1024]{1,0:T(4,128)}, u32[]{:S(2)}, u32[]{:S(2)}) collective-permute-start(s32[4,1024]{1,0:T(4,128)} %pad_add_fusion.3), channel_id=1, source_target_pairs={{0,8},{1,9},{2,10},{3,11},{4,12},{5,13},{6,14},{7,15},{8,0},{9,1},... | collective-permute-start | bytes 49160 | tf_op jit(solution)/shard_map/ppermute | solution.py:103
  43.8 2.0 %fusion.39 = f32[4,128,1024]{1,2,0:T(8,128)S(1)} fusion(bf16[512,1024]{1,0:T(8,128)(2,1)} %param.22, s32[4,128]{1,0:T(4,128)} %copy-done.21, f32[512]{0:T(512)} %param.20, f32[4]{0:T(128)} %copy-done.40, bf16[2,512]{1,0:T(2,128)(2,1)} %copy-done.14, bf16[2,512]{1,0:T(2,128)(2,1)} %param.19), kind=kOutput, calls=%fused_computation.55 | convolution fusion | flops 8409088 | bytes 3153936 | tf_op jit(solution)/shard_map/rtk,kc->rtc/dot_general | solution.py:197
  45.9 1.1 %collective-permute-done.5 = s32[4,1024]{1,0:T(4,128)} collective-permute-done((s32[4,1024]{1,0:T(4,128)}, s32[4,1024]{1,0:T(4,128)}, u32[]{:S(2)}, u32[]{:S(2)}) %collective-permute-start.5) | collective-permute-done | bytes 16416 | tf_op jit(solution)/shard_map/ppermute | solution.py:103
  47.0 0.8 %pad_add_fusion = (s32[4,2048]{1,0:T(4,128)S(1)}, s32[4,2048]{1,0:T(4,128)S(1)}) fusion(s32[4,1024]{1,0:T(4,128)} %collective-permute-done.5, s32[2,1024]{1,0:T(2,128)S(1)} %get-tuple-element.13, s32[2,1024]{1,0:T(2,128)S(1)} %get-tuple-element.12), kind=kLoop, calls=%fused_computation.100 | loop fusion | flops 32768 | bytes 98304 | tf_op jit(solution)/shard_map/concatenate | solution.py:105
  47.8 0.6 pad_add_fusion.1
  48.5 1.6 %fusion.46 = f32[4,16,16,128]{3,2,1,0:T(8,128)S(1)} fusion(f32[16]{0:T(128)} %param.26, f32[16]{0:T(128)} %copy-done.25, f32[16]{0:T(128)} %copy-done.27, f32[16]{0:T(128)} %copy-done.29, f32[16]{0:T(128)} %copy-done.23, f32[16]{0:T(128)} %copy-done.47, pred[4,16,128]{2,1,0:T(8,128)(4,1)S(1)} %get-tuple-element.7, ...), kind=kOutput, calls=%fused_computation.66 | convolution fusion | flops 203309056 | bytes 557440 | tf_op jit(solution)/shard_map/...s,st->...t/dot_general | solution.py:137
  50.8 1.4 %multiply_multiply_fusion = f32[4,16,16,128]{3,2,1,0:T(8,128)} fusion(f32[4,16,16,128]{3,2,1,0:T(8,128)S(1)} %fusion.46, f32[4,16,16]{2,1,0:T(8,128)S(1)} %exponential_select_fusion, f32[4,16,16]{2,1,0:T(8,128)S(1)} %slice_reduce_fusion, f32[16]{0:T(128)S(1)} %copy-done.33, f32[16]{0:T(128)S(1)} %copy-done.26, f32[16]{0:T(128)S(1)} %copy-done.28, ...), kind=kLoop, calls=%fused_computation.65 | loop fusion | flops 2228224 | bytes 1089856 | tf_op jit(solution)/shard_map/mul | solution.py:239
  52.2 1.9 %reshape.272 = f32[4,16,2048]{2,1,0:T(8,128)} reshape(f32[4,16,16,128]{3,2,1,0:T(8,128)} %multiply_multiply_fusion) | data formatting | bytes 1048576 | tf_op jit(solution)/shard_map/reshape | solution.py:239
  54.1 1.3 %subtract_convert_fusion = (bf16[4,16,2048]{2,1,0:T(8,128)(2,1)S(1)}, bf16[4,16,2048]{2,1,0:T(8,128)(2,1)S(1)}) fusion(f32[4,16,2048]{2,1,0:T(8,128)} %reshape.272), kind=kLoop, calls=%fused_computation.63 | loop fusion | flops 524288 | bytes 1048576 | tf_op jit(solution)/shard_map/convert_element_type | solution.py:133
  55.4 1.0 %select_select_fusion = s32[4,2048]{1,0:T(4,128)S(1)} fusion(s32[4,2048]{1,0:T(4,128)} %pad_add_fusion.1, pred[2048]{0:T(1024)(128)(4,1)S(1)} %copy-done.16, pred[2048]{0:T(1024)(128)(4,1)S(1)} %copy-done.17, pred[2048]{0:T(1024)(128)(4,1)S(1)} %copy-done.18, pred[2048]{0:T(1024)(128)(4,1)S(1)} %copy-done.19), kind=kLoop, calls=%fused_computation.104 | loop fusion | flops 106496 | bytes 73728 | tf_op jit(solution)/shard_map/jit(_where)/select_n | solution.py:90
  56.5 2.0 %fusion.2 = f32[4,32,344]{2,1,0:T(8,128)S(1)} fusion(s32[4,2048]{1,0:T(4,128)S(1)} %select_select_fusion, bf16[4,16,2048]{2,1,0:T(8,128)(2,1)S(1)} %get-tuple-element.2, bf16[4,16,2048]{2,1,0:T(8,128)(2,1)S(1)} %get-tuple-element.3), kind=kOutput, calls=%fused_computation.3 | convolution fusion | flops 184221696 | bytes 733184 | tf_op jit(solution)/shard_map/uhp,upg->uhg/dot_general | solution.py:242
  58.5 1.0 %fusion.6 = f32[16,4,64,64]{3,2,0,1:T(8,128)S(1)} fusion(bf16[16,344,64,1]{1,2,0,3:T(8,128)(2,1)S(1)} %bitcast.93, f32[344,64]{0,1:T(8,128)S(1)} %copy-done.6, f32[4,16,344]{2,1,0:T(8,128)S(1)} %slice_add_fusion), kind=kOutput, calls=%fused_computation.10 | convolution fusion | flops 187400192 | bytes 1929216 | tf_op jit(solution)/shard_map/hgp,uhgn->uhpn/dot_general | solution.py:252
  59.6 1.0 %fusion.5 = f32[16,4,64,64]{3,2,0,1:T(8,128)S(1)} fusion(bf16[16,344,64,1]{1,2,0,3:T(8,128)(2,1)S(1)} %bitcast.94, f32[344,64]{0,1:T(8,128)S(1)} %copy-done.6, f32[4,16,344]{2,1,0:T(8,128)S(1)} %slice_add_fusion), kind=kOutput, calls=%fused_computation.8 | convolution fusion | flops 183173120 | bytes 1929216 | tf_op jit(solution)/shard_map/hgp,uhgn->uhpn/dot_general | solution.py:250
  60.7 0.7 %copy-done.49 = f32[4,16,64,128]{3,2,1,0:T(8,128)S(1)} copy-done((f32[4,16,64,128]{3,2,1,0:T(8,128)S(1)}, f32[4,16,64,128]{3,2,1,0:T(8,128)}, u32[]{:S(2)}) %copy-start.49) | copy-done | bytes 2097176
  61.5 4.3 %multiply_reduce_fusion = (f32[4,128,16]{1,2,0:T(8,128)S(1)}, f32[4,128,16,64]{1,3,2,0:T(8,128)S(1)}) fusion(f32[4,128,16,64]{1,3,2,0:T(8,128)S(1)} %bitcast.90, bf16[4,128,16,64]{1,3,2,0:T(8,128)(2,1)S(1)} %bitcast.92, f32[16]{0:T(128)S(1)} %copy-done.45, f32[4,128,16]{1,2,0:T(8,128)S(1)} %copy-done.10, f32[16,4,64,64]{3,2,0,1:T(8,128)S(1)} %fusion.5, ...), kind=kOutput, calls=%fused_computation.26 | convolution fusion | flops 409198592 | bytes 11731456 | tf_op jit(solution)/shard_map/utn,uhpn->uthp/dot_general | solution.py:255
  66.4 0.7 copy-done.2
  67.0 0.7 %convolution_convert_fusion.2 = bf16[4,128,512]{2,1,0:T(8,128)(2,1)S(1)} fusion(bf16[4,128,1024]{1,2,0:T(8,128)(2,1)S(1)} %bitcast.89, bf16[1024,512]{1,0:T(8,128)(2,1)S(1)} %copy-done.2), kind=kOutput, calls=%fused_computation.38 | convolution fusion | flops 537133056 | bytes 2621440 | tf_op jit(solution)/shard_map/gre,ed->grd/dot_general | solution.py:265
  67.8 0.9 %rev.14 = bf16[2,128,512]{2,1,0:T(8,128)(2,1)S(1)} reverse(bf16[2,128,512]{2,1,0:T(8,128)(2,1)S(1)} %slice.189), dimensions={1,2} | reverse | bytes 524288 | tf_op jit(solution)/shard_map/rev | solution.py:272
  69.5 0.6 multiply_reduce_fusion.1
  (144 shorter events, 4.5 us)
Async XLA Ops:
  0.6 9.7 %copy-start = (bf16[512,1152]{1,0:T(8,128)(2,1)S(1)}, bf16[512,1152]{1,0:T(8,128)(2,1)}, u32[]{:S(2)}) copy-start(bf16[512,1152]{1,0:T(8,128)(2,1)} %param.21) | copy-start | bytes 3538948
  1.6 22.7 %collective-permute-start.1 = (s32[2,3]{1,0:T(2,128)S(1)}, s32[2,3]{1,0:T(2,128)S(1)}, u32[]{:S(2)}, u32[]{:S(2)}) collective-permute-start(s32[2,3]{1,0:T(2,128)S(1)} %slice.124), channel_id=1, source_target_pairs={{1,0},{2,1},{3,2},{4,3},{5,4},{6,5},{7,6},{8,7},{9,8},{10,9},{11,1... | collective-permute-start | bytes 80 | tf_op jit(solution)/shard_map/ppermute | solution.py:181
  3.6 20.7 %collective-permute-start = (s32[2,3]{1,0:T(2,128)S(1)}, s32[2,3]{1,0:T(2,128)S(1)}, u32[]{:S(2)}, u32[]{:S(2)}) collective-permute-start(s32[2,3]{1,0:T(2,128)S(1)} %slice.123), channel_id=1, source_target_pairs={{0,1},{1,2},{2,3},{3,4},{4,5},{5,6},{6,7},{7,8},{8,9},{9,10},{10,1... | collective-permute-start | bytes 80 | tf_op jit(solution)/shard_map/ppermute | solution.py:178
  9.5 7.1 %copy-start.14 = (bf16[2,512]{1,0:T(2,128)(2,1)}, bf16[2,512]{1,0:T(2,128)(2,1)S(1)}, u32[]{:S(2)}) copy-start(bf16[2,512]{1,0:T(2,128)(2,1)S(1)} %rev.13) | copy-start | bytes 6148
  10.4 6.2 %copy-start.40 = (f32[4]{0:T(128)}, f32[4]{0:T(128)S(1)}, u32[]{:S(2)}) copy-start(f32[4]{0:T(128)S(1)} %add_rsqrt_fusion.2) | copy-start | bytes 52
  12.2 3.8 %copy-start.7 = (s32[2,128]{1,0:T(2,128)S(1)}, s32[2,128]{1,0:T(2,128)}, u32[]{:S(2)}) copy-start(s32[2,128]{1,0:T(2,128)} %param.18) | copy-start | bytes 3076
  12.2 4.4 %copy-start.12 = (bf16[2,512]{1,0:T(2,128)(2,1)S(1)}, bf16[2,512]{1,0:T(2,128)(2,1)}, u32[]{:S(2)}) copy-start(bf16[2,512]{1,0:T(2,128)(2,1)} %param.19) | copy-start | bytes 6148
  12.2 4.4 %copy-start.20 = (f32[512]{0:T(512)S(1)}, f32[512]{0:T(512)}, u32[]{:S(2)}) copy-start(f32[512]{0:T(512)} %param.20) | copy-start | bytes 6148
  12.2 4.4 %copy-start.41 = (bf16[512,16]{0,1:T(8,128)(2,1)S(1)}, bf16[512,16]{0,1:T(8,128)(2,1)}, u32[]{:S(2)}) copy-start(bf16[512,16]{0,1:T(8,128)(2,1)} %param.23) | copy-start | bytes 49156
  12.2 4.6 %copy-start.44 = (f32[16]{0:T(128)S(1)}, f32[16]{0:T(128)}, u32[]{:S(2)}) copy-start(f32[16]{0:T(128)} %param.27) | copy-start | bytes 196
  14.8 4.1 %copy-start.32 = (f32[16]{0:T(128)S(1)}, f32[16]{0:T(128)}, u32[]{:S(2)}) copy-start(f32[16]{0:T(128)} %param.26) | copy-start | bytes 196
  14.8 6.3 %copy-start.31 = (f32[1024]{0:T(1024)S(1)}, f32[1024]{0:T(1024)}, u32[]{:S(2)}) copy-start(f32[1024]{0:T(1024)} %param.29) | copy-start | bytes 12292
  14.8 7.0 %copy-start.36 = (bf16[512,2]{0,1:T(2,128)(2,1)S(1)}, bf16[512,2]{0,1:T(2,128)(2,1)}, u32[]{:S(2)}) copy-start(bf16[512,2]{0,1:T(2,128)(2,1)} %param.32) | copy-start | bytes 6148
  14.8 8.3 %copy-start.42 = (f32[2,2,128]{2,1,0:T(2,128)S(1)}, f32[2,2,128]{2,1,0:T(2,128)}, u32[]{:S(2)}) copy-start(f32[2,2,128]{2,1,0:T(2,128)} %param.34) | copy-start | bytes 6148
  16.8 10.3 %copy-start.23 = (f32[16]{0:T(128)}, f32[16]{0:T(128)S(1)}, u32[]{:S(2)}) copy-start(f32[16]{0:T(128)S(1)} %get-tuple-element.30) | copy-start | bytes 196
  16.8 10.3 %copy-start.25 = (f32[16]{0:T(128)}, f32[16]{0:T(128)S(1)}, u32[]{:S(2)}) copy-start(f32[16]{0:T(128)S(1)} %get-tuple-element.31) | copy-start | bytes 196
  16.8 10.3 %copy-start.27 = (f32[16]{0:T(128)}, f32[16]{0:T(128)S(1)}, u32[]{:S(2)}) copy-start(f32[16]{0:T(128)S(1)} %get-tuple-element.32) | copy-start | bytes 196
  16.9 10.3 %copy-start.29 = (f32[16]{0:T(128)}, f32[16]{0:T(128)S(1)}, u32[]{:S(2)}) copy-start(f32[16]{0:T(128)S(1)} %get-tuple-element.33) | copy-start | bytes 196
  16.9 10.2 %copy-start.47 = (f32[16]{0:T(128)}, f32[16]{0:T(128)S(1)}, u32[]{:S(2)}) copy-start(f32[16]{0:T(128)S(1)} %exponential_negate_fusion) | copy-start | bytes 196
  17.0 10.1 %copy-start.34 = (pred[4,16]{1,0:T(4,128)(4,1)}, pred[4,16]{1,0:T(4,128)(4,1)S(1)}, u32[]{:S(2)}) copy-start(pred[4,16]{1,0:T(4,128)(4,1)S(1)} %iota_compare_fusion.16) | copy-start | bytes 196
  24.5 8.6 %copy-start.21 = (s32[4,128]{1,0:T(4,128)}, s32[4,128]{1,0:T(4,128)S(1)}, u32[]{:S(2)}) copy-start(s32[4,128]{1,0:T(4,128)S(1)} %get-tuple-element.24) | copy-start | bytes 6148
  24.5 6.1 %collective-permute-start.2 = (s32[4,128]{1,0:T(4,128)S(1)}, s32[4,128]{1,0:T(4,128)S(1)}, u32[]{:S(2)}, u32[]{:S(2)}) collective-permute-start(s32[4,128]{1,0:T(4,128)S(1)} %get-tuple-element.24), channel_id=1, source_target_pairs={{0,1},{1,0},{2,3},{3,2},{4,5},{5,4},{6,7},{7,6},{8,9},{9,8},{10,11... | collective-permute-start | bytes 6152 | tf_op jit(solution)/shard_map/ppermute | solution.py:103
  30.7 4.4 %collective-permute-start.3 = (s32[4,256]{1,0:T(4,128)S(1)}, s32[4,256]{1,0:T(4,128)S(1)}, u32[]{:S(2)}, u32[]{:S(2)}) collective-permute-start(s32[4,256]{1,0:T(4,128)S(1)} %pad_add_fusion.7), channel_id=1, source_target_pairs={{0,2},{1,3},{2,0},{3,1},{4,6},{5,7},{6,4},{7,5},{8,10},{9,11},{10,... | collective-permute-start | bytes 12296 | tf_op jit(solution)/shard_map/ppermute | solution.py:103
  35.1 6.2 %copy-start.3 = (bf16[4,128,1024]{1,2,0:T(8,128)(2,1)}, bf16[4,128,1024]{1,2,0:T(8,128)(2,1)S(1)}, u32[]{:S(2)}) copy-start(bf16[4,128,1024]{1,2,0:T(8,128)(2,1)S(1)} %copy.30) | copy-start | bytes 3145732
  35.1 6.2 %collective-permute-start.4 = (s32[4,512]{1,0:T(4,128)S(1)}, s32[4,512]{1,0:T(4,128)S(1)}, u32[]{:S(2)}, u32[]{:S(2)}) collective-permute-start(s32[4,512]{1,0:T(4,128)S(1)} %pad_add_fusion.5), channel_id=1, source_target_pairs={{0,4},{1,5},{2,6},{3,7},{4,0},{5,1},{6,2},{7,3},{8,12},{9,13},{10,... | collective-permute-start | bytes 24584 | tf_op jit(solution)/shard_map/ppermute | solution.py:103
  41.9 5.0 %collective-permute-start.5 = (s32[4,1024]{1,0:T(4,128)}, s32[4,1024]{1,0:T(4,128)}, u32[]{:S(2)}, u32[]{:S(2)}) collective-permute-start(s32[4,1024]{1,0:T(4,128)} %pad_add_fusion.3), channel_id=1, source_target_pairs={{0,8},{1,9},{2,10},{3,11},{4,12},{5,13},{6,14},{7,15},{8,0},{9,1},... | collective-permute-start | bytes 49160 | tf_op jit(solution)/shard_map/ppermute | solution.py:103
  45.8 4.7 %copy-start.9 = (pred[4,16,16]{2,1,0:T(8,128)(4,1)S(1)}, pred[4,16,16]{2,1,0:T(8,128)(4,1)}, u32[]{:S(2)}) copy-start(pred[4,16,16]{2,1,0:T(8,128)(4,1)} %broadcast_and_fusion) | copy-start | bytes 3076
  45.8 4.9 %copy-start.35 = (pred[4,16]{1,0:T(4,128)(4,1)S(1)}, pred[4,16]{1,0:T(4,128)(4,1)}, u32[]{:S(2)}) copy-start(pred[4,16]{1,0:T(4,128)(4,1)} %copy-done.34) | copy-start | bytes 196
  45.8 4.9 %copy-start.24 = (f32[16]{0:T(128)S(1)}, f32[16]{0:T(128)}, u32[]{:S(2)}) copy-start(f32[16]{0:T(128)} %copy-done.23) | copy-start | bytes 196
  45.8 4.9 %copy-start.26 = (f32[16]{0:T(128)S(1)}, f32[16]{0:T(128)}, u32[]{:S(2)}) copy-start(f32[16]{0:T(128)} %copy-done.25) | copy-start | bytes 196
  45.8 4.9 %copy-start.28 = (f32[16]{0:T(128)S(1)}, f32[16]{0:T(128)}, u32[]{:S(2)}) copy-start(f32[16]{0:T(128)} %copy-done.27) | copy-start | bytes 196
  45.8 4.9 %copy-start.30 = (f32[16]{0:T(128)S(1)}, f32[16]{0:T(128)}, u32[]{:S(2)}) copy-start(f32[16]{0:T(128)} %copy-done.29) | copy-start | bytes 196
  45.8 4.9 %copy-start.33 = (f32[16]{0:T(128)S(1)}, f32[16]{0:T(128)}, u32[]{:S(2)}) copy-start(f32[16]{0:T(128)} %param.26) | copy-start | bytes 196
  50.1 5.3 %copy-start.16 = (pred[2048]{0:T(1024)(128)(4,1)S(1)}, pred[2048]{0:T(1024)(128)(4,1)}, u32[]{:S(2)}) copy-start(pred[2048]{0:T(1024)(128)(4,1)} %get-tuple-element.40) | copy-start | bytes 6148
  50.1 5.3 %copy-start.17 = (pred[2048]{0:T(1024)(128)(4,1)S(1)}, pred[2048]{0:T(1024)(128)(4,1)}, u32[]{:S(2)}) copy-start(pred[2048]{0:T(1024)(128)(4,1)} %get-tuple-element.41) | copy-start | bytes 6148
  50.1 5.3 %copy-start.18 = (pred[2048]{0:T(1024)(128)(4,1)S(1)}, pred[2048]{0:T(1024)(128)(4,1)}, u32[]{:S(2)}) copy-start(pred[2048]{0:T(1024)(128)(4,1)} %get-tuple-element.42) | copy-start | bytes 6148
  50.1 5.3 %copy-start.19 = (pred[2048]{0:T(1024)(128)(4,1)S(1)}, pred[2048]{0:T(1024)(128)(4,1)}, u32[]{:S(2)}) copy-start(pred[2048]{0:T(1024)(128)(4,1)} %get-tuple-element.43) | copy-start | bytes 6148
  56.5 2.0 %copy-start.5 = (bf16[344,1024]{0,1:T(8,128)(2,1)S(1)}, bf16[344,1024]{0,1:T(8,128)(2,1)}, u32[]{:S(2)}) copy-start(bf16[344,1024]{0,1:T(8,128)(2,1)} %copy.32) | copy-start | bytes 2113540
  56.5 2.0 %copy-start.6 = (f32[344,64]{0,1:T(8,128)S(1)}, f32[344,64]{0,1:T(8,128)}, u32[]{:S(2)}) copy-start(f32[344,64]{0,1:T(8,128)} %copy.31) | copy-start | bytes 264196
  61.5 4.4 %copy-start.8 = (f32[16,64]{1,0:T(8,128)S(1)}, f32[16,64]{1,0:T(8,128)}, u32[]{:S(2)}) copy-start(f32[16,64]{1,0:T(8,128)} %mul.244) | copy-start | bytes 12292
  66.3 2.4 %copy-start.13 = (bf16[2,512]{1,0:T(2,128)(2,1)S(1)}, bf16[2,512]{1,0:T(2,128)(2,1)}, u32[]{:S(2)}) copy-start(bf16[2,512]{1,0:T(2,128)(2,1)} %param.19) | copy-start | bytes 6148
  66.3 2.4 %copy-start.15 = (bf16[2,512]{1,0:T(2,128)(2,1)S(1)}, bf16[2,512]{1,0:T(2,128)(2,1)}, u32[]{:S(2)}) copy-start(bf16[2,512]{1,0:T(2,128)(2,1)} %copy-done.14) | copy-start | bytes 6148
  66.3 2.4 %copy-start.22 = (s32[4,128]{1,0:T(4,128)S(1)}, s32[4,128]{1,0:T(4,128)}, u32[]{:S(2)}) copy-start(s32[4,128]{1,0:T(4,128)} %copy-done.21) | copy-start | bytes 6148
  67.0 2.1 %copy-start.37 = (bf16[512,2]{0,1:T(2,128)(2,1)S(1)}, bf16[512,2]{0,1:T(2,128)(2,1)}, u32[]{:S(2)}) copy-start(bf16[512,2]{0,1:T(2,128)(2,1)} %param.32) | copy-start | bytes 6148
  67.0 2.1 %copy-start.38 = (bf16[512,2]{0,1:T(2,128)(2,1)S(1)}, bf16[512,2]{0,1:T(2,128)(2,1)}, u32[]{:S(2)}) copy-start(bf16[512,2]{0,1:T(2,128)(2,1)} %rev.15) | copy-start | bytes 6148
  67.0 2.2 %copy-start.43 = (f32[512]{0:T(512)S(1)}, f32[512]{0:T(512)}, u32[]{:S(2)}) copy-start(f32[512]{0:T(512)} %param.31) | copy-start | bytes 6148
  67.0 2.4 %copy-start.39 = (s32[2,2,128]{2,1,0:T(2,128)S(1)}, s32[2,2,128]{2,1,0:T(2,128)}, u32[]{:S(2)}) copy-start(s32[2,2,128]{2,1,0:T(2,128)} %param.33) | copy-start | bytes 6148
  67.0 2.5 %copy-start.48 = (f32[2,2,128]{2,1,0:T(2,128)S(1)}, f32[2,2,128]{2,1,0:T(2,128)}, u32[]{:S(2)}) copy-start(f32[2,2,128]{2,1,0:T(2,128)} %fusion.33) | copy-start | bytes 6148
  (8 other events, 9.6 us)

commit v4 on v3

--- a/solution.py
+++ b/solution.py
@@ -175,18 +175,21 @@
     neg_rate = -jnp.exp(a_log)[:, None]
 
     rc_tok = (BASES - 1) - tokens[:, ::-1]
-    fwd_rim = lax.ppermute(
-        tokens[:, count - (KW - 1) :], "seq", [(src, src + 1) for src in range(nseq - 1)]
-    )
-    rc_rim = lax.ppermute(
-        rc_tok[:, count - (KW - 1) :], "seq", [(src, src - 1) for src in range(1, nseq)]
-    )
     local_tok = jnp.concatenate([tokens, rc_tok], axis=0)
-    ext = jnp.concatenate([jnp.concatenate([fwd_rim, rc_rim], axis=0), local_tok], axis=1)
     pos0 = jnp.concatenate(
         [jnp.full((windows, 1), place * count), jnp.full((windows, 1), (nseq - 1 - place) * count)]
     ).astype(jnp.int32)
-    local_gram = gram_ids(ext, pos0 + jnp.arange(count, dtype=jnp.int32)[None, :])
+
+    seq_tok = gather_all(tokens, rc_tok, "seq")
+    ext_all = jnp.concatenate([jnp.zeros((streams, KW - 1), seq_tok.dtype), seq_tok], axis=1)
+    gram = gram_ids(ext_all, jnp.broadcast_to(jnp.arange(total, dtype=jnp.int32), (streams, total)))
+    local_gram = jnp.concatenate(
+        [
+            lax.dynamic_slice_in_dim(gram[:windows], place * count, count, axis=1),
+            lax.dynamic_slice_in_dim(gram[windows:], (nseq - 1 - place) * count, count, axis=1),
+        ],
+        axis=0,
+    )
 
     oh_loc = onehot(local_gram, GRAMS)
     x_loc = jnp.einsum("rtg,gc->rtc", oh_loc, x_tab, preferred_element_type=jnp.float32).astype(
@@ -217,9 +220,6 @@
     weights = (scores[:, None] * decays * dt_u[:, :, None, :]).astype(jnp.bfloat16)
     y_intra = jnp.einsum("uhts,ushp->uthp", weights, x_u, preferred_element_type=jnp.float32)
 
-    seq_tok = gather_all(tokens, rc_tok, "seq")
-    ext_all = jnp.concatenate([jnp.zeros((streams, KW - 1), seq_tok.dtype), seq_tok], axis=1)
-    gram = gram_ids(ext_all, jnp.broadcast_to(jnp.arange(total, dtype=jnp.int32), (streams, total)))
     dt_all = jax.nn.softplus(heads_lookup(dt_rows, seq_tok) + dt_bias[:, None])
     ld_all = neg_rate * dt_all
     cum = block_cumsum(ld_all.reshape(streams, HEADS, nblk, BLK), tri)
@@ -236,11 +236,11 @@
     )
     span = jnp.sum(jnp.where(between[:, None], total_u[:, :, None, :], 0.0), axis=3)
     across = jnp.where(blk_idx[None, None, :] < first_blk[:, None, None], jnp.exp(span), 0.0)
-    weight = (jnp.repeat(within, nloc, axis=0) * across[..., None]).reshape(units, HEADS, total)
+    weight = jnp.repeat(within, nloc, axis=0) * across[..., None]
     w_hi, w_lo = split_bf16(weight)
-    oh_all = jnp.repeat(onehot(gram, GRAMS), nloc, axis=0)
+    oh_all = jnp.repeat(onehot(gram, GRAMS), nloc, axis=0).reshape(units, nblk, BLK, GRAMS)
     per_gram = jnp.einsum(
-        "uhp,upg->uhg",
+        "uhbs,ubsg->uhg",
         jnp.concatenate([w_hi, w_lo], axis=1),
         oh_all,
         preferred_element_type=jnp.float32,

time: 71 us -> 62.5 us (0.88)
  starting transfers between devices: 12.8 us -> 8.28 us
  other arithmetic: 12.8 us -> 9.67 us
  local copies, waits for them, and re-layouts: 15.3 us -> 12.8 us
  waiting for transfers between devices: 1.11 us -> 2.6 us
  matrix products: 26.4 us -> 27.2 us
    ppermute x2 -> x0, starting transfers between devices: 4.3 us -> none  [the longest x1 3.02 us: local(): lax.ppermute(tokens[:, count - (KW - 1):], 'seq', [(src, src + 1) for src...]
    unnamed x101 -> x60, local copies, waits for them, and re-layouts: 3.44 us -> 1.12 us
    dot_general x1, matrix products: 4.51 us -> 2.58 us  [local(): jnp.einsum('uhts,ushp->uthp', weights, x_u, preferred_element_type=jnp.fl...]
    reshape x1 -> x0, local copies, waits for them, and re-layouts: 1.92 us -> none  [local(): (jnp.repeat(within, nloc, axis=0) * across[..., None]).reshape(units, HEA...]
    ppermute x4, waiting for transfers between devices: 1.11 us -> 2.6 us  [gather_all(): lax.ppermute(held, axis, [(src, src ^ mask) for src in range(count)])]
    mul x1 -> x0, other arithmetic: 1.41 us -> none  [local(): jnp.repeat(within, nloc, axis=0) * across[..., None]]
    dot_general x1, matrix products: 0.97 us -> 2.34 us  [local(): jnp.einsum('hgp,uhgn->uhpn', x_heads, b_hi, preferred_element_type=jnp.fl...]
    dot_general x1, matrix products: 0.97 us -> 2.29 us  [local(): jnp.einsum('hgp,uhgn->uhpn', x_heads, b_lo, preferred_element_type=jnp.fl...]
  transfers between devices with their start and end apart: 6 -> 4, of which waited for: 1 -> 2; matrix products, arithmetic and copies ran while one was open for 40% -> 35% of each run, Pallas kernels for 0% -> 0%
where the time goes in v4:
time: 62.5 us; the launch traced here: 61.8 us
  matrix products  27.2 us (44%)
  local copies, waits for them, and re-layouts  12.8 us (20%)
  other arithmetic  9.67 us (15%)
  starting transfers between devices  8.28 us (13%)
  waiting for transfers between devices  2.6 us (4%)
  between operations  1.27 us (2%)
    ppermute x4, starting transfers between devices, gather_all(): lax.ppermute(held, axis, [(src, src ^ mask) for src in range(count)])  8.28 us
    dot_general x1, matrix products, local(): jnp.einsum('utn,uhpn->uthp', c_u, start_state, precision=HIGH)  4.37 us
    dot_general x1, matrix products, local(): jnp.einsum('rtk,kc->rtc', oh_tok, z_rows, preferred_element_type=jnp.floa...  2.73 us
    ppermute x4, waiting for transfers between devices, gather_all(): lax.ppermute(held, axis, [(src, src ^ mask) for src in range(count)])  2.6 us
    dot_general x1, matrix products, local(): jnp.einsum('uhts,ushp->uthp', weights, x_u, preferred_element_type=jnp.fl...  2.58 us
    rev x1, local copies, waits for them, and re-layouts, local(): head_full = jnp.concatenate([w_head_half, w_head_half[::-1, ::-1]], axis=1)  2.57 us
    dot_general x1, matrix products, local(): jnp.einsum('hgp,uhgn->uhpn', x_heads, b_hi, preferred_element_type=jnp.fl...  2.34 us
    dot_general x1, matrix products, local(): jnp.einsum('hgp,uhgn->uhpn', x_heads, b_lo, preferred_element_type=jnp.fl...  2.29 us
  transfers between devices with their start and end apart: 4, of which 2 were waited for; matrix products, arithmetic and copies ran while one was open for 35% of the time, Pallas kernels for 0%

profile of v4, /device:TPU:0, one launch (start us, length us, event | category | flops | bytes accessed | tf_op | source)
XLA Modules:
  0.0 61.8 jit_solution(16927078339521414156)
XLA Ops:
  0.7 0.9 %rev.12 = s32[2,128]{1,0:T(2,128)S(1)} reverse(s32[2,128]{1,0:T(2,128)} %param.18), dimensions={1} | reverse | bytes 2048 | tf_op jit(solution)/shard_map/rev | solution.py:177
  1.6 0.7 %pad_add_fusion.8 = s32[4,128]{1,0:T(4,128)S(1)} fusion(s32[2,128]{1,0:T(2,128)S(1)} %broadcast_subtract_fusion, s32[2,128]{1,0:T(2,128)} %param.18), kind=kLoop, calls=%fused_computation.159 | loop fusion | flops 512 | bytes 4096 | tf_op jit(solution)/shard_map/concatenate | solution.py:178
  2.3 0.5 collective-permute-start
  2.7 0.7 %broadcast_compare_fusion.7 = (pred[4,128]{1,0:T(4,128)(4,1)S(1)}, pred[4,128]{1,0:T(4,128)(4,1)S(1)}, pred[4,128]{1,0:T(4,128)(4,1)S(1)}, pred[4,128]{1,0:T(4,128)(4,1)S(1)}) fusion(s32[2,128]{1,0:T(2,128)S(1)} %broadcast_subtract_fusion, s32[2,128]{1,0:T(2,128)} %param.18), kind=kLoop, calls=%fused_computation.173 | loop fusion | flops 2560 | bytes 4096 | tf_op jit(solution)/shard_map/eq | solution.py:122
  3.4 1.6 %rev.13 = bf16[2,512]{1,0:T(2,128)(2,1)S(1)} reverse(bf16[2,512]{1,0:T(2,128)(2,1)} %param.19), dimensions={0,1} | reverse | bytes 4096 | tf_op jit(solution)/shard_map/rev | solution.py:169
  5.0 0.8 %fusion.77 = f32[4]{0:T(128)S(1)} fusion(bf16[2,512]{1,0:T(2,128)(2,1)S(1)} %rev.13, bf16[2,512]{1,0:T(2,128)(2,1)} %param.19), kind=kLoop, calls=%fused_computation.125 | loop fusion | flops 12284 | bytes 4112 | tf_op jit(solution)/shard_map/reduce_sum | solution.py:23
  5.8 0.9 %fusion.98 = f32[4,16]{1,0:T(4,128)S(1)} fusion(bf16[512,16]{0,1:T(8,128)(2,1)} %param.23, f32[512]{0:T(512)} %param.20, f32[4]{0:T(128)S(1)} %add_rsqrt_fusion.2, bf16[2,512]{1,0:T(2,128)(2,1)S(1)} %rev.13, bf16[2,512]{1,0:T(2,128)(2,1)} %param.19), kind=kOutput, calls=%fused_computation.190 | convolution fusion | flops 79872 | bytes 22800 | tf_op jit(solution)/shard_map/dot_general | solution.py:76
  6.8 0.7 %exponential_negate_fusion = f32[16]{0:T(128)S(1)} fusion(f32[16]{0:T(128)} %param.27), kind=kLoop, calls=%fused_computation.178 | loop fusion | flops 16 | bytes 128 | tf_op jit(solution)/shard_map/neg | solution.py:175
  7.5 1.0 %fusion.13 = f32[4,1152]{1,0:T(4,128)S(1)} fusion(bf16[512,1152]{1,0:T(8,128)(2,1)S(1)} %copy-done, f32[512]{0:T(512)} %param.20, f32[4]{0:T(128)S(1)} %add_rsqrt_fusion.2, bf16[2,512]{1,0:T(2,128)(2,1)S(1)} %rev.13, bf16[2,512]{1,0:T(2,128)(2,1)} %param.19), kind=kOutput, calls=%fused_computation.18 | convolution fusion | flops 4742144 | bytes 1204240 | tf_op jit(solution)/shard_map/dot_general | solution.py:74
  8.5 0.8 %broadcast_multiply_fusion = f32[4,4,1152]{2,1,0:T(4,128)S(1)} fusion(f32[4,1152]{1,0:T(4,128)S(1)} %fusion.13, f32[4,1152]{1,0:T(4,128)} %param.24), kind=kLoop, calls=%fused_computation.98 | loop fusion | flops 18432 | bytes 110592 | tf_op jit(solution)/shard_map/mul | solution.py:77
  9.4 1.4 %compare_select_fusion.2 = f32[4,16,128]{2,1,0:T(8,128)} fusion(f32[16]{0:T(128)} %param.26, f32[16]{0:T(128)S(1)} %get-tuple-element.31, f32[16]{0:T(128)S(1)} %get-tuple-element.32, f32[16]{0:T(128)S(1)} %get-tuple-element.33, f32[16]{0:T(128)S(1)} %get-tuple-element.30, pred[4,128]{1,0:T(4,128)(4,1)S(1)} %get-tuple-element.28, ...), kind=kLoop, calls=%fused_computation.91 | loop fusion | flops 114688 | bytes 35136 | tf_op jit(solution)/shard_map/jit(softplus)/select_n | solution.py:201
  10.7 0.9 %fusion.71 = f32[4,16,128]{2,1,0:T(8,128)S(1)} fusion(f32[16]{0:T(128)S(1)} %exponential_negate_fusion, f32[16]{0:T(128)} %param.26, f32[16]{0:T(128)S(1)} %get-tuple-element.31, f32[16]{0:T(128)S(1)} %get-tuple-element.32, f32[16]{0:T(128)S(1)} %get-tuple-element.33, f32[16]{0:T(128)S(1)} %get-tuple-element.30, pred[4,128]{1,0:T(4,128)(4,1)S(1)} %get-tuple-element.28, ...), kind=kOutput, calls=%fused_computation.97 | convolution fusion | flops 12722176 | bytes 35200 | tf_op jit(solution)/shard_map/...s,st->...t/dot_general | solution.py:137
  11.6 0.6 %exponential_bitcast_fusion = f32[4,128,16]{1,2,0:T(8,128)} fusion(f32[4,16,128]{2,1,0:T(8,128)S(1)} %fusion.71), kind=kLoop, calls=%fused_computation.104 | loop fusion | bytes 65536 | tf_op jit(solution)/shard_map/exp | solution.py:256
  12.3 2.7 %fusion.40 = f32[4,128,1024]{1,2,0:T(8,128)} fusion(bf16[512,1024]{1,0:T(8,128)(2,1)S(1)} %copy-done.3, s32[4,128]{1,0:T(4,128)S(1)} %pad_add_fusion.8, f32[512]{0:T(512)} %param.20, f32[4]{0:T(128)S(1)} %add_rsqrt_fusion.2, bf16[2,512]{1,0:T(2,128)(2,1)S(1)} %rev.13, bf16[2,512]{1,0:T(2,128)(2,1)} %param.19), kind=kOutput, calls=%fused_computation.56 | convolution fusion | flops 8409088 | bytes 3153936 | tf_op jit(solution)/shard_map/rtk,kc->rtc/dot_general | solution.py:200
  15.1 1.6 %divide_multiply_fusion = f32[344,1152]{1,0:T(8,128)S(1)} fusion(f32[16,1152]{1,0:T(8,128)S(1)} %mul.201, f32[344,16]{1,0:T(8,128)S(1)} %copy-done.23, f32[1152]{0:T(1024)S(1)} %copy-done.18), kind=kOutput, calls=%fused_computation.34 | convolution fusion | flops 78068736 | bytes 1685504 | tf_op jit(solution)/shard_map/dot_general | solution.py:78
  16.7 0.6 %fusion.34 = f32[2,2,128]{2,1,0:T(2,128)} fusion(f32[2,2,128]{2,1,0:T(2,128)S(1)} %copy-done.19), kind=kOutput, calls=%fused_computation.47 | output fusion | flops 769 | bytes 4096 | tf_op jit(solution)/shard_map/sub | solution.py:283
  17.4 2.6 %collective-permute-start.1 = (s32[4,256]{1,0:T(4,128)S(1)}, s32[4,256]{1,0:T(4,128)S(1)}, u32[]{:S(2)}, u32[]{:S(2)}) collective-permute-start(s32[4,256]{1,0:T(4,128)S(1)} %pad_add_fusion.7), channel_id=1, source_target_pairs={{0,2},{1,3},{2,0},{3,1},{4,6},{5,7},{6,4},{7,5},{8,10},{9,11},{10,... | collective-permute-start | bytes 12296 | tf_op jit(solution)/shard_map/ppermute | solution.py:103
  20.0 0.6 convert_compare_fusion
  20.6 1.0 %collective-permute-done.1 = s32[4,256]{1,0:T(4,128)S(1)} collective-permute-done((s32[4,256]{1,0:T(4,128)S(1)}, s32[4,256]{1,0:T(4,128)S(1)}, u32[]{:S(2)}, u32[]{:S(2)}) %collective-permute-start.1) | collective-permute-done | bytes 4128 | tf_op jit(solution)/shard_map/ppermute | solution.py:103
  21.6 2.1 %collective-permute-start.2 = (s32[4,512]{1,0:T(4,128)S(1)}, s32[4,512]{1,0:T(4,128)S(1)}, u32[]{:S(2)}, u32[]{:S(2)}) collective-permute-start(s32[4,512]{1,0:T(4,128)S(1)} %pad_add_fusion.5), channel_id=1, source_target_pairs={{0,4},{1,5},{2,6},{3,7},{4,0},{5,1},{6,2},{7,3},{8,12},{9,13},{10,... | collective-permute-start | bytes 24584 | tf_op jit(solution)/shard_map/ppermute | solution.py:103
  23.8 1.6 %collective-permute-done.2 = s32[4,512]{1,0:T(4,128)S(1)} collective-permute-done((s32[4,512]{1,0:T(4,128)S(1)}, s32[4,512]{1,0:T(4,128)S(1)}, u32[]{:S(2)}, u32[]{:S(2)}) %collective-permute-start.2) | collective-permute-done | bytes 8224 | tf_op jit(solution)/shard_map/ppermute | solution.py:103
  25.4 3.1 %collective-permute-start.3 = (s32[4,1024]{1,0:T(4,128)S(1)}, s32[4,1024]{1,0:T(4,128)}, u32[]{:S(2)}, u32[]{:S(2)}) collective-permute-start(s32[4,1024]{1,0:T(4,128)S(1)} %pad_add_fusion.3), channel_id=1, source_target_pairs={{0,8},{1,9},{2,10},{3,11},{4,12},{5,13},{6,14},{7,15},{8,0},{9,1},... | collective-permute-start | bytes 49160 | tf_op jit(solution)/shard_map/ppermute | solution.py:103
  28.7 0.7 %slice.174 = f32[344,64]{1,0:T(8,128)} slice(f32[344,1152]{1,0:T(8,128)S(1)} %divide_multiply_fusion), slice={[0:344], [1024:1088]} | slice | bytes 176128 | tf_op jit(solution)/shard_map/slice | solution.py:172
  29.3 1.2 %copy.35 = bf16[344,1024]{0,1:T(8,128)(2,1)} copy(bf16[344,1024]{1,0:T(8,128)(2,1)S(1)} %slice.219) | data formatting | bytes 1409024 | tf_op jit(solution)/shard_map/slice | solution.py:171
  30.5 1.1 %copy.34 = f32[344,64]{0,1:T(8,128)S(1)} copy(f32[344,64]{1,0:T(8,128)} %slice.174) | data formatting | bytes 176128 | tf_op jit(solution)/shard_map/slice | solution.py:172
  31.6 0.8 %mul.226 = f32[16,64]{1,0:T(8,128)S(1)} reshape(f32[1024]{0:T(1024)} %param.29) | data formatting | bytes 8192 | tf_op jit(solution)/shard_map/mul | solution.py:23
  32.3 2.6 %rev.15 = bf16[512,2]{0,1:T(2,128)(2,1)} reverse(bf16[512,2]{0,1:T(2,128)(2,1)} %param.32), dimensions={0,1} | reverse | bytes 4096 | tf_op jit(solution)/shard_map/rev | solution.py:279
  34.9 0.8 %pad_add_fusion = (s32[4,2048]{1,0:T(4,128)S(1)}, s32[4,2048]{1,0:T(4,128)S(1)}) fusion(s32[4,1024]{1,0:T(4,128)} %collective-permute-done.3, s32[2,1024]{1,0:T(2,128)S(1)} %get-tuple-element.15, s32[2,1024]{1,0:T(2,128)S(1)} %get-tuple-element.14), kind=kLoop, calls=%fused_computation.101 | loop fusion | flops 32768 | bytes 98304 | tf_op jit(solution)/shard_map/concatenate | solution.py:105
  36.1 2.1 %convolution_convert_fusion.1 = bf16[4,128,1024]{2,1,0:T(8,128)(2,1)S(1)} fusion(s32[4,128]{1,0:T(4,128)S(1)} %pad_add_fusion.9, f32[344,1152]{1,0:T(8,128)} %copy-done.1), kind=kOutput, calls=%fused_computation.36 | convolution fusion | flops 361410560 | bytes 1755136 | tf_op jit(solution)/shard_map/rtg,gc->rtc/dot_general | solution.py:195
  38.2 1.3 %fusion.39 = f32[4,128,128]{1,2,0:T(8,128)S(1)} fusion(s32[4,128]{1,0:T(4,128)S(1)} %pad_add_fusion.9, f32[344,1152]{1,0:T(8,128)} %copy-done.1), kind=kOutput, calls=%fused_computation.53 | convolution fusion | flops 270708736 | bytes 440320 | tf_op jit(solution)/shard_map/rtg,gc->rtc/dot_general | solution.py:198
  39.7 0.9 %fusion.45 = f32[4,16,16,128]{3,2,1,0:T(8,128)S(1)} fusion(f32[16]{0:T(128)S(1)} %copy-done.12, f32[16]{0:T(128)S(1)} %get-tuple-element.31, f32[16]{0:T(128)S(1)} %get-tuple-element.32, f32[16]{0:T(128)S(1)} %copy-done.11, f32[16]{0:T(128)S(1)} %get-tuple-element.30, f32[16]{0:T(128)S(1)} %copy-done.25, pred[4,16,128]{2,1,0:T(8,128)(4,1)S(1)} %get-tuple-element.7, ...), kind=kOutput, calls=%fused_computation.66 | convolution fusion | flops 203309056 | bytes 557440 | tf_op jit(solution)/shard_map/...s,st->...t/dot_general | solution.py:137
  40.6 0.4 slice_reduce_fusion
  41.2 0.7 %subtract_convert_fusion = (bf16[4,16,16,128]{3,2,1,0:T(8,128)(2,1)S(1)}, bf16[4,16,16,128]{3,2,1,0:T(8,128)(2,1)S(1)}) fusion(f32[4,16,16]{2,1,0:T(8,128)S(1)} %exponential_select_fusion, f32[16]{0:T(128)S(1)} %copy-done.12, f32[16]{0:T(128)S(1)} %get-tuple-element.31, pred[4,16,128]{2,1,0:T(8,128)(4,1)S(1)} %get-tuple-element.7, ...), kind=kLoop, calls=%fused_computation.63 | loop fusion | flops 2752512 | bytes 1089856 | tf_op jit(solution)/shard_map/convert_element_type | solution.py:133
  41.9 2.1 %fusion.32 = f32[4,32,344]{2,1,0:T(8,128)S(1)} fusion(s32[4,16,128]{2,1,0:T(8,128)S(1)} %bitcast.103, bf16[4,32,16,128]{3,2,1,0:T(8,128)(2,1)S(1)} %pad_maximum_fusion), kind=kOutput, calls=%fused_computation.44 | convolution fusion | flops 183173120 | bytes 733184 | tf_op jit(solution)/shard_map/uhbs,ubsg->uhg/dot_general | solution.py:242
  44.1 2.3 %fusion.6 = f32[16,4,64,64]{3,2,0,1:T(8,128)} fusion(bf16[16,344,64,1]{1,2,0,3:T(8,128)(2,1)S(1)} %bitcast.99, f32[344,64]{0,1:T(8,128)S(1)} %copy.34, f32[4,16,344]{2,1,0:T(8,128)S(1)} %slice_add_fusion), kind=kOutput, calls=%fused_computation.10 | convolution fusion | flops 187400192 | bytes 1929216 | tf_op jit(solution)/shard_map/hgp,uhgn->uhpn/dot_general | solution.py:252
  46.4 2.3 %fusion.5 = f32[16,4,64,64]{3,2,0,1:T(8,128)} fusion(bf16[16,344,64,1]{1,2,0,3:T(8,128)(2,1)S(1)} %bitcast.100, f32[344,64]{0,1:T(8,128)S(1)} %copy.34, f32[4,16,344]{2,1,0:T(8,128)S(1)} %slice_add_fusion), kind=kOutput, calls=%fused_computation.8 | convolution fusion | flops 183173120 | bytes 1929216 | tf_op jit(solution)/shard_map/hgp,uhgn->uhpn/dot_general | solution.py:250
  48.7 0.8 %copy.32 = bf16[4,128,1024]{1,2,0:T(8,128)(2,1)S(1)} copy(bf16[4,128,1024]{2,1,0:T(8,128)(2,1)S(1)} %convolution_convert_fusion.1) | data formatting | bytes 2097152 | tf_op jit(solution)/shard_map/convert_element_type | solution.py:195
  49.6 0.6 fusion.64
  50.2 2.6 %fusion.14 = f32[4,16,64,128]{3,2,1,0:T(8,128)S(1)} fusion(bf16[4,128,16,64]{1,3,2,0:T(8,128)(2,1)S(1)} %bitcast.97, f32[4,16,128]{2,1,0:T(8,128)} %compare_select_fusion.2, f32[4,16,128]{2,1,0:T(8,128)} %copy-done.7, f32[4,128,128]{2,1,0:T(8,128)S(1)} %fusion.64, pred[128,128]{1,0:T(8,128)(4,1)} %convert_compare_fusion), kind=kOutput, calls=%fused_computation.19 | convolution fusion | flops 140509184 | bytes 3489792 | tf_op jit(solution)/shard_map/uhts,ushp->uthp/dot_general | solution.py:221
  52.8 0.3 copy-done.28
  53.1 4.4 %multiply_reduce_fusion = (f32[4,128,16]{1,2,0:T(8,128)S(1)}, f32[4,128,16,64]{1,3,2,0:T(8,128)S(1)}) fusion(f32[4,128,16,64]{1,3,2,0:T(8,128)S(1)} %bitcast.96, bf16[4,128,16,64]{1,3,2,0:T(8,128)(2,1)S(1)} %bitcast.98, f32[16]{0:T(128)S(1)} %copy-done.21, f32[4,128,16]{1,2,0:T(8,128)S(1)} %copy-done.6, f32[16,4,64,64]{3,2,0,1:T(8,128)S(1)} %copy-done.27, ...), kind=kOutput, calls=%fused_computation.26 | convolution fusion | flops 409198592 | bytes 11731456 | tf_op jit(solution)/shard_map/utn,uhpn->uthp/dot_general | solution.py:255
  57.5 0.5 multiply_convert_fusion.4
  58.0 0.7 %copy-done.4 = bf16[1024,512]{1,0:T(8,128)(2,1)S(1)} copy-done((bf16[1024,512]{1,0:T(8,128)(2,1)S(1)}, bf16[1024,512]{1,0:T(8,128)(2,1)}, u32[]{:S(2)}) %copy-start.4) | copy-done | bytes 1048600
  58.7 0.7 %convolution_convert_fusion.2 = bf16[4,128,512]{2,1,0:T(8,128)(2,1)S(1)} fusion(bf16[4,128,1024]{1,2,0:T(8,128)(2,1)S(1)} %bitcast.95, bf16[1024,512]{1,0:T(8,128)(2,1)S(1)} %copy-done.4), kind=kOutput, calls=%fused_computation.38 | convolution fusion | flops 537133056 | bytes 2621440 | tf_op jit(solution)/shard_map/gre,ed->grd/dot_general | solution.py:265
  59.5 0.9 %rev.14 = bf16[2,128,512]{2,1,0:T(8,128)(2,1)S(1)} reverse(bf16[2,128,512]{2,1,0:T(8,128)(2,1)S(1)} %slice.176), dimensions={1,2} | reverse | bytes 524288 | tf_op jit(solution)/shard_map/rev | solution.py:272
  60.4 0.4 fusion.41
  60.9 0.2 fusion.49
  61.2 0.6 multiply_reduce_fusion.1
  (100 shorter events, 1.2 us)
Async XLA Ops:
  0.6 6.9 %copy-start = (bf16[512,1152]{1,0:T(8,128)(2,1)S(1)}, bf16[512,1152]{1,0:T(8,128)(2,1)}, u32[]{:S(2)}) copy-start(bf16[512,1152]{1,0:T(8,128)(2,1)} %param.21) | copy-start | bytes 3538948
  0.6 11.6 %copy-start.3 = (bf16[512,1024]{1,0:T(8,128)(2,1)S(1)}, bf16[512,1024]{1,0:T(8,128)(2,1)}, u32[]{:S(2)}) copy-start(bf16[512,1024]{1,0:T(8,128)(2,1)} %param.22) | copy-start | bytes 3145732
  2.3 15.1 %collective-permute-start = (s32[4,128]{1,0:T(4,128)S(1)}, s32[4,128]{1,0:T(4,128)S(1)}, u32[]{:S(2)}, u32[]{:S(2)}) collective-permute-start(s32[4,128]{1,0:T(4,128)S(1)} %pad_add_fusion.8), channel_id=1, source_target_pairs={{0,1},{1,0},{2,3},{3,2},{4,5},{5,4},{6,7},{7,6},{8,9},{9,8},{10,11... | collective-permute-start | bytes 6152 | tf_op jit(solution)/shard_map/ppermute | solution.py:103
  6.8 8.2 %copy-start.10 = (f32[16]{0:T(128)}, f32[16]{0:T(128)S(1)}, u32[]{:S(2)}) copy-start(f32[16]{0:T(128)S(1)} %get-tuple-element.33) | copy-start | bytes 196
  7.4 7.6 %copy-start.24 = (f32[16]{0:T(128)}, f32[16]{0:T(128)S(1)}, u32[]{:S(2)}) copy-start(f32[16]{0:T(128)S(1)} %exponential_negate_fusion) | copy-start | bytes 196
  7.5 7.5 %copy-start.13 = (pred[4,16]{1,0:T(4,128)(4,1)}, pred[4,16]{1,0:T(4,128)(4,1)S(1)}, u32[]{:S(2)}) copy-start(pred[4,16]{1,0:T(4,128)(4,1)S(1)} %iota_compare_fusion.18) | copy-start | bytes 196
  8.5 6.5 %copy-start.18 = (f32[1152]{0:T(1024)S(1)}, f32[1152]{0:T(1024)}, u32[]{:S(2)}) copy-start(f32[1152]{0:T(1024)} %param.25) | copy-start | bytes 13828
  8.5 6.5 %copy-start.23 = (f32[344,16]{1,0:T(8,128)S(1)}, f32[344,16]{1,0:T(8,128)}, u32[]{:S(2)}) copy-start(f32[344,16]{1,0:T(8,128)} %constant.135.clone) | copy-start | bytes 66052
  11.6 3.4 %copy-start.7 = (f32[4,16,128]{2,1,0:T(8,128)}, f32[4,16,128]{2,1,0:T(8,128)S(1)}, u32[]{:S(2)}) copy-start(f32[4,16,128]{2,1,0:T(8,128)S(1)} %fusion.71) | copy-start | bytes 98308
  15.1 1.6 %copy-start.19 = (f32[2,2,128]{2,1,0:T(2,128)S(1)}, f32[2,2,128]{2,1,0:T(2,128)}, u32[]{:S(2)}) copy-start(f32[2,2,128]{2,1,0:T(2,128)} %param.34) | copy-start | bytes 6148
  15.1 2.3 %copy-start.9 = (s32[2,128]{1,0:T(2,128)S(1)}, s32[2,128]{1,0:T(2,128)}, u32[]{:S(2)}) copy-start(s32[2,128]{1,0:T(2,128)} %param.18) | copy-start | bytes 3076
  16.7 19.0 %copy-start.1 = (f32[344,1152]{1,0:T(8,128)}, f32[344,1152]{1,0:T(8,128)S(1)}, u32[]{:S(2)}) copy-start(f32[344,1152]{1,0:T(8,128)S(1)} %divide_multiply_fusion) | copy-start | bytes 4755460
  17.4 4.2 %collective-permute-start.1 = (s32[4,256]{1,0:T(4,128)S(1)}, s32[4,256]{1,0:T(4,128)S(1)}, u32[]{:S(2)}, u32[]{:S(2)}) collective-permute-start(s32[4,256]{1,0:T(4,128)S(1)} %pad_add_fusion.7), channel_id=1, source_target_pairs={{0,2},{1,3},{2,0},{3,1},{4,6},{5,7},{6,4},{7,5},{8,10},{9,11},{10,... | collective-permute-start | bytes 12296 | tf_op jit(solution)/shard_map/ppermute | solution.py:103
  21.6 3.8 %collective-permute-start.2 = (s32[4,512]{1,0:T(4,128)S(1)}, s32[4,512]{1,0:T(4,128)S(1)}, u32[]{:S(2)}, u32[]{:S(2)}) collective-permute-start(s32[4,512]{1,0:T(4,128)S(1)} %pad_add_fusion.5), channel_id=1, source_target_pairs={{0,4},{1,5},{2,6},{3,7},{4,0},{5,1},{6,2},{7,3},{8,12},{9,13},{10,... | collective-permute-start | bytes 24584 | tf_op jit(solution)/shard_map/ppermute | solution.py:103
  25.4 9.5 %collective-permute-start.3 = (s32[4,1024]{1,0:T(4,128)S(1)}, s32[4,1024]{1,0:T(4,128)}, u32[]{:S(2)}, u32[]{:S(2)}) collective-permute-start(s32[4,1024]{1,0:T(4,128)S(1)} %pad_add_fusion.3), channel_id=1, source_target_pairs={{0,8},{1,9},{2,10},{3,11},{4,12},{5,13},{6,14},{7,15},{8,0},{9,1},... | collective-permute-start | bytes 49160 | tf_op jit(solution)/shard_map/ppermute | solution.py:103
  30.5 9.1 %copy-start.11 = (f32[16]{0:T(128)S(1)}, f32[16]{0:T(128)}, u32[]{:S(2)}) copy-start(f32[16]{0:T(128)} %copy-done.10) | copy-start | bytes 196
  30.5 9.2 %copy-start.12 = (f32[16]{0:T(128)S(1)}, f32[16]{0:T(128)}, u32[]{:S(2)}) copy-start(f32[16]{0:T(128)} %param.26) | copy-start | bytes 196
  30.5 9.2 %copy-start.25 = (f32[16]{0:T(128)S(1)}, f32[16]{0:T(128)}, u32[]{:S(2)}) copy-start(f32[16]{0:T(128)} %copy-done.24) | copy-start | bytes 196
  38.2 3.0 %copy-start.14 = (pred[4,16]{1,0:T(4,128)(4,1)S(1)}, pred[4,16]{1,0:T(4,128)(4,1)}, u32[]{:S(2)}) copy-start(pred[4,16]{1,0:T(4,128)(4,1)} %copy-done.13) | copy-start | bytes 196
  41.9 2.1 %copy-start.5 = (bf16[344,1024]{0,1:T(8,128)(2,1)S(1)}, bf16[344,1024]{0,1:T(8,128)(2,1)}, u32[]{:S(2)}) copy-start(bf16[344,1024]{0,1:T(8,128)(2,1)} %copy.35) | copy-start | bytes 2113540
  50.2 2.6 %copy-start.2 = (f32[4,128,1024]{1,2,0:T(8,128)S(1)}, f32[4,128,1024]{1,2,0:T(8,128)}, u32[]{:S(2)}) copy-start(f32[4,128,1024]{1,2,0:T(8,128)} %fusion.40) | copy-start | bytes 6291460
  50.2 2.6 %copy-start.6 = (f32[4,128,16]{1,2,0:T(8,128)S(1)}, f32[4,128,16]{1,2,0:T(8,128)}, u32[]{:S(2)}) copy-start(f32[4,128,16]{1,2,0:T(8,128)} %exponential_bitcast_fusion) | copy-start | bytes 98308
  50.2 2.6 %copy-start.21 = (f32[16]{0:T(128)S(1)}, f32[16]{0:T(128)}, u32[]{:S(2)}) copy-start(f32[16]{0:T(128)} %param.28) | copy-start | bytes 196
  50.2 2.6 %copy-start.27 = (f32[16,4,64,64]{3,2,0,1:T(8,128)S(1)}, f32[16,4,64,64]{3,2,0,1:T(8,128)}, u32[]{:S(2)}) copy-start(f32[16,4,64,64]{3,2,0,1:T(8,128)} %fusion.5) | copy-start | bytes 3145732
  50.2 2.9 %copy-start.28 = (f32[16,4,64,64]{3,2,0,1:T(8,128)S(1)}, f32[16,4,64,64]{3,2,0,1:T(8,128)}, u32[]{:S(2)}) copy-start(f32[16,4,64,64]{3,2,0,1:T(8,128)} %fusion.6) | copy-start | bytes 3145732
  57.5 1.2 %copy-start.4 = (bf16[1024,512]{1,0:T(8,128)(2,1)S(1)}, bf16[1024,512]{1,0:T(8,128)(2,1)}, u32[]{:S(2)}) copy-start(bf16[1024,512]{1,0:T(8,128)(2,1)} %param.30) | copy-start | bytes 3145732
  58.0 2.4 %copy-start.8 = (bf16[2,512]{1,0:T(2,128)(2,1)S(1)}, bf16[2,512]{1,0:T(2,128)(2,1)}, u32[]{:S(2)}) copy-start(bf16[2,512]{1,0:T(2,128)(2,1)} %param.19) | copy-start | bytes 6148
  58.7 2.1 %copy-start.15 = (bf16[512,2]{0,1:T(2,128)(2,1)S(1)}, bf16[512,2]{0,1:T(2,128)(2,1)}, u32[]{:S(2)}) copy-start(bf16[512,2]{0,1:T(2,128)(2,1)} %param.32) | copy-start | bytes 6148
  58.7 2.1 %copy-start.16 = (bf16[512,2]{0,1:T(2,128)(2,1)S(1)}, bf16[512,2]{0,1:T(2,128)(2,1)}, u32[]{:S(2)}) copy-start(bf16[512,2]{0,1:T(2,128)(2,1)} %rev.15) | copy-start | bytes 6148
  58.7 2.1 %copy-start.20 = (f32[512]{0:T(512)S(1)}, f32[512]{0:T(512)}, u32[]{:S(2)}) copy-start(f32[512]{0:T(512)} %param.31) | copy-start | bytes 6148
  58.7 2.4 %copy-start.17 = (s32[2,2,128]{2,1,0:T(2,128)S(1)}, s32[2,2,128]{2,1,0:T(2,128)}, u32[]{:S(2)}) copy-start(s32[2,2,128]{2,1,0:T(2,128)} %param.33) | copy-start | bytes 6148
  58.7 2.5 %copy-start.26 = (f32[2,2,128]{2,1,0:T(2,128)S(1)}, f32[2,2,128]{2,1,0:T(2,128)}, u32[]{:S(2)}) copy-start(f32[2,2,128]{2,1,0:T(2,128)} %fusion.34) | copy-start | bytes 6148
  60.8 1.0 %copy-start.22 = (bf16[2,128,512]{2,1,0:T(8,128)(2,1)}, bf16[2,128,512]{2,1,0:T(8,128)(2,1)S(1)}, u32[]{:S(2)}) copy-start(bf16[2,128,512]{2,1,0:T(8,128)(2,1)S(1)} %get-tuple-element.37) | copy-start | bytes 786436

commit v5 on v4

--- a/solution.py
+++ b/solution.py
@@ -126,6 +126,12 @@
 
 def onehot(ids, size):
     return (ids[..., None] == jnp.arange(size, dtype=ids.dtype)).astype(jnp.bfloat16)
+
+
+def exchange(size):
+    rows = lax.broadcasted_iota(jnp.int32, (size, size), 0)
+    cols = lax.broadcasted_iota(jnp.int32, (size, size), 1)
+    return (rows + cols == size - 1).astype(jnp.bfloat16)
 
 
 def split_bf16(values):
@@ -166,7 +172,9 @@
     units = streams * nloc
     tri = (jnp.arange(BLK)[:, None] <= jnp.arange(BLK)[None, :]).astype(jnp.float32)
 
-    emb_full = jnp.concatenate([emb_half, emb_half[::-1, ::-1]], axis=0)
+    flip_d = exchange(emb_half.shape[1])
+    emb_flip = jnp.dot(emb_half, flip_d, preferred_element_type=jnp.float32).astype(jnp.bfloat16)
+    emb_full = jnp.concatenate([emb_half, emb_flip[1:2], emb_flip[0:1]], axis=0)
     act_tab, z_rows, dt_rows = gram_tables(emb_full, norm_gain, w_xbc, w_z, w_dt, conv_w, conv_bias)
     x_tab = act_tab[:, :INNER].astype(jnp.bfloat16)
     b_tab = act_tab[:, INNER : INNER + NS]
@@ -174,7 +182,10 @@
     x_heads = x_tab.reshape(GRAMS, HEADS, HD).transpose(1, 0, 2)
     neg_rate = -jnp.exp(a_log)[:, None]
 
-    rc_tok = (BASES - 1) - tokens[:, ::-1]
+    flip_t = exchange(count)
+    rc_tok = (BASES - 1) - jnp.dot(
+        tokens.astype(jnp.bfloat16), flip_t, preferred_element_type=jnp.float32
+    ).astype(jnp.int32)
     local_tok = jnp.concatenate([tokens, rc_tok], axis=0)
     pos0 = jnp.concatenate(
         [jnp.full((windows, 1), place * count), jnp.full((windows, 1), (nseq - 1 - place) * count)]
@@ -197,7 +208,10 @@
     )
     bc_loc = jnp.einsum("rtg,gc->rtc", oh_loc, bc_tab, precision=HIGH)
     oh_tok = onehot(local_tok, BASES)
-    z_loc = jnp.einsum("rtk,kc->rtc", oh_tok, z_rows, preferred_element_type=jnp.float32)
+    gate_rows = jax.nn.silu(z_rows.astype(jnp.float32))
+    gate_loc = jnp.zeros((streams, count, INNER), jnp.float32)
+    for base in range(BASES):
+        gate_loc = gate_loc + jnp.where((local_tok == base)[..., None], gate_rows[base], 0.0)
     dt_loc = jax.nn.softplus(heads_lookup(dt_rows, local_tok) + dt_bias[:, None])
     ld_loc = neg_rate * dt_loc
 
@@ -213,7 +227,7 @@
     dt_u = per_unit(dt_loc, 2)
     cum_u = block_cumsum(per_unit(ld_loc, 2), tri)
 
-    scores = jnp.einsum("utn,usn->uts", c_u, b_u, precision=HIGH)
+    scores = jnp.einsum("utn,usn->uts", c_u, b_u, precision=lax.Precision.HIGH)
     seg_diff = cum_u[:, :, :, None] - cum_u[:, :, None, :]
     lower = tri.T > 0
     decays = jnp.where(lower, jnp.exp(jnp.where(lower, seg_diff, 0.0)), 0.0)
@@ -247,17 +261,20 @@
     )
     per_gram = per_gram[:, :HEADS] + per_gram[:, HEADS:]
     b_hi, b_lo = split_bf16(per_gram[..., None] * b_tab[None, None])
-    start_state = jnp.einsum(
-        "hgp,uhgn->uhpn", x_heads, b_hi, preferred_element_type=jnp.float32
-    ) + jnp.einsum("hgp,uhgn->uhpn", x_heads, b_lo, preferred_element_type=jnp.float32)
+    both = jnp.einsum(
+        "hgp,uhgn->uhpn",
+        x_heads,
+        jnp.concatenate([b_hi, b_lo], axis=-1),
+        preferred_element_type=jnp.float32,
+    )
+    start_state = both[..., :NS] + both[..., NS:]
 
     y_inter = (
-        jnp.einsum("utn,uhpn->uthp", c_u, start_state, precision=HIGH)
+        jnp.einsum("utn,uhpn->uthp", c_u, start_state, precision=lax.Precision.HIGH)
         * jnp.exp(cum_u).transpose(0, 2, 1)[..., None]
     )
     y_u = y_intra + y_inter + d_skip[:, None] * x_u.astype(jnp.float32)
-    z_u = per_unit(z_loc, 1).reshape(units, BLK, HEADS, HD)
-    gated_y = y_u * jax.nn.silu(z_u)
+    gated_y = y_u * per_unit(gate_loc, 1).reshape(units, BLK, HEADS, HD)
     normed = rms_gain(gated_y, inner_gain.reshape(HEADS, HD)).astype(jnp.bfloat16)
     normed = jnp.moveaxis(normed.reshape(streams, nloc, BLK, INNER), 1, 1).reshape(
         streams, count, INNER
@@ -276,7 +293,10 @@
         + returned.astype(jnp.float32)
     ).astype(jnp.bfloat16)
     final_normed = rms_gain(hidden_out.astype(jnp.float32), final_gain).astype(jnp.bfloat16)
-    head_full = jnp.concatenate([w_head_half, w_head_half[::-1, ::-1]], axis=1)
+    head_flip = jnp.dot(flip_d, w_head_half, preferred_element_type=jnp.float32).astype(
+        jnp.bfloat16
+    )
+    head_full = jnp.concatenate([w_head_half, head_flip[:, 1:2], head_flip[:, 0:1]], axis=1)
     logits = jnp.einsum("grd,db->grb", final_normed, head_full, preferred_element_type=jnp.float32)
     log_q = logits - jnp.log(jnp.sum(jnp.exp(logits), axis=-1, keepdims=True))
     top_value = jnp.max(teacher_vals, axis=1, keepdims=True)

time: 62.5 us -> 66 us (1.056)
  other arithmetic: 9.67 us -> 16.3 us
  matrix products: 27.2 us -> 21.5 us
  local copies, waits for them, and re-layouts: 12.8 us -> 15.6 us
    broadcast_in_dim x0 -> x4, local copies, waits for them, and re-layouts: none -> 5.36 us  [local(): jnp.where((local_tok == base)[..., None], gate_rows[base], 0.0)]
    rev x3 -> x0, local copies, waits for them, and re-layouts: 5.08 us -> none  [the longest x1 2.57 us: local(): head_full = jnp.concatenate([w_head_half, w_head_half[::-1, ::-1]], axis=1)]
    dot_general x5 -> x7, matrix products: 12.3 us -> 8.35 us  [the longest x1 3.35 us: local(): jnp.einsum('hgp,uhgn->uhpn', x_heads, jnp.concatenate([b_hi, b_lo], axis=...]
    convert_element_type x0 -> x1, other arithmetic: none -> 3.53 us  [split_bf16(): high = values.astype(jnp.bfloat16)]
    slice x2, local copies, waits for them, and re-layouts: 1.74 us -> 0.01 us  [local(): b_tab = act_tab[:, INNER:INNER + NS]]
    slice x0 -> x3, local copies, waits for them, and re-layouts: none -> 1.34 us  [the longest x1 0.71 us: local(): gate_rows[base]]
    eq x2, other arithmetic: 0.01 us -> 1.19 us  [gram_ids(): chosen = where_in >= real - 1 if real == KW else where_in == real - 1]
    slice x2, local copies, waits for them, and re-layouts: 1.27 us -> 2.44 us  [local(): x_tab = act_tab[:, :INNER].astype(jnp.bfloat16)]
where the time goes in v5:
time: 66 us; the launch traced here: 65.3 us
  matrix products  21.5 us (33%)
  other arithmetic  16.3 us (25%)
  local copies, waits for them, and re-layouts  15.6 us (24%)
  starting transfers between devices  8.23 us (12%)
  waiting for transfers between devices  2.01 us (3%)
  between operations  1.66 us (3%)
    ppermute x4, starting transfers between devices, gather_all(): lax.ppermute(held, axis, [(src, src ^ mask) for src in range(count)])  8.23 us
    broadcast_in_dim x4, local copies, waits for them, and re-layouts, local(): jnp.where((local_tok == base)[..., None], gate_rows[base], 0.0)  5.36 us
    convert_element_type x1, other arithmetic, split_bf16(): high = values.astype(jnp.bfloat16)  3.53 us
    dot_general x1, matrix products, local(): jnp.einsum('hgp,uhgn->uhpn', x_heads, jnp.concatenate([b_hi, b_lo], axis=...  3.35 us
    slice x2, local copies, waits for them, and re-layouts, local(): x_tab = act_tab[:, :INNER].astype(jnp.bfloat16)  2.44 us
    dot_general x1, matrix products, local(): jnp.einsum('utn,uhpn->uthp', c_u, start_state, precision=lax.Precision.HIGH)  2.28 us
    dot_general x1, matrix products, local(): jnp.einsum('rtg,gc->rtc', oh_loc, x_tab, preferred_element_type=jnp.float32)  2.22 us
    dot_general x1, matrix products, local(): jnp.einsum('uhbs,ubsg->uhg', jnp.concatenate([w_hi, w_lo], axis=1), oh_al...  2.11 us
  transfers between devices with their start and end apart: 4, of which 2 were waited for; matrix products, arithmetic and copies ran while one was open for 35% of the time, Pallas kernels for 0%

profile of v5, /device:TPU:0, one launch (start us, length us, event | category | flops | bytes accessed | tf_op | source)
XLA Modules:
  0.0 65.3 jit_solution(9386737023436092314)
XLA Ops:
  0.7 1.0 %fusion.38 = s32[2,128]{1,0:T(2,128)S(1)} fusion(s32[2,128]{1,0:T(2,128)} %param.18), kind=kOutput, calls=%fused_computation.54 | convolution fusion | flops 99072 | bytes 2048 | tf_op jit(solution)/shard_map/dot_general | solution.py:186
  1.7 0.7 %pad_add_fusion.8 = s32[4,128]{1,0:T(4,128)S(1)} fusion(s32[2,128]{1,0:T(2,128)S(1)} %fusion.38, s32[2,128]{1,0:T(2,128)} %param.18), kind=kLoop, calls=%fused_computation.174 | loop fusion | flops 512 | bytes 4096 | tf_op jit(solution)/shard_map/concatenate | solution.py:189
  2.8 0.7 %broadcast_compare_fusion.7 = (pred[4,128]{1,0:T(4,128)(4,1)S(1)}, pred[4,128]{1,0:T(4,128)(4,1)S(1)}, pred[4,128]{1,0:T(4,128)(4,1)S(1)}, pred[4,128]{1,0:T(4,128)(4,1)S(1)}) fusion(s32[2,128]{1,0:T(2,128)S(1)} %fusion.38, s32[2,128]{1,0:T(2,128)} %param.18), kind=kLoop, calls=%fused_computation.188 | loop fusion | flops 2560 | bytes 4096 | tf_op jit(solution)/shard_map/eq | solution.py:122
  3.6 0.9 %fusion.34 = bf16[2,512]{1,0:T(2,128)(2,1)S(1)} fusion(bf16[2,512]{1,0:T(2,128)(2,1)} %param.19), kind=kOutput, calls=%fused_computation.49 | convolution fusion | flops 1573888 | bytes 4096 | tf_op jit(solution)/shard_map/dot_general | solution.py:176
  4.5 0.8 %fusion.81 = (f32[4]{0:T(128)S(1)}, bf16[4,512]{1,0:T(4,128)(2,1)S(1)}) fusion(bf16[1,512]{1,0:T(2,128)(2,1)S(1)} %get-tuple-element.45, bf16[1,512]{1,0:T(2,128)(2,1)S(1)} %get-tuple-element.44, bf16[2,512]{1,0:T(2,128)(2,1)} %param.19), kind=kLoop, calls=%fused_computation.135 | loop fusion | flops 18428 | bytes 8208 | tf_op jit(solution)/shard_map/reduce_sum | solution.py:23
  5.3 0.9 %fusion.107 = f32[4,16]{1,0:T(4,128)S(1)} fusion(bf16[512,16]{0,1:T(8,128)(2,1)} %param.23, bf16[4,512]{1,0:T(4,128)(2,1)S(1)} %get-tuple-element.9, f32[512]{0:T(512)} %param.20, f32[4]{0:T(128)S(1)} %add_rsqrt_fusion.2), kind=kOutput, calls=%fused_computation.209 | convolution fusion | flops 73728 | bytes 22800 | tf_op jit(solution)/shard_map/dot_general | solution.py:76
  6.3 0.7 %exponential_negate_fusion = f32[16]{0:T(128)S(1)} fusion(f32[16]{0:T(128)} %param.27), kind=kLoop, calls=%fused_computation.193 | loop fusion | flops 16 | bytes 128 | tf_op jit(solution)/shard_map/neg | solution.py:183
  7.0 1.0 %fusion.10 = f32[4,1152]{1,0:T(4,128)S(1)} fusion(bf16[512,1152]{1,0:T(8,128)(2,1)S(1)} %copy-done, bf16[4,512]{1,0:T(4,128)(2,1)S(1)} %get-tuple-element.9, f32[512]{0:T(512)} %param.20, f32[4]{0:T(128)S(1)} %add_rsqrt_fusion.2), kind=kOutput, calls=%fused_computation.16 | convolution fusion | flops 4736000 | bytes 1204240 | tf_op jit(solution)/shard_map/dot_general | solution.py:74
  8.0 0.7 %broadcast_multiply_fusion = f32[4,4,1152]{2,1,0:T(4,128)S(1)} fusion(f32[4,1152]{1,0:T(4,128)S(1)} %fusion.10, f32[4,1152]{1,0:T(4,128)} %param.24), kind=kLoop, calls=%fused_computation.106 | loop fusion | flops 18432 | bytes 110592 | tf_op jit(solution)/shard_map/mul | solution.py:77
  8.8 0.7 %compare_select_fusion.2 = f32[4,16,128]{2,1,0:T(8,128)} fusion(f32[16]{0:T(128)S(1)} %copy-done.30, f32[16]{0:T(128)S(1)} %get-tuple-element.41, f32[16]{0:T(128)S(1)} %get-tuple-element.42, f32[16]{0:T(128)S(1)} %get-tuple-element.43, f32[16]{0:T(128)S(1)} %get-tuple-element.40, pred[4,128]{1,0:T(4,128)(4,1)S(1)} %get-tuple-element.38, ...), kind=kLoop, calls=%fused_computation.98 | loop fusion | flops 114688 | bytes 35136 | tf_op jit(solution)/shard_map/jit(softplus)/select_n | solution.py:215
  9.8 0.6 exponential_bitcast_fusion
  10.9 0.6 fusion.111
  12.2 0.6 broadcast_and_fusion
  12.8 1.6 %divide_multiply_fusion = f32[344,1152]{1,0:T(8,128)S(1)} fusion(f32[16,1152]{1,0:T(8,128)S(1)} %mul.201, f32[344,16]{1,0:T(8,128)S(1)} %copy-done.54, f32[1152]{0:T(1024)S(1)} %copy-done.47), kind=kOutput, calls=%fused_computation.33 | convolution fusion | flops 78068736 | bytes 1685504 | tf_op jit(solution)/shard_map/dot_general | solution.py:78
  14.4 0.7 %slice_reduce_fusion.4 = (f32[1024]{0:T(1024)}, f32[1024]{0:T(1024)}, f32[1024]{0:T(1024)}, f32[1024]{0:T(1024)}) fusion(f32[4,1024]{1,0:T(4,128)S(1)} %divide_multiply_fusion.1), kind=kLoop, calls=%fused_computation.155 | loop fusion | bytes 32768 | tf_op jit(solution)/shard_map/slice | solution.py:214
  15.2 2.6 %collective-permute-start.1 = (s32[4,256]{1,0:T(4,128)S(1)}, s32[4,256]{1,0:T(4,128)S(1)}, u32[]{:S(2)}, u32[]{:S(2)}) collective-permute-start(s32[4,256]{1,0:T(4,128)S(1)} %pad_add_fusion.7), channel_id=1, source_target_pairs={{0,2},{1,3},{2,0},{3,1},{4,6},{5,7},{6,4},{7,5},{8,10},{9,11},{10,... | collective-permute-start | bytes 12296 | tf_op jit(solution)/shard_map/ppermute | solution.py:103
  17.8 0.6 convert_compare_fusion
  18.4 1.0 %collective-permute-done.1 = s32[4,256]{1,0:T(4,128)S(1)} collective-permute-done((s32[4,256]{1,0:T(4,128)S(1)}, s32[4,256]{1,0:T(4,128)S(1)}, u32[]{:S(2)}, u32[]{:S(2)}) %collective-permute-start.1) | collective-permute-done | bytes 4128 | tf_op jit(solution)/shard_map/ppermute | solution.py:103
  19.4 2.1 %collective-permute-start.2 = (s32[4,512]{1,0:T(4,128)S(1)}, s32[4,512]{1,0:T(4,128)S(1)}, u32[]{:S(2)}, u32[]{:S(2)}) collective-permute-start(s32[4,512]{1,0:T(4,128)S(1)} %pad_add_fusion.5), channel_id=1, source_target_pairs={{0,4},{1,5},{2,6},{3,7},{4,0},{5,1},{6,2},{7,3},{8,12},{9,13},{10,... | collective-permute-start | bytes 24584 | tf_op jit(solution)/shard_map/ppermute | solution.py:103
  21.5 0.6 iota_compare_fusion.11
  22.1 1.0 %collective-permute-done.2 = s32[4,512]{1,0:T(4,128)S(1)} collective-permute-done((s32[4,512]{1,0:T(4,128)S(1)}, s32[4,512]{1,0:T(4,128)S(1)}, u32[]{:S(2)}, u32[]{:S(2)}) %collective-permute-start.2) | collective-permute-done | bytes 8224 | tf_op jit(solution)/shard_map/ppermute | solution.py:103
  23.8 0.6 pad_add_fusion.3
  24.4 3.0 %collective-permute-start.3 = (s32[4,1024]{1,0:T(4,128)}, s32[4,1024]{1,0:T(4,128)}, u32[]{:S(2)}, u32[]{:S(2)}) collective-permute-start(s32[4,1024]{1,0:T(4,128)} %pad_add_fusion.3), channel_id=1, source_target_pairs={{0,8},{1,9},{2,10},{3,11},{4,12},{5,13},{6,14},{7,15},{8,0},{9,1},... | collective-permute-start | bytes 49160 | tf_op jit(solution)/shard_map/ppermute | solution.py:103
  27.5 0.6 iota_compare_fusion.13
  28.1 1.0 %slice.275 = bf16[344,1024]{1,0:T(8,128)(2,1)} slice(f32[344,1152]{1,0:T(8,128)S(1)} %divide_multiply_fusion), slice={[0:344], [0:1024]} | slice | bytes 1409024 | tf_op jit(solution)/shard_map/slice | solution.py:179
  29.0 1.5 %copy.38 = bf16[344,1024]{0,1:T(8,128)(2,1)S(1)} copy(bf16[344,1024]{1,0:T(8,128)(2,1)} %slice.275) | data formatting | bytes 1409024 | tf_op jit(solution)/shard_map/slice | solution.py:179
  30.5 1.3 %broadcast_in_dim.307 = f32[16,64]{1,0:T(8,128)} reshape(f32[1024]{0:T(1024)} %get-tuple-element.2) | data formatting | bytes 8192 | tf_op jit(solution)/shard_map/jit(_where)/broadcast_in_dim | solution.py:214
  31.8 1.3 %broadcast_in_dim.311 = f32[16,64]{1,0:T(8,128)} reshape(f32[1024]{0:T(1024)} %get-tuple-element.5) | data formatting | bytes 8192 | tf_op jit(solution)/shard_map/jit(_where)/broadcast_in_dim | solution.py:214
  33.2 1.3 %broadcast_in_dim.314 = f32[16,64]{1,0:T(8,128)} reshape(f32[1024]{0:T(1024)} %get-tuple-element.4) | data formatting | bytes 8192 | tf_op jit(solution)/shard_map/jit(_where)/broadcast_in_dim | solution.py:214
  34.5 1.3 %broadcast_in_dim.317 = f32[16,64]{1,0:T(8,128)} reshape(f32[1024]{0:T(1024)} %get-tuple-element.3) | data formatting | bytes 8192 | tf_op jit(solution)/shard_map/jit(_where)/broadcast_in_dim | solution.py:214
  35.9 1.4 %mul.226 = f32[16,64]{1,0:T(8,128)} reshape(f32[1024]{0:T(1024)} %param.29) | data formatting | bytes 8192 | tf_op jit(solution)/shard_map/mul | solution.py:23
  37.3 0.9 %pad_add_fusion = (s32[4,2048]{1,0:T(4,128)S(1)}, s32[4,2048]{1,0:T(4,128)S(1)}) fusion(s32[4,1024]{1,0:T(4,128)} %collective-permute-done.3, s32[2,1024]{1,0:T(2,128)} %copy-done.8, s32[2,1024]{1,0:T(2,128)} %copy-done.7), kind=kLoop, calls=%fused_computation.109 | loop fusion | flops 32768 | bytes 98304 | tf_op jit(solution)/shard_map/concatenate | solution.py:105
  38.2 0.8 %fusion.125 = s32[1,4,16,128]{3,1,2,0:T(4,128)S(1)} fusion(s32[4,2048]{1,0:T(4,128)S(1)} %pad_add_fusion.1, pred[2048]{0:T(1024)(128)(4,1)} %get-tuple-element.50, pred[2048]{0:T(1024)(128)(4,1)} %get-tuple-element.51, pred[2048]{0:T(1024)(128)(4,1)} %get-tuple-element.52, pred[2048]{0:T(1024)(128)(4,1)} %get-tuple-element.53), kind=kLoop, calls=%fused_computation.214 | loop fusion | flops 106496 | bytes 73728
  39.0 0.8 %select_select_fusion = s32[4,2048]{1,0:T(4,128)S(1)} fusion(s32[4,2048]{1,0:T(4,128)S(1)} %pad_add_fusion.1, pred[2048]{0:T(1024)(128)(4,1)} %get-tuple-element.50, pred[2048]{0:T(1024)(128)(4,1)} %get-tuple-element.51, pred[2048]{0:T(1024)(128)(4,1)} %get-tuple-element.52, pred[2048]{0:T(1024)(128)(4,1)} %get-tuple-element.53), kind=kLoop, calls=%fused_computation.115 | loop fusion | flops 106496 | bytes 73728 | tf_op jit(solution)/shard_map/jit(_where)/select_n | solution.py:90
  39.9 2.2 %convolution_convert_fusion.1 = bf16[4,128,1024]{2,1,0:T(8,128)(2,1)S(1)} fusion(s32[4,128]{1,0:T(4,128)S(1)} %pad_add_fusion.9, f32[344,1152]{1,0:T(8,128)} %copy-done.1), kind=kOutput, calls=%fused_computation.35 | convolution fusion | flops 361410560 | bytes 1755136 | tf_op jit(solution)/shard_map/rtg,gc->rtc/dot_general | solution.py:206
  42.2 1.1 %fusion.41 = f32[4,128,128]{1,2,0:T(8,128)} fusion(s32[4,128]{1,0:T(4,128)S(1)} %pad_add_fusion.9, f32[344,1152]{1,0:T(8,128)S(1)} %copy-done.2), kind=kOutput, calls=%fused_computation.59 | convolution fusion | flops 270708736 | bytes 440320 | tf_op jit(solution)/shard_map/rtg,gc->rtc/dot_general | solution.py:209
  43.4 0.9 %fusion.46 = f32[4,16,16,128]{3,2,1,0:T(8,128)S(1)} fusion(f32[16]{0:T(128)S(1)} %copy-done.31, f32[16]{0:T(128)S(1)} %copy-done.25, f32[16]{0:T(128)S(1)} %copy-done.27, f32[16]{0:T(128)S(1)} %copy-done.29, f32[16]{0:T(128)S(1)} %copy-done.23, f32[16]{0:T(128)S(1)} %copy-done.56, pred[4,16,128]{2,1,0:T(8,128)(4,1)S(1)} %get-tuple-element.15, ...), kind=kOutput, calls=%fused_computation.71 | convolution fusion | flops 203309056 | bytes 557440 | tf_op jit(solution)/shard_map/...s,st->...t/dot_general | solution.py:143
  45.0 0.7 subtract_convert_fusion
  45.7 2.1 %fusion.31 = f32[4,32,344]{2,1,0:T(8,128)S(1)} fusion(s32[4,16,128]{2,1,0:T(8,128)S(1)} %bitcast.98, bf16[4,32,16,128]{3,2,1,0:T(8,128)(2,1)S(1)} %pad_maximum_fusion), kind=kOutput, calls=%fused_computation.43 | convolution fusion | flops 183173120 | bytes 733184 | tf_op jit(solution)/shard_map/uhbs,ubsg->uhg/dot_general | solution.py:256
  47.9 1.5 %copy.35 = bf16[4,128,1024]{1,2,0:T(8,128)(2,1)} copy(bf16[4,128,1024]{2,1,0:T(8,128)(2,1)S(1)} %convolution_convert_fusion.1) | data formatting | bytes 2097152 | tf_op jit(solution)/shard_map/convert_element_type | solution.py:206
  49.8 3.5 %multiply_convert_fusion = (bf16[4,16,344,64]{3,2,0,1:T(8,128)(2,1)S(1)}, bf16[4,16,344,64]{3,2,0,1:T(8,128)(2,1)S(1)}) fusion(f32[344,64]{1,0:T(8,128)S(1)} %slice-done, f32[4,16,344]{2,0,1:T(4,128)S(1)} %copy.37), kind=kLoop, calls=%fused_computation.3 | loop fusion | flops 7045120 | bytes 5812224 | tf_op jit(solution)/shard_map/convert_element_type | solution.py:138
  53.4 3.4 %fusion.22 = f32[4,16,64,128]{3,2,0,1:T(8,128)S(1)} fusion(bf16[16,344,64,1]{1,2,3,0:T(8,128)(2,1)S(1)} %bitcast.93, bf16[4,16,344,64]{3,2,0,1:T(8,128)(2,1)S(1)} %get-tuple-element.11, bf16[4,16,344,64]{3,2,0,1:T(8,128)(2,1)S(1)} %get-tuple-element.10), kind=kOutput, calls=%fused_computation.32 | convolution fusion | flops 371982336 | bytes 8437760 | tf_op jit(solution)/shard_map/hgp,uhgn->uhpn/dot_general | solution.py:264
  56.9 1.6 %fusion.11 = f32[4,16,64,128]{3,2,1,0:T(8,128)S(1)} fusion(bf16[4,128,16,64]{1,3,2,0:T(8,128)(2,1)S(1)} %bitcast.94, f32[4,16,128]{2,1,0:T(8,128)S(1)} %copy-done.11, f32[4,16,128]{2,1,0:T(8,128)S(1)} %copy-done.14, f32[4,128,128]{2,1,0:T(8,128)S(1)} %fusion.67, pred[128,128]{1,0:T(8,128)(4,1)S(1)} %copy-done.15), kind=kOutput, calls=%fused_computation.17 | convolution fusion | flops 140509184 | bytes 3489792 | tf_op jit(solution)/shard_map/uhts,ushp->uthp/dot_general | solution.py:235
  58.6 2.3 %multiply_reduce_fusion = (f32[4,128,16]{1,2,0:T(8,128)S(1)}, f32[4,128,16,64]{1,3,2,0:T(8,128)S(1)}) fusion(f32[16,64]{1,0:T(8,128)S(1)} %copy-done.21, pred[4,128]{1,0:T(4,128)(4,1)S(1)} %copy-done.37, f32[16,64]{1,0:T(8,128)S(1)} %copy-done.20, pred[4,128]{1,0:T(4,128)(4,1)S(1)} %copy-done.35, f32[16,64]{1,0:T(8,128)S(1)} %copy-done.19, ...), kind=kOutput, calls=%fused_computation.25 | convolution fusion | flops 209444864 | bytes 9669120 | tf_op jit(solution)/shard_map/utn,uhpn->uthp/dot_general | solution.py:273
  61.5 0.7 %copy-done.5 = bf16[1024,512]{1,0:T(8,128)(2,1)S(1)} copy-done((bf16[1024,512]{1,0:T(8,128)(2,1)S(1)}, bf16[1024,512]{1,0:T(8,128)(2,1)}, u32[]{:S(2)}) %copy-start.5) | copy-done | bytes 1048600
  62.2 0.7 %convolution_convert_fusion.2 = bf16[4,128,512]{2,1,0:T(8,128)(2,1)S(1)} fusion(bf16[4,128,1024]{1,2,0:T(8,128)(2,1)S(1)} %bitcast.92, bf16[1024,512]{1,0:T(8,128)(2,1)S(1)} %copy-done.5), kind=kOutput, calls=%fused_computation.37 | convolution fusion | flops 537133056 | bytes 2621440 | tf_op jit(solution)/shard_map/gre,ed->grd/dot_general | solution.py:282
  62.9 0.9 %rev.3 = bf16[2,128,512]{2,1,0:T(8,128)(2,1)S(1)} reverse(bf16[2,128,512]{2,1,0:T(8,128)(2,1)S(1)} %slice.224), dimensions={1,2} | reverse | bytes 524288 | tf_op jit(solution)/shard_map/rev | solution.py:289
  64.6 0.6 multiply_reduce_fusion.1
  (165 shorter events, 5.2 us)
Async XLA Ops:
  0.6 6.4 %copy-start = (bf16[512,1152]{1,0:T(8,128)(2,1)S(1)}, bf16[512,1152]{1,0:T(8,128)(2,1)}, u32[]{:S(2)}) copy-start(bf16[512,1152]{1,0:T(8,128)(2,1)} %param.21) | copy-start | bytes 3538948
  0.6 9.7 %copy-start.17 = (f32[512]{0:T(512)S(1)}, f32[512]{0:T(512)}, u32[]{:S(2)}) copy-start(f32[512]{0:T(512)} %param.20) | copy-start | bytes 6148
  0.7 8.1 %copy-start.30 = (f32[16]{0:T(128)S(1)}, f32[16]{0:T(128)}, u32[]{:S(2)}) copy-start(f32[16]{0:T(128)} %param.26) | copy-start | bytes 196
  0.7 9.7 %copy-start.4 = (bf16[512,1024]{1,0:T(8,128)(2,1)S(1)}, bf16[512,1024]{1,0:T(8,128)(2,1)}, u32[]{:S(2)}) copy-start(bf16[512,1024]{1,0:T(8,128)(2,1)} %param.22) | copy-start | bytes 3145732
  0.7 10.0 %copy-start.50 = (bf16[512,2]{0,1:T(2,128)(2,1)S(1)}, bf16[512,2]{0,1:T(2,128)(2,1)}, u32[]{:S(2)}) copy-start(bf16[512,2]{0,1:T(2,128)(2,1)} %param.32) | copy-start | bytes 6148
  1.7 9.9 %copy-start.48 = (f32[2,2,128]{2,1,0:T(2,128)S(1)}, f32[2,2,128]{2,1,0:T(2,128)}, u32[]{:S(2)}) copy-start(f32[2,2,128]{2,1,0:T(2,128)} %param.34) | copy-start | bytes 6148
  2.4 10.4 %copy-start.42 = (s32[4,128]{1,0:T(4,128)}, s32[4,128]{1,0:T(4,128)S(1)}, u32[]{:S(2)}) copy-start(s32[4,128]{1,0:T(4,128)S(1)} %pad_add_fusion.8) | copy-start | bytes 6148
  2.4 12.8 %collective-permute-start = (s32[4,128]{1,0:T(4,128)S(1)}, s32[4,128]{1,0:T(4,128)S(1)}, u32[]{:S(2)}, u32[]{:S(2)}) collective-permute-start(s32[4,128]{1,0:T(4,128)S(1)} %pad_add_fusion.8), channel_id=1, source_target_pairs={{0,1},{1,0},{2,3},{3,2},{4,5},{5,4},{6,7},{7,6},{8,9},{9,8},{10,11... | collective-permute-start | bytes 6152 | tf_op jit(solution)/shard_map/ppermute | solution.py:103
  3.5 8.6 %copy-start.32 = (pred[4,128]{1,0:T(4,128)(4,1)}, pred[4,128]{1,0:T(4,128)(4,1)S(1)}, u32[]{:S(2)}) copy-start(pred[4,128]{1,0:T(4,128)(4,1)S(1)} %get-tuple-element.36) | copy-start | bytes 1540
  3.5 8.6 %copy-start.34 = (pred[4,128]{1,0:T(4,128)(4,1)}, pred[4,128]{1,0:T(4,128)(4,1)S(1)}, u32[]{:S(2)}) copy-start(pred[4,128]{1,0:T(4,128)(4,1)S(1)} %get-tuple-element.37) | copy-start | bytes 1540
  3.5 8.6 %copy-start.36 = (pred[4,128]{1,0:T(4,128)(4,1)}, pred[4,128]{1,0:T(4,128)(4,1)S(1)}, u32[]{:S(2)}) copy-start(pred[4,128]{1,0:T(4,128)(4,1)S(1)} %get-tuple-element.38) | copy-start | bytes 1540
  3.5 8.6 %copy-start.38 = (pred[4,128]{1,0:T(4,128)(4,1)}, pred[4,128]{1,0:T(4,128)(4,1)S(1)}, u32[]{:S(2)}) copy-start(pred[4,128]{1,0:T(4,128)(4,1)S(1)} %get-tuple-element.39) | copy-start | bytes 1540
  3.6 9.2 %copy-start.47 = (f32[1152]{0:T(1024)S(1)}, f32[1152]{0:T(1024)}, u32[]{:S(2)}) copy-start(f32[1152]{0:T(1024)} %param.25) | copy-start | bytes 13828
  3.6 9.2 %copy-start.54 = (f32[344,16]{1,0:T(8,128)S(1)}, f32[344,16]{1,0:T(8,128)}, u32[]{:S(2)}) copy-start(f32[344,16]{1,0:T(8,128)} %constant.138.clone) | copy-start | bytes 66052
  6.2 5.9 %copy-start.22 = (f32[16]{0:T(128)}, f32[16]{0:T(128)S(1)}, u32[]{:S(2)}) copy-start(f32[16]{0:T(128)S(1)} %get-tuple-element.40) | copy-start | bytes 196
  6.2 5.9 %copy-start.24 = (f32[16]{0:T(128)}, f32[16]{0:T(128)S(1)}, u32[]{:S(2)}) copy-start(f32[16]{0:T(128)S(1)} %get-tuple-element.41) | copy-start | bytes 196
  6.2 5.9 %copy-start.26 = (f32[16]{0:T(128)}, f32[16]{0:T(128)S(1)}, u32[]{:S(2)}) copy-start(f32[16]{0:T(128)S(1)} %get-tuple-element.42) | copy-start | bytes 196
  6.3 5.9 %copy-start.28 = (f32[16]{0:T(128)}, f32[16]{0:T(128)S(1)}, u32[]{:S(2)}) copy-start(f32[16]{0:T(128)S(1)} %get-tuple-element.43) | copy-start | bytes 196
  6.9 5.2 %copy-start.55 = (f32[16]{0:T(128)}, f32[16]{0:T(128)S(1)}, u32[]{:S(2)}) copy-start(f32[16]{0:T(128)S(1)} %exponential_negate_fusion) | copy-start | bytes 196
  7.0 5.1 %copy-start.40 = (pred[4,16]{1,0:T(4,128)(4,1)}, pred[4,16]{1,0:T(4,128)(4,1)S(1)}, u32[]{:S(2)}) copy-start(pred[4,16]{1,0:T(4,128)(4,1)S(1)} %iota_compare_fusion.17) | copy-start | bytes 196
  9.8 2.4 %copy-start.13 = (f32[4,16,128]{2,1,0:T(8,128)}, f32[4,16,128]{2,1,0:T(8,128)S(1)}, u32[]{:S(2)}) copy-start(f32[4,16,128]{2,1,0:T(8,128)S(1)} %fusion.74) | copy-start | bytes 98308
  12.8 2.3 %copy-start.16 = (s32[2,128]{1,0:T(2,128)S(1)}, s32[2,128]{1,0:T(2,128)}, u32[]{:S(2)}) copy-start(s32[2,128]{1,0:T(2,128)} %param.18) | copy-start | bytes 3076
  14.4 25.4 %copy-start.1 = (f32[344,1152]{1,0:T(8,128)}, f32[344,1152]{1,0:T(8,128)S(1)}, u32[]{:S(2)}) copy-start(f32[344,1152]{1,0:T(8,128)S(1)} %divide_multiply_fusion) | copy-start | bytes 4755460
  15.2 4.2 %collective-permute-start.1 = (s32[4,256]{1,0:T(4,128)S(1)}, s32[4,256]{1,0:T(4,128)S(1)}, u32[]{:S(2)}, u32[]{:S(2)}) collective-permute-start(s32[4,256]{1,0:T(4,128)S(1)} %pad_add_fusion.7), channel_id=1, source_target_pairs={{0,2},{1,3},{2,0},{3,1},{4,6},{5,7},{6,4},{7,5},{8,10},{9,11},{10,... | collective-permute-start | bytes 12296 | tf_op jit(solution)/shard_map/ppermute | solution.py:103
  19.4 3.8 %collective-permute-start.2 = (s32[4,512]{1,0:T(4,128)S(1)}, s32[4,512]{1,0:T(4,128)S(1)}, u32[]{:S(2)}, u32[]{:S(2)}) collective-permute-start(s32[4,512]{1,0:T(4,128)S(1)} %pad_add_fusion.5), channel_id=1, source_target_pairs={{0,4},{1,5},{2,6},{3,7},{4,0},{5,1},{6,2},{7,3},{8,12},{9,13},{10,... | collective-permute-start | bytes 24584 | tf_op jit(solution)/shard_map/ppermute | solution.py:103
  24.4 12.8 %collective-permute-start.3 = (s32[4,1024]{1,0:T(4,128)}, s32[4,1024]{1,0:T(4,128)}, u32[]{:S(2)}, u32[]{:S(2)}) collective-permute-start(s32[4,1024]{1,0:T(4,128)} %pad_add_fusion.3), channel_id=1, source_target_pairs={{0,8},{1,9},{2,10},{3,11},{4,12},{5,13},{6,14},{7,15},{8,0},{9,1},... | collective-permute-start | bytes 49160 | tf_op jit(solution)/shard_map/ppermute | solution.py:103
  37.2 6.2 %copy-start.23 = (f32[16]{0:T(128)S(1)}, f32[16]{0:T(128)}, u32[]{:S(2)}) copy-start(f32[16]{0:T(128)} %copy-done.22) | copy-start | bytes 196
  37.2 6.2 %copy-start.25 = (f32[16]{0:T(128)S(1)}, f32[16]{0:T(128)}, u32[]{:S(2)}) copy-start(f32[16]{0:T(128)} %copy-done.24) | copy-start | bytes 196
  37.2 6.2 %copy-start.27 = (f32[16]{0:T(128)S(1)}, f32[16]{0:T(128)}, u32[]{:S(2)}) copy-start(f32[16]{0:T(128)} %copy-done.26) | copy-start | bytes 196
  37.2 6.2 %copy-start.29 = (f32[16]{0:T(128)S(1)}, f32[16]{0:T(128)}, u32[]{:S(2)}) copy-start(f32[16]{0:T(128)} %copy-done.28) | copy-start | bytes 196
  37.2 6.2 %copy-start.31 = (f32[16]{0:T(128)S(1)}, f32[16]{0:T(128)}, u32[]{:S(2)}) copy-start(f32[16]{0:T(128)} %param.26) | copy-start | bytes 196
  37.2 6.2 %copy-start.56 = (f32[16]{0:T(128)S(1)}, f32[16]{0:T(128)}, u32[]{:S(2)}) copy-start(f32[16]{0:T(128)} %copy-done.55) | copy-start | bytes 196
  39.9 2.3 %copy-start.2 = (f32[344,1152]{1,0:T(8,128)S(1)}, f32[344,1152]{1,0:T(8,128)}, u32[]{:S(2)}) copy-start(f32[344,1152]{1,0:T(8,128)} %copy-done.1) | copy-start | bytes 4755460
  42.2 2.5 %copy-start.10 = (pred[4,16,16]{2,1,0:T(8,128)(4,1)S(1)}, pred[4,16,16]{2,1,0:T(8,128)(4,1)}, u32[]{:S(2)}) copy-start(pred[4,16,16]{2,1,0:T(8,128)(4,1)} %broadcast_and_fusion) | copy-start | bytes 3076
  42.2 2.7 %copy-start.41 = (pred[4,16]{1,0:T(4,128)(4,1)S(1)}, pred[4,16]{1,0:T(4,128)(4,1)}, u32[]{:S(2)}) copy-start(pred[4,16]{1,0:T(4,128)(4,1)} %copy-done.40) | copy-start | bytes 196
  47.8 2.0 %slice-start = ((f32[344,1152]{1,0:T(8,128)}), f32[344,64]{1,0:T(8,128)S(1)}, s32[]{:S(2)}) async-start(f32[344,1152]{1,0:T(8,128)} %copy-done.1), calls=%async_computation | async-start | bytes 352256 | tf_op jit(solution)/shard_map/slice | solution.py:180
  53.3 3.4 %copy-start.6 = (bf16[4,128,1024]{1,2,0:T(8,128)(2,1)S(1)}, bf16[4,128,1024]{1,2,0:T(8,128)(2,1)}, u32[]{:S(2)}) copy-start(bf16[4,128,1024]{1,2,0:T(8,128)(2,1)} %copy.35) | copy-start | bytes 3145732
  53.3 3.4 %copy-start.11 = (f32[4,16,128]{2,1,0:T(8,128)S(1)}, f32[4,16,128]{2,1,0:T(8,128)}, u32[]{:S(2)}) copy-start(f32[4,16,128]{2,1,0:T(8,128)} %compare_select_fusion.2) | copy-start | bytes 98308
  53.4 3.4 %copy-start.14 = (f32[4,16,128]{2,1,0:T(8,128)S(1)}, f32[4,16,128]{2,1,0:T(8,128)}, u32[]{:S(2)}) copy-start(f32[4,16,128]{2,1,0:T(8,128)} %copy-done.13) | copy-start | bytes 98308
  53.4 3.4 %copy-start.15 = (pred[128,128]{1,0:T(8,128)(4,1)S(1)}, pred[128,128]{1,0:T(8,128)(4,1)}, u32[]{:S(2)}) copy-start(pred[128,128]{1,0:T(8,128)(4,1)} %convert_compare_fusion) | copy-start | bytes 49156
  58.6 2.3 %copy-start.9 = (f32[16,64]{1,0:T(8,128)S(1)}, f32[16,64]{1,0:T(8,128)}, u32[]{:S(2)}) copy-start(f32[16,64]{1,0:T(8,128)} %mul.226) | copy-start | bytes 12292
  61.5 2.4 %copy-start.43 = (s32[4,128]{1,0:T(4,128)S(1)}, s32[4,128]{1,0:T(4,128)}, u32[]{:S(2)}) copy-start(s32[4,128]{1,0:T(4,128)} %copy-done.42) | copy-start | bytes 6148
  62.1 2.1 %copy-start.45 = (bf16[512,1]{0,1:T(2,128)(2,1)S(1)}, bf16[512,1]{0,1:T(2,128)(2,1)}, u32[]{:S(2)}) copy-start(bf16[512,1]{0,1:T(2,128)(2,1)} %get-tuple-element.34) | copy-start | bytes 3076
  62.2 2.1 %copy-start.46 = (bf16[512,1]{0,1:T(2,128)(2,1)S(1)}, bf16[512,1]{0,1:T(2,128)(2,1)}, u32[]{:S(2)}) copy-start(bf16[512,1]{0,1:T(2,128)(2,1)} %get-tuple-element.35) | copy-start | bytes 3076
  62.2 2.1 %copy-start.49 = (f32[512]{0:T(512)S(1)}, f32[512]{0:T(512)}, u32[]{:S(2)}) copy-start(f32[512]{0:T(512)} %param.31) | copy-start | bytes 6148
  62.2 2.2 %copy-start.51 = (bf16[512,2]{0,1:T(2,128)(2,1)S(1)}, bf16[512,2]{0,1:T(2,128)(2,1)}, u32[]{:S(2)}) copy-start(bf16[512,2]{0,1:T(2,128)(2,1)} %param.32) | copy-start | bytes 6148
  62.2 2.4 %copy-start.44 = (s32[2,2,128]{2,1,0:T(2,128)S(1)}, s32[2,2,128]{2,1,0:T(2,128)}, u32[]{:S(2)}) copy-start(s32[2,2,128]{2,1,0:T(2,128)} %param.33) | copy-start | bytes 6148
  62.2 2.5 %copy-start.57 = (f32[2,2,128]{2,1,0:T(2,128)S(1)}, f32[2,2,128]{2,1,0:T(2,128)}, u32[]{:S(2)}) copy-start(f32[2,2,128]{2,1,0:T(2,128)} %fusion.33) | copy-start | bytes 6148
  (15 other events, 23.1 us)

commit v6 on v5

--- a/solution.py
+++ b/solution.py
@@ -208,10 +208,7 @@
     )
     bc_loc = jnp.einsum("rtg,gc->rtc", oh_loc, bc_tab, precision=HIGH)
     oh_tok = onehot(local_tok, BASES)
-    gate_rows = jax.nn.silu(z_rows.astype(jnp.float32))
-    gate_loc = jnp.zeros((streams, count, INNER), jnp.float32)
-    for base in range(BASES):
-        gate_loc = gate_loc + jnp.where((local_tok == base)[..., None], gate_rows[base], 0.0)
+    z_loc = jnp.einsum("rtk,kc->rtc", oh_tok, z_rows, preferred_element_type=jnp.float32)
     dt_loc = jax.nn.softplus(heads_lookup(dt_rows, local_tok) + dt_bias[:, None])
     ld_loc = neg_rate * dt_loc
 
@@ -274,7 +271,8 @@
         * jnp.exp(cum_u).transpose(0, 2, 1)[..., None]
     )
     y_u = y_intra + y_inter + d_skip[:, None] * x_u.astype(jnp.float32)
-    gated_y = y_u * per_unit(gate_loc, 1).reshape(units, BLK, HEADS, HD)
+    z_u = per_unit(z_loc, 1).reshape(units, BLK, HEADS, HD)
+    gated_y = y_u * jax.nn.silu(z_u)
     normed = rms_gain(gated_y, inner_gain.reshape(HEADS, HD)).astype(jnp.bfloat16)
     normed = jnp.moveaxis(normed.reshape(streams, nloc, BLK, INNER), 1, 1).reshape(
         streams, count, INNER

time: 66 us -> 61.1 us (0.926)
  local copies, waits for them, and re-layouts: 15.6 us -> 9.43 us
  matrix products: 21.5 us -> 23.1 us
    broadcast_in_dim x4 -> x0, local copies, waits for them, and re-layouts: 5.36 us -> none  [local(): jnp.where((local_tok == base)[..., None], gate_rows[base], 0.0)]
    dot_general x1, matrix products: 0.29 us -> 2.06 us  [local(): jnp.einsum('rtk,kc->rtc', oh_tok, z_rows, preferred_element_type=jnp.floa...]
    slice x1 -> x0, local copies, waits for them, and re-layouts: 0.71 us -> none  [local(): gate_rows[base]]
    unnamed x118 -> x96, local copies, waits for them, and re-layouts: 1.54 us -> 1.49 us
  transfers between devices with their start and end apart: 4 -> 4, of which waited for: 2 -> 2; matrix products, arithmetic and copies ran while one was open for 35% -> 31% of each run, Pallas kernels for 0% -> 0%
where the time goes in v6:
time: 61.1 us; the launch traced here: 60.5 us
  matrix products  23.1 us (38%)
  other arithmetic  16.3 us (27%)
  local copies, waits for them, and re-layouts  9.43 us (15%)
  starting transfers between devices  8.22 us (13%)
  waiting for transfers between devices  2.02 us (3%)
  between operations  1.48 us (2%)
    ppermute x4, starting transfers between devices, gather_all(): lax.ppermute(held, axis, [(src, src ^ mask) for src in range(count)])  8.22 us
    convert_element_type x1, other arithmetic, split_bf16(): high = values.astype(jnp.bfloat16)  3.53 us
    dot_general x1, matrix products, local(): jnp.einsum('hgp,uhgn->uhpn', x_heads, jnp.concatenate([b_hi, b_lo], axis=...  3.35 us
    slice x2, local copies, waits for them, and re-layouts, local(): x_tab = act_tab[:, :INNER].astype(jnp.bfloat16)  2.44 us
    dot_general x1, matrix products, local(): jnp.einsum('rtg,gc->rtc', oh_loc, x_tab, preferred_element_type=jnp.float32)  2.22 us
    dot_general x1, matrix products, local(): jnp.einsum('utn,uhpn->uthp', c_u, start_state, precision=lax.Precision.HIGH)  2.18 us
    dot_general x1, matrix products, local(): jnp.einsum('uhbs,ubsg->uhg', jnp.concatenate([w_hi, w_lo], axis=1), oh_al...  2.11 us
    dot_general x1, matrix products, local(): jnp.einsum('rtk,kc->rtc', oh_tok, z_rows, preferred_element_type=jnp.floa...  2.06 us
  transfers between devices with their start and end apart: 4, of which 2 were waited for; matrix products, arithmetic and copies ran while one was open for 31% of the time, Pallas kernels for 0%

profile of v6, /device:TPU:0, one launch (start us, length us, event | category | flops | bytes accessed | tf_op | source)
XLA Modules:
  0.0 60.5 jit_solution(10573748868103330240)
XLA Ops:
  0.7 1.0 %fusion.38 = s32[2,128]{1,0:T(2,128)S(1)} fusion(s32[2,128]{1,0:T(2,128)} %param.18), kind=kOutput, calls=%fused_computation.54 | convolution fusion | flops 99072 | bytes 2048 | tf_op jit(solution)/shard_map/dot_general | solution.py:186
  1.6 0.7 %pad_add_fusion.8 = s32[4,128]{1,0:T(4,128)S(1)} fusion(s32[2,128]{1,0:T(2,128)S(1)} %fusion.38, s32[2,128]{1,0:T(2,128)} %param.18), kind=kLoop, calls=%fused_computation.171 | loop fusion | flops 512 | bytes 4096 | tf_op jit(solution)/shard_map/concatenate | solution.py:189
  2.3 0.5 collective-permute-start
  2.8 0.7 %broadcast_compare_fusion.7 = (pred[4,128]{1,0:T(4,128)(4,1)S(1)}, pred[4,128]{1,0:T(4,128)(4,1)S(1)}, pred[4,128]{1,0:T(4,128)(4,1)S(1)}, pred[4,128]{1,0:T(4,128)(4,1)S(1)}) fusion(s32[2,128]{1,0:T(2,128)S(1)} %fusion.38, s32[2,128]{1,0:T(2,128)} %param.18), kind=kLoop, calls=%fused_computation.185 | loop fusion | flops 2560 | bytes 4096 | tf_op jit(solution)/shard_map/eq | solution.py:122
  3.5 0.9 %fusion.34 = bf16[2,512]{1,0:T(2,128)(2,1)S(1)} fusion(bf16[2,512]{1,0:T(2,128)(2,1)} %param.19), kind=kOutput, calls=%fused_computation.49 | convolution fusion | flops 1573888 | bytes 4096 | tf_op jit(solution)/shard_map/dot_general | solution.py:176
  4.4 0.8 %fusion.82 = (f32[4]{0:T(128)S(1)}, bf16[4,512]{1,0:T(4,128)(2,1)S(1)}) fusion(bf16[1,512]{1,0:T(2,128)(2,1)S(1)} %get-tuple-element.41, bf16[1,512]{1,0:T(2,128)(2,1)S(1)} %get-tuple-element.40, bf16[2,512]{1,0:T(2,128)(2,1)} %param.19), kind=kLoop, calls=%fused_computation.135 | loop fusion | flops 18428 | bytes 8208 | tf_op jit(solution)/shard_map/reduce_sum | solution.py:23
  5.2 0.9 %fusion.110 = f32[4,16]{1,0:T(4,128)S(1)} fusion(bf16[512,16]{0,1:T(8,128)(2,1)} %param.23, bf16[4,512]{1,0:T(4,128)(2,1)S(1)} %get-tuple-element.5, f32[512]{0:T(512)} %param.20, f32[4]{0:T(128)S(1)} %add_rsqrt_fusion.2), kind=kOutput, calls=%fused_computation.206 | convolution fusion | flops 73728 | bytes 22800 | tf_op jit(solution)/shard_map/dot_general | solution.py:76
  6.1 0.7 %exponential_negate_fusion = f32[16]{0:T(128)S(1)} fusion(f32[16]{0:T(128)} %param.27), kind=kLoop, calls=%fused_computation.190 | loop fusion | flops 16 | bytes 128 | tf_op jit(solution)/shard_map/neg | solution.py:183
  6.9 1.0 %fusion.10 = f32[4,1152]{1,0:T(4,128)S(1)} fusion(bf16[512,1152]{1,0:T(8,128)(2,1)S(1)} %copy-done, bf16[4,512]{1,0:T(4,128)(2,1)S(1)} %get-tuple-element.5, f32[512]{0:T(512)} %param.20, f32[4]{0:T(128)S(1)} %add_rsqrt_fusion.2), kind=kOutput, calls=%fused_computation.16 | convolution fusion | flops 4736000 | bytes 1204240 | tf_op jit(solution)/shard_map/dot_general | solution.py:74
  7.9 0.8 %broadcast_multiply_fusion = f32[4,4,1152]{2,1,0:T(4,128)S(1)} fusion(f32[4,1152]{1,0:T(4,128)S(1)} %fusion.10, f32[4,1152]{1,0:T(4,128)} %param.24), kind=kLoop, calls=%fused_computation.107 | loop fusion | flops 18432 | bytes 110592 | tf_op jit(solution)/shard_map/mul | solution.py:77
  8.7 0.7 %compare_select_fusion.2 = f32[4,16,128]{2,1,0:T(8,128)} fusion(f32[16]{0:T(128)S(1)} %copy-done.29, f32[16]{0:T(128)S(1)} %get-tuple-element.37, f32[16]{0:T(128)S(1)} %get-tuple-element.38, f32[16]{0:T(128)S(1)} %get-tuple-element.39, f32[16]{0:T(128)S(1)} %get-tuple-element.36, pred[4,128]{1,0:T(4,128)(4,1)S(1)} %get-tuple-element.34, ...), kind=kLoop, calls=%fused_computation.99 | loop fusion | flops 114688 | bytes 35136 | tf_op jit(solution)/shard_map/jit(softplus)/select_n | solution.py:212
  9.7 0.6 %exponential_bitcast_fusion = f32[4,128,16]{1,2,0:T(8,128)} fusion(f32[4,16,128]{2,1,0:T(8,128)S(1)} %fusion.75), kind=kLoop, calls=%fused_computation.113 | loop fusion | bytes 65536 | tf_op jit(solution)/shard_map/exp | solution.py:271
  10.3 2.1 %fusion.42 = f32[4,128,1024]{1,2,0:T(8,128)} fusion(bf16[512,1024]{1,0:T(8,128)(2,1)S(1)} %copy-done.5, s32[4,128]{1,0:T(4,128)S(1)} %pad_add_fusion.8, bf16[4,512]{1,0:T(4,128)(2,1)S(1)} %get-tuple-element.5, f32[512]{0:T(512)S(1)} %copy-done.18, f32[4]{0:T(128)S(1)} %add_rsqrt_fusion.2), kind=kOutput, calls=%fused_computation.62 | convolution fusion | flops 8402944 | bytes 3153936 | tf_op jit(solution)/shard_map/rtk,kc->rtc/dot_general | solution.py:211
  12.6 0.6 %fusion.114 = (bf16[512,1]{0,1:T(2,128)(2,1)}, bf16[512,1]{0,1:T(2,128)(2,1)}) fusion(bf16[512,2]{0,1:T(2,128)(2,1)S(1)} %convolution_convert_fusion.5), kind=kLoop, calls=%fused_computation.208 | loop fusion | bytes 4096 | tf_op jit(solution)/shard_map/slice | solution.py:297
  13.2 0.6 %broadcast_and_fusion = pred[4,16,16]{2,1,0:T(8,128)(4,1)} fusion(pred[16,16]{1,0:T(8,128)(4,1)S(1)} %iota_compare_fusion.10, pred[4,16]{1,0:T(4,128)(4,1)S(1)} %iota_compare_fusion.18), kind=kLoop, calls=%fused_computation.132 | loop fusion | flops 1024 | bytes 1344 | tf_op jit(solution)/shard_map/and | solution.py:245
  13.8 1.6 %divide_multiply_fusion = f32[344,1152]{1,0:T(8,128)S(1)} fusion(f32[16,1152]{1,0:T(8,128)S(1)} %mul.201, f32[344,16]{1,0:T(8,128)S(1)} %copy-done.43, f32[1152]{0:T(1024)S(1)} %copy-done.36), kind=kOutput, calls=%fused_computation.33 | convolution fusion | flops 78068736 | bytes 1685504 | tf_op jit(solution)/shard_map/dot_general | solution.py:78
  15.5 0.7 %fusion.33 = f32[2,2,128]{2,1,0:T(2,128)} fusion(f32[2,2,128]{2,1,0:T(2,128)S(1)} %copy-done.37), kind=kOutput, calls=%fused_computation.46 | output fusion | flops 769 | bytes 4096 | tf_op jit(solution)/shard_map/sub | solution.py:301
  16.2 2.6 %collective-permute-start.1 = (s32[4,256]{1,0:T(4,128)S(1)}, s32[4,256]{1,0:T(4,128)S(1)}, u32[]{:S(2)}, u32[]{:S(2)}) collective-permute-start(s32[4,256]{1,0:T(4,128)S(1)} %pad_add_fusion.7), channel_id=1, source_target_pairs={{0,2},{1,3},{2,0},{3,1},{4,6},{5,7},{6,4},{7,5},{8,10},{9,11},{10,... | collective-permute-start | bytes 12296 | tf_op jit(solution)/shard_map/ppermute | solution.py:103
  18.8 0.6 %convert_compare_fusion = pred[128,128]{1,0:T(8,128)(4,1)} fusion(), kind=kLoop, calls=%fused_computation.103 | loop fusion | flops 49152 | bytes 16384 | tf_op jit(solution)/shard_map/gt | solution.py:229
  19.4 1.0 %collective-permute-done.1 = s32[4,256]{1,0:T(4,128)S(1)} collective-permute-done((s32[4,256]{1,0:T(4,128)S(1)}, s32[4,256]{1,0:T(4,128)S(1)}, u32[]{:S(2)}, u32[]{:S(2)}) %collective-permute-start.1) | collective-permute-done | bytes 4128 | tf_op jit(solution)/shard_map/ppermute | solution.py:103
  20.4 2.1 %collective-permute-start.2 = (s32[4,512]{1,0:T(4,128)S(1)}, s32[4,512]{1,0:T(4,128)S(1)}, u32[]{:S(2)}, u32[]{:S(2)}) collective-permute-start(s32[4,512]{1,0:T(4,128)S(1)} %pad_add_fusion.5), channel_id=1, source_target_pairs={{0,4},{1,5},{2,6},{3,7},{4,0},{5,1},{6,2},{7,3},{8,12},{9,13},{10,... | collective-permute-start | bytes 24584 | tf_op jit(solution)/shard_map/ppermute | solution.py:103
  22.5 0.6 iota_compare_fusion.11
  23.1 1.0 %collective-permute-done.2 = s32[4,512]{1,0:T(4,128)S(1)} collective-permute-done((s32[4,512]{1,0:T(4,128)S(1)}, s32[4,512]{1,0:T(4,128)S(1)}, u32[]{:S(2)}, u32[]{:S(2)}) %collective-permute-start.2) | collective-permute-done | bytes 8224 | tf_op jit(solution)/shard_map/ppermute | solution.py:103
  24.2 0.6 copy-done.8
  24.8 0.6 %pad_add_fusion.3 = s32[4,1024]{1,0:T(4,128)} fusion(s32[2,1024]{1,0:T(2,128)S(1)} %get-tuple-element.19, s32[2,1024]{1,0:T(2,128)S(1)} %get-tuple-element.18), kind=kLoop, calls=%fused_computation.126 | loop fusion | flops 4096 | bytes 32768 | tf_op jit(solution)/shard_map/concatenate | solution.py:107
  25.4 3.0 %collective-permute-start.3 = (s32[4,1024]{1,0:T(4,128)}, s32[4,1024]{1,0:T(4,128)}, u32[]{:S(2)}, u32[]{:S(2)}) collective-permute-start(s32[4,1024]{1,0:T(4,128)} %pad_add_fusion.3), channel_id=1, source_target_pairs={{0,8},{1,9},{2,10},{3,11},{4,12},{5,13},{6,14},{7,15},{8,0},{9,1},... | collective-permute-start | bytes 49160 | tf_op jit(solution)/shard_map/ppermute | solution.py:103
  28.4 0.6 iota_compare_fusion.13
  29.0 1.0 %slice.251 = bf16[344,1024]{1,0:T(8,128)(2,1)} slice(f32[344,1152]{1,0:T(8,128)S(1)} %divide_multiply_fusion), slice={[0:344], [0:1024]} | slice | bytes 1409024 | tf_op jit(solution)/shard_map/slice | solution.py:179
  30.0 1.5 %copy.40 = bf16[344,1024]{0,1:T(8,128)(2,1)S(1)} copy(bf16[344,1024]{1,0:T(8,128)(2,1)} %slice.251) | data formatting | bytes 1409024 | tf_op jit(solution)/shard_map/slice | solution.py:179
  31.5 1.4 %mul.226 = f32[16,64]{1,0:T(8,128)} reshape(f32[1024]{0:T(1024)} %param.29) | data formatting | bytes 8192 | tf_op jit(solution)/shard_map/mul | solution.py:23
  32.9 0.8 %pad_add_fusion = (s32[4,2048]{1,0:T(4,128)S(1)}, s32[4,2048]{1,0:T(4,128)S(1)}) fusion(s32[4,1024]{1,0:T(4,128)} %collective-permute-done.3, s32[2,1024]{1,0:T(2,128)} %copy-done.9, s32[2,1024]{1,0:T(2,128)} %copy-done.8), kind=kLoop, calls=%fused_computation.110 | loop fusion | flops 32768 | bytes 98304 | tf_op jit(solution)/shard_map/concatenate | solution.py:105
  33.8 0.8 %fusion.128 = s32[1,4,16,128]{3,1,2,0:T(4,128)S(1)} fusion(s32[4,2048]{1,0:T(4,128)S(1)} %pad_add_fusion.1, pred[2048]{0:T(1024)(128)(4,1)} %get-tuple-element.46, pred[2048]{0:T(1024)(128)(4,1)} %get-tuple-element.47, pred[2048]{0:T(1024)(128)(4,1)} %get-tuple-element.48, pred[2048]{0:T(1024)(128)(4,1)} %get-tuple-element.49), kind=kLoop, calls=%fused_computation.211 | loop fusion | flops 106496 | bytes 73728
  34.6 0.8 %select_select_fusion = s32[4,2048]{1,0:T(4,128)S(1)} fusion(s32[4,2048]{1,0:T(4,128)S(1)} %pad_add_fusion.1, pred[2048]{0:T(1024)(128)(4,1)} %get-tuple-element.46, pred[2048]{0:T(1024)(128)(4,1)} %get-tuple-element.47, pred[2048]{0:T(1024)(128)(4,1)} %get-tuple-element.48, pred[2048]{0:T(1024)(128)(4,1)} %get-tuple-element.49), kind=kLoop, calls=%fused_computation.116 | loop fusion | flops 106496 | bytes 73728 | tf_op jit(solution)/shard_map/jit(_where)/select_n | solution.py:90
  35.5 2.2 %convolution_convert_fusion.1 = bf16[4,128,1024]{2,1,0:T(8,128)(2,1)S(1)} fusion(s32[4,128]{1,0:T(4,128)S(1)} %pad_add_fusion.9, f32[344,1152]{1,0:T(8,128)} %copy-done.1), kind=kOutput, calls=%fused_computation.35 | convolution fusion | flops 361410560 | bytes 1755136 | tf_op jit(solution)/shard_map/rtg,gc->rtc/dot_general | solution.py:206
  37.7 1.1 %fusion.41 = f32[4,128,128]{1,2,0:T(8,128)} fusion(s32[4,128]{1,0:T(4,128)S(1)} %pad_add_fusion.9, f32[344,1152]{1,0:T(8,128)S(1)} %copy-done.2), kind=kOutput, calls=%fused_computation.59 | convolution fusion | flops 270708736 | bytes 440320 | tf_op jit(solution)/shard_map/rtg,gc->rtc/dot_general | solution.py:209
  39.0 0.9 %fusion.47 = f32[4,16,16,128]{3,2,1,0:T(8,128)S(1)} fusion(f32[16]{0:T(128)S(1)} %copy-done.30, f32[16]{0:T(128)S(1)} %copy-done.24, f32[16]{0:T(128)S(1)} %copy-done.26, f32[16]{0:T(128)S(1)} %copy-done.28, f32[16]{0:T(128)S(1)} %copy-done.22, f32[16]{0:T(128)S(1)} %copy-done.45, pred[4,16,128]{2,1,0:T(8,128)(4,1)S(1)} %get-tuple-element.11, ...), kind=kOutput, calls=%fused_computation.72 | convolution fusion | flops 203309056 | bytes 557440 | tf_op jit(solution)/shard_map/...s,st->...t/dot_general | solution.py:143
  40.5 0.7 %subtract_convert_fusion = (bf16[4,16,16,128]{3,2,1,0:T(8,128)(2,1)S(1)}, bf16[4,16,16,128]{3,2,1,0:T(8,128)(2,1)S(1)}) fusion(f32[4,16,16]{2,1,0:T(8,128)S(1)} %exponential_select_fusion, f32[16]{0:T(128)S(1)} %copy-done.30, f32[16]{0:T(128)S(1)} %copy-done.24, pred[4,16,128]{2,1,0:T(8,128)(4,1)S(1)} %get-tuple-element.11, f32[16]{0:T(128)S(1)} %copy-done.26, ...), kind=kLoop, calls=%fused_computation.69 | loop fusion | flops 2752512 | bytes 1089856 | tf_op jit(solution)/shard_map/convert_element_type | solution.py:139
  41.2 2.1 %fusion.31 = f32[4,32,344]{2,1,0:T(8,128)S(1)} fusion(s32[4,16,128]{2,1,0:T(8,128)S(1)} %bitcast.104, bf16[4,32,16,128]{3,2,1,0:T(8,128)(2,1)S(1)} %pad_maximum_fusion), kind=kOutput, calls=%fused_computation.43 | convolution fusion | flops 183173120 | bytes 733184 | tf_op jit(solution)/shard_map/uhbs,ubsg->uhg/dot_general | solution.py:253
  43.4 1.5 %copy.37 = bf16[4,128,1024]{1,2,0:T(8,128)(2,1)} copy(bf16[4,128,1024]{2,1,0:T(8,128)(2,1)S(1)} %convolution_convert_fusion.1) | data formatting | bytes 2097152 | tf_op jit(solution)/shard_map/convert_element_type | solution.py:206
  45.3 3.5 %multiply_convert_fusion = (bf16[4,16,344,64]{3,2,0,1:T(8,128)(2,1)S(1)}, bf16[4,16,344,64]{3,2,0,1:T(8,128)(2,1)S(1)}) fusion(f32[344,64]{1,0:T(8,128)S(1)} %slice-done, f32[4,16,344]{2,0,1:T(4,128)S(1)} %copy.39), kind=kLoop, calls=%fused_computation.3 | loop fusion | flops 7045120 | bytes 5812224 | tf_op jit(solution)/shard_map/convert_element_type | solution.py:138
  48.9 3.4 %fusion.22 = f32[4,16,64,128]{3,2,0,1:T(8,128)S(1)} fusion(bf16[16,344,64,1]{1,2,3,0:T(8,128)(2,1)S(1)} %bitcast.98, bf16[4,16,344,64]{3,2,0,1:T(8,128)(2,1)S(1)} %get-tuple-element.7, bf16[4,16,344,64]{3,2,0,1:T(8,128)(2,1)S(1)} %get-tuple-element.6), kind=kOutput, calls=%fused_computation.32 | convolution fusion | flops 371982336 | bytes 8437760 | tf_op jit(solution)/shard_map/hgp,uhgn->uhpn/dot_general | solution.py:261
  52.3 1.6 %fusion.11 = f32[4,16,64,128]{3,2,1,0:T(8,128)S(1)} fusion(bf16[4,128,16,64]{1,3,2,0:T(8,128)(2,1)S(1)} %bitcast.100, f32[4,16,128]{2,1,0:T(8,128)S(1)} %copy-done.12, f32[4,16,128]{2,1,0:T(8,128)S(1)} %copy-done.15, f32[4,128,128]{2,1,0:T(8,128)S(1)} %fusion.68, pred[128,128]{1,0:T(8,128)(4,1)S(1)} %copy-done.16), kind=kOutput, calls=%fused_computation.17 | convolution fusion | flops 140509184 | bytes 3489792 | tf_op jit(solution)/shard_map/uhts,ushp->uthp/dot_general | solution.py:232
  54.0 2.2 %multiply_reduce_fusion = (f32[4,128,16]{1,2,0:T(8,128)S(1)}, f32[4,128,16,64]{1,3,2,0:T(8,128)S(1)}) fusion(f32[4,128,16,64]{1,3,2,0:T(8,128)S(1)} %bitcast.99, bf16[4,128,16,64]{1,3,2,0:T(8,128)(2,1)S(1)} %bitcast.101, f32[16]{0:T(128)S(1)} %copy-done.41, f32[4,128,16]{1,2,0:T(8,128)S(1)} %copy-done.13, f32[4,128,128]{1,2,0:T(8,128)S(1)} %copy-done.4, ...), kind=kOutput, calls=%fused_computation.25 | convolution fusion | flops 207872000 | bytes 11731456 | tf_op jit(solution)/shard_map/utn,uhpn->uthp/dot_general | solution.py:270
  56.2 0.5 multiply_convert_fusion.3
  56.7 0.7 %copy-done.6 = bf16[1024,512]{1,0:T(8,128)(2,1)S(1)} copy-done((bf16[1024,512]{1,0:T(8,128)(2,1)S(1)}, bf16[1024,512]{1,0:T(8,128)(2,1)}, u32[]{:S(2)}) %copy-start.6) | copy-done | bytes 1048600
  57.4 0.7 %convolution_convert_fusion.2 = bf16[4,128,512]{2,1,0:T(8,128)(2,1)S(1)} fusion(bf16[4,128,1024]{1,2,0:T(8,128)(2,1)S(1)} %bitcast.97, bf16[1024,512]{1,0:T(8,128)(2,1)S(1)} %copy-done.6), kind=kOutput, calls=%fused_computation.37 | convolution fusion | flops 537133056 | bytes 2621440 | tf_op jit(solution)/shard_map/gre,ed->grd/dot_general | solution.py:280
  58.2 0.9 %rev.3 = bf16[2,128,512]{2,1,0:T(8,128)(2,1)S(1)} reverse(bf16[2,128,512]{2,1,0:T(8,128)(2,1)S(1)} %slice.204), dimensions={1,2} | reverse | bytes 524288 | tf_op jit(solution)/shard_map/rev | solution.py:287
  59.9 0.6 %multiply_reduce_fusion.1 = f32[2,128]{1,0:T(2,128)} fusion(f32[2,2,128]{2,1,0:T(2,128)S(1)} %select_reduce_fusion.1, f32[2,2,128]{2,1,0:T(2,128)S(1)} %copy-done.46), kind=kOutput, calls=%fused_computation.173 | output fusion | flops 2049 | bytes 5120 | tf_op jit(solution)/shard_map/reduce_sum | solution.py:302
  (138 shorter events, 2.8 us)
Async XLA Ops:
  0.6 6.3 %copy-start = (bf16[512,1152]{1,0:T(8,128)(2,1)S(1)}, bf16[512,1152]{1,0:T(8,128)(2,1)}, u32[]{:S(2)}) copy-start(bf16[512,1152]{1,0:T(8,128)(2,1)} %param.21) | copy-start | bytes 3538948
  0.6 9.7 %copy-start.18 = (f32[512]{0:T(512)S(1)}, f32[512]{0:T(512)}, u32[]{:S(2)}) copy-start(f32[512]{0:T(512)} %param.20) | copy-start | bytes 6148
  0.7 8.1 %copy-start.29 = (f32[16]{0:T(128)S(1)}, f32[16]{0:T(128)}, u32[]{:S(2)}) copy-start(f32[16]{0:T(128)} %param.26) | copy-start | bytes 196
  0.7 9.6 %copy-start.5 = (bf16[512,1024]{1,0:T(8,128)(2,1)S(1)}, bf16[512,1024]{1,0:T(8,128)(2,1)}, u32[]{:S(2)}) copy-start(bf16[512,1024]{1,0:T(8,128)(2,1)} %param.22) | copy-start | bytes 3145732
  2.3 10.0 %copy-start.19 = (s32[4,128]{1,0:T(4,128)}, s32[4,128]{1,0:T(4,128)S(1)}, u32[]{:S(2)}) copy-start(s32[4,128]{1,0:T(4,128)S(1)} %pad_add_fusion.8) | copy-start | bytes 6148
  2.3 13.8 %collective-permute-start = (s32[4,128]{1,0:T(4,128)S(1)}, s32[4,128]{1,0:T(4,128)S(1)}, u32[]{:S(2)}, u32[]{:S(2)}) collective-permute-start(s32[4,128]{1,0:T(4,128)S(1)} %pad_add_fusion.8), channel_id=1, source_target_pairs={{0,1},{1,0},{2,3},{3,2},{4,5},{5,4},{6,7},{7,6},{8,9},{9,8},{10,11... | collective-permute-start | bytes 6152 | tf_op jit(solution)/shard_map/ppermute | solution.py:103
  6.1 6.3 %copy-start.21 = (f32[16]{0:T(128)}, f32[16]{0:T(128)S(1)}, u32[]{:S(2)}) copy-start(f32[16]{0:T(128)S(1)} %get-tuple-element.36) | copy-start | bytes 196
  6.1 6.3 %copy-start.23 = (f32[16]{0:T(128)}, f32[16]{0:T(128)S(1)}, u32[]{:S(2)}) copy-start(f32[16]{0:T(128)S(1)} %get-tuple-element.37) | copy-start | bytes 196
  6.1 6.3 %copy-start.25 = (f32[16]{0:T(128)}, f32[16]{0:T(128)S(1)}, u32[]{:S(2)}) copy-start(f32[16]{0:T(128)S(1)} %get-tuple-element.38) | copy-start | bytes 196
  6.1 6.3 %copy-start.27 = (f32[16]{0:T(128)}, f32[16]{0:T(128)S(1)}, u32[]{:S(2)}) copy-start(f32[16]{0:T(128)S(1)} %get-tuple-element.39) | copy-start | bytes 196
  6.8 5.6 %copy-start.44 = (f32[16]{0:T(128)}, f32[16]{0:T(128)S(1)}, u32[]{:S(2)}) copy-start(f32[16]{0:T(128)S(1)} %exponential_negate_fusion) | copy-start | bytes 196
  6.9 6.3 %copy-start.31 = (pred[4,16]{1,0:T(4,128)(4,1)}, pred[4,16]{1,0:T(4,128)(4,1)S(1)}, u32[]{:S(2)}) copy-start(pred[4,16]{1,0:T(4,128)(4,1)S(1)} %iota_compare_fusion.18) | copy-start | bytes 196
  7.9 4.5 %copy-start.39 = (bf16[512,2]{0,1:T(2,128)(2,1)S(1)}, bf16[512,2]{0,1:T(2,128)(2,1)}, u32[]{:S(2)}) copy-start(bf16[512,2]{0,1:T(2,128)(2,1)} %param.32) | copy-start | bytes 6148
  8.7 5.1 %copy-start.36 = (f32[1152]{0:T(1024)S(1)}, f32[1152]{0:T(1024)}, u32[]{:S(2)}) copy-start(f32[1152]{0:T(1024)} %param.25) | copy-start | bytes 13828
  8.7 5.1 %copy-start.43 = (f32[344,16]{1,0:T(8,128)S(1)}, f32[344,16]{1,0:T(8,128)}, u32[]{:S(2)}) copy-start(f32[344,16]{1,0:T(8,128)} %constant.138.clone) | copy-start | bytes 66052
  9.7 3.5 %copy-start.14 = (f32[4,16,128]{2,1,0:T(8,128)}, f32[4,16,128]{2,1,0:T(8,128)S(1)}, u32[]{:S(2)}) copy-start(f32[4,16,128]{2,1,0:T(8,128)S(1)} %fusion.75) | copy-start | bytes 98308
  13.8 1.6 %copy-start.37 = (f32[2,2,128]{2,1,0:T(2,128)S(1)}, f32[2,2,128]{2,1,0:T(2,128)}, u32[]{:S(2)}) copy-start(f32[2,2,128]{2,1,0:T(2,128)} %param.34) | copy-start | bytes 6148
  13.8 2.3 %copy-start.17 = (s32[2,128]{1,0:T(2,128)S(1)}, s32[2,128]{1,0:T(2,128)}, u32[]{:S(2)}) copy-start(s32[2,128]{1,0:T(2,128)} %param.18) | copy-start | bytes 3076
  15.5 19.9 %copy-start.1 = (f32[344,1152]{1,0:T(8,128)}, f32[344,1152]{1,0:T(8,128)S(1)}, u32[]{:S(2)}) copy-start(f32[344,1152]{1,0:T(8,128)S(1)} %divide_multiply_fusion) | copy-start | bytes 4755460
  16.2 4.2 %collective-permute-start.1 = (s32[4,256]{1,0:T(4,128)S(1)}, s32[4,256]{1,0:T(4,128)S(1)}, u32[]{:S(2)}, u32[]{:S(2)}) collective-permute-start(s32[4,256]{1,0:T(4,128)S(1)} %pad_add_fusion.7), channel_id=1, source_target_pairs={{0,2},{1,3},{2,0},{3,1},{4,6},{5,7},{6,4},{7,5},{8,10},{9,11},{10,... | collective-permute-start | bytes 12296 | tf_op jit(solution)/shard_map/ppermute | solution.py:103
  20.4 3.8 %collective-permute-start.2 = (s32[4,512]{1,0:T(4,128)S(1)}, s32[4,512]{1,0:T(4,128)S(1)}, u32[]{:S(2)}, u32[]{:S(2)}) collective-permute-start(s32[4,512]{1,0:T(4,128)S(1)} %pad_add_fusion.5), channel_id=1, source_target_pairs={{0,4},{1,5},{2,6},{3,7},{4,0},{5,1},{6,2},{7,3},{8,12},{9,13},{10,... | collective-permute-start | bytes 24584 | tf_op jit(solution)/shard_map/ppermute | solution.py:103
  25.4 7.5 %collective-permute-start.3 = (s32[4,1024]{1,0:T(4,128)}, s32[4,1024]{1,0:T(4,128)}, u32[]{:S(2)}, u32[]{:S(2)}) collective-permute-start(s32[4,1024]{1,0:T(4,128)} %pad_add_fusion.3), channel_id=1, source_target_pairs={{0,8},{1,9},{2,10},{3,11},{4,12},{5,13},{6,14},{7,15},{8,0},{9,1},... | collective-permute-start | bytes 49160 | tf_op jit(solution)/shard_map/ppermute | solution.py:103
  32.8 6.1 %copy-start.22 = (f32[16]{0:T(128)S(1)}, f32[16]{0:T(128)}, u32[]{:S(2)}) copy-start(f32[16]{0:T(128)} %copy-done.21) | copy-start | bytes 196
  32.8 6.1 %copy-start.24 = (f32[16]{0:T(128)S(1)}, f32[16]{0:T(128)}, u32[]{:S(2)}) copy-start(f32[16]{0:T(128)} %copy-done.23) | copy-start | bytes 196
  32.8 6.1 %copy-start.26 = (f32[16]{0:T(128)S(1)}, f32[16]{0:T(128)}, u32[]{:S(2)}) copy-start(f32[16]{0:T(128)} %copy-done.25) | copy-start | bytes 196
  32.8 6.1 %copy-start.28 = (f32[16]{0:T(128)S(1)}, f32[16]{0:T(128)}, u32[]{:S(2)}) copy-start(f32[16]{0:T(128)} %copy-done.27) | copy-start | bytes 196
  32.8 6.1 %copy-start.30 = (f32[16]{0:T(128)S(1)}, f32[16]{0:T(128)}, u32[]{:S(2)}) copy-start(f32[16]{0:T(128)} %param.26) | copy-start | bytes 196
  32.9 6.1 %copy-start.45 = (f32[16]{0:T(128)S(1)}, f32[16]{0:T(128)}, u32[]{:S(2)}) copy-start(f32[16]{0:T(128)} %copy-done.44) | copy-start | bytes 196
  35.4 2.3 %copy-start.2 = (f32[344,1152]{1,0:T(8,128)S(1)}, f32[344,1152]{1,0:T(8,128)}, u32[]{:S(2)}) copy-start(f32[344,1152]{1,0:T(8,128)} %copy-done.1) | copy-start | bytes 4755460
  37.7 2.5 %copy-start.11 = (pred[4,16,16]{2,1,0:T(8,128)(4,1)S(1)}, pred[4,16,16]{2,1,0:T(8,128)(4,1)}, u32[]{:S(2)}) copy-start(pred[4,16,16]{2,1,0:T(8,128)(4,1)} %broadcast_and_fusion) | copy-start | bytes 3076
  37.7 2.7 %copy-start.32 = (pred[4,16]{1,0:T(4,128)(4,1)S(1)}, pred[4,16]{1,0:T(4,128)(4,1)}, u32[]{:S(2)}) copy-start(pred[4,16]{1,0:T(4,128)(4,1)} %copy-done.31) | copy-start | bytes 196
  43.3 1.6 %copy-start.4 = (f32[4,128,128]{1,2,0:T(8,128)S(1)}, f32[4,128,128]{1,2,0:T(8,128)}, u32[]{:S(2)}) copy-start(f32[4,128,128]{1,2,0:T(8,128)} %fusion.41) | copy-start | bytes 786436
  43.3 2.0 %slice-start = ((f32[344,1152]{1,0:T(8,128)}), f32[344,64]{1,0:T(8,128)S(1)}, s32[]{:S(2)}) async-start(f32[344,1152]{1,0:T(8,128)} %copy-done.1), calls=%async_computation | async-start | bytes 352256 | tf_op jit(solution)/shard_map/slice | solution.py:180
  48.8 3.4 %copy-start.7 = (bf16[4,128,1024]{1,2,0:T(8,128)(2,1)S(1)}, bf16[4,128,1024]{1,2,0:T(8,128)(2,1)}, u32[]{:S(2)}) copy-start(bf16[4,128,1024]{1,2,0:T(8,128)(2,1)} %copy.37) | copy-start | bytes 3145732
  48.9 3.4 %copy-start.12 = (f32[4,16,128]{2,1,0:T(8,128)S(1)}, f32[4,16,128]{2,1,0:T(8,128)}, u32[]{:S(2)}) copy-start(f32[4,16,128]{2,1,0:T(8,128)} %compare_select_fusion.2) | copy-start | bytes 98308
  48.9 3.4 %copy-start.15 = (f32[4,16,128]{2,1,0:T(8,128)S(1)}, f32[4,16,128]{2,1,0:T(8,128)}, u32[]{:S(2)}) copy-start(f32[4,16,128]{2,1,0:T(8,128)} %copy-done.14) | copy-start | bytes 98308
  48.9 3.4 %copy-start.16 = (pred[128,128]{1,0:T(8,128)(4,1)S(1)}, pred[128,128]{1,0:T(8,128)(4,1)}, u32[]{:S(2)}) copy-start(pred[128,128]{1,0:T(8,128)(4,1)} %convert_compare_fusion) | copy-start | bytes 49156
  52.3 1.7 %copy-start.3 = (f32[4,128,1024]{1,2,0:T(8,128)S(1)}, f32[4,128,1024]{1,2,0:T(8,128)}, u32[]{:S(2)}) copy-start(f32[4,128,1024]{1,2,0:T(8,128)} %fusion.42) | copy-start | bytes 6291460
  52.3 1.7 %copy-start.13 = (f32[4,128,16]{1,2,0:T(8,128)S(1)}, f32[4,128,16]{1,2,0:T(8,128)}, u32[]{:S(2)}) copy-start(f32[4,128,16]{1,2,0:T(8,128)} %exponential_bitcast_fusion) | copy-start | bytes 98308
  52.3 1.7 %copy-start.41 = (f32[16]{0:T(128)S(1)}, f32[16]{0:T(128)}, u32[]{:S(2)}) copy-start(f32[16]{0:T(128)} %param.28) | copy-start | bytes 196
  54.0 2.2 %copy-start.10 = (f32[16,64]{1,0:T(8,128)S(1)}, f32[16,64]{1,0:T(8,128)}, u32[]{:S(2)}) copy-start(f32[16,64]{1,0:T(8,128)} %mul.226) | copy-start | bytes 12292
  56.7 2.4 %copy-start.20 = (s32[4,128]{1,0:T(4,128)S(1)}, s32[4,128]{1,0:T(4,128)}, u32[]{:S(2)}) copy-start(s32[4,128]{1,0:T(4,128)} %copy-done.19) | copy-start | bytes 6148
  57.4 2.1 %copy-start.34 = (bf16[512,1]{0,1:T(2,128)(2,1)S(1)}, bf16[512,1]{0,1:T(2,128)(2,1)}, u32[]{:S(2)}) copy-start(bf16[512,1]{0,1:T(2,128)(2,1)} %get-tuple-element.30) | copy-start | bytes 3076
  57.4 2.1 %copy-start.35 = (bf16[512,1]{0,1:T(2,128)(2,1)S(1)}, bf16[512,1]{0,1:T(2,128)(2,1)}, u32[]{:S(2)}) copy-start(bf16[512,1]{0,1:T(2,128)(2,1)} %get-tuple-element.31) | copy-start | bytes 3076
  57.4 2.2 %copy-start.38 = (f32[512]{0:T(512)S(1)}, f32[512]{0:T(512)}, u32[]{:S(2)}) copy-start(f32[512]{0:T(512)} %param.31) | copy-start | bytes 6148
  57.4 2.2 %copy-start.40 = (bf16[512,2]{0,1:T(2,128)(2,1)S(1)}, bf16[512,2]{0,1:T(2,128)(2,1)}, u32[]{:S(2)}) copy-start(bf16[512,2]{0,1:T(2,128)(2,1)} %param.32) | copy-start | bytes 6148
  57.4 2.5 %copy-start.33 = (s32[2,2,128]{2,1,0:T(2,128)S(1)}, s32[2,2,128]{2,1,0:T(2,128)}, u32[]{:S(2)}) copy-start(s32[2,2,128]{2,1,0:T(2,128)} %param.33) | copy-start | bytes 6148
  57.4 2.5 %copy-start.46 = (f32[2,2,128]{2,1,0:T(2,128)S(1)}, f32[2,2,128]{2,1,0:T(2,128)}, u32[]{:S(2)}) copy-start(f32[2,2,128]{2,1,0:T(2,128)} %fusion.33) | copy-start | bytes 6148
  (4 other events, 4.0 us)

commit v7 on v6

--- a/solution.py
+++ b/solution.py
@@ -208,7 +208,9 @@
     )
     bc_loc = jnp.einsum("rtg,gc->rtc", oh_loc, bc_tab, precision=HIGH)
     oh_tok = onehot(local_tok, BASES)
-    z_loc = jnp.einsum("rtk,kc->rtc", oh_tok, z_rows, preferred_element_type=jnp.float32)
+    z_loc = jnp.einsum("rtk,kc->rtc", oh_tok, z_rows, preferred_element_type=jnp.float32).astype(
+        jnp.bfloat16
+    )
     dt_loc = jax.nn.softplus(heads_lookup(dt_rows, local_tok) + dt_bias[:, None])
     ld_loc = neg_rate * dt_loc
 
@@ -258,13 +260,9 @@
     )
     per_gram = per_gram[:, :HEADS] + per_gram[:, HEADS:]
     b_hi, b_lo = split_bf16(per_gram[..., None] * b_tab[None, None])
-    both = jnp.einsum(
-        "hgp,uhgn->uhpn",
-        x_heads,
-        jnp.concatenate([b_hi, b_lo], axis=-1),
-        preferred_element_type=jnp.float32,
-    )
-    start_state = both[..., :NS] + both[..., NS:]
+    start_state = jnp.einsum(
+        "hgp,uhgn->uhpn", x_heads, b_hi, preferred_element_type=jnp.float32
+    ) + jnp.einsum("hgp,uhgn->uhpn", x_heads, b_lo, preferred_element_type=jnp.float32)
 
     y_inter = (
         jnp.einsum("utn,uhpn->uthp", c_u, start_state, precision=lax.Precision.HIGH)
@@ -272,11 +270,9 @@
     )
     y_u = y_intra + y_inter + d_skip[:, None] * x_u.astype(jnp.float32)
     z_u = per_unit(z_loc, 1).reshape(units, BLK, HEADS, HD)
-    gated_y = y_u * jax.nn.silu(z_u)
-    normed = rms_gain(gated_y, inner_gain.reshape(HEADS, HD)).astype(jnp.bfloat16)
-    normed = jnp.moveaxis(normed.reshape(streams, nloc, BLK, INNER), 1, 1).reshape(
-        streams, count, INNER
-    )
+    gated_y = y_u * jax.nn.silu(z_u.astype(jnp.float32))
+    scaled_y = gated_y * lax.rsqrt(jnp.mean(gated_y * gated_y, axis=-1, keepdims=True) + EPS)
+    normed = (scaled_y.reshape(streams, count, INNER) * inner_gain).astype(jnp.bfloat16)
     outputs = jnp.einsum("gre,ed->grd", normed, w_out, preferred_element_type=jnp.float32).astype(
         jnp.bfloat16
     )

time: 61.1 us -> 63.1 us (1.033)
  other arithmetic: 16.3 us -> 10.5 us
  matrix products: 23.1 us -> 28.1 us
  local copies, waits for them, and re-layouts: 9.43 us -> 12.3 us
    convert_element_type x2 -> x0, other arithmetic: 4.01 us -> none  [the longest x1 3.53 us: split_bf16(): high = values.astype(jnp.bfloat16)]
    dot_general x1, matrix products: 1.64 us -> 4.62 us  [local(): jnp.einsum('uhts,ushp->uthp', weights, x_u, preferred_element_type=jnp.fl...]
    dot_general x1, matrix products: 1.6 us -> 3.73 us  [gram_tables(): jnp.dot(jnp.asarray(gram_layout()), taps, precision=HIGH)]
    reshape x0 -> x1, local copies, waits for them, and re-layouts: none -> 1.85 us  [local(): scaled_y.reshape(streams, count, INNER) * inner_gain]
    convert_element_type x0 -> x1, local copies, waits for them, and re-layouts: none -> 1.85 us  [local(): gated_y = y_u * jax.nn.silu(z_u.astype(jnp.float32))]
    dot_general x1, matrix products: 0.73 us -> 2.58 us  [local(): jnp.einsum('gre,ed->grd', normed, w_out, preferred_element_type=jnp.float32)]
    dot_general x1, matrix products: 2.22 us -> 0.76 us  [local(): jnp.einsum('rtg,gc->rtc', oh_loc, x_tab, preferred_element_type=jnp.float32)]
    mul x1 -> x0, local copies, waits for them, and re-layouts: 1.36 us -> none  [rms_gain(): values * lax.rsqrt(jnp.mean(values * values, axis=-1, keepdims=True) + EPS)]
  transfers between devices with their start and end apart: 4 -> 4, of which waited for: 2 -> 2; matrix products, arithmetic and copies ran while one was open for 31% -> 32% of each run, Pallas kernels for 0% -> 0%
where the time goes in v7:
time: 63.1 us; the launch traced here: 62.7 us
  matrix products  28.1 us (45%)
  local copies, waits for them, and re-layouts  12.3 us (19%)
  other arithmetic  10.5 us (17%)
  starting transfers between devices  8.21 us (13%)
  waiting for transfers between devices  2 us (3%)
  between operations  1.55 us (2%)
    ppermute x4, starting transfers between devices, gather_all(): lax.ppermute(held, axis, [(src, src ^ mask) for src in range(count)])  8.21 us
    dot_general x1, matrix products, local(): jnp.einsum('uhts,ushp->uthp', weights, x_u, preferred_element_type=jnp.fl...  4.62 us
    slice x2, local copies, waits for them, and re-layouts, local(): x_tab = act_tab[:, :INNER].astype(jnp.bfloat16)  3.78 us
    dot_general x1, matrix products, gram_tables(): jnp.dot(jnp.asarray(gram_layout()), taps, precision=HIGH)  3.73 us
    dot_general x1, matrix products, local(): jnp.einsum('utn,uhpn->uthp', c_u, start_state, precision=lax.Precision.HIGH)  2.75 us
    dot_general x1, matrix products, local(): jnp.einsum('gre,ed->grd', normed, w_out, preferred_element_type=jnp.float32)  2.58 us
    dot_general x1, matrix products, local(): jnp.einsum('hgp,uhgn->uhpn', x_heads, b_lo, preferred_element_type=jnp.fl...  2.36 us
    dot_general x1, matrix products, local(): jnp.einsum('hgp,uhgn->uhpn', x_heads, b_hi, preferred_element_type=jnp.fl...  2.31 us
  transfers between devices with their start and end apart: 4, of which 2 were waited for; matrix products, arithmetic and copies ran while one was open for 32% of the time, Pallas kernels for 0%

profile of v7, /device:TPU:0, one launch (start us, length us, event | category | flops | bytes accessed | tf_op | source)
XLA Modules:
  0.0 62.7 jit_solution(7871893840801331172)
XLA Ops:
  0.7 0.9 %fusion.40 = s32[2,128]{1,0:T(2,128)S(1)} fusion(s32[2,128]{1,0:T(2,128)} %param.18), kind=kOutput, calls=%fused_computation.57 | convolution fusion | flops 99072 | bytes 2048 | tf_op jit(solution)/shard_map/dot_general | solution.py:186
  1.6 0.7 %pad_add_fusion.8 = s32[4,128]{1,0:T(4,128)S(1)} fusion(s32[2,128]{1,0:T(2,128)S(1)} %fusion.40, s32[2,128]{1,0:T(2,128)} %param.18), kind=kLoop, calls=%fused_computation.175 | loop fusion | flops 512 | bytes 4096 | tf_op jit(solution)/shard_map/concatenate | solution.py:189
  2.3 0.5 collective-permute-start
  2.7 0.7 %broadcast_compare_fusion.7 = (pred[4,128]{1,0:T(4,128)(4,1)S(1)}, pred[4,128]{1,0:T(4,128)(4,1)S(1)}, pred[4,128]{1,0:T(4,128)(4,1)S(1)}, pred[4,128]{1,0:T(4,128)(4,1)S(1)}) fusion(s32[2,128]{1,0:T(2,128)S(1)} %fusion.40, s32[2,128]{1,0:T(2,128)} %param.18), kind=kLoop, calls=%fused_computation.189 | loop fusion | flops 2560 | bytes 4096 | tf_op jit(solution)/shard_map/eq | solution.py:122
  3.4 0.9 %fusion.36 = bf16[2,512]{1,0:T(2,128)(2,1)S(1)} fusion(bf16[2,512]{1,0:T(2,128)(2,1)} %param.19), kind=kOutput, calls=%fused_computation.52 | convolution fusion | flops 1573888 | bytes 4096 | tf_op jit(solution)/shard_map/dot_general | solution.py:176
  4.3 0.8 %fusion.84 = (f32[4]{0:T(128)S(1)}, bf16[4,512]{1,0:T(4,128)(2,1)S(1)}) fusion(bf16[1,512]{1,0:T(2,128)(2,1)S(1)} %get-tuple-element.39, bf16[1,512]{1,0:T(2,128)(2,1)S(1)} %get-tuple-element.38, bf16[2,512]{1,0:T(2,128)(2,1)} %param.19), kind=kLoop, calls=%fused_computation.139 | loop fusion | flops 18428 | bytes 8208 | tf_op jit(solution)/shard_map/reduce_sum | solution.py:23
  5.2 1.9 %fusion.28 = f32[4,128,1024]{2,1,0:T(8,128)S(1)} fusion(bf16[512,1024]{1,0:T(8,128)(2,1)} %param.22, s32[4,128]{1,0:T(4,128)S(1)} %pad_add_fusion.8, bf16[4,512]{1,0:T(4,128)(2,1)S(1)} %get-tuple-element.5, f32[512]{0:T(512)} %param.20, f32[4]{0:T(128)S(1)} %add_rsqrt_fusion.2), kind=kOutput, calls=%fused_computation.37 | convolution fusion | flops 9451520 | bytes 3153936 | tf_op jit(solution)/shard_map/rtk,kc->rtc/dot_general | solution.py:211
  7.1 0.3 fusion.13
  7.7 0.7 %compare_select_fusion.2 = f32[4,16,128]{2,1,0:T(8,128)} fusion(f32[16]{0:T(128)S(1)} %copy-done.27, f32[16]{0:T(128)S(1)} %get-tuple-element.35, f32[16]{0:T(128)S(1)} %get-tuple-element.36, f32[16]{0:T(128)S(1)} %get-tuple-element.37, f32[16]{0:T(128)S(1)} %get-tuple-element.34, pred[4,128]{1,0:T(4,128)(4,1)S(1)} %get-tuple-element.32, ...), kind=kLoop, calls=%fused_computation.103 | loop fusion | flops 114688 | bytes 35136 | tf_op jit(solution)/shard_map/jit(softplus)/select_n | solution.py:214
  8.7 0.6 exponential_bitcast_fusion
  9.6 0.6 fusion.115
  10.2 0.6 broadcast_and_fusion
  10.8 3.7 %divide_multiply_fusion = f32[344,1152]{1,0:T(8,128)} fusion(f32[16,1152]{1,0:T(8,128)S(1)} %mul.199, f32[344,16]{1,0:T(8,128)} %constant.138.clone, f32[1152]{0:T(1024)S(1)} %copy-done.35), kind=kOutput, calls=%fused_computation.34 | convolution fusion | flops 78068736 | bytes 1685504 | tf_op jit(solution)/shard_map/dot_general | solution.py:78
  14.6 0.6 fusion.35
  15.3 2.6 %collective-permute-start.1 = (s32[4,256]{1,0:T(4,128)S(1)}, s32[4,256]{1,0:T(4,128)S(1)}, u32[]{:S(2)}, u32[]{:S(2)}) collective-permute-start(s32[4,256]{1,0:T(4,128)S(1)} %pad_add_fusion.7), channel_id=1, source_target_pairs={{0,2},{1,3},{2,0},{3,1},{4,6},{5,7},{6,4},{7,5},{8,10},{9,11},{10,... | collective-permute-start | bytes 12296 | tf_op jit(solution)/shard_map/ppermute | solution.py:103
  17.9 0.6 convert_compare_fusion
  18.5 1.0 %collective-permute-done.1 = s32[4,256]{1,0:T(4,128)S(1)} collective-permute-done((s32[4,256]{1,0:T(4,128)S(1)}, s32[4,256]{1,0:T(4,128)S(1)}, u32[]{:S(2)}, u32[]{:S(2)}) %collective-permute-start.1) | collective-permute-done | bytes 4128 | tf_op jit(solution)/shard_map/ppermute | solution.py:103
  19.5 2.1 %collective-permute-start.2 = (s32[4,512]{1,0:T(4,128)S(1)}, s32[4,512]{1,0:T(4,128)S(1)}, u32[]{:S(2)}, u32[]{:S(2)}) collective-permute-start(s32[4,512]{1,0:T(4,128)S(1)} %pad_add_fusion.5), channel_id=1, source_target_pairs={{0,4},{1,5},{2,6},{3,7},{4,0},{5,1},{6,2},{7,3},{8,12},{9,13},{10,... | collective-permute-start | bytes 24584 | tf_op jit(solution)/shard_map/ppermute | solution.py:103
  21.6 0.6 iota_compare_fusion.11
  22.2 1.0 %collective-permute-done.2 = s32[4,512]{1,0:T(4,128)S(1)} collective-permute-done((s32[4,512]{1,0:T(4,128)S(1)}, s32[4,512]{1,0:T(4,128)S(1)}, u32[]{:S(2)}, u32[]{:S(2)}) %collective-permute-start.2) | collective-permute-done | bytes 8224 | tf_op jit(solution)/shard_map/ppermute | solution.py:103
  23.3 0.6 copy-done.4
  23.9 0.6 pad_add_fusion.3
  24.5 3.0 %collective-permute-start.3 = (s32[4,1024]{1,0:T(4,128)}, s32[4,1024]{1,0:T(4,128)}, u32[]{:S(2)}, u32[]{:S(2)}) collective-permute-start(s32[4,1024]{1,0:T(4,128)} %pad_add_fusion.3), channel_id=1, source_target_pairs={{0,8},{1,9},{2,10},{3,11},{4,12},{5,13},{6,14},{7,15},{8,0},{9,1},... | collective-permute-start | bytes 49160 | tf_op jit(solution)/shard_map/ppermute | solution.py:103
  27.5 0.6 iota_compare_fusion.13
  28.1 2.3 %slice.239 = bf16[344,1024]{1,0:T(8,128)(2,1)} slice(f32[344,1152]{1,0:T(8,128)} %divide_multiply_fusion), slice={[0:344], [0:1024]} | slice | bytes 1409024 | tf_op jit(solution)/shard_map/slice | solution.py:179
  30.4 1.8 %copy.37 = f32[4,128,1024]{1,2,0:T(8,128)} copy(f32[4,128,1024]{2,1,0:T(8,128)S(1)} %fusion.28) | data formatting | bytes 4194304 | tf_op jit(solution)/shard_map/convert_element_type | solution.py:273
  32.4 1.5 %copy.35 = bf16[344,1024]{0,1:T(8,128)(2,1)S(1)} copy(bf16[344,1024]{1,0:T(8,128)(2,1)} %slice.239) | data formatting | bytes 1409024 | tf_op jit(solution)/shard_map/slice | solution.py:179
  34.0 0.8 %pad_add_fusion = (s32[4,2048]{1,0:T(4,128)S(1)}, s32[4,2048]{1,0:T(4,128)S(1)}) fusion(s32[4,1024]{1,0:T(4,128)} %collective-permute-done.3, s32[2,1024]{1,0:T(2,128)} %copy-done.5, s32[2,1024]{1,0:T(2,128)} %copy-done.4), kind=kLoop, calls=%fused_computation.114 | loop fusion | flops 32768 | bytes 98304 | tf_op jit(solution)/shard_map/concatenate | solution.py:105
  34.9 0.8 %select_select_fusion = s32[4,2048]{1,0:T(4,128)S(1)} fusion(s32[4,2048]{1,0:T(4,128)S(1)} %pad_add_fusion.1, pred[2048]{0:T(1024)(128)(4,1)} %get-tuple-element.44, pred[2048]{0:T(1024)(128)(4,1)} %get-tuple-element.45, pred[2048]{0:T(1024)(128)(4,1)} %get-tuple-element.46, pred[2048]{0:T(1024)(128)(4,1)} %get-tuple-element.47), kind=kLoop, calls=%fused_computation.120 | loop fusion | flops 106496 | bytes 73728 | tf_op jit(solution)/shard_map/jit(_where)/select_n | solution.py:90
  36.0 0.9 %fusion.49 = f32[4,16,16,128]{3,2,1,0:T(8,128)S(1)} fusion(f32[16]{0:T(128)S(1)} %copy-done.28, f32[16]{0:T(128)S(1)} %copy-done.21, f32[16]{0:T(128)S(1)} %copy-done.23, f32[16]{0:T(128)S(1)} %copy-done.25, f32[16]{0:T(128)S(1)} %copy-done.19, f32[16]{0:T(128)S(1)} %copy-done.44, pred[4,16,128]{2,1,0:T(8,128)(4,1)S(1)} %get-tuple-element.9, ...), kind=kOutput, calls=%fused_computation.76 | convolution fusion | flops 203309056 | bytes 557440 | tf_op jit(solution)/shard_map/...s,st->...t/dot_general | solution.py:143
  36.9 0.4 slice_reduce_fusion
  37.5 0.7 %subtract_convert_fusion = (bf16[4,16,16,128]{3,2,1,0:T(8,128)(2,1)S(1)}, bf16[4,16,16,128]{3,2,1,0:T(8,128)(2,1)S(1)}) fusion(f32[4,16,16]{2,1,0:T(8,128)S(1)} %exponential_select_fusion, f32[16]{0:T(128)S(1)} %copy-done.28, f32[16]{0:T(128)S(1)} %copy-done.21, pred[4,16,128]{2,1,0:T(8,128)(4,1)S(1)} %get-tuple-element.9, f32[16]{0:T(128)S(1)} %copy-done.23, ...), kind=kLoop, calls=%fused_computation.73 | loop fusion | flops 2752512 | bytes 1089856 | tf_op jit(solution)/shard_map/convert_element_type | solution.py:139
  38.2 2.1 %fusion.33 = f32[4,32,344]{2,1,0:T(8,128)S(1)} fusion(s32[4,16,128]{2,1,0:T(8,128)S(1)} %bitcast.108, bf16[4,32,16,128]{3,2,1,0:T(8,128)(2,1)S(1)} %pad_maximum_fusion), kind=kOutput, calls=%fused_computation.46 | convolution fusion | flops 183173120 | bytes 733184 | tf_op jit(solution)/shard_map/uhbs,ubsg->uhg/dot_general | solution.py:255
  40.4 2.3 %fusion.5 = f32[16,4,64,64]{3,2,0,1:T(8,128)} fusion(bf16[16,344,64,1]{1,2,0,3:T(8,128)(2,1)S(1)} %bitcast.104, f32[344,64]{0,1:T(8,128)S(1)} %copy.34, f32[4,16,344]{2,1,0:T(8,128)S(1)} %slice_add_fusion), kind=kOutput, calls=%fused_computation.8 | convolution fusion | flops 183173120 | bytes 1929216 | tf_op jit(solution)/shard_map/hgp,uhgn->uhpn/dot_general | solution.py:263
  42.7 2.4 %fusion.6 = f32[16,4,64,64]{3,2,0,1:T(8,128)} fusion(bf16[16,344,64,1]{1,2,0,3:T(8,128)(2,1)S(1)} %bitcast.105, f32[344,64]{0,1:T(8,128)S(1)} %copy.34, f32[4,16,344]{2,1,0:T(8,128)S(1)} %slice_add_fusion), kind=kOutput, calls=%fused_computation.10 | convolution fusion | flops 187400192 | bytes 1929216 | tf_op jit(solution)/shard_map/hgp,uhgn->uhpn/dot_general | solution.py:265
  45.1 0.8 %convolution_convert_fusion.2 = bf16[4,128,1024]{2,1,0:T(8,128)(2,1)S(1)} fusion(s32[4,128]{1,0:T(4,128)S(1)} %pad_add_fusion.9, f32[344,1152]{1,0:T(8,128)S(1)} %copy-done.1), kind=kOutput, calls=%fused_computation.38 | convolution fusion | flops 361410560 | bytes 1755136 | tf_op jit(solution)/shard_map/rtg,gc->rtc/dot_general | solution.py:206
  45.9 0.4 fusion.44
  46.3 1.3 %copy.32 = bf16[4,128,1024]{1,2,0:T(8,128)(2,1)} copy(bf16[4,128,1024]{2,1,0:T(8,128)(2,1)S(1)} %convolution_convert_fusion.2) | data formatting | bytes 2097152 | tf_op jit(solution)/shard_map/convert_element_type | solution.py:206
  47.6 0.4 fusion.70
  48.1 4.6 %fusion.14 = f32[4,16,64,128]{3,2,1,0:T(8,128)S(1)} fusion(bf16[4,128,16,64]{1,3,2,0:T(8,128)(2,1)} %bitcast.102, f32[4,16,128]{2,1,0:T(8,128)} %compare_select_fusion.2, f32[4,16,128]{2,1,0:T(8,128)} %copy-done.8, f32[4,128,128]{2,1,0:T(8,128)S(1)} %fusion.70, pred[128,128]{1,0:T(8,128)(4,1)} %convert_compare_fusion), kind=kOutput, calls=%fused_computation.19 | convolution fusion | flops 140509184 | bytes 3489792 | tf_op jit(solution)/shard_map/uhts,ushp->uthp/dot_general | solution.py:234
  52.8 2.8 %multiply_reduce_fusion = (f32[4,128,16]{1,2,0:T(8,128)S(1)}, f32[4,128,16,64]{1,3,2,0:T(8,128)S(1)}) fusion(f32[4,128,16,64]{1,3,2,0:T(8,128)S(1)} %bitcast.101, bf16[4,128,16,64]{1,3,2,0:T(8,128)(2,1)S(1)} %bitcast.103, f32[16]{0:T(128)S(1)} %copy-done.41, f32[4,128,16]{1,2,0:T(8,128)S(1)} %copy-done.7, f32[16,4,64,64]{3,2,0,1:T(8,128)S(1)} %copy-done.46, ...), kind=kOutput, calls=%fused_computation.26 | convolution fusion | flops 207872000 | bytes 11731456 | tf_op jit(solution)/shard_map/utn,uhpn->uthp/dot_general | solution.py:268
  55.5 0.3 broadcast_multiply_fusion
  55.8 1.9 %copy.38 = f32[4,128,1024]{2,1,0:T(8,128)} copy(f32[4,128,1024]{1,2,0:T(8,128)S(1)} %bitcast.100) | data formatting | bytes 4194304 | tf_op jit(solution)/shard_map/reshape | solution.py:275
  57.7 2.6 %convolution_convert_fusion.3 = bf16[4,128,512]{2,1,0:T(8,128)(2,1)S(1)} fusion(f32[4,128,1024]{2,1,0:T(8,128)} %copy.38, bf16[1024,512]{1,0:T(8,128)(2,1)} %param.30, f32[1024]{0:T(1024)S(1)} %copy-done.26), kind=kOutput, calls=%fused_computation.40 | convolution fusion | flops 538181632 | bytes 3674112 | tf_op jit(solution)/shard_map/gre,ed->grd/dot_general | solution.py:276
  60.4 0.9 %rev.3 = bf16[2,128,512]{2,1,0:T(8,128)(2,1)S(1)} reverse(bf16[2,128,512]{2,1,0:T(8,128)(2,1)S(1)} %slice.194), dimensions={1,2} | reverse | bytes 524288 | tf_op jit(solution)/shard_map/rev | solution.py:283
  61.3 0.4 fusion.45
  61.7 0.2 fusion.55
  62.1 0.6 multiply_reduce_fusion.1
  (141 shorter events, 1.8 us)
Async XLA Ops:
  0.6 6.5 %copy-start = (bf16[512,1152]{1,0:T(8,128)(2,1)S(1)}, bf16[512,1152]{1,0:T(8,128)(2,1)}, u32[]{:S(2)}) copy-start(bf16[512,1152]{1,0:T(8,128)(2,1)} %param.21) | copy-start | bytes 3538948
  0.6 6.5 %copy-start.15 = (f32[512]{0:T(512)S(1)}, f32[512]{0:T(512)}, u32[]{:S(2)}) copy-start(f32[512]{0:T(512)} %param.20) | copy-start | bytes 6148
  2.3 5.2 %copy-start.16 = (s32[4,128]{1,0:T(4,128)}, s32[4,128]{1,0:T(4,128)S(1)}, u32[]{:S(2)}) copy-start(s32[4,128]{1,0:T(4,128)S(1)} %pad_add_fusion.8) | copy-start | bytes 6148
  2.3 13.0 %collective-permute-start = (s32[4,128]{1,0:T(4,128)S(1)}, s32[4,128]{1,0:T(4,128)S(1)}, u32[]{:S(2)}, u32[]{:S(2)}) collective-permute-start(s32[4,128]{1,0:T(4,128)S(1)} %pad_add_fusion.8), channel_id=1, source_target_pairs={{0,1},{1,0},{2,3},{3,2},{4,5},{5,4},{6,7},{7,6},{8,9},{9,8},{10,11... | collective-permute-start | bytes 6152 | tf_op jit(solution)/shard_map/ppermute | solution.py:103
  5.1 2.3 %copy-start.9 = (f32[4,1152]{1,0:T(4,128)S(1)}, f32[4,1152]{1,0:T(4,128)}, u32[]{:S(2)}) copy-start(f32[4,1152]{1,0:T(4,128)} %param.24) | copy-start | bytes 55300
  5.1 2.4 %copy-start.40 = (f32[16]{0:T(128)S(1)}, f32[16]{0:T(128)}, u32[]{:S(2)}) copy-start(f32[16]{0:T(128)} %param.27) | copy-start | bytes 196
  5.1 2.4 %copy-start.34 = (bf16[512,16]{0,1:T(8,128)(2,1)S(1)}, bf16[512,16]{0,1:T(8,128)(2,1)}, u32[]{:S(2)}) copy-start(bf16[512,16]{0,1:T(8,128)(2,1)} %param.23) | copy-start | bytes 49156
  5.1 2.6 %copy-start.27 = (f32[16]{0:T(128)S(1)}, f32[16]{0:T(128)}, u32[]{:S(2)}) copy-start(f32[16]{0:T(128)} %param.26) | copy-start | bytes 196
  5.2 4.3 %copy-start.38 = (bf16[512,2]{0,1:T(2,128)(2,1)S(1)}, bf16[512,2]{0,1:T(2,128)(2,1)}, u32[]{:S(2)}) copy-start(bf16[512,2]{0,1:T(2,128)(2,1)} %param.32) | copy-start | bytes 6148
  5.2 5.7 %copy-start.35 = (f32[1152]{0:T(1024)S(1)}, f32[1152]{0:T(1024)}, u32[]{:S(2)}) copy-start(f32[1152]{0:T(1024)} %param.25) | copy-start | bytes 13828
  7.5 7.1 %copy-start.43 = (f32[16]{0:T(128)}, f32[16]{0:T(128)S(1)}, u32[]{:S(2)}) copy-start(f32[16]{0:T(128)S(1)} %exponential_negate_fusion) | copy-start | bytes 196
  7.7 6.9 %copy-start.20 = (f32[16]{0:T(128)}, f32[16]{0:T(128)S(1)}, u32[]{:S(2)}) copy-start(f32[16]{0:T(128)S(1)} %get-tuple-element.35) | copy-start | bytes 196
  7.7 6.9 %copy-start.22 = (f32[16]{0:T(128)}, f32[16]{0:T(128)S(1)}, u32[]{:S(2)}) copy-start(f32[16]{0:T(128)S(1)} %get-tuple-element.36) | copy-start | bytes 196
  7.7 6.9 %copy-start.24 = (f32[16]{0:T(128)}, f32[16]{0:T(128)S(1)}, u32[]{:S(2)}) copy-start(f32[16]{0:T(128)S(1)} %get-tuple-element.37) | copy-start | bytes 196
  8.7 5.9 %copy-start.8 = (f32[4,16,128]{2,1,0:T(8,128)}, f32[4,16,128]{2,1,0:T(8,128)S(1)}, u32[]{:S(2)}) copy-start(f32[4,16,128]{2,1,0:T(8,128)S(1)} %fusion.77) | copy-start | bytes 98308
  9.4 5.2 %copy-start.29 = (pred[4,16]{1,0:T(4,128)(4,1)}, pred[4,16]{1,0:T(4,128)(4,1)S(1)}, u32[]{:S(2)}) copy-start(pred[4,16]{1,0:T(4,128)(4,1)S(1)} %iota_compare_fusion.18) | copy-start | bytes 196
  10.8 3.8 %copy-start.36 = (f32[2,2,128]{2,1,0:T(2,128)S(1)}, f32[2,2,128]{2,1,0:T(2,128)}, u32[]{:S(2)}) copy-start(f32[2,2,128]{2,1,0:T(2,128)} %param.34) | copy-start | bytes 6148
  10.8 4.4 %copy-start.14 = (s32[2,128]{1,0:T(2,128)S(1)}, s32[2,128]{1,0:T(2,128)}, u32[]{:S(2)}) copy-start(s32[2,128]{1,0:T(2,128)} %param.18) | copy-start | bytes 3076
  15.3 4.2 %collective-permute-start.1 = (s32[4,256]{1,0:T(4,128)S(1)}, s32[4,256]{1,0:T(4,128)S(1)}, u32[]{:S(2)}, u32[]{:S(2)}) collective-permute-start(s32[4,256]{1,0:T(4,128)S(1)} %pad_add_fusion.7), channel_id=1, source_target_pairs={{0,2},{1,3},{2,0},{3,1},{4,6},{5,7},{6,4},{7,5},{8,10},{9,11},{10,... | collective-permute-start | bytes 12296 | tf_op jit(solution)/shard_map/ppermute | solution.py:103
  19.5 3.8 %collective-permute-start.2 = (s32[4,512]{1,0:T(4,128)S(1)}, s32[4,512]{1,0:T(4,128)S(1)}, u32[]{:S(2)}, u32[]{:S(2)}) collective-permute-start(s32[4,512]{1,0:T(4,128)S(1)} %pad_add_fusion.5), channel_id=1, source_target_pairs={{0,4},{1,5},{2,6},{3,7},{4,0},{5,1},{6,2},{7,3},{8,12},{9,13},{10,... | collective-permute-start | bytes 24584 | tf_op jit(solution)/shard_map/ppermute | solution.py:103
  24.5 9.5 %collective-permute-start.3 = (s32[4,1024]{1,0:T(4,128)}, s32[4,1024]{1,0:T(4,128)}, u32[]{:S(2)}, u32[]{:S(2)}) collective-permute-start(s32[4,1024]{1,0:T(4,128)} %pad_add_fusion.3), channel_id=1, source_target_pairs={{0,8},{1,9},{2,10},{3,11},{4,12},{5,13},{6,14},{7,15},{8,0},{9,1},... | collective-permute-start | bytes 49160 | tf_op jit(solution)/shard_map/ppermute | solution.py:103
  30.4 3.4 %slice-start = ((f32[344,1152]{1,0:T(8,128)}), f32[344,64]{1,0:T(8,128)S(1)}, s32[]{:S(2)}) async-start(f32[344,1152]{1,0:T(8,128)} %divide_multiply_fusion), calls=%async_computation | async-start | bytes 352256 | tf_op jit(solution)/shard_map/slice | solution.py:180
  32.3 3.4 %copy-start.10 = (pred[2048]{0:T(1024)(128)(4,1)S(1)}, pred[2048]{0:T(1024)(128)(4,1)}, u32[]{:S(2)}) copy-start(pred[2048]{0:T(1024)(128)(4,1)} %get-tuple-element.44) | copy-start | bytes 6148
  32.3 3.4 %copy-start.11 = (pred[2048]{0:T(1024)(128)(4,1)S(1)}, pred[2048]{0:T(1024)(128)(4,1)}, u32[]{:S(2)}) copy-start(pred[2048]{0:T(1024)(128)(4,1)} %get-tuple-element.45) | copy-start | bytes 6148
  32.3 3.4 %copy-start.12 = (pred[2048]{0:T(1024)(128)(4,1)S(1)}, pred[2048]{0:T(1024)(128)(4,1)}, u32[]{:S(2)}) copy-start(pred[2048]{0:T(1024)(128)(4,1)} %get-tuple-element.46) | copy-start | bytes 6148
  32.3 3.4 %copy-start.13 = (pred[2048]{0:T(1024)(128)(4,1)S(1)}, pred[2048]{0:T(1024)(128)(4,1)}, u32[]{:S(2)}) copy-start(pred[2048]{0:T(1024)(128)(4,1)} %get-tuple-element.47) | copy-start | bytes 6148
  32.3 3.6 %copy-start.19 = (f32[16]{0:T(128)S(1)}, f32[16]{0:T(128)}, u32[]{:S(2)}) copy-start(f32[16]{0:T(128)} %copy-done.18) | copy-start | bytes 196
  32.3 3.6 %copy-start.21 = (f32[16]{0:T(128)S(1)}, f32[16]{0:T(128)}, u32[]{:S(2)}) copy-start(f32[16]{0:T(128)} %copy-done.20) | copy-start | bytes 196
  32.3 3.6 %copy-start.23 = (f32[16]{0:T(128)S(1)}, f32[16]{0:T(128)}, u32[]{:S(2)}) copy-start(f32[16]{0:T(128)} %copy-done.22) | copy-start | bytes 196
  32.3 3.6 %copy-start.25 = (f32[16]{0:T(128)S(1)}, f32[16]{0:T(128)}, u32[]{:S(2)}) copy-start(f32[16]{0:T(128)} %copy-done.24) | copy-start | bytes 196
  32.3 3.6 %copy-start.28 = (f32[16]{0:T(128)S(1)}, f32[16]{0:T(128)}, u32[]{:S(2)}) copy-start(f32[16]{0:T(128)} %param.26) | copy-start | bytes 196
  32.3 3.6 %copy-start.44 = (f32[16]{0:T(128)S(1)}, f32[16]{0:T(128)}, u32[]{:S(2)}) copy-start(f32[16]{0:T(128)} %copy-done.43) | copy-start | bytes 196
  33.8 3.4 %copy-start.6 = (pred[4,16,16]{2,1,0:T(8,128)(4,1)S(1)}, pred[4,16,16]{2,1,0:T(8,128)(4,1)}, u32[]{:S(2)}) copy-start(pred[4,16,16]{2,1,0:T(8,128)(4,1)} %broadcast_and_fusion) | copy-start | bytes 3076
  34.0 3.5 %copy-start.30 = (pred[4,16]{1,0:T(4,128)(4,1)S(1)}, pred[4,16]{1,0:T(4,128)(4,1)}, u32[]{:S(2)}) copy-start(pred[4,16]{1,0:T(4,128)(4,1)} %copy-done.29) | copy-start | bytes 196
  42.7 2.4 %copy-start.1 = (f32[344,1152]{1,0:T(8,128)S(1)}, f32[344,1152]{1,0:T(8,128)}, u32[]{:S(2)}) copy-start(f32[344,1152]{1,0:T(8,128)} %divide_multiply_fusion) | copy-start | bytes 4755460
  48.0 4.7 %copy-start.2 = (f32[4,128,1024]{1,2,0:T(8,128)S(1)}, f32[4,128,1024]{1,2,0:T(8,128)}, u32[]{:S(2)}) copy-start(f32[4,128,1024]{1,2,0:T(8,128)} %copy.37) | copy-start | bytes 6291460
  48.0 4.7 %copy-start.3 = (bf16[4,128,1024]{1,2,0:T(8,128)(2,1)S(1)}, bf16[4,128,1024]{1,2,0:T(8,128)(2,1)}, u32[]{:S(2)}) copy-start(bf16[4,128,1024]{1,2,0:T(8,128)(2,1)} %copy.32) | copy-start | bytes 3145732
  48.0 4.7 %copy-start.7 = (f32[4,128,16]{1,2,0:T(8,128)S(1)}, f32[4,128,16]{1,2,0:T(8,128)}, u32[]{:S(2)}) copy-start(f32[4,128,16]{1,2,0:T(8,128)} %exponential_bitcast_fusion) | copy-start | bytes 98308
  48.0 4.7 %copy-start.41 = (f32[16]{0:T(128)S(1)}, f32[16]{0:T(128)}, u32[]{:S(2)}) copy-start(f32[16]{0:T(128)} %param.28) | copy-start | bytes 196
  48.0 4.7 %copy-start.46 = (f32[16,4,64,64]{3,2,0,1:T(8,128)S(1)}, f32[16,4,64,64]{3,2,0,1:T(8,128)}, u32[]{:S(2)}) copy-start(f32[16,4,64,64]{3,2,0,1:T(8,128)} %fusion.5) | copy-start | bytes 3145732
  48.1 4.7 %copy-start.47 = (f32[16,4,64,64]{3,2,0,1:T(8,128)S(1)}, f32[16,4,64,64]{3,2,0,1:T(8,128)}, u32[]{:S(2)}) copy-start(f32[16,4,64,64]{3,2,0,1:T(8,128)} %fusion.6) | copy-start | bytes 3145732
  55.8 1.9 %copy-start.26 = (f32[1024]{0:T(1024)S(1)}, f32[1024]{0:T(1024)}, u32[]{:S(2)}) copy-start(f32[1024]{0:T(1024)} %param.29) | copy-start | bytes 12292
  57.7 3.6 %copy-start.17 = (s32[4,128]{1,0:T(4,128)S(1)}, s32[4,128]{1,0:T(4,128)}, u32[]{:S(2)}) copy-start(s32[4,128]{1,0:T(4,128)} %copy-done.16) | copy-start | bytes 6148
  57.7 4.0 %copy-start.32 = (bf16[512,1]{0,1:T(2,128)(2,1)S(1)}, bf16[512,1]{0,1:T(2,128)(2,1)}, u32[]{:S(2)}) copy-start(bf16[512,1]{0,1:T(2,128)(2,1)} %get-tuple-element.28) | copy-start | bytes 3076
  57.7 4.0 %copy-start.33 = (bf16[512,1]{0,1:T(2,128)(2,1)S(1)}, bf16[512,1]{0,1:T(2,128)(2,1)}, u32[]{:S(2)}) copy-start(bf16[512,1]{0,1:T(2,128)(2,1)} %get-tuple-element.29) | copy-start | bytes 3076
  57.7 4.0 %copy-start.37 = (f32[512]{0:T(512)S(1)}, f32[512]{0:T(512)}, u32[]{:S(2)}) copy-start(f32[512]{0:T(512)} %param.31) | copy-start | bytes 6148
  57.7 4.0 %copy-start.39 = (bf16[512,2]{0,1:T(2,128)(2,1)S(1)}, bf16[512,2]{0,1:T(2,128)(2,1)}, u32[]{:S(2)}) copy-start(bf16[512,2]{0,1:T(2,128)(2,1)} %param.32) | copy-start | bytes 6148
  60.3 1.7 %copy-start.45 = (f32[2,2,128]{2,1,0:T(2,128)S(1)}, f32[2,2,128]{2,1,0:T(2,128)}, u32[]{:S(2)}) copy-start(f32[2,2,128]{2,1,0:T(2,128)} %fusion.35) | copy-start | bytes 6148
  (5 other events, 6.1 us)

commit v8 on v6

--- a/solution.py
+++ b/solution.py
@@ -258,13 +258,9 @@
     )
     per_gram = per_gram[:, :HEADS] + per_gram[:, HEADS:]
     b_hi, b_lo = split_bf16(per_gram[..., None] * b_tab[None, None])
-    both = jnp.einsum(
-        "hgp,uhgn->uhpn",
-        x_heads,
-        jnp.concatenate([b_hi, b_lo], axis=-1),
-        preferred_element_type=jnp.float32,
-    )
-    start_state = both[..., :NS] + both[..., NS:]
+    start_state = jnp.einsum(
+        "hgp,uhgn->uhpn", x_heads, b_hi, preferred_element_type=jnp.float32
+    ) + jnp.einsum("hgp,uhgn->uhpn", x_heads, b_lo, preferred_element_type=jnp.float32)
 
     y_inter = (
         jnp.einsum("utn,uhpn->uthp", c_u, start_state, precision=lax.Precision.HIGH)

time: 61.1 us -> 55.9 us (0.915)
  other arithmetic: 16.3 us -> 8.98 us
  matrix products: 23.1 us -> 26 us
  local copies, waits for them, and re-layouts: 9.43 us -> 8.18 us
    convert_element_type x1 -> x0, other arithmetic: 3.53 us -> none  [split_bf16(): high = values.astype(jnp.bfloat16)]
    slice x2, local copies, waits for them, and re-layouts: 0.01 us -> 1.74 us  [local(): b_tab = act_tab[:, INNER:INNER + NS]]
    dot_general x1 -> x2, matrix products: 3.35 us -> 4.63 us  [the longest x1 2.35 us: local(): jnp.einsum('hgp,uhgn->uhpn', x_heads, b_hi, preferred_element_type=jnp.fl...]
    slice x2, local copies, waits for them, and re-layouts: 2.44 us -> 1.25 us  [local(): x_tab = act_tab[:, :INNER].astype(jnp.bfloat16)]
    eq x2, other arithmetic: 1.17 us -> 0.01 us  [gram_ids(): chosen = where_in >= real - 1 if real == KW else where_in == real - 1]
    dot_general x1, matrix products: 1.64 us -> 2.58 us  [local(): jnp.einsum('uhts,ushp->uthp', weights, x_u, preferred_element_type=jnp.fl...]
    convert_element_type x1, local copies, waits for them, and re-layouts: 1.49 us -> 0.65 us  [local(): jnp.einsum('rtg,gc->rtc', oh_loc, x_tab, preferred_element_type=jnp.float32)]
    select_n x1, other arithmetic: 0.8 us -> 0.12 us  [gram_ids(): ids = jnp.where(chosen, offset_of + code, ids)]
  transfers between devices with their start and end apart: 4 -> 4, of which waited for: 2 -> 2; matrix products, arithmetic and copies ran while one was open for 31% -> 30% of each run, Pallas kernels for 0% -> 0%
where the time goes in v8:
time: 55.9 us; the launch traced here: 55.3 us
  matrix products  26 us (47%)
  other arithmetic  8.98 us (16%)
  starting transfers between devices  8.28 us (15%)
  local copies, waits for them, and re-layouts  8.18 us (15%)
  waiting for transfers between devices  2.6 us (5%)
  between operations  1.3 us (2%)
    ppermute x4, starting transfers between devices, gather_all(): lax.ppermute(held, axis, [(src, src ^ mask) for src in range(count)])  8.28 us
    dot_general x1, matrix products, local(): jnp.einsum('utn,uhpn->uthp', c_u, start_state, precision=lax.Precision.HIGH)  2.76 us
    ppermute x4, waiting for transfers between devices, gather_all(): lax.ppermute(held, axis, [(src, src ^ mask) for src in range(count)])  2.6 us
    dot_general x1, matrix products, local(): jnp.einsum('uhts,ushp->uthp', weights, x_u, preferred_element_type=jnp.fl...  2.58 us
    dot_general x1, matrix products, local(): jnp.einsum('hgp,uhgn->uhpn', x_heads, b_hi, preferred_element_type=jnp.fl...  2.35 us
    dot_general x1, matrix products, local(): jnp.einsum('hgp,uhgn->uhpn', x_heads, b_lo, preferred_element_type=jnp.fl...  2.28 us
    dot_general x1, matrix products, local(): jnp.einsum('rtg,gc->rtc', oh_loc, x_tab, preferred_element_type=jnp.float32)  2.11 us
    dot_general x1, matrix products, local(): jnp.einsum('uhbs,ubsg->uhg', jnp.concatenate([w_hi, w_lo], axis=1), oh_al...  2.11 us
  transfers between devices with their start and end apart: 4, of which 2 were waited for; matrix products, arithmetic and copies ran while one was open for 30% of the time, Pallas kernels for 0%

profile of v8, /device:TPU:0, one launch (start us, length us, event | category | flops | bytes accessed | tf_op | source)
XLA Modules:
  0.0 55.3 jit_solution(9811386782879855388)
XLA Ops:
  0.7 1.0 %fusion.39 = s32[2,128]{1,0:T(2,128)S(1)} fusion(s32[2,128]{1,0:T(2,128)} %param.18), kind=kOutput, calls=%fused_computation.55 | convolution fusion | flops 99072 | bytes 2048 | tf_op jit(solution)/shard_map/dot_general | solution.py:186
  1.6 0.7 %pad_add_fusion.8 = s32[4,128]{1,0:T(4,128)S(1)} fusion(s32[2,128]{1,0:T(2,128)S(1)} %fusion.39, s32[2,128]{1,0:T(2,128)} %param.18), kind=kLoop, calls=%fused_computation.172 | loop fusion | flops 512 | bytes 4096 | tf_op jit(solution)/shard_map/concatenate | solution.py:189
  2.3 0.5 collective-permute-start
  2.8 0.7 %broadcast_compare_fusion.7 = (pred[4,128]{1,0:T(4,128)(4,1)S(1)}, pred[4,128]{1,0:T(4,128)(4,1)S(1)}, pred[4,128]{1,0:T(4,128)(4,1)S(1)}, pred[4,128]{1,0:T(4,128)(4,1)S(1)}) fusion(s32[2,128]{1,0:T(2,128)S(1)} %fusion.39, s32[2,128]{1,0:T(2,128)} %param.18), kind=kLoop, calls=%fused_computation.186 | loop fusion | flops 2560 | bytes 4096 | tf_op jit(solution)/shard_map/eq | solution.py:122
  3.5 0.9 %fusion.35 = bf16[2,512]{1,0:T(2,128)(2,1)S(1)} fusion(bf16[2,512]{1,0:T(2,128)(2,1)} %param.19), kind=kOutput, calls=%fused_computation.50 | convolution fusion | flops 1573888 | bytes 4096 | tf_op jit(solution)/shard_map/dot_general | solution.py:176
  4.4 0.8 %fusion.83 = (f32[4]{0:T(128)S(1)}, bf16[4,512]{1,0:T(4,128)(2,1)S(1)}) fusion(bf16[1,512]{1,0:T(2,128)(2,1)S(1)} %get-tuple-element.39, bf16[1,512]{1,0:T(2,128)(2,1)S(1)} %get-tuple-element.38, bf16[2,512]{1,0:T(2,128)(2,1)} %param.19), kind=kLoop, calls=%fused_computation.136 | loop fusion | flops 18428 | bytes 8208 | tf_op jit(solution)/shard_map/reduce_sum | solution.py:23
  5.2 0.9 %fusion.110 = f32[4,16]{1,0:T(4,128)S(1)} fusion(bf16[512,16]{0,1:T(8,128)(2,1)} %param.23, bf16[4,512]{1,0:T(4,128)(2,1)S(1)} %get-tuple-element.5, f32[512]{0:T(512)} %param.20, f32[4]{0:T(128)S(1)} %add_rsqrt_fusion.2), kind=kOutput, calls=%fused_computation.206 | convolution fusion | flops 73728 | bytes 22800 | tf_op jit(solution)/shard_map/dot_general | solution.py:76
  6.1 0.7 %exponential_negate_fusion = f32[16]{0:T(128)S(1)} fusion(f32[16]{0:T(128)} %param.27), kind=kLoop, calls=%fused_computation.191 | loop fusion | flops 16 | bytes 128 | tf_op jit(solution)/shard_map/neg | solution.py:183
  6.9 1.0 %fusion.13 = f32[4,1152]{1,0:T(4,128)S(1)} fusion(bf16[512,1152]{1,0:T(8,128)(2,1)S(1)} %copy-done, bf16[4,512]{1,0:T(4,128)(2,1)S(1)} %get-tuple-element.5, f32[512]{0:T(512)} %param.20, f32[4]{0:T(128)S(1)} %add_rsqrt_fusion.2), kind=kOutput, calls=%fused_computation.18 | convolution fusion | flops 4736000 | bytes 1204240 | tf_op jit(solution)/shard_map/dot_general | solution.py:74
  7.9 0.8 %broadcast_multiply_fusion = f32[4,4,1152]{2,1,0:T(4,128)S(1)} fusion(f32[4,1152]{1,0:T(4,128)S(1)} %fusion.13, f32[4,1152]{1,0:T(4,128)} %param.24), kind=kLoop, calls=%fused_computation.108 | loop fusion | flops 18432 | bytes 110592 | tf_op jit(solution)/shard_map/mul | solution.py:77
  8.7 0.7 %compare_select_fusion.2 = f32[4,16,128]{2,1,0:T(8,128)} fusion(f32[16]{0:T(128)S(1)} %copy-done.12, f32[16]{0:T(128)S(1)} %get-tuple-element.35, f32[16]{0:T(128)S(1)} %get-tuple-element.36, f32[16]{0:T(128)S(1)} %get-tuple-element.37, f32[16]{0:T(128)S(1)} %get-tuple-element.34, pred[4,128]{1,0:T(4,128)(4,1)S(1)} %get-tuple-element.32, ...), kind=kLoop, calls=%fused_computation.100 | loop fusion | flops 114688 | bytes 35136 | tf_op jit(solution)/shard_map/jit(softplus)/select_n | solution.py:212
  9.4 0.2 fusion.76
  9.7 0.6 %exponential_bitcast_fusion = f32[4,128,16]{1,2,0:T(8,128)} fusion(f32[4,16,128]{2,1,0:T(8,128)S(1)} %fusion.76), kind=kLoop, calls=%fused_computation.114 | loop fusion | bytes 65536 | tf_op jit(solution)/shard_map/exp | solution.py:267
  10.3 2.0 %fusion.43 = f32[4,128,1024]{1,2,0:T(8,128)} fusion(bf16[512,1024]{1,0:T(8,128)(2,1)S(1)} %copy-done.3, s32[4,128]{1,0:T(4,128)S(1)} %pad_add_fusion.8, bf16[4,512]{1,0:T(4,128)(2,1)S(1)} %get-tuple-element.5, f32[512]{0:T(512)S(1)} %copy-done.9, f32[4]{0:T(128)S(1)} %add_rsqrt_fusion.2), kind=kOutput, calls=%fused_computation.63 | convolution fusion | flops 8402944 | bytes 3153936 | tf_op jit(solution)/shard_map/rtk,kc->rtc/dot_general | solution.py:211
  12.5 0.6 %fusion.114 = (bf16[512,1]{0,1:T(2,128)(2,1)}, bf16[512,1]{0,1:T(2,128)(2,1)}) fusion(bf16[512,2]{0,1:T(2,128)(2,1)S(1)} %convolution_convert_fusion.5), kind=kLoop, calls=%fused_computation.208 | loop fusion | bytes 4096 | tf_op jit(solution)/shard_map/slice | solution.py:293
  13.2 1.6 %divide_multiply_fusion = f32[344,1152]{1,0:T(8,128)S(1)} fusion(f32[16,1152]{1,0:T(8,128)S(1)} %mul.201, f32[344,16]{1,0:T(8,128)S(1)} %copy-done.26, f32[1152]{0:T(1024)S(1)} %copy-done.19), kind=kOutput, calls=%fused_computation.34 | convolution fusion | flops 78068736 | bytes 1685504 | tf_op jit(solution)/shard_map/dot_general | solution.py:78
  14.8 0.6 %fusion.34 = f32[2,2,128]{2,1,0:T(2,128)} fusion(f32[2,2,128]{2,1,0:T(2,128)S(1)} %copy-done.20), kind=kOutput, calls=%fused_computation.47 | output fusion | flops 769 | bytes 4096 | tf_op jit(solution)/shard_map/sub | solution.py:297
  15.5 2.6 %collective-permute-start.1 = (s32[4,256]{1,0:T(4,128)S(1)}, s32[4,256]{1,0:T(4,128)S(1)}, u32[]{:S(2)}, u32[]{:S(2)}) collective-permute-start(s32[4,256]{1,0:T(4,128)S(1)} %pad_add_fusion.7), channel_id=1, source_target_pairs={{0,2},{1,3},{2,0},{3,1},{4,6},{5,7},{6,4},{7,5},{8,10},{9,11},{10,... | collective-permute-start | bytes 12296 | tf_op jit(solution)/shard_map/ppermute | solution.py:103
  18.1 0.6 %convert_compare_fusion = pred[128,128]{1,0:T(8,128)(4,1)} fusion(), kind=kLoop, calls=%fused_computation.104 | loop fusion | flops 49152 | bytes 16384 | tf_op jit(solution)/shard_map/gt | solution.py:229
  18.7 1.0 %collective-permute-done.1 = s32[4,256]{1,0:T(4,128)S(1)} collective-permute-done((s32[4,256]{1,0:T(4,128)S(1)}, s32[4,256]{1,0:T(4,128)S(1)}, u32[]{:S(2)}, u32[]{:S(2)}) %collective-permute-start.1) | collective-permute-done | bytes 4128 | tf_op jit(solution)/shard_map/ppermute | solution.py:103
  19.7 2.1 %collective-permute-start.2 = (s32[4,512]{1,0:T(4,128)S(1)}, s32[4,512]{1,0:T(4,128)S(1)}, u32[]{:S(2)}, u32[]{:S(2)}) collective-permute-start(s32[4,512]{1,0:T(4,128)S(1)} %pad_add_fusion.5), channel_id=1, source_target_pairs={{0,4},{1,5},{2,6},{3,7},{4,0},{5,1},{6,2},{7,3},{8,12},{9,13},{10,... | collective-permute-start | bytes 24584 | tf_op jit(solution)/shard_map/ppermute | solution.py:103
  21.8 1.6 %collective-permute-done.2 = s32[4,512]{1,0:T(4,128)S(1)} collective-permute-done((s32[4,512]{1,0:T(4,128)S(1)}, s32[4,512]{1,0:T(4,128)S(1)}, u32[]{:S(2)}, u32[]{:S(2)}) %collective-permute-start.2) | collective-permute-done | bytes 8224 | tf_op jit(solution)/shard_map/ppermute | solution.py:103
  23.5 3.1 %collective-permute-start.3 = (s32[4,1024]{1,0:T(4,128)S(1)}, s32[4,1024]{1,0:T(4,128)}, u32[]{:S(2)}, u32[]{:S(2)}) collective-permute-start(s32[4,1024]{1,0:T(4,128)S(1)} %pad_add_fusion.3), channel_id=1, source_target_pairs={{0,8},{1,9},{2,10},{3,11},{4,12},{5,13},{6,14},{7,15},{8,0},{9,1},... | collective-permute-start | bytes 49160 | tf_op jit(solution)/shard_map/ppermute | solution.py:103
  26.7 0.7 %slice.192 = f32[344,64]{1,0:T(8,128)} slice(f32[344,1152]{1,0:T(8,128)S(1)} %divide_multiply_fusion), slice={[0:344], [1024:1088]} | slice | bytes 176128 | tf_op jit(solution)/shard_map/slice | solution.py:180
  27.4 1.2 %copy.35 = bf16[344,1024]{0,1:T(8,128)(2,1)} copy(bf16[344,1024]{1,0:T(8,128)(2,1)S(1)} %slice.239) | data formatting | bytes 1409024 | tf_op jit(solution)/shard_map/slice | solution.py:179
  28.6 1.1 %copy.34 = f32[344,64]{0,1:T(8,128)S(1)} copy(f32[344,64]{1,0:T(8,128)} %slice.192) | data formatting | bytes 176128 | tf_op jit(solution)/shard_map/slice | solution.py:180
  29.6 0.8 %mul.226 = f32[16,64]{1,0:T(8,128)S(1)} reshape(f32[1024]{0:T(1024)} %param.29) | data formatting | bytes 8192 | tf_op jit(solution)/shard_map/mul | solution.py:23
  30.4 0.8 %pad_add_fusion = (s32[4,2048]{1,0:T(4,128)S(1)}, s32[4,2048]{1,0:T(4,128)S(1)}) fusion(s32[4,1024]{1,0:T(4,128)} %collective-permute-done.3, s32[2,1024]{1,0:T(2,128)S(1)} %get-tuple-element.17, s32[2,1024]{1,0:T(2,128)S(1)} %get-tuple-element.16), kind=kLoop, calls=%fused_computation.111 | loop fusion | flops 32768 | bytes 98304 | tf_op jit(solution)/shard_map/concatenate | solution.py:105
  31.6 2.1 %convolution_convert_fusion.1 = bf16[4,128,1024]{2,1,0:T(8,128)(2,1)S(1)} fusion(s32[4,128]{1,0:T(4,128)S(1)} %pad_add_fusion.9, f32[344,1152]{1,0:T(8,128)} %copy-done.1), kind=kOutput, calls=%fused_computation.36 | convolution fusion | flops 361410560 | bytes 1755136 | tf_op jit(solution)/shard_map/rtg,gc->rtc/dot_general | solution.py:206
  33.7 1.3 %fusion.42 = f32[4,128,128]{1,2,0:T(8,128)S(1)} fusion(s32[4,128]{1,0:T(4,128)S(1)} %pad_add_fusion.9, f32[344,1152]{1,0:T(8,128)} %copy-done.1), kind=kOutput, calls=%fused_computation.60 | convolution fusion | flops 270708736 | bytes 440320 | tf_op jit(solution)/shard_map/rtg,gc->rtc/dot_general | solution.py:209
  35.2 0.9 %fusion.48 = f32[4,16,16,128]{3,2,1,0:T(8,128)S(1)} fusion(f32[16]{0:T(128)S(1)} %copy-done.13, f32[16]{0:T(128)S(1)} %get-tuple-element.35, f32[16]{0:T(128)S(1)} %get-tuple-element.36, f32[16]{0:T(128)S(1)} %copy-done.11, f32[16]{0:T(128)S(1)} %get-tuple-element.34, f32[16]{0:T(128)S(1)} %copy-done.28, pred[4,16,128]{2,1,0:T(8,128)(4,1)S(1)} %get-tuple-element.9, ...), kind=kOutput, calls=%fused_computation.73 | convolution fusion | flops 203309056 | bytes 557440 | tf_op jit(solution)/shard_map/...s,st->...t/dot_general | solution.py:143
  36.1 0.4 slice_reduce_fusion
  36.7 0.7 %subtract_convert_fusion = (bf16[4,16,16,128]{3,2,1,0:T(8,128)(2,1)S(1)}, bf16[4,16,16,128]{3,2,1,0:T(8,128)(2,1)S(1)}) fusion(f32[4,16,16]{2,1,0:T(8,128)S(1)} %exponential_select_fusion, f32[16]{0:T(128)S(1)} %copy-done.13, f32[16]{0:T(128)S(1)} %get-tuple-element.35, pred[4,16,128]{2,1,0:T(8,128)(4,1)S(1)} %get-tuple-element.9, ...), kind=kLoop, calls=%fused_computation.70 | loop fusion | flops 2752512 | bytes 1089856 | tf_op jit(solution)/shard_map/convert_element_type | solution.py:139
  37.4 2.1 %fusion.32 = f32[4,32,344]{2,1,0:T(8,128)S(1)} fusion(s32[4,16,128]{2,1,0:T(8,128)S(1)} %bitcast.109, bf16[4,32,16,128]{3,2,1,0:T(8,128)(2,1)S(1)} %pad_maximum_fusion), kind=kOutput, calls=%fused_computation.44 | convolution fusion | flops 183173120 | bytes 733184 | tf_op jit(solution)/shard_map/uhbs,ubsg->uhg/dot_general | solution.py:253
  39.6 2.3 %fusion.6 = f32[16,4,64,64]{3,2,0,1:T(8,128)} fusion(bf16[16,344,64,1]{1,2,0,3:T(8,128)(2,1)S(1)} %bitcast.105, f32[344,64]{0,1:T(8,128)S(1)} %copy.34, f32[4,16,344]{2,1,0:T(8,128)S(1)} %slice_add_fusion), kind=kOutput, calls=%fused_computation.10 | convolution fusion | flops 187400192 | bytes 1929216 | tf_op jit(solution)/shard_map/hgp,uhgn->uhpn/dot_general | solution.py:263
  41.9 2.3 %fusion.5 = f32[16,4,64,64]{3,2,0,1:T(8,128)} fusion(bf16[16,344,64,1]{1,2,0,3:T(8,128)(2,1)S(1)} %bitcast.106, f32[344,64]{0,1:T(8,128)S(1)} %copy.34, f32[4,16,344]{2,1,0:T(8,128)S(1)} %slice_add_fusion), kind=kOutput, calls=%fused_computation.8 | convolution fusion | flops 183173120 | bytes 1929216 | tf_op jit(solution)/shard_map/hgp,uhgn->uhpn/dot_general | solution.py:261
  44.2 0.7 %copy.32 = bf16[4,128,1024]{1,2,0:T(8,128)(2,1)S(1)} copy(bf16[4,128,1024]{2,1,0:T(8,128)(2,1)S(1)} %convolution_convert_fusion.1) | data formatting | bytes 2097152 | tf_op jit(solution)/shard_map/convert_element_type | solution.py:206
  44.9 0.4 fusion.69
  45.3 2.6 %fusion.14 = f32[4,16,64,128]{3,2,1,0:T(8,128)S(1)} fusion(bf16[4,128,16,64]{1,3,2,0:T(8,128)(2,1)S(1)} %bitcast.103, f32[4,16,128]{2,1,0:T(8,128)} %compare_select_fusion.2, f32[4,16,128]{2,1,0:T(8,128)} %copy-done.7, f32[4,128,128]{2,1,0:T(8,128)S(1)} %fusion.69, pred[128,128]{1,0:T(8,128)(4,1)} %convert_compare_fusion), kind=kOutput, calls=%fused_computation.19 | convolution fusion | flops 140509184 | bytes 3489792 | tf_op jit(solution)/shard_map/uhts,ushp->uthp/dot_general | solution.py:232
  48.0 0.3 copy-done.31
  48.2 2.8 %multiply_reduce_fusion = (f32[4,128,16]{1,2,0:T(8,128)S(1)}, f32[4,128,16,64]{1,3,2,0:T(8,128)S(1)}) fusion(f32[4,128,16,64]{1,3,2,0:T(8,128)S(1)} %bitcast.102, bf16[4,128,16,64]{1,3,2,0:T(8,128)(2,1)S(1)} %bitcast.104, f32[16]{0:T(128)S(1)} %copy-done.24, f32[4,128,16]{1,2,0:T(8,128)S(1)} %copy-done.6, f32[16,4,64,64]{3,2,0,1:T(8,128)S(1)} %copy-done.30, ...), kind=kOutput, calls=%fused_computation.26 | convolution fusion | flops 207872000 | bytes 11731456 | tf_op jit(solution)/shard_map/utn,uhpn->uthp/dot_general | solution.py:266
  51.0 0.5 multiply_convert_fusion.4
  51.5 0.7 %copy-done.4 = bf16[1024,512]{1,0:T(8,128)(2,1)S(1)} copy-done((bf16[1024,512]{1,0:T(8,128)(2,1)S(1)}, bf16[1024,512]{1,0:T(8,128)(2,1)}, u32[]{:S(2)}) %copy-start.4) | copy-done | bytes 1048600
  52.3 0.7 %convolution_convert_fusion.2 = bf16[4,128,512]{2,1,0:T(8,128)(2,1)S(1)} fusion(bf16[4,128,1024]{1,2,0:T(8,128)(2,1)S(1)} %bitcast.101, bf16[1024,512]{1,0:T(8,128)(2,1)S(1)} %copy-done.4), kind=kOutput, calls=%fused_computation.38 | convolution fusion | flops 537133056 | bytes 2621440 | tf_op jit(solution)/shard_map/gre,ed->grd/dot_general | solution.py:276
  53.0 0.9 %rev.3 = bf16[2,128,512]{2,1,0:T(8,128)(2,1)S(1)} reverse(bf16[2,128,512]{2,1,0:T(8,128)(2,1)S(1)} %slice.194), dimensions={1,2} | reverse | bytes 524288 | tf_op jit(solution)/shard_map/rev | solution.py:283
  53.9 0.4 fusion.44
  54.4 0.2 fusion.54
  54.7 0.6 %multiply_reduce_fusion.1 = f32[2,128]{1,0:T(2,128)} fusion(f32[2,2,128]{2,1,0:T(2,128)S(1)} %select_reduce_fusion.1, f32[2,2,128]{2,1,0:T(2,128)S(1)} %copy-done.29), kind=kOutput, calls=%fused_computation.174 | output fusion | flops 2049 | bytes 5120 | tf_op jit(solution)/shard_map/reduce_sum | solution.py:298
  (107 shorter events, 1.4 us)
Async XLA Ops:
  0.6 6.2 %copy-start = (bf16[512,1152]{1,0:T(8,128)(2,1)S(1)}, bf16[512,1152]{1,0:T(8,128)(2,1)}, u32[]{:S(2)}) copy-start(bf16[512,1152]{1,0:T(8,128)(2,1)} %param.21) | copy-start | bytes 3538948
  0.6 9.7 %copy-start.9 = (f32[512]{0:T(512)S(1)}, f32[512]{0:T(512)}, u32[]{:S(2)}) copy-start(f32[512]{0:T(512)} %param.20) | copy-start | bytes 6148
  0.7 8.0 %copy-start.12 = (f32[16]{0:T(128)S(1)}, f32[16]{0:T(128)}, u32[]{:S(2)}) copy-start(f32[16]{0:T(128)} %param.26) | copy-start | bytes 196
  0.7 9.6 %copy-start.3 = (bf16[512,1024]{1,0:T(8,128)(2,1)S(1)}, bf16[512,1024]{1,0:T(8,128)(2,1)}, u32[]{:S(2)}) copy-start(bf16[512,1024]{1,0:T(8,128)(2,1)} %param.22) | copy-start | bytes 3145732
  2.3 13.1 %collective-permute-start = (s32[4,128]{1,0:T(4,128)S(1)}, s32[4,128]{1,0:T(4,128)S(1)}, u32[]{:S(2)}, u32[]{:S(2)}) collective-permute-start(s32[4,128]{1,0:T(4,128)S(1)} %pad_add_fusion.8), channel_id=1, source_target_pairs={{0,1},{1,0},{2,3},{3,2},{4,5},{5,4},{6,7},{7,6},{8,9},{9,8},{10,11... | collective-permute-start | bytes 6152 | tf_op jit(solution)/shard_map/ppermute | solution.py:103
  6.1 4.2 %copy-start.10 = (f32[16]{0:T(128)}, f32[16]{0:T(128)S(1)}, u32[]{:S(2)}) copy-start(f32[16]{0:T(128)S(1)} %get-tuple-element.37) | copy-start | bytes 196
  6.8 5.6 %copy-start.27 = (f32[16]{0:T(128)}, f32[16]{0:T(128)S(1)}, u32[]{:S(2)}) copy-start(f32[16]{0:T(128)S(1)} %exponential_negate_fusion) | copy-start | bytes 196
  6.9 6.3 %copy-start.14 = (pred[4,16]{1,0:T(4,128)(4,1)}, pred[4,16]{1,0:T(4,128)(4,1)S(1)}, u32[]{:S(2)}) copy-start(pred[4,16]{1,0:T(4,128)(4,1)S(1)} %iota_compare_fusion.18) | copy-start | bytes 196
  7.9 4.5 %copy-start.22 = (bf16[512,2]{0,1:T(2,128)(2,1)S(1)}, bf16[512,2]{0,1:T(2,128)(2,1)}, u32[]{:S(2)}) copy-start(bf16[512,2]{0,1:T(2,128)(2,1)} %param.32) | copy-start | bytes 6148
  8.7 4.5 %copy-start.19 = (f32[1152]{0:T(1024)S(1)}, f32[1152]{0:T(1024)}, u32[]{:S(2)}) copy-start(f32[1152]{0:T(1024)} %param.25) | copy-start | bytes 13828
  8.7 4.5 %copy-start.26 = (f32[344,16]{1,0:T(8,128)S(1)}, f32[344,16]{1,0:T(8,128)}, u32[]{:S(2)}) copy-start(f32[344,16]{1,0:T(8,128)} %constant.138.clone) | copy-start | bytes 66052
  9.7 3.5 %copy-start.7 = (f32[4,16,128]{2,1,0:T(8,128)}, f32[4,16,128]{2,1,0:T(8,128)S(1)}, u32[]{:S(2)}) copy-start(f32[4,16,128]{2,1,0:T(8,128)S(1)} %fusion.76) | copy-start | bytes 98308
  13.2 1.6 %copy-start.20 = (f32[2,2,128]{2,1,0:T(2,128)S(1)}, f32[2,2,128]{2,1,0:T(2,128)}, u32[]{:S(2)}) copy-start(f32[2,2,128]{2,1,0:T(2,128)} %param.34) | copy-start | bytes 6148
  13.2 2.3 %copy-start.8 = (s32[2,128]{1,0:T(2,128)S(1)}, s32[2,128]{1,0:T(2,128)}, u32[]{:S(2)}) copy-start(s32[2,128]{1,0:T(2,128)} %param.18) | copy-start | bytes 3076
  14.8 16.4 %copy-start.1 = (f32[344,1152]{1,0:T(8,128)}, f32[344,1152]{1,0:T(8,128)S(1)}, u32[]{:S(2)}) copy-start(f32[344,1152]{1,0:T(8,128)S(1)} %divide_multiply_fusion) | copy-start | bytes 4755460
  15.5 4.2 %collective-permute-start.1 = (s32[4,256]{1,0:T(4,128)S(1)}, s32[4,256]{1,0:T(4,128)S(1)}, u32[]{:S(2)}, u32[]{:S(2)}) collective-permute-start(s32[4,256]{1,0:T(4,128)S(1)} %pad_add_fusion.7), channel_id=1, source_target_pairs={{0,2},{1,3},{2,0},{3,1},{4,6},{5,7},{6,4},{7,5},{8,10},{9,11},{10,... | collective-permute-start | bytes 12296 | tf_op jit(solution)/shard_map/ppermute | solution.py:103
  19.7 3.8 %collective-permute-start.2 = (s32[4,512]{1,0:T(4,128)S(1)}, s32[4,512]{1,0:T(4,128)S(1)}, u32[]{:S(2)}, u32[]{:S(2)}) collective-permute-start(s32[4,512]{1,0:T(4,128)S(1)} %pad_add_fusion.5), channel_id=1, source_target_pairs={{0,4},{1,5},{2,6},{3,7},{4,0},{5,1},{6,2},{7,3},{8,12},{9,13},{10,... | collective-permute-start | bytes 24584 | tf_op jit(solution)/shard_map/ppermute | solution.py:103
  23.5 6.9 %collective-permute-start.3 = (s32[4,1024]{1,0:T(4,128)S(1)}, s32[4,1024]{1,0:T(4,128)}, u32[]{:S(2)}, u32[]{:S(2)}) collective-permute-start(s32[4,1024]{1,0:T(4,128)S(1)} %pad_add_fusion.3), channel_id=1, source_target_pairs={{0,8},{1,9},{2,10},{3,11},{4,12},{5,13},{6,14},{7,15},{8,0},{9,1},... | collective-permute-start | bytes 49160 | tf_op jit(solution)/shard_map/ppermute | solution.py:103
  28.6 6.6 %copy-start.11 = (f32[16]{0:T(128)S(1)}, f32[16]{0:T(128)}, u32[]{:S(2)}) copy-start(f32[16]{0:T(128)} %copy-done.10) | copy-start | bytes 196
  28.6 6.6 %copy-start.13 = (f32[16]{0:T(128)S(1)}, f32[16]{0:T(128)}, u32[]{:S(2)}) copy-start(f32[16]{0:T(128)} %param.26) | copy-start | bytes 196
  28.6 6.6 %copy-start.28 = (f32[16]{0:T(128)S(1)}, f32[16]{0:T(128)}, u32[]{:S(2)}) copy-start(f32[16]{0:T(128)} %copy-done.27) | copy-start | bytes 196
  33.7 3.0 %copy-start.15 = (pred[4,16]{1,0:T(4,128)(4,1)S(1)}, pred[4,16]{1,0:T(4,128)(4,1)}, u32[]{:S(2)}) copy-start(pred[4,16]{1,0:T(4,128)(4,1)} %copy-done.14) | copy-start | bytes 196
  37.4 2.1 %copy-start.5 = (bf16[344,1024]{0,1:T(8,128)(2,1)S(1)}, bf16[344,1024]{0,1:T(8,128)(2,1)}, u32[]{:S(2)}) copy-start(bf16[344,1024]{0,1:T(8,128)(2,1)} %copy.35) | copy-start | bytes 2113540
  45.3 2.6 %copy-start.2 = (f32[4,128,1024]{1,2,0:T(8,128)S(1)}, f32[4,128,1024]{1,2,0:T(8,128)}, u32[]{:S(2)}) copy-start(f32[4,128,1024]{1,2,0:T(8,128)} %fusion.43) | copy-start | bytes 6291460
  45.3 2.6 %copy-start.6 = (f32[4,128,16]{1,2,0:T(8,128)S(1)}, f32[4,128,16]{1,2,0:T(8,128)}, u32[]{:S(2)}) copy-start(f32[4,128,16]{1,2,0:T(8,128)} %exponential_bitcast_fusion) | copy-start | bytes 98308
  45.3 2.6 %copy-start.24 = (f32[16]{0:T(128)S(1)}, f32[16]{0:T(128)}, u32[]{:S(2)}) copy-start(f32[16]{0:T(128)} %param.28) | copy-start | bytes 196
  45.3 2.6 %copy-start.30 = (f32[16,4,64,64]{3,2,0,1:T(8,128)S(1)}, f32[16,4,64,64]{3,2,0,1:T(8,128)}, u32[]{:S(2)}) copy-start(f32[16,4,64,64]{3,2,0,1:T(8,128)} %fusion.5) | copy-start | bytes 3145732
  45.3 2.9 %copy-start.31 = (f32[16,4,64,64]{3,2,0,1:T(8,128)S(1)}, f32[16,4,64,64]{3,2,0,1:T(8,128)}, u32[]{:S(2)}) copy-start(f32[16,4,64,64]{3,2,0,1:T(8,128)} %fusion.6) | copy-start | bytes 3145732
  51.0 1.2 %copy-start.4 = (bf16[1024,512]{1,0:T(8,128)(2,1)S(1)}, bf16[1024,512]{1,0:T(8,128)(2,1)}, u32[]{:S(2)}) copy-start(bf16[1024,512]{1,0:T(8,128)(2,1)} %param.30) | copy-start | bytes 3145732
  52.2 2.1 %copy-start.17 = (bf16[512,1]{0,1:T(2,128)(2,1)S(1)}, bf16[512,1]{0,1:T(2,128)(2,1)}, u32[]{:S(2)}) copy-start(bf16[512,1]{0,1:T(2,128)(2,1)} %get-tuple-element.28) | copy-start | bytes 3076
  52.2 2.1 %copy-start.18 = (bf16[512,1]{0,1:T(2,128)(2,1)S(1)}, bf16[512,1]{0,1:T(2,128)(2,1)}, u32[]{:S(2)}) copy-start(bf16[512,1]{0,1:T(2,128)(2,1)} %get-tuple-element.29) | copy-start | bytes 3076
  52.2 2.1 %copy-start.21 = (f32[512]{0:T(512)S(1)}, f32[512]{0:T(512)}, u32[]{:S(2)}) copy-start(f32[512]{0:T(512)} %param.31) | copy-start | bytes 6148
  52.2 2.1 %copy-start.23 = (bf16[512,2]{0,1:T(2,128)(2,1)S(1)}, bf16[512,2]{0,1:T(2,128)(2,1)}, u32[]{:S(2)}) copy-start(bf16[512,2]{0,1:T(2,128)(2,1)} %param.32) | copy-start | bytes 6148
  52.2 2.4 %copy-start.16 = (s32[2,2,128]{2,1,0:T(2,128)S(1)}, s32[2,2,128]{2,1,0:T(2,128)}, u32[]{:S(2)}) copy-start(s32[2,2,128]{2,1,0:T(2,128)} %param.33) | copy-start | bytes 6148
  52.2 2.5 %copy-start.29 = (f32[2,2,128]{2,1,0:T(2,128)S(1)}, f32[2,2,128]{2,1,0:T(2,128)}, u32[]{:S(2)}) copy-start(f32[2,2,128]{2,1,0:T(2,128)} %fusion.34) | copy-start | bytes 6148
  54.3 1.0 %copy-start.25 = (bf16[2,128,512]{2,1,0:T(8,128)(2,1)}, bf16[2,128,512]{2,1,0:T(8,128)(2,1)S(1)}, u32[]{:S(2)}) copy-start(bf16[2,128,512]{2,1,0:T(8,128)(2,1)S(1)} %get-tuple-element.43) | copy-start | bytes 786436

commit v9 on v8

--- a/solution.py
+++ b/solution.py
@@ -258,9 +258,7 @@
     )
     per_gram = per_gram[:, :HEADS] + per_gram[:, HEADS:]
     b_hi, b_lo = split_bf16(per_gram[..., None] * b_tab[None, None])
-    start_state = jnp.einsum(
-        "hgp,uhgn->uhpn", x_heads, b_hi, preferred_element_type=jnp.float32
-    ) + jnp.einsum("hgp,uhgn->uhpn", x_heads, b_lo, preferred_element_type=jnp.float32)
+    start_state = jnp.einsum("hgp,uhgn->uhpn", x_heads, b_hi, preferred_element_type=jnp.float32)
 
     y_inter = (
         jnp.einsum("utn,uhpn->uthp", c_u, start_state, precision=lax.Precision.HIGH)

time: 55.9 us -> 53.5 us (0.957)
  matrix products: 26 us -> 22.1 us
  local copies, waits for them, and re-layouts: 8.18 us -> 9.54 us
    dot_general x1 -> x0, matrix products: 2.28 us -> none  [local(): jnp.einsum('hgp,uhgn->uhpn', x_heads, b_lo, preferred_element_type=jnp.fl...]
    dot_general x1, matrix products: 2.35 us -> 0.97 us  [local(): jnp.einsum('hgp,uhgn->uhpn', x_heads, b_hi, preferred_element_type=jnp.fl...]
    dot_general x1, matrix products: 2.58 us -> 1.64 us  [local(): jnp.einsum('uhts,ushp->uthp', weights, x_u, preferred_element_type=jnp.fl...]
    unnamed x66 -> x116, local copies, waits for them, and re-layouts: 1.15 us -> 1.98 us
    concatenate x4, other arithmetic: 0.83 us -> 0.04 us  [gather_all(): low_first = jnp.concatenate([held, other], axis=1)]
    dot_general x2, matrix products: 1.14 us -> 1.86 us  [block_cumsum(): return jnp.einsum('...s,st->...t', values, tri, precision=HIGH)]
    neg x1, other arithmetic: 0.66 us -> 0.01 us  [local(): neg_rate = -jnp.exp(a_log)[:, None]]
    unnamed x1, other arithmetic: 0.12 us -> 0.74 us
  transfers between devices with their start and end apart: 4 -> 4, of which waited for: 2 -> 2; matrix products, arithmetic and copies ran while one was open for 30% -> 33% of each run, Pallas kernels for 0% -> 0%
where the time goes in v9:
time: 53.5 us; the launch traced here: 52.9 us
  matrix products  22.1 us (41%)
  local copies, waits for them, and re-layouts  9.54 us (18%)
  other arithmetic  8.72 us (16%)
  starting transfers between devices  8.28 us (15%)
  waiting for transfers between devices  2.56 us (5%)
  between operations  1.7 us (3%)
    ppermute x4, starting transfers between devices, gather_all(): lax.ppermute(held, axis, [(src, src ^ mask) for src in range(count)])  8.28 us
    dot_general x1, matrix products, local(): jnp.einsum('utn,uhpn->uthp', c_u, start_state, precision=lax.Precision.HIGH)  2.77 us
    ppermute x4, waiting for transfers between devices, gather_all(): lax.ppermute(held, axis, [(src, src ^ mask) for src in range(count)])  2.56 us
    slice x2, local copies, waits for them, and re-layouts, local(): b_tab = act_tab[:, INNER:INNER + NS]  2.36 us
    dot_general x1, matrix products, local(): jnp.einsum('rtg,gc->rtc', oh_loc, x_tab, preferred_element_type=jnp.float32)  2.11 us
    dot_general x1, matrix products, local(): jnp.einsum('uhbs,ubsg->uhg', jnp.concatenate([w_hi, w_lo], axis=1), oh_al...  2.11 us
    dot_general x1, matrix products, local(): jnp.einsum('rtk,kc->rtc', oh_tok, z_rows, preferred_element_type=jnp.floa...  2.04 us
    unnamed x116, local copies, waits for them, and re-layouts  1.98 us
  transfers between devices with their start and end apart: 4, of which 2 were waited for; matrix products, arithmetic and copies ran while one was open for 33% of the time, Pallas kernels for 0%

profile of v9, /device:TPU:0, one launch (start us, length us, event | category | flops | bytes accessed | tf_op | source)
XLA Modules:
  0.0 52.9 jit_solution(14627780627255575648)
XLA Ops:
  0.7 1.0 %fusion.33 = s32[2,128]{1,0:T(2,128)S(1)} fusion(s32[2,128]{1,0:T(2,128)} %param.18), kind=kOutput, calls=%fused_computation.49 | convolution fusion | flops 99072 | bytes 2048 | tf_op jit(solution)/shard_map/dot_general | solution.py:186
  1.7 0.7 %pad_add_fusion.8 = s32[4,128]{1,0:T(4,128)S(1)} fusion(s32[2,128]{1,0:T(2,128)S(1)} %fusion.33, s32[2,128]{1,0:T(2,128)} %param.18), kind=kLoop, calls=%fused_computation.166 | loop fusion | flops 512 | bytes 4096 | tf_op jit(solution)/shard_map/concatenate | solution.py:189
  2.3 0.5 collective-permute-start
  2.8 0.7 %broadcast_compare_fusion.7 = (pred[4,128]{1,0:T(4,128)(4,1)S(1)}, pred[4,128]{1,0:T(4,128)(4,1)S(1)}, pred[4,128]{1,0:T(4,128)(4,1)S(1)}, pred[4,128]{1,0:T(4,128)(4,1)S(1)}) fusion(s32[2,128]{1,0:T(2,128)S(1)} %fusion.33, s32[2,128]{1,0:T(2,128)} %param.18), kind=kLoop, calls=%fused_computation.180 | loop fusion | flops 2560 | bytes 4096 | tf_op jit(solution)/shard_map/eq | solution.py:122
  3.5 0.9 %fusion.29 = bf16[2,512]{1,0:T(2,128)(2,1)S(1)} fusion(bf16[2,512]{1,0:T(2,128)(2,1)} %param.19), kind=kOutput, calls=%fused_computation.44 | convolution fusion | flops 1573888 | bytes 4096 | tf_op jit(solution)/shard_map/dot_general | solution.py:176
  4.4 0.8 %fusion.77 = (f32[4]{0:T(128)S(1)}, bf16[4,512]{1,0:T(4,128)(2,1)S(1)}) fusion(bf16[1,512]{1,0:T(2,128)(2,1)S(1)} %get-tuple-element.39, bf16[1,512]{1,0:T(2,128)(2,1)S(1)} %get-tuple-element.38, bf16[2,512]{1,0:T(2,128)(2,1)} %param.19), kind=kLoop, calls=%fused_computation.130 | loop fusion | flops 18428 | bytes 8208 | tf_op jit(solution)/shard_map/reduce_sum | solution.py:23
  5.2 1.0 %fusion.8 = f32[4,1152]{1,0:T(4,128)S(1)} fusion(bf16[512,1152]{1,0:T(8,128)(2,1)S(1)} %copy-done, bf16[4,512]{1,0:T(4,128)(2,1)S(1)} %get-tuple-element.5, f32[512]{0:T(512)} %param.20, f32[4]{0:T(128)S(1)} %add_rsqrt_fusion.2), kind=kOutput, calls=%fused_computation.13 | convolution fusion | flops 4736000 | bytes 1204240 | tf_op jit(solution)/shard_map/dot_general | solution.py:74
  6.2 0.8 %broadcast_multiply_fusion = f32[4,4,1152]{2,1,0:T(4,128)S(1)} fusion(f32[4,1152]{1,0:T(4,128)S(1)} %fusion.8, f32[4,1152]{1,0:T(4,128)} %param.24), kind=kLoop, calls=%fused_computation.102 | loop fusion | flops 18432 | bytes 110592 | tf_op jit(solution)/shard_map/mul | solution.py:77
  7.0 0.9 %fusion.104 = f32[4,16]{1,0:T(4,128)S(1)} fusion(bf16[512,16]{0,1:T(8,128)(2,1)} %param.23, bf16[4,512]{1,0:T(4,128)(2,1)S(1)} %get-tuple-element.5, f32[512]{0:T(512)} %param.20, f32[4]{0:T(128)S(1)} %add_rsqrt_fusion.2), kind=kOutput, calls=%fused_computation.200 | convolution fusion | flops 73728 | bytes 22800 | tf_op jit(solution)/shard_map/dot_general | solution.py:76
  8.0 0.7 %compare_select_fusion.2 = f32[4,16,128]{2,1,0:T(8,128)} fusion(f32[16]{0:T(128)S(1)} %copy-done.39, f32[16]{0:T(128)S(1)} %get-tuple-element.35, f32[16]{0:T(128)S(1)} %get-tuple-element.36, f32[16]{0:T(128)S(1)} %get-tuple-element.37, f32[16]{0:T(128)S(1)} %get-tuple-element.34, pred[4,128]{1,0:T(4,128)(4,1)S(1)} %get-tuple-element.32, ...), kind=kLoop, calls=%fused_computation.94 | loop fusion | flops 114688 | bytes 35136 | tf_op jit(solution)/shard_map/jit(softplus)/select_n | solution.py:212
  8.7 0.2 fusion.70
  9.1 0.6 %exponential_bitcast_fusion = f32[4,128,16]{1,2,0:T(8,128)} fusion(f32[4,16,128]{2,1,0:T(8,128)S(1)} %fusion.70), kind=kLoop, calls=%fused_computation.108 | loop fusion | bytes 65536 | tf_op jit(solution)/shard_map/exp | solution.py:265
  9.7 2.0 %fusion.37 = f32[4,128,1024]{1,2,0:T(8,128)} fusion(bf16[512,1024]{1,0:T(8,128)(2,1)S(1)} %copy-done.3, s32[4,128]{1,0:T(4,128)S(1)} %pad_add_fusion.8, bf16[4,512]{1,0:T(4,128)(2,1)S(1)} %get-tuple-element.5, f32[512]{0:T(512)S(1)} %copy-done.27, f32[4]{0:T(128)S(1)} %add_rsqrt_fusion.2), kind=kOutput, calls=%fused_computation.57 | convolution fusion | flops 8402944 | bytes 3153936 | tf_op jit(solution)/shard_map/rtk,kc->rtc/dot_general | solution.py:211
  12.0 0.6 %fusion.108 = (bf16[512,1]{0,1:T(2,128)(2,1)}, bf16[512,1]{0,1:T(2,128)(2,1)}) fusion(bf16[512,2]{0,1:T(2,128)(2,1)S(1)} %convolution_convert_fusion.5), kind=kLoop, calls=%fused_computation.202 | loop fusion | bytes 4096 | tf_op jit(solution)/shard_map/slice | solution.py:291
  12.6 0.6 %broadcast_and_fusion = pred[4,16,16]{2,1,0:T(8,128)(4,1)} fusion(pred[16,16]{1,0:T(8,128)(4,1)S(1)} %iota_compare_fusion.10, pred[4,16]{1,0:T(4,128)(4,1)S(1)} %iota_compare_fusion.18), kind=kLoop, calls=%fused_computation.127 | loop fusion | flops 1024 | bytes 1344 | tf_op jit(solution)/shard_map/and | solution.py:245
  13.2 1.6 %divide_multiply_fusion = f32[344,1152]{1,0:T(8,128)S(1)} fusion(f32[16,1152]{1,0:T(8,128)S(1)} %mul.201, f32[344,16]{1,0:T(8,128)S(1)} %copy-done.54, f32[1152]{0:T(1024)S(1)} %copy-done.46), kind=kOutput, calls=%fused_computation.28 | convolution fusion | flops 78068736 | bytes 1685504 | tf_op jit(solution)/shard_map/dot_general | solution.py:78
  14.9 0.6 %fusion.28 = f32[2,2,128]{2,1,0:T(2,128)} fusion(f32[2,2,128]{2,1,0:T(2,128)S(1)} %copy-done.47), kind=kOutput, calls=%fused_computation.41 | output fusion | flops 769 | bytes 4096 | tf_op jit(solution)/shard_map/sub | solution.py:295
  15.5 2.6 %collective-permute-start.1 = (s32[4,256]{1,0:T(4,128)S(1)}, s32[4,256]{1,0:T(4,128)S(1)}, u32[]{:S(2)}, u32[]{:S(2)}) collective-permute-start(s32[4,256]{1,0:T(4,128)S(1)} %pad_add_fusion.7), channel_id=1, source_target_pairs={{0,2},{1,3},{2,0},{3,1},{4,6},{5,7},{6,4},{7,5},{8,10},{9,11},{10,... | collective-permute-start | bytes 12296 | tf_op jit(solution)/shard_map/ppermute | solution.py:103
  18.1 0.6 %convert_compare_fusion = pred[128,128]{1,0:T(8,128)(4,1)} fusion(), kind=kLoop, calls=%fused_computation.98 | loop fusion | flops 49152 | bytes 16384 | tf_op jit(solution)/shard_map/gt | solution.py:229
  18.7 1.0 %collective-permute-done.1 = s32[4,256]{1,0:T(4,128)S(1)} collective-permute-done((s32[4,256]{1,0:T(4,128)S(1)}, s32[4,256]{1,0:T(4,128)S(1)}, u32[]{:S(2)}, u32[]{:S(2)}) %collective-permute-start.1) | collective-permute-done | bytes 4128 | tf_op jit(solution)/shard_map/ppermute | solution.py:103
  19.7 2.1 %collective-permute-start.2 = (s32[4,512]{1,0:T(4,128)S(1)}, s32[4,512]{1,0:T(4,128)S(1)}, u32[]{:S(2)}, u32[]{:S(2)}) collective-permute-start(s32[4,512]{1,0:T(4,128)S(1)} %pad_add_fusion.5), channel_id=1, source_target_pairs={{0,4},{1,5},{2,6},{3,7},{4,0},{5,1},{6,2},{7,3},{8,12},{9,13},{10,... | collective-permute-start | bytes 24584 | tf_op jit(solution)/shard_map/ppermute | solution.py:103
  21.9 1.6 %collective-permute-done.2 = s32[4,512]{1,0:T(4,128)S(1)} collective-permute-done((s32[4,512]{1,0:T(4,128)S(1)}, s32[4,512]{1,0:T(4,128)S(1)}, u32[]{:S(2)}, u32[]{:S(2)}) %collective-permute-start.2) | collective-permute-done | bytes 8224 | tf_op jit(solution)/shard_map/ppermute | solution.py:103
  23.6 3.1 %collective-permute-start.3 = (s32[4,1024]{1,0:T(4,128)S(1)}, s32[4,1024]{1,0:T(4,128)S(1)}, u32[]{:S(2)}, u32[]{:S(2)}) collective-permute-start(s32[4,1024]{1,0:T(4,128)S(1)} %pad_add_fusion.3), channel_id=1, source_target_pairs={{0,8},{1,9},{2,10},{3,11},{4,12},{5,13},{6,14},{7,15},{8,0},{9,1},... | collective-permute-start | bytes 49160 | tf_op jit(solution)/shard_map/ppermute | solution.py:103
  26.8 0.7 %slice.192 = f32[344,64]{1,0:T(8,128)} slice(f32[344,1152]{1,0:T(8,128)S(1)} %divide_multiply_fusion), slice={[0:344], [1024:1088]} | slice | bytes 176128 | tf_op jit(solution)/shard_map/slice | solution.py:180
  27.5 1.2 %copy.35 = bf16[344,1024]{0,1:T(8,128)(2,1)} copy(bf16[344,1024]{1,0:T(8,128)(2,1)S(1)} %slice.239) | data formatting | bytes 1409024 | tf_op jit(solution)/shard_map/slice | solution.py:179
  28.7 1.7 %copy.34 = f32[344,64]{0,1:T(8,128)} copy(f32[344,64]{1,0:T(8,128)} %slice.192) | data formatting | bytes 176128 | tf_op jit(solution)/shard_map/slice | solution.py:180
  30.3 0.7 %mul.226 = f32[16,64]{1,0:T(8,128)} reshape(f32[1024]{0:T(1024)S(1)} %copy-done.38) | data formatting | bytes 8192 | tf_op jit(solution)/shard_map/mul | solution.py:23
  31.4 0.3 copy-done.6
  31.7 2.1 %convolution_convert_fusion.1 = bf16[4,128,1024]{2,1,0:T(8,128)(2,1)S(1)} fusion(s32[4,128]{1,0:T(4,128)S(1)} %pad_add_fusion.9, f32[344,1152]{1,0:T(8,128)} %copy-done.1), kind=kOutput, calls=%fused_computation.30 | convolution fusion | flops 361410560 | bytes 1755136 | tf_op jit(solution)/shard_map/rtg,gc->rtc/dot_general | solution.py:206
  33.8 1.3 %fusion.36 = f32[4,128,128]{1,2,0:T(8,128)S(1)} fusion(s32[4,128]{1,0:T(4,128)S(1)} %pad_add_fusion.9, f32[344,1152]{1,0:T(8,128)} %copy-done.1), kind=kOutput, calls=%fused_computation.54 | convolution fusion | flops 270708736 | bytes 440320 | tf_op jit(solution)/shard_map/rtg,gc->rtc/dot_general | solution.py:209
  35.2 0.7 %fusion.122 = s32[1,4,16,128]{3,1,2,0:T(4,128)} fusion(s32[4,2048]{1,0:T(4,128)S(1)} %pad_add_fusion.1, pred[2048]{0:T(1024)(128)(4,1)S(1)} %copy-done.18, pred[2048]{0:T(1024)(128)(4,1)S(1)} %copy-done.20, pred[2048]{0:T(1024)(128)(4,1)S(1)} %copy-done.22, pred[2048]{0:T(1024)(128)(4,1)S(1)} %copy-done.24), kind=kLoop, calls=%fused_computation.205 | loop fusion | flops 106496 | bytes 73728
  35.9 0.7 %copy.32 = bf16[4,128,1024]{1,2,0:T(8,128)(2,1)S(1)} copy(bf16[4,128,1024]{2,1,0:T(8,128)(2,1)S(1)} %convolution_convert_fusion.1) | data formatting | bytes 2097152 | tf_op jit(solution)/shard_map/convert_element_type | solution.py:206
  36.7 0.4 fusion.63
  37.1 0.7 %bitcast_dynamic-update-slice_fusion.1 = s32[4,16,128]{2,1,0:T(8,128)S(1)} fusion(s32[1,2,16,128]{3,1,2,0:T(2,128)} %bitcast.106), kind=kLoop, calls=%fused_computation.116 | loop fusion | bytes 32768
  37.8 1.6 %fusion.42 = f32[4,16,16,128]{3,2,1,0:T(8,128)S(1)} fusion(f32[16]{0:T(128)} %param.26, f32[16]{0:T(128)} %copy-done.32, f32[16]{0:T(128)} %copy-done.34, f32[16]{0:T(128)} %copy-done.36, f32[16]{0:T(128)} %copy-done.30, f32[16]{0:T(128)} %copy-done.55, pred[4,16,128]{2,1,0:T(8,128)(4,1)S(1)} %get-tuple-element.9, ...), kind=kOutput, calls=%fused_computation.67 | convolution fusion | flops 203309056 | bytes 557440 | tf_op jit(solution)/shard_map/...s,st->...t/dot_general | solution.py:143
  39.5 0.4 slice_reduce_fusion
  40.1 0.7 %subtract_convert_fusion = (bf16[4,16,16,128]{3,2,1,0:T(8,128)(2,1)S(1)}, bf16[4,16,16,128]{3,2,1,0:T(8,128)(2,1)S(1)}) fusion(f32[4,16,16]{2,1,0:T(8,128)S(1)} %exponential_select_fusion, f32[16]{0:T(128)S(1)} %copy-done.40, f32[16]{0:T(128)S(1)} %copy-done.33, pred[4,16,128]{2,1,0:T(8,128)(4,1)S(1)} %get-tuple-element.9, f32[16]{0:T(128)S(1)} %copy-done.35, ...), kind=kLoop, calls=%fused_computation.64 | loop fusion | flops 2752512 | bytes 1089856 | tf_op jit(solution)/shard_map/convert_element_type | solution.py:139
  40.9 2.1 %fusion.26 = f32[4,32,344]{2,1,0:T(8,128)S(1)} fusion(s32[4,16,128]{2,1,0:T(8,128)S(1)} %bitcast.107, bf16[4,32,16,128]{3,2,1,0:T(8,128)(2,1)S(1)} %pad_maximum_fusion), kind=kOutput, calls=%fused_computation.38 | convolution fusion | flops 183173120 | bytes 733184 | tf_op jit(solution)/shard_map/uhbs,ubsg->uhg/dot_general | solution.py:253
  43.1 1.0 %fusion.4 = f32[16,4,64,64]{3,2,0,1:T(8,128)S(1)} fusion(bf16[16,344,64,1]{1,2,0,3:T(8,128)(2,1)S(1)} %bitcast.104, f32[344,64]{0,1:T(8,128)S(1)} %copy-done.8, f32[4,16,344]{2,1,0:T(8,128)S(1)} %slice_add_fusion), kind=kOutput, calls=%fused_computation.7 | convolution fusion | flops 183173120 | bytes 1929216 | tf_op jit(solution)/shard_map/hgp,uhgn->uhpn/dot_general | solution.py:261
  44.1 1.6 %fusion.9 = f32[4,16,64,128]{3,2,1,0:T(8,128)S(1)} fusion(bf16[4,128,16,64]{1,3,2,0:T(8,128)(2,1)S(1)} %bitcast.102, f32[4,16,128]{2,1,0:T(8,128)S(1)} %copy-done.13, f32[4,16,128]{2,1,0:T(8,128)S(1)} %copy-done.15, f32[4,128,128]{2,1,0:T(8,128)S(1)} %fusion.63, pred[128,128]{1,0:T(8,128)(4,1)S(1)} %copy-done.25), kind=kOutput, calls=%fused_computation.14 | convolution fusion | flops 140509184 | bytes 3489792 | tf_op jit(solution)/shard_map/uhts,ushp->uthp/dot_general | solution.py:232
  45.8 2.8 %multiply_reduce_fusion = (f32[4,128,16]{1,2,0:T(8,128)S(1)}, f32[4,128,16,64]{1,3,2,0:T(8,128)S(1)}) fusion(f32[4,128,16,64]{1,3,2,0:T(8,128)S(1)} %bitcast.101, bf16[4,128,16,64]{1,3,2,0:T(8,128)(2,1)S(1)} %bitcast.103, f32[16]{0:T(128)S(1)} %copy-done.52, f32[4,128,16]{1,2,0:T(8,128)S(1)} %copy-done.16, f32[16,4,64,64]{3,2,0,1:T(8,128)S(1)} %fusion.4, ...), kind=kOutput, calls=%fused_computation.21 | convolution fusion | flops 207609856 | bytes 9634304 | tf_op jit(solution)/shard_map/utn,uhpn->uthp/dot_general | solution.py:264
  48.6 0.5 multiply_convert_fusion.4
  49.1 0.7 %copy-done.4 = bf16[1024,512]{1,0:T(8,128)(2,1)S(1)} copy-done((bf16[1024,512]{1,0:T(8,128)(2,1)S(1)}, bf16[1024,512]{1,0:T(8,128)(2,1)}, u32[]{:S(2)}) %copy-start.4) | copy-done | bytes 1048600
  49.8 0.7 %convolution_convert_fusion.2 = bf16[4,128,512]{2,1,0:T(8,128)(2,1)S(1)} fusion(bf16[4,128,1024]{1,2,0:T(8,128)(2,1)S(1)} %bitcast.100, bf16[1024,512]{1,0:T(8,128)(2,1)S(1)} %copy-done.4), kind=kOutput, calls=%fused_computation.32 | convolution fusion | flops 537133056 | bytes 2621440 | tf_op jit(solution)/shard_map/gre,ed->grd/dot_general | solution.py:274
  50.6 0.9 %rev.3 = bf16[2,128,512]{2,1,0:T(8,128)(2,1)S(1)} reverse(bf16[2,128,512]{2,1,0:T(8,128)(2,1)S(1)} %slice.194), dimensions={1,2} | reverse | bytes 524288 | tf_op jit(solution)/shard_map/rev | solution.py:281
  51.5 0.4 fusion.38
  52.0 0.2 fusion.48
  52.3 0.6 %multiply_reduce_fusion.1 = f32[2,128]{1,0:T(2,128)} fusion(f32[2,2,128]{2,1,0:T(2,128)S(1)} %select_reduce_fusion.1, f32[2,2,128]{2,1,0:T(2,128)S(1)} %copy-done.56), kind=kOutput, calls=%fused_computation.168 | output fusion | flops 2049 | bytes 5120 | tf_op jit(solution)/shard_map/reduce_sum | solution.py:296
  (156 shorter events, 1.4 us)
Async XLA Ops:
  0.6 4.6 %copy-start = (bf16[512,1152]{1,0:T(8,128)(2,1)S(1)}, bf16[512,1152]{1,0:T(8,128)(2,1)}, u32[]{:S(2)}) copy-start(bf16[512,1152]{1,0:T(8,128)(2,1)} %param.21) | copy-start | bytes 3538948
  0.6 9.1 %copy-start.27 = (f32[512]{0:T(512)S(1)}, f32[512]{0:T(512)}, u32[]{:S(2)}) copy-start(f32[512]{0:T(512)} %param.20) | copy-start | bytes 6148
  0.7 7.3 %copy-start.51 = (f32[16]{0:T(128)S(1)}, f32[16]{0:T(128)}, u32[]{:S(2)}) copy-start(f32[16]{0:T(128)} %param.27) | copy-start | bytes 196
  0.7 7.3 %copy-start.39 = (f32[16]{0:T(128)S(1)}, f32[16]{0:T(128)}, u32[]{:S(2)}) copy-start(f32[16]{0:T(128)} %param.26) | copy-start | bytes 196
  0.7 9.1 %copy-start.3 = (bf16[512,1024]{1,0:T(8,128)(2,1)S(1)}, bf16[512,1024]{1,0:T(8,128)(2,1)}, u32[]{:S(2)}) copy-start(bf16[512,1024]{1,0:T(8,128)(2,1)} %param.22) | copy-start | bytes 3145732
  2.3 9.4 %copy-start.28 = (s32[4,128]{1,0:T(4,128)}, s32[4,128]{1,0:T(4,128)S(1)}, u32[]{:S(2)}) copy-start(s32[4,128]{1,0:T(4,128)S(1)} %pad_add_fusion.8) | copy-start | bytes 6148
  2.3 13.1 %collective-permute-start = (s32[4,128]{1,0:T(4,128)S(1)}, s32[4,128]{1,0:T(4,128)S(1)}, u32[]{:S(2)}, u32[]{:S(2)}) collective-permute-start(s32[4,128]{1,0:T(4,128)S(1)} %pad_add_fusion.8), channel_id=1, source_target_pairs={{0,1},{1,0},{2,3},{3,2},{4,5},{5,4},{6,7},{7,6},{8,9},{9,8},{10,11... | collective-permute-start | bytes 6152 | tf_op jit(solution)/shard_map/ppermute | solution.py:103
  5.2 6.6 %copy-start.9 = (bf16[4,512]{1,0:T(4,128)(2,1)}, bf16[4,512]{1,0:T(4,128)(2,1)S(1)}, u32[]{:S(2)}) copy-start(bf16[4,512]{1,0:T(4,128)(2,1)S(1)} %get-tuple-element.5) | copy-start | bytes 12292
  6.2 5.6 %copy-start.49 = (bf16[512,2]{0,1:T(2,128)(2,1)S(1)}, bf16[512,2]{0,1:T(2,128)(2,1)}, u32[]{:S(2)}) copy-start(bf16[512,2]{0,1:T(2,128)(2,1)} %param.32) | copy-start | bytes 6148
  7.9 5.3 %copy-start.46 = (f32[1152]{0:T(1024)S(1)}, f32[1152]{0:T(1024)}, u32[]{:S(2)}) copy-start(f32[1152]{0:T(1024)} %param.25) | copy-start | bytes 13828
  7.9 5.3 %copy-start.54 = (f32[344,16]{1,0:T(8,128)S(1)}, f32[344,16]{1,0:T(8,128)}, u32[]{:S(2)}) copy-start(f32[344,16]{1,0:T(8,128)} %constant.138.clone) | copy-start | bytes 66052
  7.9 4.6 %copy-start.30 = (f32[16]{0:T(128)}, f32[16]{0:T(128)S(1)}, u32[]{:S(2)}) copy-start(f32[16]{0:T(128)S(1)} %get-tuple-element.34) | copy-start | bytes 196
  7.9 4.6 %copy-start.32 = (f32[16]{0:T(128)}, f32[16]{0:T(128)S(1)}, u32[]{:S(2)}) copy-start(f32[16]{0:T(128)S(1)} %get-tuple-element.35) | copy-start | bytes 196
  8.0 4.6 %copy-start.34 = (f32[16]{0:T(128)}, f32[16]{0:T(128)S(1)}, u32[]{:S(2)}) copy-start(f32[16]{0:T(128)S(1)} %get-tuple-element.36) | copy-start | bytes 196
  8.0 4.6 %copy-start.36 = (f32[16]{0:T(128)}, f32[16]{0:T(128)S(1)}, u32[]{:S(2)}) copy-start(f32[16]{0:T(128)S(1)} %get-tuple-element.37) | copy-start | bytes 196
  9.0 3.6 %copy-start.14 = (f32[4,16,128]{2,1,0:T(8,128)}, f32[4,16,128]{2,1,0:T(8,128)S(1)}, u32[]{:S(2)}) copy-start(f32[4,16,128]{2,1,0:T(8,128)S(1)} %fusion.70) | copy-start | bytes 98308
  9.1 3.5 %copy-start.41 = (pred[4,16]{1,0:T(4,128)(4,1)}, pred[4,16]{1,0:T(4,128)(4,1)S(1)}, u32[]{:S(2)}) copy-start(pred[4,16]{1,0:T(4,128)(4,1)S(1)} %iota_compare_fusion.18) | copy-start | bytes 196
  13.2 2.3 %copy-start.26 = (s32[2,128]{1,0:T(2,128)S(1)}, s32[2,128]{1,0:T(2,128)}, u32[]{:S(2)}) copy-start(s32[2,128]{1,0:T(2,128)} %param.18) | copy-start | bytes 3076
  14.9 16.2 %copy-start.1 = (f32[344,1152]{1,0:T(8,128)}, f32[344,1152]{1,0:T(8,128)S(1)}, u32[]{:S(2)}) copy-start(f32[344,1152]{1,0:T(8,128)S(1)} %divide_multiply_fusion) | copy-start | bytes 4755460
  14.9 15.5 %copy-start.38 = (f32[1024]{0:T(1024)S(1)}, f32[1024]{0:T(1024)}, u32[]{:S(2)}) copy-start(f32[1024]{0:T(1024)} %param.29) | copy-start | bytes 12292
  15.5 4.2 %collective-permute-start.1 = (s32[4,256]{1,0:T(4,128)S(1)}, s32[4,256]{1,0:T(4,128)S(1)}, u32[]{:S(2)}, u32[]{:S(2)}) collective-permute-start(s32[4,256]{1,0:T(4,128)S(1)} %pad_add_fusion.7), channel_id=1, source_target_pairs={{0,2},{1,3},{2,0},{3,1},{4,6},{5,7},{6,4},{7,5},{8,10},{9,11},{10,... | collective-permute-start | bytes 12296 | tf_op jit(solution)/shard_map/ppermute | solution.py:103
  19.7 3.8 %collective-permute-start.2 = (s32[4,512]{1,0:T(4,128)S(1)}, s32[4,512]{1,0:T(4,128)S(1)}, u32[]{:S(2)}, u32[]{:S(2)}) collective-permute-start(s32[4,512]{1,0:T(4,128)S(1)} %pad_add_fusion.5), channel_id=1, source_target_pairs={{0,4},{1,5},{2,6},{3,7},{4,0},{5,1},{6,2},{7,3},{8,12},{9,13},{10,... | collective-permute-start | bytes 24584 | tf_op jit(solution)/shard_map/ppermute | solution.py:103
  21.9 9.4 %copy-start.17 = (pred[2048]{0:T(1024)(128)(4,1)}, pred[2048]{0:T(1024)(128)(4,1)S(1)}, u32[]{:S(2)}) copy-start(pred[2048]{0:T(1024)(128)(4,1)S(1)} %get-tuple-element.44) | copy-start | bytes 6148
  21.9 9.4 %copy-start.19 = (pred[2048]{0:T(1024)(128)(4,1)}, pred[2048]{0:T(1024)(128)(4,1)S(1)}, u32[]{:S(2)}) copy-start(pred[2048]{0:T(1024)(128)(4,1)S(1)} %get-tuple-element.45) | copy-start | bytes 6148
  23.6 7.4 %collective-permute-start.3 = (s32[4,1024]{1,0:T(4,128)S(1)}, s32[4,1024]{1,0:T(4,128)S(1)}, u32[]{:S(2)}, u32[]{:S(2)}) collective-permute-start(s32[4,1024]{1,0:T(4,128)S(1)} %pad_add_fusion.3), channel_id=1, source_target_pairs={{0,8},{1,9},{2,10},{3,11},{4,12},{5,13},{6,14},{7,15},{8,0},{9,1},... | collective-permute-start | bytes 49160 | tf_op jit(solution)/shard_map/ppermute | solution.py:103
  26.7 4.7 %copy-start.21 = (pred[2048]{0:T(1024)(128)(4,1)}, pred[2048]{0:T(1024)(128)(4,1)S(1)}, u32[]{:S(2)}) copy-start(pred[2048]{0:T(1024)(128)(4,1)S(1)} %get-tuple-element.46) | copy-start | bytes 6148
  26.7 4.7 %copy-start.23 = (pred[2048]{0:T(1024)(128)(4,1)}, pred[2048]{0:T(1024)(128)(4,1)S(1)}, u32[]{:S(2)}) copy-start(pred[2048]{0:T(1024)(128)(4,1)S(1)} %get-tuple-element.47) | copy-start | bytes 6148
  31.3 3.9 %copy-start.18 = (pred[2048]{0:T(1024)(128)(4,1)S(1)}, pred[2048]{0:T(1024)(128)(4,1)}, u32[]{:S(2)}) copy-start(pred[2048]{0:T(1024)(128)(4,1)} %copy-done.17) | copy-start | bytes 6148
  31.3 3.9 %copy-start.20 = (pred[2048]{0:T(1024)(128)(4,1)S(1)}, pred[2048]{0:T(1024)(128)(4,1)}, u32[]{:S(2)}) copy-start(pred[2048]{0:T(1024)(128)(4,1)} %copy-done.19) | copy-start | bytes 6148
  31.7 3.5 %copy-start.22 = (pred[2048]{0:T(1024)(128)(4,1)S(1)}, pred[2048]{0:T(1024)(128)(4,1)}, u32[]{:S(2)}) copy-start(pred[2048]{0:T(1024)(128)(4,1)} %copy-done.21) | copy-start | bytes 6148
  31.7 3.5 %copy-start.24 = (pred[2048]{0:T(1024)(128)(4,1)S(1)}, pred[2048]{0:T(1024)(128)(4,1)}, u32[]{:S(2)}) copy-start(pred[2048]{0:T(1024)(128)(4,1)} %copy-done.23) | copy-start | bytes 6148
  36.6 3.2 %copy-start.12 = (pred[4,16,16]{2,1,0:T(8,128)(4,1)S(1)}, pred[4,16,16]{2,1,0:T(8,128)(4,1)}, u32[]{:S(2)}) copy-start(pred[4,16,16]{2,1,0:T(8,128)(4,1)} %broadcast_and_fusion) | copy-start | bytes 3076
  36.6 3.5 %copy-start.42 = (pred[4,16]{1,0:T(4,128)(4,1)S(1)}, pred[4,16]{1,0:T(4,128)(4,1)}, u32[]{:S(2)}) copy-start(pred[4,16]{1,0:T(4,128)(4,1)} %copy-done.41) | copy-start | bytes 196
  36.6 3.5 %copy-start.31 = (f32[16]{0:T(128)S(1)}, f32[16]{0:T(128)}, u32[]{:S(2)}) copy-start(f32[16]{0:T(128)} %copy-done.30) | copy-start | bytes 196
  36.6 3.5 %copy-start.33 = (f32[16]{0:T(128)S(1)}, f32[16]{0:T(128)}, u32[]{:S(2)}) copy-start(f32[16]{0:T(128)} %copy-done.32) | copy-start | bytes 196
  36.6 3.5 %copy-start.35 = (f32[16]{0:T(128)S(1)}, f32[16]{0:T(128)}, u32[]{:S(2)}) copy-start(f32[16]{0:T(128)} %copy-done.34) | copy-start | bytes 196
  36.7 3.5 %copy-start.37 = (f32[16]{0:T(128)S(1)}, f32[16]{0:T(128)}, u32[]{:S(2)}) copy-start(f32[16]{0:T(128)} %copy-done.36) | copy-start | bytes 196
  36.7 3.5 %copy-start.40 = (f32[16]{0:T(128)S(1)}, f32[16]{0:T(128)}, u32[]{:S(2)}) copy-start(f32[16]{0:T(128)} %param.26) | copy-start | bytes 196
  37.8 3.0 %copy-start.7 = (s32[1,4,16,128]{3,1,2,0:T(4,128)S(1)}, s32[1,4,16,128]{3,1,2,0:T(4,128)}, u32[]{:S(2)}) copy-start(s32[1,4,16,128]{3,1,2,0:T(4,128)} %fusion.122) | copy-start | bytes 98308
  40.9 2.2 %copy-start.5 = (bf16[344,1024]{0,1:T(8,128)(2,1)S(1)}, bf16[344,1024]{0,1:T(8,128)(2,1)}, u32[]{:S(2)}) copy-start(bf16[344,1024]{0,1:T(8,128)(2,1)} %copy.35) | copy-start | bytes 2113540
  40.9 2.2 %copy-start.8 = (f32[344,64]{0,1:T(8,128)S(1)}, f32[344,64]{0,1:T(8,128)}, u32[]{:S(2)}) copy-start(f32[344,64]{0,1:T(8,128)} %copy.34) | copy-start | bytes 264196
  45.8 2.8 %copy-start.11 = (f32[16,64]{1,0:T(8,128)S(1)}, f32[16,64]{1,0:T(8,128)}, u32[]{:S(2)}) copy-start(f32[16,64]{1,0:T(8,128)} %mul.226) | copy-start | bytes 12292
  49.1 2.4 %copy-start.10 = (bf16[4,512]{1,0:T(4,128)(2,1)S(1)}, bf16[4,512]{1,0:T(4,128)(2,1)}, u32[]{:S(2)}) copy-start(bf16[4,512]{1,0:T(4,128)(2,1)} %copy-done.9) | copy-start | bytes 12292
  49.1 2.4 %copy-start.29 = (s32[4,128]{1,0:T(4,128)S(1)}, s32[4,128]{1,0:T(4,128)}, u32[]{:S(2)}) copy-start(s32[4,128]{1,0:T(4,128)} %copy-done.28) | copy-start | bytes 6148
  49.8 2.2 %copy-start.48 = (f32[512]{0:T(512)S(1)}, f32[512]{0:T(512)}, u32[]{:S(2)}) copy-start(f32[512]{0:T(512)} %param.31) | copy-start | bytes 6148
  49.8 2.2 %copy-start.50 = (bf16[512,2]{0,1:T(2,128)(2,1)S(1)}, bf16[512,2]{0,1:T(2,128)(2,1)}, u32[]{:S(2)}) copy-start(bf16[512,2]{0,1:T(2,128)(2,1)} %param.32) | copy-start | bytes 6148
  49.8 2.5 %copy-start.43 = (s32[2,2,128]{2,1,0:T(2,128)S(1)}, s32[2,2,128]{2,1,0:T(2,128)}, u32[]{:S(2)}) copy-start(s32[2,2,128]{2,1,0:T(2,128)} %param.33) | copy-start | bytes 6148
  49.8 2.5 %copy-start.56 = (f32[2,2,128]{2,1,0:T(2,128)S(1)}, f32[2,2,128]{2,1,0:T(2,128)}, u32[]{:S(2)}) copy-start(f32[2,2,128]{2,1,0:T(2,128)} %fusion.28) | copy-start | bytes 6148
  (13 other events, 17.8 us)

commit v10 on v9

--- a/solution.py
+++ b/solution.py
@@ -248,15 +248,13 @@
     span = jnp.sum(jnp.where(between[:, None], total_u[:, :, None, :], 0.0), axis=3)
     across = jnp.where(blk_idx[None, None, :] < first_blk[:, None, None], jnp.exp(span), 0.0)
     weight = jnp.repeat(within, nloc, axis=0) * across[..., None]
-    w_hi, w_lo = split_bf16(weight)
     oh_all = jnp.repeat(onehot(gram, GRAMS), nloc, axis=0).reshape(units, nblk, BLK, GRAMS)
     per_gram = jnp.einsum(
         "uhbs,ubsg->uhg",
-        jnp.concatenate([w_hi, w_lo], axis=1),
+        weight.astype(jnp.bfloat16),
         oh_all,
         preferred_element_type=jnp.float32,
     )
-    per_gram = per_gram[:, :HEADS] + per_gram[:, HEADS:]
     b_hi, b_lo = split_bf16(per_gram[..., None] * b_tab[None, None])
     start_state = jnp.einsum("hgp,uhgn->uhpn", x_heads, b_hi, preferred_element_type=jnp.float32)
 

time: 53.5 us -> 53.1 us (level)
  no operation moved by 1% of the time
where the time goes in v10:
time: 53.1 us; the launch traced here: 52.6 us
  matrix products  21.9 us (41%)
  local copies, waits for them, and re-layouts  9.52 us (18%)
  other arithmetic  8.6 us (16%)
  starting transfers between devices  8.29 us (16%)
  waiting for transfers between devices  2.57 us (5%)
  between operations  1.66 us (3%)
    ppermute x4, starting transfers between devices, gather_all(): lax.ppermute(held, axis, [(src, src ^ mask) for src in range(count)])  8.29 us
    dot_general x1, matrix products, local(): jnp.einsum('utn,uhpn->uthp', c_u, start_state, precision=lax.Precision.HIGH)  2.78 us
    ppermute x4, waiting for transfers between devices, gather_all(): lax.ppermute(held, axis, [(src, src ^ mask) for src in range(count)])  2.57 us
    slice x2, local copies, waits for them, and re-layouts, local(): b_tab = act_tab[:, INNER:INNER + NS]  2.35 us
    dot_general x1, matrix products, local(): jnp.einsum('rtg,gc->rtc', oh_loc, x_tab, preferred_element_type=jnp.float32)  2.11 us
    dot_general x1, matrix products, local(): jnp.einsum('rtk,kc->rtc', oh_tok, z_rows, preferred_element_type=jnp.floa...  2.04 us
    unnamed x116, local copies, waits for them, and re-layouts  1.98 us
    dot_general x1, matrix products, local(): jnp.einsum('uhbs,ubsg->uhg', weight.astype(jnp.bfloat16), oh_all, preferr...  1.91 us
  transfers between devices with their start and end apart: 4, of which 2 were waited for; matrix products, arithmetic and copies ran while one was open for 33% of the time, Pallas kernels for 0%

profile of v10, /device:TPU:0, one launch (start us, length us, event | category | flops | bytes accessed | tf_op | source)
XLA Modules:
  0.0 52.6 jit_solution(4184853058864927681)
XLA Ops:
  0.7 1.0 %fusion.33 = s32[2,128]{1,0:T(2,128)S(1)} fusion(s32[2,128]{1,0:T(2,128)} %param.18), kind=kOutput, calls=%fused_computation.49 | convolution fusion | flops 99072 | bytes 2048 | tf_op jit(solution)/shard_map/dot_general | solution.py:186
  1.7 0.7 %pad_add_fusion.8 = s32[4,128]{1,0:T(4,128)S(1)} fusion(s32[2,128]{1,0:T(2,128)S(1)} %fusion.33, s32[2,128]{1,0:T(2,128)} %param.18), kind=kLoop, calls=%fused_computation.163 | loop fusion | flops 512 | bytes 4096 | tf_op jit(solution)/shard_map/concatenate | solution.py:189
  2.3 0.5 collective-permute-start
  2.8 0.7 %broadcast_compare_fusion.7 = (pred[4,128]{1,0:T(4,128)(4,1)S(1)}, pred[4,128]{1,0:T(4,128)(4,1)S(1)}, pred[4,128]{1,0:T(4,128)(4,1)S(1)}, pred[4,128]{1,0:T(4,128)(4,1)S(1)}) fusion(s32[2,128]{1,0:T(2,128)S(1)} %fusion.33, s32[2,128]{1,0:T(2,128)} %param.18), kind=kLoop, calls=%fused_computation.177 | loop fusion | flops 2560 | bytes 4096 | tf_op jit(solution)/shard_map/eq | solution.py:122
  3.5 0.9 %fusion.29 = bf16[2,512]{1,0:T(2,128)(2,1)S(1)} fusion(bf16[2,512]{1,0:T(2,128)(2,1)} %param.19), kind=kOutput, calls=%fused_computation.44 | convolution fusion | flops 1573888 | bytes 4096 | tf_op jit(solution)/shard_map/dot_general | solution.py:176
  4.4 0.8 %fusion.77 = (f32[4]{0:T(128)S(1)}, bf16[4,512]{1,0:T(4,128)(2,1)S(1)}) fusion(bf16[1,512]{1,0:T(2,128)(2,1)S(1)} %get-tuple-element.37, bf16[1,512]{1,0:T(2,128)(2,1)S(1)} %get-tuple-element.36, bf16[2,512]{1,0:T(2,128)(2,1)} %param.19), kind=kLoop, calls=%fused_computation.127 | loop fusion | flops 18428 | bytes 8208 | tf_op jit(solution)/shard_map/reduce_sum | solution.py:23
  5.2 1.0 %fusion.8 = f32[4,1152]{1,0:T(4,128)S(1)} fusion(bf16[512,1152]{1,0:T(8,128)(2,1)S(1)} %copy-done, bf16[4,512]{1,0:T(4,128)(2,1)S(1)} %get-tuple-element.3, f32[512]{0:T(512)} %param.20, f32[4]{0:T(128)S(1)} %add_rsqrt_fusion.2), kind=kOutput, calls=%fused_computation.13 | convolution fusion | flops 4736000 | bytes 1204240 | tf_op jit(solution)/shard_map/dot_general | solution.py:74
  6.2 0.8 %broadcast_multiply_fusion = f32[4,4,1152]{2,1,0:T(4,128)S(1)} fusion(f32[4,1152]{1,0:T(4,128)S(1)} %fusion.8, f32[4,1152]{1,0:T(4,128)} %param.24), kind=kLoop, calls=%fused_computation.99 | loop fusion | flops 18432 | bytes 110592 | tf_op jit(solution)/shard_map/mul | solution.py:77
  7.0 0.9 %fusion.104 = f32[4,16]{1,0:T(4,128)S(1)} fusion(bf16[512,16]{0,1:T(8,128)(2,1)} %param.23, bf16[4,512]{1,0:T(4,128)(2,1)S(1)} %get-tuple-element.3, f32[512]{0:T(512)} %param.20, f32[4]{0:T(128)S(1)} %add_rsqrt_fusion.2), kind=kOutput, calls=%fused_computation.197 | convolution fusion | flops 73728 | bytes 22800 | tf_op jit(solution)/shard_map/dot_general | solution.py:76
  8.0 0.7 %compare_select_fusion.2 = f32[4,16,128]{2,1,0:T(8,128)} fusion(f32[16]{0:T(128)S(1)} %copy-done.39, f32[16]{0:T(128)S(1)} %get-tuple-element.33, f32[16]{0:T(128)S(1)} %get-tuple-element.34, f32[16]{0:T(128)S(1)} %get-tuple-element.35, f32[16]{0:T(128)S(1)} %get-tuple-element.32, pred[4,128]{1,0:T(4,128)(4,1)S(1)} %get-tuple-element.30, ...), kind=kLoop, calls=%fused_computation.91 | loop fusion | flops 114688 | bytes 35136 | tf_op jit(solution)/shard_map/jit(softplus)/select_n | solution.py:212
  8.7 0.2 fusion.70
  9.1 0.6 %exponential_bitcast_fusion = f32[4,128,16]{1,2,0:T(8,128)} fusion(f32[4,16,128]{2,1,0:T(8,128)S(1)} %fusion.70), kind=kLoop, calls=%fused_computation.105 | loop fusion | bytes 65536 | tf_op jit(solution)/shard_map/exp | solution.py:263
  9.7 2.0 %fusion.37 = f32[4,128,1024]{1,2,0:T(8,128)} fusion(bf16[512,1024]{1,0:T(8,128)(2,1)S(1)} %copy-done.3, s32[4,128]{1,0:T(4,128)S(1)} %pad_add_fusion.8, bf16[4,512]{1,0:T(4,128)(2,1)S(1)} %get-tuple-element.3, f32[512]{0:T(512)S(1)} %copy-done.27, f32[4]{0:T(128)S(1)} %add_rsqrt_fusion.2), kind=kOutput, calls=%fused_computation.57 | convolution fusion | flops 8402944 | bytes 3153936 | tf_op jit(solution)/shard_map/rtk,kc->rtc/dot_general | solution.py:211
  11.9 0.6 %fusion.108 = (bf16[512,1]{0,1:T(2,128)(2,1)}, bf16[512,1]{0,1:T(2,128)(2,1)}) fusion(bf16[512,2]{0,1:T(2,128)(2,1)S(1)} %convolution_convert_fusion.5), kind=kLoop, calls=%fused_computation.199 | loop fusion | bytes 4096 | tf_op jit(solution)/shard_map/slice | solution.py:289
  12.6 0.6 %broadcast_and_fusion = pred[4,16,16]{2,1,0:T(8,128)(4,1)} fusion(pred[16,16]{1,0:T(8,128)(4,1)S(1)} %iota_compare_fusion.10, pred[4,16]{1,0:T(4,128)(4,1)S(1)} %iota_compare_fusion.18), kind=kLoop, calls=%fused_computation.124 | loop fusion | flops 1024 | bytes 1344 | tf_op jit(solution)/shard_map/and | solution.py:245
  13.2 1.6 %divide_multiply_fusion = f32[344,1152]{1,0:T(8,128)S(1)} fusion(f32[16,1152]{1,0:T(8,128)S(1)} %mul.201, f32[344,16]{1,0:T(8,128)S(1)} %copy-done.54, f32[1152]{0:T(1024)S(1)} %copy-done.46), kind=kOutput, calls=%fused_computation.28 | convolution fusion | flops 78068736 | bytes 1685504 | tf_op jit(solution)/shard_map/dot_general | solution.py:78
  14.9 0.6 %fusion.28 = f32[2,2,128]{2,1,0:T(2,128)} fusion(f32[2,2,128]{2,1,0:T(2,128)S(1)} %copy-done.47), kind=kOutput, calls=%fused_computation.41 | output fusion | flops 769 | bytes 4096 | tf_op jit(solution)/shard_map/sub | solution.py:293
  15.5 2.6 %collective-permute-start.1 = (s32[4,256]{1,0:T(4,128)S(1)}, s32[4,256]{1,0:T(4,128)S(1)}, u32[]{:S(2)}, u32[]{:S(2)}) collective-permute-start(s32[4,256]{1,0:T(4,128)S(1)} %pad_add_fusion.7), channel_id=1, source_target_pairs={{0,2},{1,3},{2,0},{3,1},{4,6},{5,7},{6,4},{7,5},{8,10},{9,11},{10,... | collective-permute-start | bytes 12296 | tf_op jit(solution)/shard_map/ppermute | solution.py:103
  18.1 0.6 %convert_compare_fusion = pred[128,128]{1,0:T(8,128)(4,1)} fusion(), kind=kLoop, calls=%fused_computation.95 | loop fusion | flops 49152 | bytes 16384 | tf_op jit(solution)/shard_map/gt | solution.py:229
  18.7 1.0 %collective-permute-done.1 = s32[4,256]{1,0:T(4,128)S(1)} collective-permute-done((s32[4,256]{1,0:T(4,128)S(1)}, s32[4,256]{1,0:T(4,128)S(1)}, u32[]{:S(2)}, u32[]{:S(2)}) %collective-permute-start.1) | collective-permute-done | bytes 4128 | tf_op jit(solution)/shard_map/ppermute | solution.py:103
  19.7 2.1 %collective-permute-start.2 = (s32[4,512]{1,0:T(4,128)S(1)}, s32[4,512]{1,0:T(4,128)S(1)}, u32[]{:S(2)}, u32[]{:S(2)}) collective-permute-start(s32[4,512]{1,0:T(4,128)S(1)} %pad_add_fusion.5), channel_id=1, source_target_pairs={{0,4},{1,5},{2,6},{3,7},{4,0},{5,1},{6,2},{7,3},{8,12},{9,13},{10,... | collective-permute-start | bytes 24584 | tf_op jit(solution)/shard_map/ppermute | solution.py:103
  21.9 1.6 %collective-permute-done.2 = s32[4,512]{1,0:T(4,128)S(1)} collective-permute-done((s32[4,512]{1,0:T(4,128)S(1)}, s32[4,512]{1,0:T(4,128)S(1)}, u32[]{:S(2)}, u32[]{:S(2)}) %collective-permute-start.2) | collective-permute-done | bytes 8224 | tf_op jit(solution)/shard_map/ppermute | solution.py:103
  23.6 3.1 %collective-permute-start.3 = (s32[4,1024]{1,0:T(4,128)S(1)}, s32[4,1024]{1,0:T(4,128)S(1)}, u32[]{:S(2)}, u32[]{:S(2)}) collective-permute-start(s32[4,1024]{1,0:T(4,128)S(1)} %pad_add_fusion.3), channel_id=1, source_target_pairs={{0,8},{1,9},{2,10},{3,11},{4,12},{5,13},{6,14},{7,15},{8,0},{9,1},... | collective-permute-start | bytes 49160 | tf_op jit(solution)/shard_map/ppermute | solution.py:103
  26.8 0.7 %slice.182 = f32[344,64]{1,0:T(8,128)} slice(f32[344,1152]{1,0:T(8,128)S(1)} %divide_multiply_fusion), slice={[0:344], [1024:1088]} | slice | bytes 176128 | tf_op jit(solution)/shard_map/slice | solution.py:180
  27.5 1.2 %copy.33 = bf16[344,1024]{0,1:T(8,128)(2,1)} copy(bf16[344,1024]{1,0:T(8,128)(2,1)S(1)} %slice.227) | data formatting | bytes 1409024 | tf_op jit(solution)/shard_map/slice | solution.py:179
  28.7 1.7 %copy.32 = f32[344,64]{0,1:T(8,128)} copy(f32[344,64]{1,0:T(8,128)} %slice.182) | data formatting | bytes 176128 | tf_op jit(solution)/shard_map/slice | solution.py:180
  30.3 0.7 %mul.226 = f32[16,64]{1,0:T(8,128)} reshape(f32[1024]{0:T(1024)S(1)} %copy-done.38) | data formatting | bytes 8192 | tf_op jit(solution)/shard_map/mul | solution.py:23
  31.3 0.3 copy-done.6
  31.7 2.1 %convolution_convert_fusion.1 = bf16[4,128,1024]{2,1,0:T(8,128)(2,1)S(1)} fusion(s32[4,128]{1,0:T(4,128)S(1)} %pad_add_fusion.9, f32[344,1152]{1,0:T(8,128)} %copy-done.1), kind=kOutput, calls=%fused_computation.30 | convolution fusion | flops 361410560 | bytes 1755136 | tf_op jit(solution)/shard_map/rtg,gc->rtc/dot_general | solution.py:206
  33.8 1.3 %fusion.36 = f32[4,128,128]{1,2,0:T(8,128)S(1)} fusion(s32[4,128]{1,0:T(4,128)S(1)} %pad_add_fusion.9, f32[344,1152]{1,0:T(8,128)} %copy-done.1), kind=kOutput, calls=%fused_computation.54 | convolution fusion | flops 270708736 | bytes 440320 | tf_op jit(solution)/shard_map/rtg,gc->rtc/dot_general | solution.py:209
  35.2 0.7 %fusion.122 = s32[1,4,16,128]{3,1,2,0:T(4,128)} fusion(s32[4,2048]{1,0:T(4,128)S(1)} %pad_add_fusion.1, pred[2048]{0:T(1024)(128)(4,1)S(1)} %copy-done.18, pred[2048]{0:T(1024)(128)(4,1)S(1)} %copy-done.20, pred[2048]{0:T(1024)(128)(4,1)S(1)} %copy-done.22, pred[2048]{0:T(1024)(128)(4,1)S(1)} %copy-done.24), kind=kLoop, calls=%fused_computation.202 | loop fusion | flops 106496 | bytes 73728
  35.9 0.7 %copy.30 = bf16[4,128,1024]{1,2,0:T(8,128)(2,1)S(1)} copy(bf16[4,128,1024]{2,1,0:T(8,128)(2,1)S(1)} %convolution_convert_fusion.1) | data formatting | bytes 2097152 | tf_op jit(solution)/shard_map/convert_element_type | solution.py:206
  36.7 0.4 fusion.63
  37.0 0.7 %bitcast_dynamic-update-slice_fusion.1 = s32[4,16,128]{2,1,0:T(8,128)S(1)} fusion(s32[1,2,16,128]{3,1,2,0:T(2,128)} %bitcast.106), kind=kLoop, calls=%fused_computation.113 | loop fusion | bytes 32768
  37.8 1.6 %fusion.41 = f32[4,16,16,128]{3,2,1,0:T(8,128)S(1)} fusion(f32[16]{0:T(128)} %param.26, f32[16]{0:T(128)} %copy-done.32, f32[16]{0:T(128)} %copy-done.34, f32[16]{0:T(128)} %copy-done.36, f32[16]{0:T(128)} %copy-done.30, f32[16]{0:T(128)} %copy-done.55, pred[4,16,128]{2,1,0:T(8,128)(4,1)S(1)} %get-tuple-element.7, ...), kind=kOutput, calls=%fused_computation.64 | convolution fusion | flops 203309056 | bytes 557440 | tf_op jit(solution)/shard_map/...s,st->...t/dot_general | solution.py:143
  39.4 0.4 slice_reduce_fusion
  40.1 0.6 %multiply_convert_fusion.5 = bf16[4,16,16,128]{3,2,1,0:T(8,128)(2,1)S(1)} fusion(f32[4,16,16,128]{3,2,1,0:T(8,128)S(1)} %fusion.41, f32[4,16,16]{2,1,0:T(8,128)S(1)} %exponential_select_fusion, f32[4,16,16]{2,1,0:T(8,128)S(1)} %slice_reduce_fusion, f32[16]{0:T(128)S(1)} %copy-done.40, f32[16]{0:T(128)S(1)} %copy-done.33, f32[16]{0:T(128)S(1)} %copy-done.35, ...), kind=kLoop, calls=%fused_computation.62 | loop fusion | flops 2359296 | bytes 827712 | tf_op jit(solution)/shard_map/convert_element_type | solution.py:254
  40.8 1.9 %fusion.26 = f32[4,16,344]{2,1,0:T(8,128)S(1)} fusion(s32[4,16,128]{2,1,0:T(8,128)S(1)} %bitcast.107, bf16[4,16,16,128]{3,2,1,0:T(8,128)(2,1)S(1)} %multiply_convert_fusion.5), kind=kOutput, calls=%fused_computation.38 | convolution fusion | flops 92995584 | bytes 382976 | tf_op jit(solution)/shard_map/uhbs,ubsg->uhg/dot_general | solution.py:252
  42.7 1.0 %fusion.4 = f32[16,4,64,64]{3,2,0,1:T(8,128)S(1)} fusion(bf16[16,344,64,1]{1,2,0,3:T(8,128)(2,1)S(1)} %bitcast.104, f32[344,64]{0,1:T(8,128)S(1)} %copy-done.8, f32[4,16,344]{2,1,0:T(8,128)S(1)} %fusion.26), kind=kOutput, calls=%fused_computation.7 | convolution fusion | flops 183173120 | bytes 1929216 | tf_op jit(solution)/shard_map/hgp,uhgn->uhpn/dot_general | solution.py:259
  43.8 1.6 %fusion.9 = f32[4,16,64,128]{3,2,1,0:T(8,128)S(1)} fusion(bf16[4,128,16,64]{1,3,2,0:T(8,128)(2,1)S(1)} %bitcast.102, f32[4,16,128]{2,1,0:T(8,128)S(1)} %copy-done.13, f32[4,16,128]{2,1,0:T(8,128)S(1)} %copy-done.15, f32[4,128,128]{2,1,0:T(8,128)S(1)} %fusion.63, pred[128,128]{1,0:T(8,128)(4,1)S(1)} %copy-done.25), kind=kOutput, calls=%fused_computation.14 | convolution fusion | flops 140509184 | bytes 3489792 | tf_op jit(solution)/shard_map/uhts,ushp->uthp/dot_general | solution.py:232
  45.4 2.8 %multiply_reduce_fusion = (f32[4,128,16]{1,2,0:T(8,128)S(1)}, f32[4,128,16,64]{1,3,2,0:T(8,128)S(1)}) fusion(f32[4,128,16,64]{1,3,2,0:T(8,128)S(1)} %bitcast.101, bf16[4,128,16,64]{1,3,2,0:T(8,128)(2,1)S(1)} %bitcast.103, f32[16]{0:T(128)S(1)} %copy-done.52, f32[4,128,16]{1,2,0:T(8,128)S(1)} %copy-done.16, f32[16,4,64,64]{3,2,0,1:T(8,128)S(1)} %fusion.4, ...), kind=kOutput, calls=%fused_computation.21 | convolution fusion | flops 207609856 | bytes 9634304 | tf_op jit(solution)/shard_map/utn,uhpn->uthp/dot_general | solution.py:262
  48.3 0.5 multiply_convert_fusion.4
  48.8 0.7 %copy-done.4 = bf16[1024,512]{1,0:T(8,128)(2,1)S(1)} copy-done((bf16[1024,512]{1,0:T(8,128)(2,1)S(1)}, bf16[1024,512]{1,0:T(8,128)(2,1)}, u32[]{:S(2)}) %copy-start.4) | copy-done | bytes 1048600
  49.5 0.7 %convolution_convert_fusion.2 = bf16[4,128,512]{2,1,0:T(8,128)(2,1)S(1)} fusion(bf16[4,128,1024]{1,2,0:T(8,128)(2,1)S(1)} %bitcast.100, bf16[1024,512]{1,0:T(8,128)(2,1)S(1)} %copy-done.4), kind=kOutput, calls=%fused_computation.32 | convolution fusion | flops 537133056 | bytes 2621440 | tf_op jit(solution)/shard_map/gre,ed->grd/dot_general | solution.py:272
  50.2 0.9 %rev.3 = bf16[2,128,512]{2,1,0:T(8,128)(2,1)S(1)} reverse(bf16[2,128,512]{2,1,0:T(8,128)(2,1)S(1)} %slice.184), dimensions={1,2} | reverse | bytes 524288 | tf_op jit(solution)/shard_map/rev | solution.py:279
  51.2 0.4 fusion.38
  51.6 0.2 fusion.47
  52.0 0.6 %multiply_reduce_fusion.1 = f32[2,128]{1,0:T(2,128)} fusion(f32[2,2,128]{2,1,0:T(2,128)S(1)} %select_reduce_fusion.1, f32[2,2,128]{2,1,0:T(2,128)S(1)} %copy-done.56), kind=kOutput, calls=%fused_computation.165 | output fusion | flops 2049 | bytes 5120 | tf_op jit(solution)/shard_map/reduce_sum | solution.py:294
  (154 shorter events, 1.4 us)
Async XLA Ops:
  0.6 4.6 %copy-start = (bf16[512,1152]{1,0:T(8,128)(2,1)S(1)}, bf16[512,1152]{1,0:T(8,128)(2,1)}, u32[]{:S(2)}) copy-start(bf16[512,1152]{1,0:T(8,128)(2,1)} %param.21) | copy-start | bytes 3538948
  0.6 9.1 %copy-start.27 = (f32[512]{0:T(512)S(1)}, f32[512]{0:T(512)}, u32[]{:S(2)}) copy-start(f32[512]{0:T(512)} %param.20) | copy-start | bytes 6148
  0.7 7.3 %copy-start.51 = (f32[16]{0:T(128)S(1)}, f32[16]{0:T(128)}, u32[]{:S(2)}) copy-start(f32[16]{0:T(128)} %param.27) | copy-start | bytes 196
  0.7 7.3 %copy-start.39 = (f32[16]{0:T(128)S(1)}, f32[16]{0:T(128)}, u32[]{:S(2)}) copy-start(f32[16]{0:T(128)} %param.26) | copy-start | bytes 196
  0.7 9.0 %copy-start.3 = (bf16[512,1024]{1,0:T(8,128)(2,1)S(1)}, bf16[512,1024]{1,0:T(8,128)(2,1)}, u32[]{:S(2)}) copy-start(bf16[512,1024]{1,0:T(8,128)(2,1)} %param.22) | copy-start | bytes 3145732
  2.3 9.4 %copy-start.28 = (s32[4,128]{1,0:T(4,128)}, s32[4,128]{1,0:T(4,128)S(1)}, u32[]{:S(2)}) copy-start(s32[4,128]{1,0:T(4,128)S(1)} %pad_add_fusion.8) | copy-start | bytes 6148
  2.3 13.1 %collective-permute-start = (s32[4,128]{1,0:T(4,128)S(1)}, s32[4,128]{1,0:T(4,128)S(1)}, u32[]{:S(2)}, u32[]{:S(2)}) collective-permute-start(s32[4,128]{1,0:T(4,128)S(1)} %pad_add_fusion.8), channel_id=1, source_target_pairs={{0,1},{1,0},{2,3},{3,2},{4,5},{5,4},{6,7},{7,6},{8,9},{9,8},{10,11... | collective-permute-start | bytes 6152 | tf_op jit(solution)/shard_map/ppermute | solution.py:103
  5.2 6.6 %copy-start.9 = (bf16[4,512]{1,0:T(4,128)(2,1)}, bf16[4,512]{1,0:T(4,128)(2,1)S(1)}, u32[]{:S(2)}) copy-start(bf16[4,512]{1,0:T(4,128)(2,1)S(1)} %get-tuple-element.3) | copy-start | bytes 12292
  6.2 5.6 %copy-start.49 = (bf16[512,2]{0,1:T(2,128)(2,1)S(1)}, bf16[512,2]{0,1:T(2,128)(2,1)}, u32[]{:S(2)}) copy-start(bf16[512,2]{0,1:T(2,128)(2,1)} %param.32) | copy-start | bytes 6148
  7.9 5.3 %copy-start.46 = (f32[1152]{0:T(1024)S(1)}, f32[1152]{0:T(1024)}, u32[]{:S(2)}) copy-start(f32[1152]{0:T(1024)} %param.25) | copy-start | bytes 13828
  7.9 5.3 %copy-start.54 = (f32[344,16]{1,0:T(8,128)S(1)}, f32[344,16]{1,0:T(8,128)}, u32[]{:S(2)}) copy-start(f32[344,16]{1,0:T(8,128)} %constant.138.clone) | copy-start | bytes 66052
  7.9 4.6 %copy-start.30 = (f32[16]{0:T(128)}, f32[16]{0:T(128)S(1)}, u32[]{:S(2)}) copy-start(f32[16]{0:T(128)S(1)} %get-tuple-element.32) | copy-start | bytes 196
  7.9 4.6 %copy-start.32 = (f32[16]{0:T(128)}, f32[16]{0:T(128)S(1)}, u32[]{:S(2)}) copy-start(f32[16]{0:T(128)S(1)} %get-tuple-element.33) | copy-start | bytes 196
  8.0 4.6 %copy-start.34 = (f32[16]{0:T(128)}, f32[16]{0:T(128)S(1)}, u32[]{:S(2)}) copy-start(f32[16]{0:T(128)S(1)} %get-tuple-element.34) | copy-start | bytes 196
  8.0 4.6 %copy-start.36 = (f32[16]{0:T(128)}, f32[16]{0:T(128)S(1)}, u32[]{:S(2)}) copy-start(f32[16]{0:T(128)S(1)} %get-tuple-element.35) | copy-start | bytes 196
  9.0 3.6 %copy-start.14 = (f32[4,16,128]{2,1,0:T(8,128)}, f32[4,16,128]{2,1,0:T(8,128)S(1)}, u32[]{:S(2)}) copy-start(f32[4,16,128]{2,1,0:T(8,128)S(1)} %fusion.70) | copy-start | bytes 98308
  9.1 3.5 %copy-start.41 = (pred[4,16]{1,0:T(4,128)(4,1)}, pred[4,16]{1,0:T(4,128)(4,1)S(1)}, u32[]{:S(2)}) copy-start(pred[4,16]{1,0:T(4,128)(4,1)S(1)} %iota_compare_fusion.18) | copy-start | bytes 196
  13.2 2.3 %copy-start.26 = (s32[2,128]{1,0:T(2,128)S(1)}, s32[2,128]{1,0:T(2,128)}, u32[]{:S(2)}) copy-start(s32[2,128]{1,0:T(2,128)} %param.18) | copy-start | bytes 3076
  14.8 16.2 %copy-start.1 = (f32[344,1152]{1,0:T(8,128)}, f32[344,1152]{1,0:T(8,128)S(1)}, u32[]{:S(2)}) copy-start(f32[344,1152]{1,0:T(8,128)S(1)} %divide_multiply_fusion) | copy-start | bytes 4755460
  14.8 15.5 %copy-start.38 = (f32[1024]{0:T(1024)S(1)}, f32[1024]{0:T(1024)}, u32[]{:S(2)}) copy-start(f32[1024]{0:T(1024)} %param.29) | copy-start | bytes 12292
  15.5 4.2 %collective-permute-start.1 = (s32[4,256]{1,0:T(4,128)S(1)}, s32[4,256]{1,0:T(4,128)S(1)}, u32[]{:S(2)}, u32[]{:S(2)}) collective-permute-start(s32[4,256]{1,0:T(4,128)S(1)} %pad_add_fusion.7), channel_id=1, source_target_pairs={{0,2},{1,3},{2,0},{3,1},{4,6},{5,7},{6,4},{7,5},{8,10},{9,11},{10,... | collective-permute-start | bytes 12296 | tf_op jit(solution)/shard_map/ppermute | solution.py:103
  19.7 3.8 %collective-permute-start.2 = (s32[4,512]{1,0:T(4,128)S(1)}, s32[4,512]{1,0:T(4,128)S(1)}, u32[]{:S(2)}, u32[]{:S(2)}) collective-permute-start(s32[4,512]{1,0:T(4,128)S(1)} %pad_add_fusion.5), channel_id=1, source_target_pairs={{0,4},{1,5},{2,6},{3,7},{4,0},{5,1},{6,2},{7,3},{8,12},{9,13},{10,... | collective-permute-start | bytes 24584 | tf_op jit(solution)/shard_map/ppermute | solution.py:103
  21.9 9.4 %copy-start.17 = (pred[2048]{0:T(1024)(128)(4,1)}, pred[2048]{0:T(1024)(128)(4,1)S(1)}, u32[]{:S(2)}) copy-start(pred[2048]{0:T(1024)(128)(4,1)S(1)} %get-tuple-element.42) | copy-start | bytes 6148
  21.9 9.4 %copy-start.19 = (pred[2048]{0:T(1024)(128)(4,1)}, pred[2048]{0:T(1024)(128)(4,1)S(1)}, u32[]{:S(2)}) copy-start(pred[2048]{0:T(1024)(128)(4,1)S(1)} %get-tuple-element.43) | copy-start | bytes 6148
  23.6 7.4 %collective-permute-start.3 = (s32[4,1024]{1,0:T(4,128)S(1)}, s32[4,1024]{1,0:T(4,128)S(1)}, u32[]{:S(2)}, u32[]{:S(2)}) collective-permute-start(s32[4,1024]{1,0:T(4,128)S(1)} %pad_add_fusion.3), channel_id=1, source_target_pairs={{0,8},{1,9},{2,10},{3,11},{4,12},{5,13},{6,14},{7,15},{8,0},{9,1},... | collective-permute-start | bytes 49160 | tf_op jit(solution)/shard_map/ppermute | solution.py:103
  26.7 4.7 %copy-start.21 = (pred[2048]{0:T(1024)(128)(4,1)}, pred[2048]{0:T(1024)(128)(4,1)S(1)}, u32[]{:S(2)}) copy-start(pred[2048]{0:T(1024)(128)(4,1)S(1)} %get-tuple-element.44) | copy-start | bytes 6148
  26.7 4.7 %copy-start.23 = (pred[2048]{0:T(1024)(128)(4,1)}, pred[2048]{0:T(1024)(128)(4,1)S(1)}, u32[]{:S(2)}) copy-start(pred[2048]{0:T(1024)(128)(4,1)S(1)} %get-tuple-element.45) | copy-start | bytes 6148
  31.3 3.9 %copy-start.18 = (pred[2048]{0:T(1024)(128)(4,1)S(1)}, pred[2048]{0:T(1024)(128)(4,1)}, u32[]{:S(2)}) copy-start(pred[2048]{0:T(1024)(128)(4,1)} %copy-done.17) | copy-start | bytes 6148
  31.3 3.9 %copy-start.20 = (pred[2048]{0:T(1024)(128)(4,1)S(1)}, pred[2048]{0:T(1024)(128)(4,1)}, u32[]{:S(2)}) copy-start(pred[2048]{0:T(1024)(128)(4,1)} %copy-done.19) | copy-start | bytes 6148
  31.6 3.5 %copy-start.22 = (pred[2048]{0:T(1024)(128)(4,1)S(1)}, pred[2048]{0:T(1024)(128)(4,1)}, u32[]{:S(2)}) copy-start(pred[2048]{0:T(1024)(128)(4,1)} %copy-done.21) | copy-start | bytes 6148
  31.6 3.5 %copy-start.24 = (pred[2048]{0:T(1024)(128)(4,1)S(1)}, pred[2048]{0:T(1024)(128)(4,1)}, u32[]{:S(2)}) copy-start(pred[2048]{0:T(1024)(128)(4,1)} %copy-done.23) | copy-start | bytes 6148
  36.6 3.2 %copy-start.12 = (pred[4,16,16]{2,1,0:T(8,128)(4,1)S(1)}, pred[4,16,16]{2,1,0:T(8,128)(4,1)}, u32[]{:S(2)}) copy-start(pred[4,16,16]{2,1,0:T(8,128)(4,1)} %broadcast_and_fusion) | copy-start | bytes 3076
  36.6 3.5 %copy-start.42 = (pred[4,16]{1,0:T(4,128)(4,1)S(1)}, pred[4,16]{1,0:T(4,128)(4,1)}, u32[]{:S(2)}) copy-start(pred[4,16]{1,0:T(4,128)(4,1)} %copy-done.41) | copy-start | bytes 196
  36.6 3.5 %copy-start.31 = (f32[16]{0:T(128)S(1)}, f32[16]{0:T(128)}, u32[]{:S(2)}) copy-start(f32[16]{0:T(128)} %copy-done.30) | copy-start | bytes 196
  36.6 3.5 %copy-start.33 = (f32[16]{0:T(128)S(1)}, f32[16]{0:T(128)}, u32[]{:S(2)}) copy-start(f32[16]{0:T(128)} %copy-done.32) | copy-start | bytes 196
  36.6 3.5 %copy-start.35 = (f32[16]{0:T(128)S(1)}, f32[16]{0:T(128)}, u32[]{:S(2)}) copy-start(f32[16]{0:T(128)} %copy-done.34) | copy-start | bytes 196
  36.6 3.5 %copy-start.37 = (f32[16]{0:T(128)S(1)}, f32[16]{0:T(128)}, u32[]{:S(2)}) copy-start(f32[16]{0:T(128)} %copy-done.36) | copy-start | bytes 196
  36.6 3.5 %copy-start.40 = (f32[16]{0:T(128)S(1)}, f32[16]{0:T(128)}, u32[]{:S(2)}) copy-start(f32[16]{0:T(128)} %param.26) | copy-start | bytes 196
  37.8 3.0 %copy-start.7 = (s32[1,4,16,128]{3,1,2,0:T(4,128)S(1)}, s32[1,4,16,128]{3,1,2,0:T(4,128)}, u32[]{:S(2)}) copy-start(s32[1,4,16,128]{3,1,2,0:T(4,128)} %fusion.122) | copy-start | bytes 98308
  40.1 2.6 %copy-start.5 = (bf16[344,1024]{0,1:T(8,128)(2,1)S(1)}, bf16[344,1024]{0,1:T(8,128)(2,1)}, u32[]{:S(2)}) copy-start(bf16[344,1024]{0,1:T(8,128)(2,1)} %copy.33) | copy-start | bytes 2113540
  40.1 2.6 %copy-start.8 = (f32[344,64]{0,1:T(8,128)S(1)}, f32[344,64]{0,1:T(8,128)}, u32[]{:S(2)}) copy-start(f32[344,64]{0,1:T(8,128)} %copy.32) | copy-start | bytes 264196
  45.4 2.8 %copy-start.11 = (f32[16,64]{1,0:T(8,128)S(1)}, f32[16,64]{1,0:T(8,128)}, u32[]{:S(2)}) copy-start(f32[16,64]{1,0:T(8,128)} %mul.226) | copy-start | bytes 12292
  48.7 2.4 %copy-start.10 = (bf16[4,512]{1,0:T(4,128)(2,1)S(1)}, bf16[4,512]{1,0:T(4,128)(2,1)}, u32[]{:S(2)}) copy-start(bf16[4,512]{1,0:T(4,128)(2,1)} %copy-done.9) | copy-start | bytes 12292
  48.8 2.4 %copy-start.29 = (s32[4,128]{1,0:T(4,128)S(1)}, s32[4,128]{1,0:T(4,128)}, u32[]{:S(2)}) copy-start(s32[4,128]{1,0:T(4,128)} %copy-done.28) | copy-start | bytes 6148
  49.5 2.2 %copy-start.48 = (f32[512]{0:T(512)S(1)}, f32[512]{0:T(512)}, u32[]{:S(2)}) copy-start(f32[512]{0:T(512)} %param.31) | copy-start | bytes 6148
  49.5 2.2 %copy-start.50 = (bf16[512,2]{0,1:T(2,128)(2,1)S(1)}, bf16[512,2]{0,1:T(2,128)(2,1)}, u32[]{:S(2)}) copy-start(bf16[512,2]{0,1:T(2,128)(2,1)} %param.32) | copy-start | bytes 6148
  49.5 2.5 %copy-start.43 = (s32[2,2,128]{2,1,0:T(2,128)S(1)}, s32[2,2,128]{2,1,0:T(2,128)}, u32[]{:S(2)}) copy-start(s32[2,2,128]{2,1,0:T(2,128)} %param.33) | copy-start | bytes 6148
  49.5 2.5 %copy-start.56 = (f32[2,2,128]{2,1,0:T(2,128)S(1)}, f32[2,2,128]{2,1,0:T(2,128)}, u32[]{:S(2)}) copy-start(f32[2,2,128]{2,1,0:T(2,128)} %fusion.28) | copy-start | bytes 6148
  (13 other events, 17.8 us)

commit v11 on v9

--- a/solution.py
+++ b/solution.py
@@ -208,7 +208,8 @@
     )
     bc_loc = jnp.einsum("rtg,gc->rtc", oh_loc, bc_tab, precision=HIGH)
     oh_tok = onehot(local_tok, BASES)
-    z_loc = jnp.einsum("rtk,kc->rtc", oh_tok, z_rows, preferred_element_type=jnp.float32)
+    gate_rows = jax.nn.silu(z_rows.astype(jnp.float32))
+    gate_loc = jnp.einsum("rtk,kc->rtc", oh_tok, gate_rows, precision=HIGH)
     dt_loc = jax.nn.softplus(heads_lookup(dt_rows, local_tok) + dt_bias[:, None])
     ld_loc = neg_rate * dt_loc
 
@@ -265,8 +266,7 @@
         * jnp.exp(cum_u).transpose(0, 2, 1)[..., None]
     )
     y_u = y_intra + y_inter + d_skip[:, None] * x_u.astype(jnp.float32)
-    z_u = per_unit(z_loc, 1).reshape(units, BLK, HEADS, HD)
-    gated_y = y_u * jax.nn.silu(z_u)
+    gated_y = y_u * per_unit(gate_loc, 1).reshape(units, BLK, HEADS, HD)
     normed = rms_gain(gated_y, inner_gain.reshape(HEADS, HD)).astype(jnp.bfloat16)
     normed = jnp.moveaxis(normed.reshape(streams, nloc, BLK, INNER), 1, 1).reshape(
         streams, count, INNER

time: 53.5 us -> 58.2 us (1.088)
  local copies, waits for them, and re-layouts: 9.54 us -> 13.4 us
  other arithmetic: 8.72 us -> 9.36 us
    slice x2, local copies, waits for them, and re-layouts: 1.27 us -> 4.61 us  [local(): x_tab = act_tab[:, :INNER].astype(jnp.bfloat16)]
    convert_element_type x1, local copies, waits for them, and re-layouts: 0.65 us -> 2.28 us  [local(): jnp.einsum('rtg,gc->rtc', oh_loc, x_tab, preferred_element_type=jnp.float32)]
    slice x2 -> x3, local copies, waits for them, and re-layouts: 2.36 us -> 0.76 us  [local(): b_tab = act_tab[:, INNER:INNER + NS]]
    dot_general x1, matrix products: 1.6 us -> 2.78 us  [gram_tables(): jnp.dot(jnp.asarray(gram_layout()), taps, precision=HIGH)]
    dot_general x1, matrix products: 2.11 us -> 3.1 us  [local(): jnp.einsum('rtg,gc->rtc', oh_loc, x_tab, preferred_element_type=jnp.float32)]
    dot_general x1, matrix products: 1.35 us -> 0.43 us  [local(): bc_loc = jnp.einsum('rtg,gc->rtc', oh_loc, bc_tab, precision=HIGH)]
    dot_general x1 -> x2, matrix products: 2.04 us -> 1.33 us  [the longest x1 1.05 us: local(): gate_loc = jnp.einsum('rtk,kc->rtc', oh_tok, gate_rows, precision=HIGH)]
    unnamed x1, other arithmetic: 0.74 us -> 1.4 us
  transfers between devices with their start and end apart: 4 -> 4, of which waited for: 2 -> 2; matrix products, arithmetic and copies ran while one was open for 33% -> 34% of each run, Pallas kernels for 0% -> 0%
where the time goes in v11:
time: 58.2 us; the launch traced here: 57.5 us
  matrix products  22.3 us (38%)
  local copies, waits for them, and re-layouts  13.4 us (23%)
  other arithmetic  9.36 us (16%)
  starting transfers between devices  8.29 us (14%)
  waiting for transfers between devices  2.56 us (4%)
  between operations  1.59 us (3%)
    ppermute x4, starting transfers between devices, gather_all(): lax.ppermute(held, axis, [(src, src ^ mask) for src in range(count)])  8.29 us
    slice x2, local copies, waits for them, and re-layouts, local(): x_tab = act_tab[:, :INNER].astype(jnp.bfloat16)  4.61 us
    dot_general x1, matrix products, local(): jnp.einsum('rtg,gc->rtc', oh_loc, x_tab, preferred_element_type=jnp.float32)  3.1 us
    dot_general x1, matrix products, gram_tables(): jnp.dot(jnp.asarray(gram_layout()), taps, precision=HIGH)  2.78 us
    ppermute x4, waiting for transfers between devices, gather_all(): lax.ppermute(held, axis, [(src, src ^ mask) for src in range(count)])  2.56 us
    unnamed x112, local copies, waits for them, and re-layouts  2.46 us
    dot_general x1, matrix products, local(): jnp.einsum('utn,uhpn->uthp', c_u, start_state, precision=lax.Precision.HIGH)  2.45 us
    convert_element_type x1, local copies, waits for them, and re-layouts, local(): jnp.einsum('rtg,gc->rtc', oh_loc, x_tab, preferred_element_type=jnp.float32)  2.28 us
  transfers between devices with their start and end apart: 4, of which 2 were waited for; matrix products, arithmetic and copies ran while one was open for 34% of the time, Pallas kernels for 0%

profile of v11, /device:TPU:0, one launch (start us, length us, event | category | flops | bytes accessed | tf_op | source)
XLA Modules:
  0.0 57.5 jit_solution(5568632028454362901)
XLA Ops:
  0.7 1.0 %fusion.33 = s32[2,128]{1,0:T(2,128)S(1)} fusion(s32[2,128]{1,0:T(2,128)} %param.18), kind=kOutput, calls=%fused_computation.49 | convolution fusion | flops 99072 | bytes 2048 | tf_op jit(solution)/shard_map/dot_general | solution.py:186
  1.7 0.7 %pad_add_fusion.8 = s32[4,128]{1,0:T(4,128)S(1)} fusion(s32[2,128]{1,0:T(2,128)S(1)} %fusion.33, s32[2,128]{1,0:T(2,128)} %param.18), kind=kLoop, calls=%fused_computation.171 | loop fusion | flops 512 | bytes 4096 | tf_op jit(solution)/shard_map/concatenate | solution.py:189
  2.3 0.5 collective-permute-start
  2.8 0.7 %broadcast_compare_fusion.7 = (pred[4,128]{1,0:T(4,128)(4,1)S(1)}, pred[4,128]{1,0:T(4,128)(4,1)S(1)}, pred[4,128]{1,0:T(4,128)(4,1)S(1)}, pred[4,128]{1,0:T(4,128)(4,1)S(1)}) fusion(s32[2,128]{1,0:T(2,128)S(1)} %fusion.33, s32[2,128]{1,0:T(2,128)} %param.18), kind=kLoop, calls=%fused_computation.185 | loop fusion | flops 2560 | bytes 4096 | tf_op jit(solution)/shard_map/eq | solution.py:122
  3.5 0.9 %fusion.29 = bf16[2,512]{1,0:T(2,128)(2,1)S(1)} fusion(bf16[2,512]{1,0:T(2,128)(2,1)} %param.19), kind=kOutput, calls=%fused_computation.44 | convolution fusion | flops 1573888 | bytes 4096 | tf_op jit(solution)/shard_map/dot_general | solution.py:176
  4.4 0.8 %fusion.80 = (f32[4]{0:T(128)S(1)}, bf16[4,512]{1,0:T(4,128)(2,1)S(1)}) fusion(bf16[1,512]{1,0:T(2,128)(2,1)S(1)} %get-tuple-element.39, bf16[1,512]{1,0:T(2,128)(2,1)S(1)} %get-tuple-element.38, bf16[2,512]{1,0:T(2,128)(2,1)} %param.19), kind=kLoop, calls=%fused_computation.134 | loop fusion | flops 18428 | bytes 8208 | tf_op jit(solution)/shard_map/reduce_sum | solution.py:23
  5.2 1.0 %fusion.8 = f32[4,1152]{1,0:T(4,128)S(1)} fusion(bf16[512,1152]{1,0:T(8,128)(2,1)S(1)} %copy-done, bf16[4,512]{1,0:T(4,128)(2,1)S(1)} %get-tuple-element.5, f32[512]{0:T(512)} %param.20, f32[4]{0:T(128)S(1)} %add_rsqrt_fusion.2), kind=kOutput, calls=%fused_computation.13 | convolution fusion | flops 4736000 | bytes 1204240 | tf_op jit(solution)/shard_map/dot_general | solution.py:74
  6.2 0.8 %broadcast_multiply_fusion = f32[4,4,1152]{2,1,0:T(4,128)S(1)} fusion(f32[4,1152]{1,0:T(4,128)S(1)} %fusion.8, f32[4,1152]{1,0:T(4,128)} %param.24), kind=kLoop, calls=%fused_computation.101 | loop fusion | flops 18432 | bytes 110592 | tf_op jit(solution)/shard_map/mul | solution.py:77
  7.0 0.9 %fusion.108 = f32[4,16]{1,0:T(4,128)S(1)} fusion(bf16[512,16]{0,1:T(8,128)(2,1)} %param.23, bf16[4,512]{1,0:T(4,128)(2,1)S(1)} %get-tuple-element.5, f32[512]{0:T(512)} %param.20, f32[4]{0:T(128)S(1)} %add_rsqrt_fusion.2), kind=kOutput, calls=%fused_computation.206 | convolution fusion | flops 73728 | bytes 22800 | tf_op jit(solution)/shard_map/dot_general | solution.py:76
  8.0 0.7 %compare_select_fusion.2 = f32[4,16,128]{2,1,0:T(8,128)} fusion(f32[16]{0:T(128)S(1)} %copy-done.37, f32[16]{0:T(128)S(1)} %get-tuple-element.35, f32[16]{0:T(128)S(1)} %get-tuple-element.36, f32[16]{0:T(128)S(1)} %get-tuple-element.37, f32[16]{0:T(128)S(1)} %get-tuple-element.34, pred[4,128]{1,0:T(4,128)(4,1)S(1)} %get-tuple-element.32, ...), kind=kLoop, calls=%fused_computation.93 | loop fusion | flops 114688 | bytes 35136 | tf_op jit(solution)/shard_map/jit(softplus)/select_n | solution.py:213
  9.1 0.6 %exponential_bitcast_fusion = f32[4,128,16]{1,2,0:T(8,128)} fusion(f32[4,16,128]{2,1,0:T(8,128)S(1)} %fusion.69), kind=kLoop, calls=%fused_computation.107 | loop fusion | bytes 65536 | tf_op jit(solution)/shard_map/exp | solution.py:266
  9.8 0.3 fusion.27
  10.1 1.1 %fusion.75 = f32[4,128,1024]{1,2,0:T(8,128)S(1)} fusion(f32[4,1024]{1,0:T(4,128)S(1)} %fusion.27, s32[4,128]{1,0:T(4,128)S(1)} %pad_add_fusion.8), kind=kOutput, calls=%fused_computation.122 | convolution fusion | flops 25184256 | bytes 2115584 | tf_op jit(solution)/shard_map/rtk,kc->rtc/dot_general | solution.py:212
  11.3 0.6 %fusion.112 = (bf16[512,1]{0,1:T(2,128)(2,1)}, bf16[512,1]{0,1:T(2,128)(2,1)}) fusion(bf16[512,2]{0,1:T(2,128)(2,1)S(1)} %convolution_convert_fusion.5), kind=kLoop, calls=%fused_computation.208 | loop fusion | bytes 4096 | tf_op jit(solution)/shard_map/slice | solution.py:291
  11.9 0.6 %broadcast_and_fusion = pred[4,16,16]{2,1,0:T(8,128)(4,1)} fusion(pred[16,16]{1,0:T(8,128)(4,1)S(1)} %iota_compare_fusion.10, pred[4,16]{1,0:T(4,128)(4,1)S(1)} %iota_compare_fusion.18), kind=kLoop, calls=%fused_computation.131 | loop fusion | flops 1024 | bytes 1344 | tf_op jit(solution)/shard_map/and | solution.py:246
  12.6 2.8 %divide_multiply_fusion = f32[344,1152]{1,0:T(8,128)} fusion(f32[16,1152]{1,0:T(8,128)S(1)} %mul.201, f32[344,16]{1,0:T(8,128)S(1)} %copy-done.52, f32[1152]{0:T(1024)S(1)} %copy-done.45), kind=kOutput, calls=%fused_computation.28 | convolution fusion | flops 78068736 | bytes 1685504 | tf_op jit(solution)/shard_map/dot_general | solution.py:78
  15.4 0.6 %fusion.28 = f32[2,2,128]{2,1,0:T(2,128)} fusion(f32[2,2,128]{2,1,0:T(2,128)S(1)} %copy-done.46), kind=kOutput, calls=%fused_computation.41 | output fusion | flops 769 | bytes 4096 | tf_op jit(solution)/shard_map/sub | solution.py:295
  16.0 2.6 %collective-permute-start.1 = (s32[4,256]{1,0:T(4,128)S(1)}, s32[4,256]{1,0:T(4,128)S(1)}, u32[]{:S(2)}, u32[]{:S(2)}) collective-permute-start(s32[4,256]{1,0:T(4,128)S(1)} %pad_add_fusion.7), channel_id=1, source_target_pairs={{0,2},{1,3},{2,0},{3,1},{4,6},{5,7},{6,4},{7,5},{8,10},{9,11},{10,... | collective-permute-start | bytes 12296 | tf_op jit(solution)/shard_map/ppermute | solution.py:103
  18.6 0.6 %convert_compare_fusion = pred[128,128]{1,0:T(8,128)(4,1)} fusion(), kind=kLoop, calls=%fused_computation.97 | loop fusion | flops 49152 | bytes 16384 | tf_op jit(solution)/shard_map/gt | solution.py:230
  19.2 1.0 %collective-permute-done.1 = s32[4,256]{1,0:T(4,128)S(1)} collective-permute-done((s32[4,256]{1,0:T(4,128)S(1)}, s32[4,256]{1,0:T(4,128)S(1)}, u32[]{:S(2)}, u32[]{:S(2)}) %collective-permute-start.1) | collective-permute-done | bytes 4128 | tf_op jit(solution)/shard_map/ppermute | solution.py:103
  20.2 2.1 %collective-permute-start.2 = (s32[4,512]{1,0:T(4,128)S(1)}, s32[4,512]{1,0:T(4,128)S(1)}, u32[]{:S(2)}, u32[]{:S(2)}) collective-permute-start(s32[4,512]{1,0:T(4,128)S(1)} %pad_add_fusion.5), channel_id=1, source_target_pairs={{0,4},{1,5},{2,6},{3,7},{4,0},{5,1},{6,2},{7,3},{8,12},{9,13},{10,... | collective-permute-start | bytes 24584 | tf_op jit(solution)/shard_map/ppermute | solution.py:103
  22.4 1.6 %collective-permute-done.2 = s32[4,512]{1,0:T(4,128)S(1)} collective-permute-done((s32[4,512]{1,0:T(4,128)S(1)}, s32[4,512]{1,0:T(4,128)S(1)}, u32[]{:S(2)}, u32[]{:S(2)}) %collective-permute-start.2) | collective-permute-done | bytes 8224 | tf_op jit(solution)/shard_map/ppermute | solution.py:103
  24.0 3.1 %collective-permute-start.3 = (s32[4,1024]{1,0:T(4,128)S(1)}, s32[4,1024]{1,0:T(4,128)S(1)}, u32[]{:S(2)}, u32[]{:S(2)}) collective-permute-start(s32[4,1024]{1,0:T(4,128)S(1)} %pad_add_fusion.3), channel_id=1, source_target_pairs={{0,8},{1,9},{2,10},{3,11},{4,12},{5,13},{6,14},{7,15},{8,0},{9,1},... | collective-permute-start | bytes 49160 | tf_op jit(solution)/shard_map/ppermute | solution.py:103
  27.2 2.3 %slice.239 = bf16[344,1024]{1,0:T(8,128)(2,1)} slice(f32[344,1152]{1,0:T(8,128)} %divide_multiply_fusion), slice={[0:344], [0:1024]} | slice | bytes 1409024 | tf_op jit(solution)/shard_map/slice | solution.py:179
  29.5 2.3 %copy.35 = bf16[344,1024]{0,1:T(8,128)(2,1)} copy(bf16[344,1024]{1,0:T(8,128)(2,1)} %slice.239) | data formatting | bytes 1409024 | tf_op jit(solution)/shard_map/slice | solution.py:179
  31.8 0.8 %copy.34 = f32[344,64]{0,1:T(8,128)} copy(f32[344,64]{1,0:T(8,128)S(1)} %slice-done) | data formatting | bytes 176128 | tf_op jit(solution)/shard_map/slice | solution.py:180
  32.5 0.7 %mul.226 = f32[16,64]{1,0:T(8,128)} reshape(f32[1024]{0:T(1024)S(1)} %copy-done.36) | data formatting | bytes 8192 | tf_op jit(solution)/shard_map/mul | solution.py:23
  33.3 0.6 %copy-done.6 = s32[2,2048]{1,0:T(2,128)} copy-done((s32[2,2048]{1,0:T(2,128)}, s32[2,2048]{1,0:T(2,128)S(1)}, u32[]{:S(2)}) %copy-start.6) | copy-done | bytes 16408
  34.1 3.1 %convolution_convert_fusion.1 = bf16[4,128,1024]{2,1,0:T(8,128)(2,1)} fusion(s32[4,128]{1,0:T(4,128)S(1)} %pad_add_fusion.9, f32[344,1152]{1,0:T(8,128)} %divide_multiply_fusion), kind=kOutput, calls=%fused_computation.30 | convolution fusion | flops 361410560 | bytes 1755136 | tf_op jit(solution)/shard_map/rtg,gc->rtc/dot_general | solution.py:206
  37.2 0.4 fusion.36
  37.7 1.4 %fusion.126 = s32[1,4,16,128]{3,1,2,0:T(4,128)} fusion(s32[4,2048]{1,0:T(4,128)S(1)} %pad_add_fusion.1, pred[2048]{0:T(1024)(128)(4,1)S(1)} %copy-done.18, pred[2048]{0:T(1024)(128)(4,1)S(1)} %copy-done.20, pred[2048]{0:T(1024)(128)(4,1)} %copy-done.21, pred[2048]{0:T(1024)(128)(4,1)} %copy-done.22), kind=kLoop, calls=%fused_computation.211 | loop fusion | flops 106496 | bytes 73728
  39.1 2.3 %copy.32 = bf16[4,128,1024]{1,2,0:T(8,128)(2,1)} copy(bf16[4,128,1024]{2,1,0:T(8,128)(2,1)} %convolution_convert_fusion.1) | data formatting | bytes 2097152 | tf_op jit(solution)/shard_map/convert_element_type | solution.py:206
  41.4 0.4 fusion.62
  41.8 0.7 %bitcast_dynamic-update-slice_fusion.1 = s32[4,16,128]{2,1,0:T(8,128)S(1)} fusion(s32[1,2,16,128]{3,1,2,0:T(2,128)} %bitcast.105), kind=kLoop, calls=%fused_computation.116 | loop fusion | bytes 32768
  42.6 1.6 %fusion.41 = f32[4,16,16,128]{3,2,1,0:T(8,128)S(1)} fusion(f32[16]{0:T(128)} %param.26, f32[16]{0:T(128)} %copy-done.30, f32[16]{0:T(128)} %copy-done.32, f32[16]{0:T(128)} %copy-done.34, f32[16]{0:T(128)} %copy-done.28, f32[16]{0:T(128)} %copy-done.53, pred[4,16,128]{2,1,0:T(8,128)(4,1)S(1)} %get-tuple-element.9, ...), kind=kOutput, calls=%fused_computation.66 | convolution fusion | flops 203309056 | bytes 557440 | tf_op jit(solution)/shard_map/...s,st->...t/dot_general | solution.py:143
  44.2 0.4 slice_reduce_fusion
  44.9 0.7 %subtract_convert_fusion = (bf16[4,16,16,128]{3,2,1,0:T(8,128)(2,1)S(1)}, bf16[4,16,16,128]{3,2,1,0:T(8,128)(2,1)S(1)}) fusion(f32[4,16,16]{2,1,0:T(8,128)S(1)} %exponential_select_fusion, f32[16]{0:T(128)S(1)} %copy-done.38, f32[16]{0:T(128)S(1)} %copy-done.31, pred[4,16,128]{2,1,0:T(8,128)(4,1)S(1)} %get-tuple-element.9, f32[16]{0:T(128)S(1)} %copy-done.33, ...), kind=kLoop, calls=%fused_computation.63 | loop fusion | flops 2752512 | bytes 1089856 | tf_op jit(solution)/shard_map/convert_element_type | solution.py:139
  45.6 2.1 %fusion.26 = f32[4,32,344]{2,1,0:T(8,128)S(1)} fusion(s32[4,16,128]{2,1,0:T(8,128)S(1)} %bitcast.106, bf16[4,32,16,128]{3,2,1,0:T(8,128)(2,1)S(1)} %pad_maximum_fusion), kind=kOutput, calls=%fused_computation.38 | convolution fusion | flops 183173120 | bytes 733184 | tf_op jit(solution)/shard_map/uhbs,ubsg->uhg/dot_general | solution.py:254
  47.8 1.0 %fusion.4 = f32[16,4,64,64]{3,2,0,1:T(8,128)S(1)} fusion(bf16[16,344,64,1]{1,2,0,3:T(8,128)(2,1)S(1)} %bitcast.103, f32[344,64]{0,1:T(8,128)S(1)} %copy-done.9, f32[4,16,344]{2,1,0:T(8,128)S(1)} %slice_add_fusion), kind=kOutput, calls=%fused_computation.7 | convolution fusion | flops 183173120 | bytes 1929216 | tf_op jit(solution)/shard_map/hgp,uhgn->uhpn/dot_general | solution.py:262
  49.0 1.6 %fusion.9 = f32[4,16,64,128]{3,2,1,0:T(8,128)S(1)} fusion(bf16[4,128,16,64]{1,3,2,0:T(8,128)(2,1)S(1)} %bitcast.100, f32[4,16,128]{2,1,0:T(8,128)S(1)} %copy-done.14, f32[4,16,128]{2,1,0:T(8,128)S(1)} %copy-done.16, f32[4,128,128]{2,1,0:T(8,128)S(1)} %fusion.62, pred[128,128]{1,0:T(8,128)(4,1)S(1)} %copy-done.23), kind=kOutput, calls=%fused_computation.14 | convolution fusion | flops 140509184 | bytes 3489792 | tf_op jit(solution)/shard_map/uhts,ushp->uthp/dot_general | solution.py:233
  50.7 2.4 %multiply_reduce_fusion = (f32[4,128,16]{1,2,0:T(8,128)S(1)}, f32[4,128,16,64]{1,3,2,0:T(8,128)S(1)}) fusion(f32[4,128,16,64]{1,3,2,0:T(8,128)S(1)} %bitcast.99, bf16[4,128,16,64]{1,3,2,0:T(8,128)(2,1)S(1)} %bitcast.101, f32[16]{0:T(128)S(1)} %copy-done.44, f32[4,128,16]{1,2,0:T(8,128)S(1)} %copy-done.7, f32[16,4,64,64]{3,2,0,1:T(8,128)S(1)} %fusion.4, ...), kind=kOutput, calls=%fused_computation.21 | convolution fusion | flops 205512704 | bytes 9634304 | tf_op jit(solution)/shard_map/utn,uhpn->uthp/dot_general | solution.py:265
  53.2 0.5 multiply_convert_fusion.4
  53.7 0.7 %copy-done.4 = bf16[1024,512]{1,0:T(8,128)(2,1)S(1)} copy-done((bf16[1024,512]{1,0:T(8,128)(2,1)S(1)}, bf16[1024,512]{1,0:T(8,128)(2,1)}, u32[]{:S(2)}) %copy-start.4) | copy-done | bytes 1048600
  54.4 0.7 %convolution_convert_fusion.2 = bf16[4,128,512]{2,1,0:T(8,128)(2,1)S(1)} fusion(bf16[4,128,1024]{1,2,0:T(8,128)(2,1)S(1)} %bitcast.102, bf16[1024,512]{1,0:T(8,128)(2,1)S(1)} %copy-done.4), kind=kOutput, calls=%fused_computation.32 | convolution fusion | flops 537133056 | bytes 2621440 | tf_op jit(solution)/shard_map/gre,ed->grd/dot_general | solution.py:274
  55.2 0.9 %rev.3 = bf16[2,128,512]{2,1,0:T(8,128)(2,1)S(1)} reverse(bf16[2,128,512]{2,1,0:T(8,128)(2,1)S(1)} %slice.194), dimensions={1,2} | reverse | bytes 524288 | tf_op jit(solution)/shard_map/rev | solution.py:281
  56.1 0.4 fusion.37
  56.6 0.2 fusion.47
  56.9 0.6 %multiply_reduce_fusion.1 = f32[2,128]{1,0:T(2,128)} fusion(f32[2,2,128]{2,1,0:T(2,128)S(1)} %select_reduce_fusion.1, f32[2,2,128]{2,1,0:T(2,128)S(1)} %copy-done.54), kind=kOutput, calls=%fused_computation.173 | output fusion | flops 2049 | bytes 5120 | tf_op jit(solution)/shard_map/reduce_sum | solution.py:296
  (154 shorter events, 1.8 us)
Async XLA Ops:
  0.6 4.6 %copy-start = (bf16[512,1152]{1,0:T(8,128)(2,1)S(1)}, bf16[512,1152]{1,0:T(8,128)(2,1)}, u32[]{:S(2)}) copy-start(bf16[512,1152]{1,0:T(8,128)(2,1)} %param.21) | copy-start | bytes 3538948
  0.6 9.1 %copy-start.25 = (f32[512]{0:T(512)S(1)}, f32[512]{0:T(512)}, u32[]{:S(2)}) copy-start(f32[512]{0:T(512)} %param.20) | copy-start | bytes 6148
  0.7 7.3 %copy-start.50 = (f32[16]{0:T(128)S(1)}, f32[16]{0:T(128)}, u32[]{:S(2)}) copy-start(f32[16]{0:T(128)} %param.27) | copy-start | bytes 196
  0.7 7.3 %copy-start.37 = (f32[16]{0:T(128)S(1)}, f32[16]{0:T(128)}, u32[]{:S(2)}) copy-start(f32[16]{0:T(128)} %param.26) | copy-start | bytes 196
  0.7 9.1 %copy-start.3 = (bf16[512,1024]{1,0:T(8,128)(2,1)S(1)}, bf16[512,1024]{1,0:T(8,128)(2,1)}, u32[]{:S(2)}) copy-start(bf16[512,1024]{1,0:T(8,128)(2,1)} %param.22) | copy-start | bytes 3145732
  2.3 8.8 %copy-start.26 = (s32[4,128]{1,0:T(4,128)}, s32[4,128]{1,0:T(4,128)S(1)}, u32[]{:S(2)}) copy-start(s32[4,128]{1,0:T(4,128)S(1)} %pad_add_fusion.8) | copy-start | bytes 6148
  2.3 13.6 %collective-permute-start = (s32[4,128]{1,0:T(4,128)S(1)}, s32[4,128]{1,0:T(4,128)S(1)}, u32[]{:S(2)}, u32[]{:S(2)}) collective-permute-start(s32[4,128]{1,0:T(4,128)S(1)} %pad_add_fusion.8), channel_id=1, source_target_pairs={{0,1},{1,0},{2,3},{3,2},{4,5},{5,4},{6,7},{7,6},{8,9},{9,8},{10,11... | collective-permute-start | bytes 6152 | tf_op jit(solution)/shard_map/ppermute | solution.py:103
  5.2 4.5 %copy-start.10 = (bf16[4,512]{1,0:T(4,128)(2,1)}, bf16[4,512]{1,0:T(4,128)(2,1)S(1)}, u32[]{:S(2)}) copy-start(bf16[4,512]{1,0:T(4,128)(2,1)S(1)} %get-tuple-element.5) | copy-start | bytes 12292
  6.2 4.9 %copy-start.48 = (bf16[512,2]{0,1:T(2,128)(2,1)S(1)}, bf16[512,2]{0,1:T(2,128)(2,1)}, u32[]{:S(2)}) copy-start(bf16[512,2]{0,1:T(2,128)(2,1)} %param.32) | copy-start | bytes 6148
  7.9 1.8 %copy-start.30 = (f32[16]{0:T(128)}, f32[16]{0:T(128)S(1)}, u32[]{:S(2)}) copy-start(f32[16]{0:T(128)S(1)} %get-tuple-element.35) | copy-start | bytes 196
  7.9 1.8 %copy-start.32 = (f32[16]{0:T(128)}, f32[16]{0:T(128)S(1)}, u32[]{:S(2)}) copy-start(f32[16]{0:T(128)S(1)} %get-tuple-element.36) | copy-start | bytes 196
  7.9 3.4 %copy-start.28 = (f32[16]{0:T(128)}, f32[16]{0:T(128)S(1)}, u32[]{:S(2)}) copy-start(f32[16]{0:T(128)S(1)} %get-tuple-element.34) | copy-start | bytes 196
  8.0 4.6 %copy-start.45 = (f32[1152]{0:T(1024)S(1)}, f32[1152]{0:T(1024)}, u32[]{:S(2)}) copy-start(f32[1152]{0:T(1024)} %param.25) | copy-start | bytes 13828
  8.0 4.5 %copy-start.52 = (f32[344,16]{1,0:T(8,128)S(1)}, f32[344,16]{1,0:T(8,128)}, u32[]{:S(2)}) copy-start(f32[344,16]{1,0:T(8,128)} %constant.138.clone) | copy-start | bytes 66052
  9.1 3.4 %copy-start.39 = (pred[4,16]{1,0:T(4,128)(4,1)}, pred[4,16]{1,0:T(4,128)(4,1)S(1)}, u32[]{:S(2)}) copy-start(pred[4,16]{1,0:T(4,128)(4,1)S(1)} %iota_compare_fusion.18) | copy-start | bytes 196
  12.5 2.8 %copy-start.46 = (f32[2,2,128]{2,1,0:T(2,128)S(1)}, f32[2,2,128]{2,1,0:T(2,128)}, u32[]{:S(2)}) copy-start(f32[2,2,128]{2,1,0:T(2,128)} %param.34) | copy-start | bytes 6148
  12.6 3.4 %copy-start.24 = (s32[2,128]{1,0:T(2,128)S(1)}, s32[2,128]{1,0:T(2,128)}, u32[]{:S(2)}) copy-start(s32[2,128]{1,0:T(2,128)} %param.18) | copy-start | bytes 3076
  15.3 16.4 %slice-start = ((f32[344,1152]{1,0:T(8,128)}), f32[344,64]{1,0:T(8,128)S(1)}, s32[]{:S(2)}) async-start(f32[344,1152]{1,0:T(8,128)} %divide_multiply_fusion), calls=%async_computation | async-start | bytes 352256 | tf_op jit(solution)/shard_map/slice | solution.py:180
  15.4 17.2 %copy-start.36 = (f32[1024]{0:T(1024)S(1)}, f32[1024]{0:T(1024)}, u32[]{:S(2)}) copy-start(f32[1024]{0:T(1024)} %param.29) | copy-start | bytes 12292
  16.0 4.2 %collective-permute-start.1 = (s32[4,256]{1,0:T(4,128)S(1)}, s32[4,256]{1,0:T(4,128)S(1)}, u32[]{:S(2)}, u32[]{:S(2)}) collective-permute-start(s32[4,256]{1,0:T(4,128)S(1)} %pad_add_fusion.7), channel_id=1, source_target_pairs={{0,2},{1,3},{2,0},{3,1},{4,6},{5,7},{6,4},{7,5},{8,10},{9,11},{10,... | collective-permute-start | bytes 12296 | tf_op jit(solution)/shard_map/ppermute | solution.py:103
  20.2 3.8 %collective-permute-start.2 = (s32[4,512]{1,0:T(4,128)S(1)}, s32[4,512]{1,0:T(4,128)S(1)}, u32[]{:S(2)}, u32[]{:S(2)}) collective-permute-start(s32[4,512]{1,0:T(4,128)S(1)} %pad_add_fusion.5), channel_id=1, source_target_pairs={{0,4},{1,5},{2,6},{3,7},{4,0},{5,1},{6,2},{7,3},{8,12},{9,13},{10,... | collective-permute-start | bytes 24584 | tf_op jit(solution)/shard_map/ppermute | solution.py:103
  22.3 11.7 %copy-start.17 = (pred[2048]{0:T(1024)(128)(4,1)}, pred[2048]{0:T(1024)(128)(4,1)S(1)}, u32[]{:S(2)}) copy-start(pred[2048]{0:T(1024)(128)(4,1)S(1)} %get-tuple-element.44) | copy-start | bytes 6148
  22.3 11.7 %copy-start.19 = (pred[2048]{0:T(1024)(128)(4,1)}, pred[2048]{0:T(1024)(128)(4,1)S(1)}, u32[]{:S(2)}) copy-start(pred[2048]{0:T(1024)(128)(4,1)S(1)} %get-tuple-element.45) | copy-start | bytes 6148
  24.0 9.2 %collective-permute-start.3 = (s32[4,1024]{1,0:T(4,128)S(1)}, s32[4,1024]{1,0:T(4,128)S(1)}, u32[]{:S(2)}, u32[]{:S(2)}) collective-permute-start(s32[4,1024]{1,0:T(4,128)S(1)} %pad_add_fusion.3), channel_id=1, source_target_pairs={{0,8},{1,9},{2,10},{3,11},{4,12},{5,13},{6,14},{7,15},{8,0},{9,1},... | collective-permute-start | bytes 49160 | tf_op jit(solution)/shard_map/ppermute | solution.py:103
  27.1 7.0 %copy-start.21 = (pred[2048]{0:T(1024)(128)(4,1)}, pred[2048]{0:T(1024)(128)(4,1)S(1)}, u32[]{:S(2)}) copy-start(pred[2048]{0:T(1024)(128)(4,1)S(1)} %get-tuple-element.46) | copy-start | bytes 6148
  27.1 7.0 %copy-start.22 = (pred[2048]{0:T(1024)(128)(4,1)}, pred[2048]{0:T(1024)(128)(4,1)S(1)}, u32[]{:S(2)}) copy-start(pred[2048]{0:T(1024)(128)(4,1)S(1)} %get-tuple-element.47) | copy-start | bytes 6148
  33.2 4.0 %copy-start.2 = (f32[344,1152]{1,0:T(8,128)S(1)}, f32[344,1152]{1,0:T(8,128)}, u32[]{:S(2)}) copy-start(f32[344,1152]{1,0:T(8,128)} %divide_multiply_fusion) | copy-start | bytes 4755460
  34.0 3.6 %copy-start.18 = (pred[2048]{0:T(1024)(128)(4,1)S(1)}, pred[2048]{0:T(1024)(128)(4,1)}, u32[]{:S(2)}) copy-start(pred[2048]{0:T(1024)(128)(4,1)} %copy-done.17) | copy-start | bytes 6148
  34.1 3.6 %copy-start.20 = (pred[2048]{0:T(1024)(128)(4,1)S(1)}, pred[2048]{0:T(1024)(128)(4,1)}, u32[]{:S(2)}) copy-start(pred[2048]{0:T(1024)(128)(4,1)} %copy-done.19) | copy-start | bytes 6148
  41.4 3.2 %copy-start.13 = (pred[4,16,16]{2,1,0:T(8,128)(4,1)S(1)}, pred[4,16,16]{2,1,0:T(8,128)(4,1)}, u32[]{:S(2)}) copy-start(pred[4,16,16]{2,1,0:T(8,128)(4,1)} %broadcast_and_fusion) | copy-start | bytes 3076
  41.4 3.4 %copy-start.40 = (pred[4,16]{1,0:T(4,128)(4,1)S(1)}, pred[4,16]{1,0:T(4,128)(4,1)}, u32[]{:S(2)}) copy-start(pred[4,16]{1,0:T(4,128)(4,1)} %copy-done.39) | copy-start | bytes 196
  41.4 3.4 %copy-start.29 = (f32[16]{0:T(128)S(1)}, f32[16]{0:T(128)}, u32[]{:S(2)}) copy-start(f32[16]{0:T(128)} %copy-done.28) | copy-start | bytes 196
  41.4 3.4 %copy-start.31 = (f32[16]{0:T(128)S(1)}, f32[16]{0:T(128)}, u32[]{:S(2)}) copy-start(f32[16]{0:T(128)} %copy-done.30) | copy-start | bytes 196
  41.4 3.4 %copy-start.33 = (f32[16]{0:T(128)S(1)}, f32[16]{0:T(128)}, u32[]{:S(2)}) copy-start(f32[16]{0:T(128)} %copy-done.32) | copy-start | bytes 196
  41.4 3.4 %copy-start.35 = (f32[16]{0:T(128)S(1)}, f32[16]{0:T(128)}, u32[]{:S(2)}) copy-start(f32[16]{0:T(128)} %copy-done.34) | copy-start | bytes 196
  41.4 3.4 %copy-start.38 = (f32[16]{0:T(128)S(1)}, f32[16]{0:T(128)}, u32[]{:S(2)}) copy-start(f32[16]{0:T(128)} %param.26) | copy-start | bytes 196
  42.6 3.0 %copy-start.8 = (s32[1,4,16,128]{3,1,2,0:T(4,128)S(1)}, s32[1,4,16,128]{3,1,2,0:T(4,128)}, u32[]{:S(2)}) copy-start(s32[1,4,16,128]{3,1,2,0:T(4,128)} %fusion.126) | copy-start | bytes 98308
  45.6 2.2 %copy-start.5 = (bf16[344,1024]{0,1:T(8,128)(2,1)S(1)}, bf16[344,1024]{0,1:T(8,128)(2,1)}, u32[]{:S(2)}) copy-start(bf16[344,1024]{0,1:T(8,128)(2,1)} %copy.35) | copy-start | bytes 2113540
  45.6 2.2 %copy-start.9 = (f32[344,64]{0,1:T(8,128)S(1)}, f32[344,64]{0,1:T(8,128)}, u32[]{:S(2)}) copy-start(f32[344,64]{0,1:T(8,128)} %copy.34) | copy-start | bytes 264196
  50.7 2.5 %copy-start.12 = (f32[16,64]{1,0:T(8,128)S(1)}, f32[16,64]{1,0:T(8,128)}, u32[]{:S(2)}) copy-start(f32[16,64]{1,0:T(8,128)} %mul.226) | copy-start | bytes 12292
  53.7 2.4 %copy-start.11 = (bf16[4,512]{1,0:T(4,128)(2,1)S(1)}, bf16[4,512]{1,0:T(4,128)(2,1)}, u32[]{:S(2)}) copy-start(bf16[4,512]{1,0:T(4,128)(2,1)} %copy-done.10) | copy-start | bytes 12292
  53.7 2.4 %copy-start.27 = (s32[4,128]{1,0:T(4,128)S(1)}, s32[4,128]{1,0:T(4,128)}, u32[]{:S(2)}) copy-start(s32[4,128]{1,0:T(4,128)} %copy-done.26) | copy-start | bytes 6148
  54.4 2.2 %copy-start.42 = (bf16[512,1]{0,1:T(2,128)(2,1)S(1)}, bf16[512,1]{0,1:T(2,128)(2,1)}, u32[]{:S(2)}) copy-start(bf16[512,1]{0,1:T(2,128)(2,1)} %get-tuple-element.28) | copy-start | bytes 3076
  54.4 2.2 %copy-start.43 = (bf16[512,1]{0,1:T(2,128)(2,1)S(1)}, bf16[512,1]{0,1:T(2,128)(2,1)}, u32[]{:S(2)}) copy-start(bf16[512,1]{0,1:T(2,128)(2,1)} %get-tuple-element.29) | copy-start | bytes 3076
  54.4 2.2 %copy-start.47 = (f32[512]{0:T(512)S(1)}, f32[512]{0:T(512)}, u32[]{:S(2)}) copy-start(f32[512]{0:T(512)} %param.31) | copy-start | bytes 6148
  54.4 2.2 %copy-start.49 = (bf16[512,2]{0,1:T(2,128)(2,1)S(1)}, bf16[512,2]{0,1:T(2,128)(2,1)}, u32[]{:S(2)}) copy-start(bf16[512,2]{0,1:T(2,128)(2,1)} %param.32) | copy-start | bytes 6148
  54.4 2.5 %copy-start.41 = (s32[2,2,128]{2,1,0:T(2,128)S(1)}, s32[2,2,128]{2,1,0:T(2,128)}, u32[]{:S(2)}) copy-start(s32[2,2,128]{2,1,0:T(2,128)} %param.33) | copy-start | bytes 6148
  54.4 2.5 %copy-start.54 = (f32[2,2,128]{2,1,0:T(2,128)S(1)}, f32[2,2,128]{2,1,0:T(2,128)}, u32[]{:S(2)}) copy-start(f32[2,2,128]{2,1,0:T(2,128)} %fusion.28) | copy-start | bytes 6148
  (12 other events, 15.3 us)

commit v12 on v10

--- a/solution.py
+++ b/solution.py
@@ -141,6 +141,44 @@
 
 def block_cumsum(values, tri):
     return jnp.einsum("...s,st->...t", values, tri, precision=HIGH)
+
+
+def needed_per_gram(seq_tok, gram, dt_rows, dt_bias, neg_rate, tri, place, windows, nblk):
+    need = nblk - 1
+
+    def arranged(values):
+        fwd = values[:windows].reshape(windows, nblk, BLK)
+        rc = values[windows:].reshape(windows, nblk, BLK)[:, ::-1]
+        joined = jnp.concatenate([rc, fwd], axis=1)
+        return lax.dynamic_slice_in_dim(joined, place + 1, need, axis=1)
+
+    tok_n = arranged(seq_tok)
+    gram_n = arranged(gram)
+    dt_n = jax.nn.softplus(
+        heads_lookup(dt_rows, tok_n.reshape(windows, need * BLK)) + dt_bias[:, None]
+    ).reshape(windows, HEADS, need, BLK)
+    cum = block_cumsum(neg_rate[:, :, None] * dt_n, tri)
+    blk_total = cum[..., -1]
+    within = jnp.exp(blk_total[..., None] - cum) * dt_n
+    idx = jnp.arange(need)
+    is_fwd = idx >= (nblk - 1 - place)
+    pick = jnp.where(is_fwd[:, None], idx[None, :] > idx[:, None], idx[None, :] < idx[:, None])
+    span = jnp.sum(jnp.where(pick[None, None], blk_total[:, :, None, :], 0.0), axis=3)
+    weight = within * jnp.exp(span)[..., None]
+    fwd_part = is_fwd[None, None, :, None]
+    w_hi, w_lo = split_bf16(
+        jnp.concatenate(
+            [jnp.where(fwd_part, weight, 0.0), jnp.where(fwd_part, 0.0, weight)], axis=1
+        )
+    )
+    summed = jnp.einsum(
+        "whbs,wbsg->whg",
+        jnp.concatenate([w_hi, w_lo], axis=1),
+        onehot(gram_n, GRAMS),
+        preferred_element_type=jnp.float32,
+    )
+    summed = summed[:, : 2 * HEADS] + summed[:, 2 * HEADS :]
+    return jnp.concatenate([summed[:, :HEADS], summed[:, HEADS:]], axis=0)
 
 
 def local(
@@ -231,30 +269,37 @@
     weights = (scores[:, None] * decays * dt_u[:, :, None, :]).astype(jnp.bfloat16)
     y_intra = jnp.einsum("uhts,ushp->uthp", weights, x_u, preferred_element_type=jnp.float32)
 
-    dt_all = jax.nn.softplus(heads_lookup(dt_rows, seq_tok) + dt_bias[:, None])
-    ld_all = neg_rate * dt_all
-    cum = block_cumsum(ld_all.reshape(streams, HEADS, nblk, BLK), tri)
-    blk_total = cum[..., -1]
-    within = jnp.exp(blk_total[..., None] - cum) * dt_all.reshape(streams, HEADS, nblk, BLK)
-
-    first_blk = (
-        jnp.repeat(pos0[:, 0] // BLK, nloc) + jnp.tile(jnp.arange(nloc, dtype=jnp.int32), streams)
-    )
-    blk_idx = jnp.arange(nblk)
-    total_u = jnp.repeat(blk_total, nloc, axis=0)
-    between = (blk_idx[:, None] < blk_idx[None, :])[None] & (
-        blk_idx[None, None, :] < first_blk[:, None, None]
-    )
-    span = jnp.sum(jnp.where(between[:, None], total_u[:, :, None, :], 0.0), axis=3)
-    across = jnp.where(blk_idx[None, None, :] < first_blk[:, None, None], jnp.exp(span), 0.0)
-    weight = jnp.repeat(within, nloc, axis=0) * across[..., None]
-    oh_all = jnp.repeat(onehot(gram, GRAMS), nloc, axis=0).reshape(units, nblk, BLK, GRAMS)
-    per_gram = jnp.einsum(
-        "uhbs,ubsg->uhg",
-        weight.astype(jnp.bfloat16),
-        oh_all,
-        preferred_element_type=jnp.float32,
-    )
+    if nloc == 1:
+        per_gram = needed_per_gram(
+            seq_tok, gram, dt_rows, dt_bias, neg_rate, tri, place, windows, nblk
+        )
+    else:
+        dt_all = jax.nn.softplus(heads_lookup(dt_rows, seq_tok) + dt_bias[:, None])
+        ld_all = neg_rate * dt_all
+        cum = block_cumsum(ld_all.reshape(streams, HEADS, nblk, BLK), tri)
+        blk_total = cum[..., -1]
+        within = jnp.exp(blk_total[..., None] - cum) * dt_all.reshape(streams, HEADS, nblk, BLK)
+
+        first_blk = (
+            jnp.repeat(pos0[:, 0] // BLK, nloc) + jnp.tile(jnp.arange(nloc, dtype=jnp.int32), streams)
+        )
+        blk_idx = jnp.arange(nblk)
+        total_u = jnp.repeat(blk_total, nloc, axis=0)
+        between = (blk_idx[:, None] < blk_idx[None, :])[None] & (
+            blk_idx[None, None, :] < first_blk[:, None, None]
+        )
+        span = jnp.sum(jnp.where(between[:, None], total_u[:, :, None, :], 0.0), axis=3)
+        across = jnp.where(blk_idx[None, None, :] < first_blk[:, None, None], jnp.exp(span), 0.0)
+        weight = jnp.repeat(within, nloc, axis=0) * across[..., None]
+        w_hi, w_lo = split_bf16(weight)
+        oh_all = jnp.repeat(onehot(gram, GRAMS), nloc, axis=0).reshape(units, nblk, BLK, GRAMS)
+        per_gram = jnp.einsum(
+            "uhbs,ubsg->uhg",
+            jnp.concatenate([w_hi, w_lo], axis=1),
+            oh_all,
+            preferred_element_type=jnp.float32,
+        )
+        per_gram = per_gram[:, :HEADS] + per_gram[:, HEADS:]
     b_hi, b_lo = split_bf16(per_gram[..., None] * b_tab[None, None])
     start_state = jnp.einsum("hgp,uhgn->uhpn", x_heads, b_hi, preferred_element_type=jnp.float32)
 

time: 53.1 us -> 53.3 us (level)
    dot_general x2, matrix products: 1.86 us -> 0.79 us  [block_cumsum(): return jnp.einsum('...s,st->...t', values, tri, precision=HIGH)]
    convert_element_type x1 -> x2, other arithmetic: 0.61 us -> 1.5 us  [the longest x1 0.75 us: split_bf16(): high = values.astype(jnp.bfloat16)]
    unnamed x1 -> x0, other arithmetic: 0.74 us -> none
    dot_general x1, matrix products: 0.39 us -> 1.09 us  [local(): scores = jnp.einsum('utn,usn->uts', c_u, b_u, precision=lax.Precision.HIGH)]
    and x1 -> x0, other arithmetic: 0.61 us -> none  [local(): (blk_idx[:, None] < blk_idx[None, :])[None]]
    unnamed x116 -> x101, local copies, waits for them, and re-layouts: 1.98 us -> 2.25 us
  transfers between devices with their start and end apart: 4 -> 4, of which waited for: 2 -> 2; matrix products, arithmetic and copies ran while one was open for 33% -> 32% of each run, Pallas kernels for 0% -> 0%
where the time goes in v12:
time: 53.3 us; the launch traced here: 52.7 us
  matrix products  21.7 us (41%)
  local copies, waits for them, and re-layouts  9.79 us (18%)
  other arithmetic  8.79 us (16%)
  starting transfers between devices  8.29 us (16%)
  waiting for transfers between devices  2.6 us (5%)
  between operations  1.54 us (3%)
    ppermute x4, starting transfers between devices, gather_all(): lax.ppermute(held, axis, [(src, src ^ mask) for src in range(count)])  8.29 us
    dot_general x1, matrix products, local(): jnp.einsum('utn,uhpn->uthp', c_u, start_state, precision=lax.Precision.HIGH)  2.75 us
    ppermute x4, waiting for transfers between devices, gather_all(): lax.ppermute(held, axis, [(src, src ^ mask) for src in range(count)])  2.6 us
    slice x2, local copies, waits for them, and re-layouts, local(): b_tab = act_tab[:, INNER:INNER + NS]  2.36 us
    unnamed x101, local copies, waits for them, and re-layouts  2.25 us
    dot_general x1, matrix products, local(): jnp.einsum('rtg,gc->rtc', oh_loc, x_tab, preferred_element_type=jnp.float32)  2.12 us
    dot_general x1, matrix products, needed_per_gram(): jnp.einsum('whbs,wbsg->whg', jnp.concatenate([w_hi, w_lo], axis=1), oneho...  2.09 us
    dot_general x1, matrix products, local(): jnp.einsum('rtk,kc->rtc', oh_tok, z_rows, preferred_element_type=jnp.floa...  2.04 us
  transfers between devices with their start and end apart: 4, of which 2 were waited for; matrix products, arithmetic and copies ran while one was open for 32% of the time, Pallas kernels for 0%

profile of v12, /device:TPU:0, one launch (start us, length us, event | category | flops | bytes accessed | tf_op | source)
XLA Modules:
  0.0 52.7 jit_solution(9364066883281957499)
XLA Ops:
  0.7 1.0 %fusion.33 = s32[2,128]{1,0:T(2,128)S(1)} fusion(s32[2,128]{1,0:T(2,128)} %param.18), kind=kOutput, calls=%fused_computation.48 | convolution fusion | flops 99072 | bytes 2048 | tf_op jit(solution)/shard_map/dot_general | solution.py:224
  1.7 0.7 %pad_add_fusion.8 = s32[4,128]{1,0:T(4,128)S(1)} fusion(s32[2,128]{1,0:T(2,128)S(1)} %fusion.33, s32[2,128]{1,0:T(2,128)} %param.18), kind=kLoop, calls=%fused_computation.178 | loop fusion | flops 512 | bytes 4096 | tf_op jit(solution)/shard_map/concatenate | solution.py:227
  2.3 0.5 collective-permute-start
  2.8 0.7 %broadcast_compare_fusion.7 = (pred[4,128]{1,0:T(4,128)(4,1)S(1)}, pred[4,128]{1,0:T(4,128)(4,1)S(1)}, pred[4,128]{1,0:T(4,128)(4,1)S(1)}, pred[4,128]{1,0:T(4,128)(4,1)S(1)}) fusion(s32[2,128]{1,0:T(2,128)S(1)} %fusion.33, s32[2,128]{1,0:T(2,128)} %param.18), kind=kLoop, calls=%fused_computation.189 | loop fusion | flops 2560 | bytes 4096 | tf_op jit(solution)/shard_map/eq | solution.py:122
  3.5 0.9 %fusion.29 = bf16[2,512]{1,0:T(2,128)(2,1)S(1)} fusion(bf16[2,512]{1,0:T(2,128)(2,1)} %param.19), kind=kOutput, calls=%fused_computation.43 | convolution fusion | flops 1573888 | bytes 4096 | tf_op jit(solution)/shard_map/dot_general | solution.py:214
  4.4 0.8 %fusion.82 = (f32[4]{0:T(128)S(1)}, bf16[4,512]{1,0:T(4,128)(2,1)S(1)}) fusion(bf16[1,512]{1,0:T(2,128)(2,1)S(1)} %get-tuple-element.44, bf16[1,512]{1,0:T(2,128)(2,1)S(1)} %get-tuple-element.43, bf16[2,512]{1,0:T(2,128)(2,1)} %param.19), kind=kLoop, calls=%fused_computation.136 | loop fusion | flops 18428 | bytes 8208 | tf_op jit(solution)/shard_map/reduce_sum | solution.py:23
  5.2 1.0 %fusion.8 = f32[4,1152]{1,0:T(4,128)S(1)} fusion(bf16[512,1152]{1,0:T(8,128)(2,1)S(1)} %copy-done, bf16[4,512]{1,0:T(4,128)(2,1)S(1)} %get-tuple-element.7, f32[512]{0:T(512)} %param.20, f32[4]{0:T(128)S(1)} %add_rsqrt_fusion.2), kind=kOutput, calls=%fused_computation.13 | convolution fusion | flops 4736000 | bytes 1204240 | tf_op jit(solution)/shard_map/dot_general | solution.py:74
  6.2 0.8 %broadcast_multiply_fusion = f32[4,4,1152]{2,1,0:T(4,128)S(1)} fusion(f32[4,1152]{1,0:T(4,128)S(1)} %fusion.8, f32[4,1152]{1,0:T(4,128)} %param.24), kind=kLoop, calls=%fused_computation.107 | loop fusion | flops 18432 | bytes 110592 | tf_op jit(solution)/shard_map/mul | solution.py:77
  7.0 0.9 %fusion.111 = f32[4,16]{1,0:T(4,128)S(1)} fusion(bf16[512,16]{0,1:T(8,128)(2,1)} %param.23, bf16[4,512]{1,0:T(4,128)(2,1)S(1)} %get-tuple-element.7, f32[512]{0:T(512)} %param.20, f32[4]{0:T(128)S(1)} %add_rsqrt_fusion.2), kind=kOutput, calls=%fused_computation.211 | convolution fusion | flops 73728 | bytes 22800 | tf_op jit(solution)/shard_map/dot_general | solution.py:76
  8.0 0.7 %compare_select_fusion.2 = f32[4,16,128]{2,1,0:T(8,128)} fusion(f32[16]{0:T(128)S(1)} %copy-done.31, f32[16]{0:T(128)S(1)} %get-tuple-element.40, f32[16]{0:T(128)S(1)} %get-tuple-element.41, f32[16]{0:T(128)S(1)} %get-tuple-element.42, f32[16]{0:T(128)S(1)} %get-tuple-element.39, pred[4,128]{1,0:T(4,128)(4,1)S(1)} %get-tuple-element.37, ...), kind=kLoop, calls=%fused_computation.99 | loop fusion | flops 114688 | bytes 35136 | tf_op jit(solution)/shard_map/jit(softplus)/select_n | solution.py:250
  8.7 0.2 fusion.73
  9.0 0.6 %exponential_bitcast_fusion = f32[4,128,16]{1,2,0:T(8,128)} fusion(f32[4,16,128]{2,1,0:T(8,128)S(1)} %fusion.73), kind=kLoop, calls=%fused_computation.116 | loop fusion | bytes 65536 | tf_op jit(solution)/shard_map/exp | solution.py:308
  9.6 2.0 %fusion.37 = f32[4,128,1024]{1,2,0:T(8,128)} fusion(bf16[512,1024]{1,0:T(8,128)(2,1)S(1)} %copy-done.3, s32[4,128]{1,0:T(4,128)S(1)} %pad_add_fusion.8, bf16[4,512]{1,0:T(4,128)(2,1)S(1)} %get-tuple-element.7, f32[512]{0:T(512)S(1)} %copy-done.17, f32[4]{0:T(128)S(1)} %add_rsqrt_fusion.2), kind=kOutput, calls=%fused_computation.57 | convolution fusion | flops 8402944 | bytes 3153936 | tf_op jit(solution)/shard_map/rtk,kc->rtc/dot_general | solution.py:249
  11.9 0.6 %fusion.116 = (bf16[512,1]{0,1:T(2,128)(2,1)}, bf16[512,1]{0,1:T(2,128)(2,1)}) fusion(bf16[512,2]{0,1:T(2,128)(2,1)S(1)} %convolution_convert_fusion.5), kind=kLoop, calls=%fused_computation.213 | loop fusion | bytes 4096 | tf_op jit(solution)/shard_map/slice | solution.py:334
  12.5 0.6 %fusion.28 = f32[2,2,128]{2,1,0:T(2,128)} fusion(f32[2,2,128]{2,1,0:T(2,128)S(1)} %copy-done.37), kind=kOutput, calls=%fused_computation.40 | output fusion | flops 769 | bytes 4096 | tf_op jit(solution)/shard_map/sub | solution.py:338
  13.1 1.6 %divide_multiply_fusion = f32[344,1152]{1,0:T(8,128)S(1)} fusion(f32[16,1152]{1,0:T(8,128)S(1)} %mul.198, f32[344,16]{1,0:T(8,128)S(1)} %copy-done.44, f32[1152]{0:T(1024)S(1)} %copy-done.36), kind=kOutput, calls=%fused_computation.28 | convolution fusion | flops 78068736 | bytes 1685504 | tf_op jit(solution)/shard_map/dot_general | solution.py:78
  14.9 2.6 %collective-permute-start.1 = (s32[4,256]{1,0:T(4,128)S(1)}, s32[4,256]{1,0:T(4,128)S(1)}, u32[]{:S(2)}, u32[]{:S(2)}) collective-permute-start(s32[4,256]{1,0:T(4,128)S(1)} %pad_add_fusion.7), channel_id=1, source_target_pairs={{0,2},{1,3},{2,0},{3,1},{4,6},{5,7},{6,4},{7,5},{8,10},{9,11},{10,... | collective-permute-start | bytes 12296 | tf_op jit(solution)/shard_map/ppermute | solution.py:103
  17.5 0.6 %convert_compare_fusion = pred[128,128]{1,0:T(8,128)(4,1)} fusion(), kind=kLoop, calls=%fused_computation.103 | loop fusion | flops 49152 | bytes 16384 | tf_op jit(solution)/shard_map/gt | solution.py:267
  18.1 1.0 %collective-permute-done.1 = s32[4,256]{1,0:T(4,128)S(1)} collective-permute-done((s32[4,256]{1,0:T(4,128)S(1)}, s32[4,256]{1,0:T(4,128)S(1)}, u32[]{:S(2)}, u32[]{:S(2)}) %collective-permute-start.1) | collective-permute-done | bytes 4128 | tf_op jit(solution)/shard_map/ppermute | solution.py:103
  19.1 2.1 %collective-permute-start.2 = (s32[4,512]{1,0:T(4,128)S(1)}, s32[4,512]{1,0:T(4,128)S(1)}, u32[]{:S(2)}, u32[]{:S(2)}) collective-permute-start(s32[4,512]{1,0:T(4,128)S(1)} %pad_add_fusion.5), channel_id=1, source_target_pairs={{0,4},{1,5},{2,6},{3,7},{4,0},{5,1},{6,2},{7,3},{8,12},{9,13},{10,... | collective-permute-start | bytes 24584 | tf_op jit(solution)/shard_map/ppermute | solution.py:103
  21.3 1.6 %collective-permute-done.2 = s32[4,512]{1,0:T(4,128)S(1)} collective-permute-done((s32[4,512]{1,0:T(4,128)S(1)}, s32[4,512]{1,0:T(4,128)S(1)}, u32[]{:S(2)}, u32[]{:S(2)}) %collective-permute-start.2) | collective-permute-done | bytes 8224 | tf_op jit(solution)/shard_map/ppermute | solution.py:103
  22.9 3.1 %collective-permute-start.3 = (s32[4,1024]{1,0:T(4,128)S(1)}, s32[4,1024]{1,0:T(4,128)S(1)}, u32[]{:S(2)}, u32[]{:S(2)}) collective-permute-start(s32[4,1024]{1,0:T(4,128)S(1)} %pad_add_fusion.3), channel_id=1, source_target_pairs={{0,8},{1,9},{2,10},{3,11},{4,12},{5,13},{6,14},{7,15},{8,0},{9,1},... | collective-permute-start | bytes 49160 | tf_op jit(solution)/shard_map/ppermute | solution.py:103
  26.2 0.7 %slice.204 = f32[344,64]{1,0:T(8,128)} slice(f32[344,1152]{1,0:T(8,128)S(1)} %divide_multiply_fusion), slice={[0:344], [1024:1088]} | slice | bytes 176128 | tf_op jit(solution)/shard_map/slice | solution.py:218
  26.8 1.2 %copy.39 = bf16[344,1024]{0,1:T(8,128)(2,1)} copy(bf16[344,1024]{1,0:T(8,128)(2,1)S(1)} %slice.252) | data formatting | bytes 1409024 | tf_op jit(solution)/shard_map/slice | solution.py:217
  28.0 1.7 %copy.38 = f32[344,64]{0,1:T(8,128)} copy(f32[344,64]{1,0:T(8,128)} %slice.204) | data formatting | bytes 176128 | tf_op jit(solution)/shard_map/slice | solution.py:218
  29.7 0.7 %mul.223 = f32[16,64]{1,0:T(8,128)} reshape(f32[1024]{0:T(1024)S(1)} %copy-done.30) | data formatting | bytes 8192 | tf_op jit(solution)/shard_map/mul | solution.py:23
  30.6 0.6 %slice_bitcast_fusion.7 = (s32[1,2,16,128]{3,1,2,0:T(2,128)S(1)}, s32[1,2,16,128]{3,1,2,0:T(2,128)}, s32[2,2048]{1,0:T(2,128)S(1)}, s32[2,2048]{1,0:T(2,128)S(1)}) fusion(s32[4,2048]{1,0:T(4,128)S(1)} %select_select_fusion), kind=kLoop, calls=%fused_computation.210 | loop fusion | bytes 98304
  31.2 2.1 %convolution_convert_fusion.1 = bf16[4,128,1024]{2,1,0:T(8,128)(2,1)S(1)} fusion(s32[4,128]{1,0:T(4,128)S(1)} %pad_add_fusion.9, f32[344,1152]{1,0:T(8,128)} %copy-done.1), kind=kOutput, calls=%fused_computation.29 | convolution fusion | flops 361410560 | bytes 1755136 | tf_op jit(solution)/shard_map/rtg,gc->rtc/dot_general | solution.py:244
  33.4 1.3 %fusion.36 = f32[4,128,128]{1,2,0:T(8,128)S(1)} fusion(s32[4,128]{1,0:T(4,128)S(1)} %pad_add_fusion.9, f32[344,1152]{1,0:T(8,128)} %copy-done.1), kind=kOutput, calls=%fused_computation.54 | convolution fusion | flops 270708736 | bytes 440320 | tf_op jit(solution)/shard_map/rtg,gc->rtc/dot_general | solution.py:247
  34.9 0.5 %fusion.53 = f32[2,16,15,128]{3,1,2,0:T(8,128)S(1)} fusion(f32[16]{0:T(128)S(1)} %copy-done.32, f32[16]{0:T(128)S(1)} %copy-done.25, f32[16]{0:T(128)S(1)} %copy-done.27, f32[16]{0:T(128)S(1)} %copy-done.29, f32[16]{0:T(128)S(1)} %copy-done.23, f32[16]{0:T(128)S(1)} %copy-done.46, pred[2,15,128]{2,1,0:T(8,128)(4,1)S(1)} %get-tuple-element.22, ...), kind=kOutput, calls=%fused_computation.75 | convolution fusion | flops 95309824 | bytes 261504 | tf_op jit(solution)/shard_map/...s,st->...t/dot_general | solution.py:143
  35.8 0.3 select_reduce_fusion
  36.2 0.4 broadcast_select_fusion
  36.7 0.8 %fusion.46 = bf16[2,32,15,128]{3,1,2,0:T(8,128)(2,1)} fusion(f32[2,16,15,128]{3,1,2,0:T(8,128)S(1)} %broadcast_select_fusion.1, f32[2,16,15,128]{3,1,2,0:T(8,128)S(1)} %get-tuple-element.2), kind=kLoop, calls=%fused_computation.68 | loop fusion | flops 491520 | bytes 737280 | tf_op jit(solution)/shard_map/convert_element_type | solution.py:138
  37.4 0.7 %subtract_convert_fusion = bf16[2,32,15,128]{3,1,2,0:T(8,128)(2,1)} fusion(f32[2,16,15,128]{3,1,2,0:T(8,128)S(1)} %broadcast_select_fusion.1, f32[2,16,15,128]{3,1,2,0:T(8,128)S(1)} %get-tuple-element.2), kind=kLoop, calls=%fused_computation.67 | loop fusion | flops 614400 | bytes 737280 | tf_op jit(solution)/shard_map/convert_element_type | solution.py:139
  38.1 0.7 %copy.34 = bf16[4,128,1024]{1,2,0:T(8,128)(2,1)S(1)} copy(bf16[4,128,1024]{2,1,0:T(8,128)(2,1)S(1)} %convolution_convert_fusion.1) | data formatting | bytes 2097152 | tf_op jit(solution)/shard_map/convert_element_type | solution.py:244
  38.8 1.1 %fusion.55 = f32[4,128,128]{2,1,0:T(8,128)} fusion(f32[4,128,128]{1,2,0:T(8,128)S(1)} %fusion.36), kind=kOutput, calls=%fused_computation.79 | convolution fusion | flops 25165824 | bytes 524288 | tf_op jit(solution)/shard_map/utn,usn->uts/dot_general | solution.py:265
  39.9 0.7 %copy.58 = s32[1,2,16,128]{3,2,1,0:T(8,128)S(1)} copy(s32[1,2,16,128]{3,1,2,0:T(2,128)} %get-tuple-element.13) | data formatting | bytes 32768
  40.7 2.1 %fusion.26 = f32[2,64,344]{2,1,0:T(8,128)S(1)} fusion(s32[2,15,128]{2,1,0:T(8,128)S(1)} %fusion.79, bf16[2,32,15,128]{3,1,2,0:T(8,128)(2,1)} %subtract_convert_fusion, bf16[2,32,15,128]{3,1,2,0:T(8,128)(2,1)} %fusion.46), kind=kOutput, calls=%fused_computation.37 | convolution fusion | flops 171386880 | bytes 683008 | tf_op jit(solution)/shard_map/whbs,wbsg->whg/dot_general | solution.py:174
  42.9 1.0 %fusion.3 = f32[16,4,64,64]{3,2,0,1:T(8,128)S(1)} fusion(bf16[16,344,64,1]{1,2,0,3:T(8,128)(2,1)S(1)} %bitcast.112, f32[344,64]{0,1:T(8,128)S(1)} %copy-done.7, f32[4,16,344]{2,1,0:T(8,128)S(1)} %pad_maximum_fusion.1), kind=kOutput, calls=%fused_computation.6 | convolution fusion | flops 183173120 | bytes 1929216 | tf_op jit(solution)/shard_map/hgp,uhgn->uhpn/dot_general | solution.py:304
  43.9 1.6 %fusion.9 = f32[4,16,64,128]{3,2,1,0:T(8,128)S(1)} fusion(bf16[4,128,16,64]{1,3,2,0:T(8,128)(2,1)S(1)} %bitcast.110, f32[4,16,128]{2,1,0:T(8,128)S(1)} %copy-done.11, f32[4,16,128]{2,1,0:T(8,128)S(1)} %copy-done.13, f32[4,128,128]{2,1,0:T(8,128)S(1)} %copy-done.6, pred[128,128]{1,0:T(8,128)(4,1)S(1)} %copy-done.15), kind=kOutput, calls=%fused_computation.14 | convolution fusion | flops 140509184 | bytes 3489792 | tf_op jit(solution)/shard_map/uhts,ushp->uthp/dot_general | solution.py:270
  45.6 2.8 %multiply_reduce_fusion = (f32[4,128,16]{1,2,0:T(8,128)S(1)}, f32[4,128,16,64]{1,3,2,0:T(8,128)S(1)}) fusion(f32[4,128,16,64]{1,3,2,0:T(8,128)S(1)} %bitcast.109, bf16[4,128,16,64]{1,3,2,0:T(8,128)(2,1)S(1)} %bitcast.111, f32[16]{0:T(128)S(1)} %copy-done.42, f32[4,128,16]{1,2,0:T(8,128)S(1)} %copy-done.14, f32[16,4,64,64]{3,2,0,1:T(8,128)S(1)} %fusion.3, ...), kind=kOutput, calls=%fused_computation.21 | convolution fusion | flops 207609856 | bytes 9634304 | tf_op jit(solution)/shard_map/utn,uhpn->uthp/dot_general | solution.py:307
  48.4 0.5 multiply_convert_fusion.4
  48.9 0.7 %copy-done.4 = bf16[1024,512]{1,0:T(8,128)(2,1)S(1)} copy-done((bf16[1024,512]{1,0:T(8,128)(2,1)S(1)}, bf16[1024,512]{1,0:T(8,128)(2,1)}, u32[]{:S(2)}) %copy-start.4) | copy-done | bytes 1048600
  49.6 0.7 %convolution_convert_fusion.2 = bf16[4,128,512]{2,1,0:T(8,128)(2,1)S(1)} fusion(bf16[4,128,1024]{1,2,0:T(8,128)(2,1)S(1)} %bitcast.108, bf16[1024,512]{1,0:T(8,128)(2,1)S(1)} %copy-done.4), kind=kOutput, calls=%fused_computation.31 | convolution fusion | flops 537133056 | bytes 2621440 | tf_op jit(solution)/shard_map/gre,ed->grd/dot_general | solution.py:317
  50.4 0.9 %rev.11 = bf16[2,128,512]{2,1,0:T(8,128)(2,1)S(1)} reverse(bf16[2,128,512]{2,1,0:T(8,128)(2,1)S(1)} %slice.206), dimensions={1,2} | reverse | bytes 524288 | tf_op jit(solution)/shard_map/rev | solution.py:324
  51.4 0.4 fusion.38
  51.8 0.2 fusion.49
  52.1 0.6 %multiply_reduce_fusion.1 = f32[2,128]{1,0:T(2,128)} fusion(f32[2,2,128]{2,1,0:T(2,128)S(1)} %select_reduce_fusion.1, f32[2,2,128]{2,1,0:T(2,128)S(1)} %copy-done.47), kind=kOutput, calls=%fused_computation.180 | output fusion | flops 2049 | bytes 5120 | tf_op jit(solution)/shard_map/reduce_sum | solution.py:339
  (146 shorter events, 1.6 us)
Async XLA Ops:
  0.6 4.6 %copy-start = (bf16[512,1152]{1,0:T(8,128)(2,1)S(1)}, bf16[512,1152]{1,0:T(8,128)(2,1)}, u32[]{:S(2)}) copy-start(bf16[512,1152]{1,0:T(8,128)(2,1)} %param.21) | copy-start | bytes 3538948
  0.6 9.0 %copy-start.17 = (f32[512]{0:T(512)S(1)}, f32[512]{0:T(512)}, u32[]{:S(2)}) copy-start(f32[512]{0:T(512)} %param.20) | copy-start | bytes 6148
  0.7 7.3 %copy-start.41 = (f32[16]{0:T(128)S(1)}, f32[16]{0:T(128)}, u32[]{:S(2)}) copy-start(f32[16]{0:T(128)} %param.27) | copy-start | bytes 196
  0.7 7.3 %copy-start.31 = (f32[16]{0:T(128)S(1)}, f32[16]{0:T(128)}, u32[]{:S(2)}) copy-start(f32[16]{0:T(128)} %param.26) | copy-start | bytes 196
  0.7 8.9 %copy-start.3 = (bf16[512,1024]{1,0:T(8,128)(2,1)S(1)}, bf16[512,1024]{1,0:T(8,128)(2,1)}, u32[]{:S(2)}) copy-start(bf16[512,1024]{1,0:T(8,128)(2,1)} %param.22) | copy-start | bytes 3145732
  2.3 9.3 %copy-start.18 = (s32[4,128]{1,0:T(4,128)}, s32[4,128]{1,0:T(4,128)S(1)}, u32[]{:S(2)}) copy-start(s32[4,128]{1,0:T(4,128)S(1)} %pad_add_fusion.8) | copy-start | bytes 6148
  2.3 12.5 %collective-permute-start = (s32[4,128]{1,0:T(4,128)S(1)}, s32[4,128]{1,0:T(4,128)S(1)}, u32[]{:S(2)}, u32[]{:S(2)}) collective-permute-start(s32[4,128]{1,0:T(4,128)S(1)} %pad_add_fusion.8), channel_id=1, source_target_pairs={{0,1},{1,0},{2,3},{3,2},{4,5},{5,4},{6,7},{7,6},{8,9},{9,8},{10,11... | collective-permute-start | bytes 6152 | tf_op jit(solution)/shard_map/ppermute | solution.py:103
  5.2 6.5 %copy-start.8 = (bf16[4,512]{1,0:T(4,128)(2,1)}, bf16[4,512]{1,0:T(4,128)(2,1)S(1)}, u32[]{:S(2)}) copy-start(bf16[4,512]{1,0:T(4,128)(2,1)S(1)} %get-tuple-element.7) | copy-start | bytes 12292
  6.2 5.5 %copy-start.39 = (bf16[512,2]{0,1:T(2,128)(2,1)S(1)}, bf16[512,2]{0,1:T(2,128)(2,1)}, u32[]{:S(2)}) copy-start(bf16[512,2]{0,1:T(2,128)(2,1)} %param.32) | copy-start | bytes 6148
  7.9 4.6 %copy-start.37 = (f32[2,2,128]{2,1,0:T(2,128)S(1)}, f32[2,2,128]{2,1,0:T(2,128)}, u32[]{:S(2)}) copy-start(f32[2,2,128]{2,1,0:T(2,128)} %param.34) | copy-start | bytes 6148
  7.9 5.2 %copy-start.36 = (f32[1152]{0:T(1024)S(1)}, f32[1152]{0:T(1024)}, u32[]{:S(2)}) copy-start(f32[1152]{0:T(1024)} %param.25) | copy-start | bytes 13828
  7.9 5.2 %copy-start.44 = (f32[344,16]{1,0:T(8,128)S(1)}, f32[344,16]{1,0:T(8,128)}, u32[]{:S(2)}) copy-start(f32[344,16]{1,0:T(8,128)} %constant.135.clone) | copy-start | bytes 66052
  7.9 4.5 %copy-start.22 = (f32[16]{0:T(128)}, f32[16]{0:T(128)S(1)}, u32[]{:S(2)}) copy-start(f32[16]{0:T(128)S(1)} %get-tuple-element.39) | copy-start | bytes 196
  7.9 4.5 %copy-start.24 = (f32[16]{0:T(128)}, f32[16]{0:T(128)S(1)}, u32[]{:S(2)}) copy-start(f32[16]{0:T(128)S(1)} %get-tuple-element.40) | copy-start | bytes 196
  7.9 4.5 %copy-start.26 = (f32[16]{0:T(128)}, f32[16]{0:T(128)S(1)}, u32[]{:S(2)}) copy-start(f32[16]{0:T(128)S(1)} %get-tuple-element.41) | copy-start | bytes 196
  8.0 4.5 %copy-start.28 = (f32[16]{0:T(128)}, f32[16]{0:T(128)S(1)}, u32[]{:S(2)}) copy-start(f32[16]{0:T(128)S(1)} %get-tuple-element.42) | copy-start | bytes 196
  8.0 4.5 %copy-start.45 = (f32[16]{0:T(128)}, f32[16]{0:T(128)S(1)}, u32[]{:S(2)}) copy-start(f32[16]{0:T(128)S(1)} %exponential_negate_fusion) | copy-start | bytes 196
  9.0 3.5 %copy-start.12 = (f32[4,16,128]{2,1,0:T(8,128)}, f32[4,16,128]{2,1,0:T(8,128)S(1)}, u32[]{:S(2)}) copy-start(f32[4,16,128]{2,1,0:T(8,128)S(1)} %fusion.73) | copy-start | bytes 98308
  9.0 5.7 %copy-start.20 = (pred[15]{0:T(512)(128)(4,1)}, pred[15]{0:T(512)(128)(4,1)S(1)}, u32[]{:S(2)}) copy-start(pred[15]{0:T(512)(128)(4,1)S(1)} %iota_compare_fusion.19) | copy-start | bytes 49
  13.1 1.7 %copy-start.16 = (s32[2,128]{1,0:T(2,128)S(1)}, s32[2,128]{1,0:T(2,128)}, u32[]{:S(2)}) copy-start(s32[2,128]{1,0:T(2,128)} %param.18) | copy-start | bytes 3076
  14.7 15.7 %copy-start.1 = (f32[344,1152]{1,0:T(8,128)}, f32[344,1152]{1,0:T(8,128)S(1)}, u32[]{:S(2)}) copy-start(f32[344,1152]{1,0:T(8,128)S(1)} %divide_multiply_fusion) | copy-start | bytes 4755460
  14.7 15.0 %copy-start.30 = (f32[1024]{0:T(1024)S(1)}, f32[1024]{0:T(1024)}, u32[]{:S(2)}) copy-start(f32[1024]{0:T(1024)} %param.29) | copy-start | bytes 12292
  14.9 4.2 %collective-permute-start.1 = (s32[4,256]{1,0:T(4,128)S(1)}, s32[4,256]{1,0:T(4,128)S(1)}, u32[]{:S(2)}, u32[]{:S(2)}) collective-permute-start(s32[4,256]{1,0:T(4,128)S(1)} %pad_add_fusion.7), channel_id=1, source_target_pairs={{0,2},{1,3},{2,0},{3,1},{4,6},{5,7},{6,4},{7,5},{8,10},{9,11},{10,... | collective-permute-start | bytes 12296 | tf_op jit(solution)/shard_map/ppermute | solution.py:103
  19.1 3.8 %collective-permute-start.2 = (s32[4,512]{1,0:T(4,128)S(1)}, s32[4,512]{1,0:T(4,128)S(1)}, u32[]{:S(2)}, u32[]{:S(2)}) collective-permute-start(s32[4,512]{1,0:T(4,128)S(1)} %pad_add_fusion.5), channel_id=1, source_target_pairs={{0,4},{1,5},{2,6},{3,7},{4,0},{5,1},{6,2},{7,3},{8,12},{9,13},{10,... | collective-permute-start | bytes 24584 | tf_op jit(solution)/shard_map/ppermute | solution.py:103
  22.9 7.4 %collective-permute-start.3 = (s32[4,1024]{1,0:T(4,128)S(1)}, s32[4,1024]{1,0:T(4,128)S(1)}, u32[]{:S(2)}, u32[]{:S(2)}) collective-permute-start(s32[4,1024]{1,0:T(4,128)S(1)} %pad_add_fusion.3), channel_id=1, source_target_pairs={{0,8},{1,9},{2,10},{3,11},{4,12},{5,13},{6,14},{7,15},{8,0},{9,1},... | collective-permute-start | bytes 49160 | tf_op jit(solution)/shard_map/ppermute | solution.py:103
  28.0 6.8 %copy-start.23 = (f32[16]{0:T(128)S(1)}, f32[16]{0:T(128)}, u32[]{:S(2)}) copy-start(f32[16]{0:T(128)} %copy-done.22) | copy-start | bytes 196
  28.0 6.8 %copy-start.25 = (f32[16]{0:T(128)S(1)}, f32[16]{0:T(128)}, u32[]{:S(2)}) copy-start(f32[16]{0:T(128)} %copy-done.24) | copy-start | bytes 196
  28.0 6.8 %copy-start.27 = (f32[16]{0:T(128)S(1)}, f32[16]{0:T(128)}, u32[]{:S(2)}) copy-start(f32[16]{0:T(128)} %copy-done.26) | copy-start | bytes 196
  28.0 6.8 %copy-start.29 = (f32[16]{0:T(128)S(1)}, f32[16]{0:T(128)}, u32[]{:S(2)}) copy-start(f32[16]{0:T(128)} %copy-done.28) | copy-start | bytes 196
  28.0 6.8 %copy-start.32 = (f32[16]{0:T(128)S(1)}, f32[16]{0:T(128)}, u32[]{:S(2)}) copy-start(f32[16]{0:T(128)} %param.26) | copy-start | bytes 196
  28.0 6.8 %copy-start.46 = (f32[16]{0:T(128)S(1)}, f32[16]{0:T(128)}, u32[]{:S(2)}) copy-start(f32[16]{0:T(128)} %copy-done.45) | copy-start | bytes 196
  31.2 4.9 %copy-start.21 = (pred[15]{0:T(512)(128)(4,1)S(1)}, pred[15]{0:T(512)(128)(4,1)}, u32[]{:S(2)}) copy-start(pred[15]{0:T(512)(128)(4,1)} %copy-done.20) | copy-start | bytes 49
  38.8 4.0 %copy-start.5 = (bf16[344,1024]{0,1:T(8,128)(2,1)S(1)}, bf16[344,1024]{0,1:T(8,128)(2,1)}, u32[]{:S(2)}) copy-start(bf16[344,1024]{0,1:T(8,128)(2,1)} %copy.39) | copy-start | bytes 2113540
  40.6 2.2 %copy-start.7 = (f32[344,64]{0,1:T(8,128)S(1)}, f32[344,64]{0,1:T(8,128)}, u32[]{:S(2)}) copy-start(f32[344,64]{0,1:T(8,128)} %copy.38) | copy-start | bytes 264196
  42.9 1.0 %copy-start.6 = (f32[4,128,128]{2,1,0:T(8,128)S(1)}, f32[4,128,128]{2,1,0:T(8,128)}, u32[]{:S(2)}) copy-start(f32[4,128,128]{2,1,0:T(8,128)} %fusion.55) | copy-start | bytes 786436
  43.9 1.7 %copy-start.2 = (f32[4,128,1024]{1,2,0:T(8,128)S(1)}, f32[4,128,1024]{1,2,0:T(8,128)}, u32[]{:S(2)}) copy-start(f32[4,128,1024]{1,2,0:T(8,128)} %fusion.37) | copy-start | bytes 6291460
  43.9 1.7 %copy-start.14 = (f32[4,128,16]{1,2,0:T(8,128)S(1)}, f32[4,128,16]{1,2,0:T(8,128)}, u32[]{:S(2)}) copy-start(f32[4,128,16]{1,2,0:T(8,128)} %exponential_bitcast_fusion) | copy-start | bytes 98308
  43.9 1.7 %copy-start.42 = (f32[16]{0:T(128)S(1)}, f32[16]{0:T(128)}, u32[]{:S(2)}) copy-start(f32[16]{0:T(128)} %param.28) | copy-start | bytes 196
  45.6 2.8 %copy-start.10 = (f32[16,64]{1,0:T(8,128)S(1)}, f32[16,64]{1,0:T(8,128)}, u32[]{:S(2)}) copy-start(f32[16,64]{1,0:T(8,128)} %mul.223) | copy-start | bytes 12292
  48.4 1.2 %copy-start.4 = (bf16[1024,512]{1,0:T(8,128)(2,1)S(1)}, bf16[1024,512]{1,0:T(8,128)(2,1)}, u32[]{:S(2)}) copy-start(bf16[1024,512]{1,0:T(8,128)(2,1)} %param.30) | copy-start | bytes 3145732
  48.9 2.4 %copy-start.9 = (bf16[4,512]{1,0:T(4,128)(2,1)S(1)}, bf16[4,512]{1,0:T(4,128)(2,1)}, u32[]{:S(2)}) copy-start(bf16[4,512]{1,0:T(4,128)(2,1)} %copy-done.8) | copy-start | bytes 12292
  48.9 2.4 %copy-start.19 = (s32[4,128]{1,0:T(4,128)S(1)}, s32[4,128]{1,0:T(4,128)}, u32[]{:S(2)}) copy-start(s32[4,128]{1,0:T(4,128)} %copy-done.18) | copy-start | bytes 6148
  49.6 2.1 %copy-start.34 = (bf16[512,1]{0,1:T(2,128)(2,1)S(1)}, bf16[512,1]{0,1:T(2,128)(2,1)}, u32[]{:S(2)}) copy-start(bf16[512,1]{0,1:T(2,128)(2,1)} %get-tuple-element.33) | copy-start | bytes 3076
  49.6 2.2 %copy-start.35 = (bf16[512,1]{0,1:T(2,128)(2,1)S(1)}, bf16[512,1]{0,1:T(2,128)(2,1)}, u32[]{:S(2)}) copy-start(bf16[512,1]{0,1:T(2,128)(2,1)} %get-tuple-element.34) | copy-start | bytes 3076
  49.6 2.2 %copy-start.38 = (f32[512]{0:T(512)S(1)}, f32[512]{0:T(512)}, u32[]{:S(2)}) copy-start(f32[512]{0:T(512)} %param.31) | copy-start | bytes 6148
  49.6 2.2 %copy-start.40 = (bf16[512,2]{0,1:T(2,128)(2,1)S(1)}, bf16[512,2]{0,1:T(2,128)(2,1)}, u32[]{:S(2)}) copy-start(bf16[512,2]{0,1:T(2,128)(2,1)} %param.32) | copy-start | bytes 6148
  49.6 2.5 %copy-start.33 = (s32[2,2,128]{2,1,0:T(2,128)S(1)}, s32[2,2,128]{2,1,0:T(2,128)}, u32[]{:S(2)}) copy-start(s32[2,2,128]{2,1,0:T(2,128)} %param.33) | copy-start | bytes 6148
  49.6 2.5 %copy-start.47 = (f32[2,2,128]{2,1,0:T(2,128)S(1)}, f32[2,2,128]{2,1,0:T(2,128)}, u32[]{:S(2)}) copy-start(f32[2,2,128]{2,1,0:T(2,128)} %fusion.28) | copy-start | bytes 6148
  (4 other events, 4.1 us)

commit v13 on v12

--- a/solution.py
+++ b/solution.py
@@ -246,7 +246,9 @@
     )
     bc_loc = jnp.einsum("rtg,gc->rtc", oh_loc, bc_tab, precision=HIGH)
     oh_tok = onehot(local_tok, BASES)
-    z_loc = jnp.einsum("rtk,kc->rtc", oh_tok, z_rows, preferred_element_type=jnp.float32)
+    z_loc = jnp.einsum("rtk,kc->rtc", oh_tok, z_rows, preferred_element_type=jnp.float32).astype(
+        jnp.bfloat16
+    )
     dt_loc = jax.nn.softplus(heads_lookup(dt_rows, local_tok) + dt_bias[:, None])
     ld_loc = neg_rate * dt_loc
 
@@ -309,7 +311,7 @@
     )
     y_u = y_intra + y_inter + d_skip[:, None] * x_u.astype(jnp.float32)
     z_u = per_unit(z_loc, 1).reshape(units, BLK, HEADS, HD)
-    gated_y = y_u * jax.nn.silu(z_u)
+    gated_y = y_u * jax.nn.silu(z_u.astype(jnp.float32))
     normed = rms_gain(gated_y, inner_gain.reshape(HEADS, HD)).astype(jnp.bfloat16)
     normed = jnp.moveaxis(normed.reshape(streams, nloc, BLK, INNER), 1, 1).reshape(
         streams, count, INNER

time: 53.3 us -> 54.6 us (1.024)
  local copies, waits for them, and re-layouts: 9.79 us -> 13.4 us
  matrix products: 21.7 us -> 20.6 us
  other arithmetic: 8.79 us -> 7.97 us
    slice x2, local copies, waits for them, and re-layouts: 1.26 us -> 4.6 us  [local(): x_tab = act_tab[:, :INNER].astype(jnp.bfloat16)]
    dot_general x1, matrix products: 1.6 us -> 3.68 us  [gram_tables(): jnp.dot(jnp.asarray(gram_layout()), taps, precision=HIGH)]
    convert_element_type x0 -> x1, local copies, waits for them, and re-layouts: none -> 1.83 us  [local(): gated_y = y_u * jax.nn.silu(z_u.astype(jnp.float32))]
    slice x2 -> x3, local copies, waits for them, and re-layouts: 2.36 us -> 0.75 us  [local(): b_tab = act_tab[:, INNER:INNER + NS]]
    dot_general x1, matrix products: 1.35 us -> 0.43 us  [local(): bc_loc = jnp.einsum('rtg,gc->rtc', oh_loc, bc_tab, precision=HIGH)]
    mul x1, other arithmetic: 0.76 us -> 0.02 us  [gram_tables(): conv_w[:, None, :] * xbc_rows.astype(jnp.float32)[None]]
    dot_general x1, matrix products: 0.92 us -> 0.19 us  [gram_tables(): dt_rows = jnp.dot(row_norm, w_dt, preferred_element_type=jnp.float32)]
    dot_general x1, matrix products: 1.09 us -> 0.39 us  [local(): scores = jnp.einsum('utn,usn->uts', c_u, b_u, precision=lax.Precision.HIGH)]
  transfers between devices with their start and end apart: 4 -> 4, of which waited for: 2 -> 2; matrix products, arithmetic and copies ran while one was open for 32% -> 37% of each run, Pallas kernels for 0% -> 0%
where the time goes in v13:
time: 54.6 us; the launch traced here: 54.2 us
  matrix products  20.6 us (38%)
  local copies, waits for them, and re-layouts  13.4 us (25%)
  starting transfers between devices  8.3 us (15%)
  other arithmetic  7.97 us (15%)
  waiting for transfers between devices  2.6 us (5%)
  between operations  1.39 us (3%)
    ppermute x4, starting transfers between devices, gather_all(): lax.ppermute(held, axis, [(src, src ^ mask) for src in range(count)])  8.3 us
    slice x2, local copies, waits for them, and re-layouts, local(): x_tab = act_tab[:, :INNER].astype(jnp.bfloat16)  4.6 us
    dot_general x1, matrix products, gram_tables(): jnp.dot(jnp.asarray(gram_layout()), taps, precision=HIGH)  3.68 us
    dot_general x1, matrix products, local(): jnp.einsum('utn,uhpn->uthp', c_u, start_state, precision=lax.Precision.HIGH)  2.78 us
    ppermute x4, waiting for transfers between devices, gather_all(): lax.ppermute(held, axis, [(src, src ^ mask) for src in range(count)])  2.6 us
    unnamed x73, local copies, waits for them, and re-layouts  2.27 us
    dot_general x1, matrix products, local(): jnp.einsum('rtg,gc->rtc', oh_loc, x_tab, preferred_element_type=jnp.float32)  2.11 us
    dot_general x1, matrix products, needed_per_gram(): jnp.einsum('whbs,wbsg->whg', jnp.concatenate([w_hi, w_lo], axis=1), oneho...  2.06 us
  transfers between devices with their start and end apart: 4, of which 2 were waited for; matrix products, arithmetic and copies ran while one was open for 37% of the time, Pallas kernels for 0%

profile of v13, /device:TPU:0, one launch (start us, length us, event | category | flops | bytes accessed | tf_op | source)
XLA Modules:
  0.0 54.2 jit_solution(9268759302979664331)
XLA Ops:
  0.7 0.9 %fusion.34 = s32[2,128]{1,0:T(2,128)S(1)} fusion(s32[2,128]{1,0:T(2,128)} %param.18), kind=kOutput, calls=%fused_computation.50 | convolution fusion | flops 99072 | bytes 2048 | tf_op jit(solution)/shard_map/dot_general | solution.py:224
  1.6 0.7 %pad_add_fusion.8 = s32[4,128]{1,0:T(4,128)S(1)} fusion(s32[2,128]{1,0:T(2,128)S(1)} %fusion.34, s32[2,128]{1,0:T(2,128)} %param.18), kind=kLoop, calls=%fused_computation.179 | loop fusion | flops 512 | bytes 4096 | tf_op jit(solution)/shard_map/concatenate | solution.py:227
  2.3 0.5 collective-permute-start
  2.7 0.7 %broadcast_compare_fusion.7 = (pred[4,128]{1,0:T(4,128)(4,1)S(1)}, pred[4,128]{1,0:T(4,128)(4,1)S(1)}, pred[4,128]{1,0:T(4,128)(4,1)S(1)}, pred[4,128]{1,0:T(4,128)(4,1)S(1)}) fusion(s32[2,128]{1,0:T(2,128)S(1)} %fusion.34, s32[2,128]{1,0:T(2,128)} %param.18), kind=kLoop, calls=%fused_computation.190 | loop fusion | flops 2560 | bytes 4096 | tf_op jit(solution)/shard_map/eq | solution.py:122
  3.4 0.9 %fusion.30 = bf16[2,512]{1,0:T(2,128)(2,1)S(1)} fusion(bf16[2,512]{1,0:T(2,128)(2,1)} %param.19), kind=kOutput, calls=%fused_computation.45 | convolution fusion | flops 1573888 | bytes 4096 | tf_op jit(solution)/shard_map/dot_general | solution.py:214
  4.3 0.8 %fusion.82 = (f32[4]{0:T(128)S(1)}, bf16[4,512]{1,0:T(4,128)(2,1)S(1)}) fusion(bf16[1,512]{1,0:T(2,128)(2,1)S(1)} %get-tuple-element.44, bf16[1,512]{1,0:T(2,128)(2,1)S(1)} %get-tuple-element.43, bf16[2,512]{1,0:T(2,128)(2,1)} %param.19), kind=kLoop, calls=%fused_computation.137 | loop fusion | flops 18428 | bytes 8208 | tf_op jit(solution)/shard_map/reduce_sum | solution.py:23
  5.2 1.9 %fusion.22 = f32[4,128,1024]{2,1,0:T(8,128)S(1)} fusion(bf16[512,1024]{1,0:T(8,128)(2,1)} %param.22, s32[4,128]{1,0:T(4,128)S(1)} %pad_add_fusion.8, bf16[4,512]{1,0:T(4,128)(2,1)S(1)} %get-tuple-element.7, f32[512]{0:T(512)} %param.20, f32[4]{0:T(128)S(1)} %add_rsqrt_fusion.2), kind=kOutput, calls=%fused_computation.30 | convolution fusion | flops 9451520 | bytes 3153936 | tf_op jit(solution)/shard_map/rtk,kc->rtc/dot_general | solution.py:249
  7.1 0.3 fusion.8
  7.7 0.7 %compare_select_fusion.2 = f32[4,16,128]{2,1,0:T(8,128)} fusion(f32[16]{0:T(128)S(1)} %copy-done.20, f32[16]{0:T(128)S(1)} %get-tuple-element.40, f32[16]{0:T(128)S(1)} %get-tuple-element.41, f32[16]{0:T(128)S(1)} %get-tuple-element.42, f32[16]{0:T(128)S(1)} %get-tuple-element.39, pred[4,128]{1,0:T(4,128)(4,1)S(1)} %get-tuple-element.37, ...), kind=kLoop, calls=%fused_computation.100 | loop fusion | flops 114688 | bytes 35136 | tf_op jit(solution)/shard_map/jit(softplus)/select_n | solution.py:252
  8.4 0.2 fusion.73
  8.7 0.6 %exponential_bitcast_fusion = f32[4,128,16]{1,2,0:T(8,128)} fusion(f32[4,16,128]{2,1,0:T(8,128)S(1)} %fusion.73), kind=kLoop, calls=%fused_computation.117 | loop fusion | bytes 65536 | tf_op jit(solution)/shard_map/exp | solution.py:310
  9.5 0.6 %fusion.116 = (bf16[512,1]{0,1:T(2,128)(2,1)}, bf16[512,1]{0,1:T(2,128)(2,1)}) fusion(bf16[512,2]{0,1:T(2,128)(2,1)S(1)} %convolution_convert_fusion.6), kind=kLoop, calls=%fused_computation.214 | loop fusion | bytes 4096 | tf_op jit(solution)/shard_map/slice | solution.py:336
  10.1 0.6 %fusion.29 = f32[2,2,128]{2,1,0:T(2,128)} fusion(f32[2,2,128]{2,1,0:T(2,128)S(1)} %copy-done.26), kind=kOutput, calls=%fused_computation.42 | output fusion | flops 769 | bytes 4096 | tf_op jit(solution)/shard_map/sub | solution.py:340
  10.7 3.7 %divide_multiply_fusion = f32[344,1152]{1,0:T(8,128)} fusion(f32[16,1152]{1,0:T(8,128)S(1)} %mul.198, f32[344,16]{1,0:T(8,128)} %constant.135.clone, f32[1152]{0:T(1024)S(1)} %copy-done.25), kind=kOutput, calls=%fused_computation.28 | convolution fusion | flops 78068736 | bytes 1685504 | tf_op jit(solution)/shard_map/dot_general | solution.py:78
  14.5 2.6 %collective-permute-start.1 = (s32[4,256]{1,0:T(4,128)S(1)}, s32[4,256]{1,0:T(4,128)S(1)}, u32[]{:S(2)}, u32[]{:S(2)}) collective-permute-start(s32[4,256]{1,0:T(4,128)S(1)} %pad_add_fusion.7), channel_id=1, source_target_pairs={{0,2},{1,3},{2,0},{3,1},{4,6},{5,7},{6,4},{7,5},{8,10},{9,11},{10,... | collective-permute-start | bytes 12296 | tf_op jit(solution)/shard_map/ppermute | solution.py:103
  17.1 0.6 %convert_compare_fusion = pred[128,128]{1,0:T(8,128)(4,1)} fusion(), kind=kLoop, calls=%fused_computation.104 | loop fusion | flops 49152 | bytes 16384 | tf_op jit(solution)/shard_map/gt | solution.py:269
  17.7 1.0 %collective-permute-done.1 = s32[4,256]{1,0:T(4,128)S(1)} collective-permute-done((s32[4,256]{1,0:T(4,128)S(1)}, s32[4,256]{1,0:T(4,128)S(1)}, u32[]{:S(2)}, u32[]{:S(2)}) %collective-permute-start.1) | collective-permute-done | bytes 4128 | tf_op jit(solution)/shard_map/ppermute | solution.py:103
  18.7 2.1 %collective-permute-start.2 = (s32[4,512]{1,0:T(4,128)S(1)}, s32[4,512]{1,0:T(4,128)S(1)}, u32[]{:S(2)}, u32[]{:S(2)}) collective-permute-start(s32[4,512]{1,0:T(4,128)S(1)} %pad_add_fusion.5), channel_id=1, source_target_pairs={{0,4},{1,5},{2,6},{3,7},{4,0},{5,1},{6,2},{7,3},{8,12},{9,13},{10,... | collective-permute-start | bytes 24584 | tf_op jit(solution)/shard_map/ppermute | solution.py:103
  20.9 1.6 %collective-permute-done.2 = s32[4,512]{1,0:T(4,128)S(1)} collective-permute-done((s32[4,512]{1,0:T(4,128)S(1)}, s32[4,512]{1,0:T(4,128)S(1)}, u32[]{:S(2)}, u32[]{:S(2)}) %collective-permute-start.2) | collective-permute-done | bytes 8224 | tf_op jit(solution)/shard_map/ppermute | solution.py:103
  22.5 3.1 %collective-permute-start.3 = (s32[4,1024]{1,0:T(4,128)S(1)}, s32[4,1024]{1,0:T(4,128)S(1)}, u32[]{:S(2)}, u32[]{:S(2)}) collective-permute-start(s32[4,1024]{1,0:T(4,128)S(1)} %pad_add_fusion.3), channel_id=1, source_target_pairs={{0,8},{1,9},{2,10},{3,11},{4,12},{5,13},{6,14},{7,15},{8,0},{9,1},... | collective-permute-start | bytes 49160 | tf_op jit(solution)/shard_map/ppermute | solution.py:103
  25.7 2.3 %slice.252 = bf16[344,1024]{1,0:T(8,128)(2,1)} slice(f32[344,1152]{1,0:T(8,128)} %divide_multiply_fusion), slice={[0:344], [0:1024]} | slice | bytes 1409024 | tf_op jit(solution)/shard_map/slice | solution.py:217
  28.0 1.8 %copy.41 = f32[4,128,1024]{1,2,0:T(8,128)} copy(f32[4,128,1024]{2,1,0:T(8,128)S(1)} %fusion.22) | data formatting | bytes 4194304 | tf_op jit(solution)/shard_map/convert_element_type | solution.py:314
  29.8 2.3 %copy.39 = bf16[344,1024]{0,1:T(8,128)(2,1)} copy(bf16[344,1024]{1,0:T(8,128)(2,1)} %slice.252) | data formatting | bytes 1409024 | tf_op jit(solution)/shard_map/slice | solution.py:217
  32.1 0.7 %copy.38 = f32[344,64]{0,1:T(8,128)} copy(f32[344,64]{1,0:T(8,128)S(1)} %slice-done) | data formatting | bytes 176128 | tf_op jit(solution)/shard_map/slice | solution.py:218
  32.8 0.7 %mul.223 = f32[16,64]{1,0:T(8,128)} reshape(f32[1024]{0:T(1024)S(1)} %copy-done.19) | data formatting | bytes 8192 | tf_op jit(solution)/shard_map/mul | solution.py:23
  33.7 0.5 %fusion.53 = f32[2,16,15,128]{3,1,2,0:T(8,128)S(1)} fusion(f32[16]{0:T(128)S(1)} %copy-done.20, f32[16]{0:T(128)S(1)} %get-tuple-element.40, f32[16]{0:T(128)S(1)} %get-tuple-element.41, f32[16]{0:T(128)S(1)} %get-tuple-element.42, f32[16]{0:T(128)S(1)} %get-tuple-element.39, f32[16]{0:T(128)S(1)} %exponential_negate_fusion, ...), kind=kOutput, calls=%fused_computation.76 | convolution fusion | flops 95309824 | bytes 261504 | tf_op jit(solution)/shard_map/...s,st->...t/dot_general | solution.py:143
  34.4 0.2 copy.35
  34.6 0.3 select_reduce_fusion
  35.0 0.4 broadcast_select_fusion
  35.5 0.7 %subtract_convert_fusion = bf16[2,32,15,128]{3,1,2,0:T(8,128)(2,1)} fusion(f32[2,16,15,128]{3,1,2,0:T(8,128)S(1)} %broadcast_select_fusion.1, f32[2,16,15,128]{3,1,2,0:T(8,128)S(1)} %get-tuple-element.2), kind=kLoop, calls=%fused_computation.68 | loop fusion | flops 614400 | bytes 737280 | tf_op jit(solution)/shard_map/convert_element_type | solution.py:139
  36.2 0.7 %fusion.46 = bf16[2,32,15,128]{3,1,2,0:T(8,128)(2,1)} fusion(f32[2,16,15,128]{3,1,2,0:T(8,128)S(1)} %broadcast_select_fusion.1, f32[2,16,15,128]{3,1,2,0:T(8,128)S(1)} %get-tuple-element.2), kind=kLoop, calls=%fused_computation.69 | loop fusion | flops 491520 | bytes 737280 | tf_op jit(solution)/shard_map/convert_element_type | solution.py:138
  37.1 0.6 %slice_bitcast_fusion.7 = (s32[1,2,16,128]{3,1,2,0:T(2,128)S(1)}, s32[1,2,16,128]{3,1,2,0:T(2,128)}, s32[2,2048]{1,0:T(2,128)S(1)}, s32[2,2048]{1,0:T(2,128)S(1)}) fusion(s32[4,2048]{1,0:T(4,128)S(1)} %select_select_fusion), kind=kLoop, calls=%fused_computation.211 | loop fusion | bytes 98304
  37.7 2.1 %convolution_convert_fusion.2 = bf16[4,128,1024]{2,1,0:T(8,128)(2,1)S(1)} fusion(s32[4,128]{1,0:T(4,128)S(1)} %pad_add_fusion.9, f32[344,1152]{1,0:T(8,128)} %divide_multiply_fusion), kind=kOutput, calls=%fused_computation.31 | convolution fusion | flops 361410560 | bytes 1755136 | tf_op jit(solution)/shard_map/rtg,gc->rtc/dot_general | solution.py:244
  39.8 0.4 fusion.37
  40.3 0.7 %copy.34 = bf16[4,128,1024]{1,2,0:T(8,128)(2,1)S(1)} copy(bf16[4,128,1024]{2,1,0:T(8,128)(2,1)S(1)} %convolution_convert_fusion.2) | data formatting | bytes 2097152 | tf_op jit(solution)/shard_map/convert_element_type | solution.py:244
  40.9 0.8 %copy.57 = s32[1,2,16,128]{3,2,1,0:T(8,128)S(1)} copy(s32[1,2,16,128]{3,1,2,0:T(2,128)} %get-tuple-element.13) | data formatting | bytes 32768
  41.8 2.1 %fusion.27 = f32[2,64,344]{2,1,0:T(8,128)S(1)} fusion(s32[2,15,128]{2,1,0:T(8,128)S(1)} %fusion.79, bf16[2,32,15,128]{3,1,2,0:T(8,128)(2,1)} %subtract_convert_fusion, bf16[2,32,15,128]{3,1,2,0:T(8,128)(2,1)} %fusion.46), kind=kOutput, calls=%fused_computation.39 | convolution fusion | flops 171386880 | bytes 683008 | tf_op jit(solution)/shard_map/whbs,wbsg->whg/dot_general | solution.py:174
  43.9 0.4 fusion.55
  44.3 1.0 %fusion.3 = f32[16,4,64,64]{3,2,0,1:T(8,128)S(1)} fusion(bf16[16,344,64,1]{1,2,0,3:T(8,128)(2,1)S(1)} %bitcast.112, f32[344,64]{0,1:T(8,128)S(1)} %copy-done.5, f32[4,16,344]{2,1,0:T(8,128)S(1)} %pad_maximum_fusion.1), kind=kOutput, calls=%fused_computation.6 | convolution fusion | flops 183173120 | bytes 1929216 | tf_op jit(solution)/shard_map/hgp,uhgn->uhpn/dot_general | solution.py:306
  45.4 1.6 %fusion.9 = f32[4,16,64,128]{3,2,1,0:T(8,128)S(1)} fusion(bf16[4,128,16,64]{1,3,2,0:T(8,128)(2,1)S(1)} %bitcast.110, f32[4,16,128]{2,1,0:T(8,128)S(1)} %copy-done.9, f32[4,16,128]{2,1,0:T(8,128)S(1)} %copy-done.12, f32[4,128,128]{2,1,0:T(8,128)S(1)} %fusion.55, pred[128,128]{1,0:T(8,128)(4,1)S(1)} %copy-done.14), kind=kOutput, calls=%fused_computation.14 | convolution fusion | flops 140509184 | bytes 3489792 | tf_op jit(solution)/shard_map/uhts,ushp->uthp/dot_general | solution.py:272
  47.1 2.8 %multiply_reduce_fusion = (f32[4,128,16]{1,2,0:T(8,128)S(1)}, f32[4,128,16,64]{1,3,2,0:T(8,128)S(1)}) fusion(f32[4,128,16,64]{1,3,2,0:T(8,128)S(1)} %bitcast.109, bf16[4,128,16,64]{1,3,2,0:T(8,128)(2,1)S(1)} %bitcast.111, f32[16]{0:T(128)S(1)} %copy-done.31, f32[4,128,16]{1,2,0:T(8,128)S(1)} %copy-done.10, f32[16,4,64,64]{3,2,0,1:T(8,128)S(1)} %fusion.3, ...), kind=kOutput, calls=%fused_computation.21 | convolution fusion | flops 207609856 | bytes 9634304 | tf_op jit(solution)/shard_map/utn,uhpn->uthp/dot_general | solution.py:309
  49.9 0.5 multiply_convert_fusion.4
  50.4 0.7 %copy-done.3 = bf16[1024,512]{1,0:T(8,128)(2,1)S(1)} copy-done((bf16[1024,512]{1,0:T(8,128)(2,1)S(1)}, bf16[1024,512]{1,0:T(8,128)(2,1)}, u32[]{:S(2)}) %copy-start.3) | copy-done | bytes 1048600
  51.1 0.7 %convolution_convert_fusion.3 = bf16[4,128,512]{2,1,0:T(8,128)(2,1)S(1)} fusion(bf16[4,128,1024]{1,2,0:T(8,128)(2,1)S(1)} %bitcast.108, bf16[1024,512]{1,0:T(8,128)(2,1)S(1)} %copy-done.3), kind=kOutput, calls=%fused_computation.33 | convolution fusion | flops 537133056 | bytes 2621440 | tf_op jit(solution)/shard_map/gre,ed->grd/dot_general | solution.py:319
  51.9 0.9 %rev.11 = bf16[2,128,512]{2,1,0:T(8,128)(2,1)S(1)} reverse(bf16[2,128,512]{2,1,0:T(8,128)(2,1)S(1)} %slice.206), dimensions={1,2} | reverse | bytes 524288 | tf_op jit(solution)/shard_map/rev | solution.py:326
  52.8 0.4 fusion.38
  53.3 0.2 fusion.49
  53.6 0.6 %multiply_reduce_fusion.1 = f32[2,128]{1,0:T(2,128)} fusion(f32[2,2,128]{2,1,0:T(2,128)S(1)} %select_reduce_fusion.1, f32[2,2,128]{2,1,0:T(2,128)S(1)} %copy-done.33), kind=kOutput, calls=%fused_computation.181 | output fusion | flops 2049 | bytes 5120 | tf_op jit(solution)/shard_map/reduce_sum | solution.py:341
  (120 shorter events, 1.4 us)
Async XLA Ops:
  0.6 6.5 %copy-start = (bf16[512,1152]{1,0:T(8,128)(2,1)S(1)}, bf16[512,1152]{1,0:T(8,128)(2,1)}, u32[]{:S(2)}) copy-start(bf16[512,1152]{1,0:T(8,128)(2,1)} %param.21) | copy-start | bytes 3538948
  0.6 6.5 %copy-start.16 = (f32[512]{0:T(512)S(1)}, f32[512]{0:T(512)}, u32[]{:S(2)}) copy-start(f32[512]{0:T(512)} %param.20) | copy-start | bytes 6148
  2.3 5.2 %copy-start.17 = (s32[4,128]{1,0:T(4,128)}, s32[4,128]{1,0:T(4,128)S(1)}, u32[]{:S(2)}) copy-start(s32[4,128]{1,0:T(4,128)S(1)} %pad_add_fusion.8) | copy-start | bytes 6148
  2.3 12.2 %collective-permute-start = (s32[4,128]{1,0:T(4,128)S(1)}, s32[4,128]{1,0:T(4,128)S(1)}, u32[]{:S(2)}, u32[]{:S(2)}) collective-permute-start(s32[4,128]{1,0:T(4,128)S(1)} %pad_add_fusion.8), channel_id=1, source_target_pairs={{0,1},{1,0},{2,3},{3,2},{4,5},{5,4},{6,7},{7,6},{8,9},{9,8},{10,11... | collective-permute-start | bytes 6152 | tf_op jit(solution)/shard_map/ppermute | solution.py:103
  5.1 2.4 %copy-start.6 = (bf16[4,512]{1,0:T(4,128)(2,1)}, bf16[4,512]{1,0:T(4,128)(2,1)S(1)}, u32[]{:S(2)}) copy-start(bf16[4,512]{1,0:T(4,128)(2,1)S(1)} %get-tuple-element.7) | copy-start | bytes 12292
  5.1 2.3 %copy-start.13 = (f32[4,1152]{1,0:T(4,128)S(1)}, f32[4,1152]{1,0:T(4,128)}, u32[]{:S(2)}) copy-start(f32[4,1152]{1,0:T(4,128)} %param.24) | copy-start | bytes 55300
  5.1 2.4 %copy-start.30 = (f32[16]{0:T(128)S(1)}, f32[16]{0:T(128)}, u32[]{:S(2)}) copy-start(f32[16]{0:T(128)} %param.27) | copy-start | bytes 196
  5.1 2.4 %copy-start.24 = (bf16[512,16]{0,1:T(8,128)(2,1)S(1)}, bf16[512,16]{0,1:T(8,128)(2,1)}, u32[]{:S(2)}) copy-start(bf16[512,16]{0,1:T(8,128)(2,1)} %param.23) | copy-start | bytes 49156
  5.1 2.6 %copy-start.20 = (f32[16]{0:T(128)S(1)}, f32[16]{0:T(128)}, u32[]{:S(2)}) copy-start(f32[16]{0:T(128)} %param.26) | copy-start | bytes 196
  5.1 4.2 %copy-start.28 = (bf16[512,2]{0,1:T(2,128)(2,1)S(1)}, bf16[512,2]{0,1:T(2,128)(2,1)}, u32[]{:S(2)}) copy-start(bf16[512,2]{0,1:T(2,128)(2,1)} %param.32) | copy-start | bytes 6148
  5.2 5.0 %copy-start.26 = (f32[2,2,128]{2,1,0:T(2,128)S(1)}, f32[2,2,128]{2,1,0:T(2,128)}, u32[]{:S(2)}) copy-start(f32[2,2,128]{2,1,0:T(2,128)} %param.34) | copy-start | bytes 6148
  5.2 5.5 %copy-start.25 = (f32[1152]{0:T(1024)S(1)}, f32[1152]{0:T(1024)}, u32[]{:S(2)}) copy-start(f32[1152]{0:T(1024)} %param.25) | copy-start | bytes 13828
  8.7 5.7 %copy-start.11 = (f32[4,16,128]{2,1,0:T(8,128)}, f32[4,16,128]{2,1,0:T(8,128)S(1)}, u32[]{:S(2)}) copy-start(f32[4,16,128]{2,1,0:T(8,128)S(1)} %fusion.73) | copy-start | bytes 98308
  10.7 3.8 %copy-start.15 = (s32[2,128]{1,0:T(2,128)S(1)}, s32[2,128]{1,0:T(2,128)}, u32[]{:S(2)}) copy-start(s32[2,128]{1,0:T(2,128)} %param.18) | copy-start | bytes 3076
  14.5 4.2 %collective-permute-start.1 = (s32[4,256]{1,0:T(4,128)S(1)}, s32[4,256]{1,0:T(4,128)S(1)}, u32[]{:S(2)}, u32[]{:S(2)}) collective-permute-start(s32[4,256]{1,0:T(4,128)S(1)} %pad_add_fusion.7), channel_id=1, source_target_pairs={{0,2},{1,3},{2,0},{3,1},{4,6},{5,7},{6,4},{7,5},{8,10},{9,11},{10,... | collective-permute-start | bytes 12296 | tf_op jit(solution)/shard_map/ppermute | solution.py:103
  18.7 3.8 %collective-permute-start.2 = (s32[4,512]{1,0:T(4,128)S(1)}, s32[4,512]{1,0:T(4,128)S(1)}, u32[]{:S(2)}, u32[]{:S(2)}) collective-permute-start(s32[4,512]{1,0:T(4,128)S(1)} %pad_add_fusion.5), channel_id=1, source_target_pairs={{0,4},{1,5},{2,6},{3,7},{4,0},{5,1},{6,2},{7,3},{8,12},{9,13},{10,... | collective-permute-start | bytes 24584 | tf_op jit(solution)/shard_map/ppermute | solution.py:103
  22.5 11.0 %collective-permute-start.3 = (s32[4,1024]{1,0:T(4,128)S(1)}, s32[4,1024]{1,0:T(4,128)S(1)}, u32[]{:S(2)}, u32[]{:S(2)}) collective-permute-start(s32[4,1024]{1,0:T(4,128)S(1)} %pad_add_fusion.3), channel_id=1, source_target_pairs={{0,8},{1,9},{2,10},{3,11},{4,12},{5,13},{6,14},{7,15},{8,0},{9,1},... | collective-permute-start | bytes 49160 | tf_op jit(solution)/shard_map/ppermute | solution.py:103
  28.0 4.1 %slice-start = ((f32[344,1152]{1,0:T(8,128)}), f32[344,64]{1,0:T(8,128)S(1)}, s32[]{:S(2)}) async-start(f32[344,1152]{1,0:T(8,128)} %divide_multiply_fusion), calls=%async_computation | async-start | bytes 352256 | tf_op jit(solution)/shard_map/slice | solution.py:218
  28.0 4.9 %copy-start.19 = (f32[1024]{0:T(1024)S(1)}, f32[1024]{0:T(1024)}, u32[]{:S(2)}) copy-start(f32[1024]{0:T(1024)} %param.29) | copy-start | bytes 12292
  35.5 4.4 %copy-start.1 = (f32[344,1152]{1,0:T(8,128)S(1)}, f32[344,1152]{1,0:T(8,128)}, u32[]{:S(2)}) copy-start(f32[344,1152]{1,0:T(8,128)} %divide_multiply_fusion) | copy-start | bytes 4755460
  40.9 3.4 %copy-start.4 = (bf16[344,1024]{0,1:T(8,128)(2,1)S(1)}, bf16[344,1024]{0,1:T(8,128)(2,1)}, u32[]{:S(2)}) copy-start(bf16[344,1024]{0,1:T(8,128)(2,1)} %copy.39) | copy-start | bytes 2113540
  41.7 2.6 %copy-start.5 = (f32[344,64]{0,1:T(8,128)S(1)}, f32[344,64]{0,1:T(8,128)}, u32[]{:S(2)}) copy-start(f32[344,64]{0,1:T(8,128)} %copy.38) | copy-start | bytes 264196
  44.3 1.0 %copy-start.9 = (f32[4,16,128]{2,1,0:T(8,128)S(1)}, f32[4,16,128]{2,1,0:T(8,128)}, u32[]{:S(2)}) copy-start(f32[4,16,128]{2,1,0:T(8,128)} %compare_select_fusion.2) | copy-start | bytes 98308
  44.3 1.0 %copy-start.12 = (f32[4,16,128]{2,1,0:T(8,128)S(1)}, f32[4,16,128]{2,1,0:T(8,128)}, u32[]{:S(2)}) copy-start(f32[4,16,128]{2,1,0:T(8,128)} %copy-done.11) | copy-start | bytes 98308
  44.3 1.0 %copy-start.14 = (pred[128,128]{1,0:T(8,128)(4,1)S(1)}, pred[128,128]{1,0:T(8,128)(4,1)}, u32[]{:S(2)}) copy-start(pred[128,128]{1,0:T(8,128)(4,1)} %convert_compare_fusion) | copy-start | bytes 49156
  45.4 1.7 %copy-start.2 = (f32[4,128,1024]{1,2,0:T(8,128)S(1)}, f32[4,128,1024]{1,2,0:T(8,128)}, u32[]{:S(2)}) copy-start(f32[4,128,1024]{1,2,0:T(8,128)} %copy.41) | copy-start | bytes 6291460
  45.4 1.7 %copy-start.10 = (f32[4,128,16]{1,2,0:T(8,128)S(1)}, f32[4,128,16]{1,2,0:T(8,128)}, u32[]{:S(2)}) copy-start(f32[4,128,16]{1,2,0:T(8,128)} %exponential_bitcast_fusion) | copy-start | bytes 98308
  45.4 1.7 %copy-start.31 = (f32[16]{0:T(128)S(1)}, f32[16]{0:T(128)}, u32[]{:S(2)}) copy-start(f32[16]{0:T(128)} %param.28) | copy-start | bytes 196
  47.1 2.8 %copy-start.8 = (f32[16,64]{1,0:T(8,128)S(1)}, f32[16,64]{1,0:T(8,128)}, u32[]{:S(2)}) copy-start(f32[16,64]{1,0:T(8,128)} %mul.223) | copy-start | bytes 12292
  49.9 1.2 %copy-start.3 = (bf16[1024,512]{1,0:T(8,128)(2,1)S(1)}, bf16[1024,512]{1,0:T(8,128)(2,1)}, u32[]{:S(2)}) copy-start(bf16[1024,512]{1,0:T(8,128)(2,1)} %param.30) | copy-start | bytes 3145732
  50.4 2.4 %copy-start.7 = (bf16[4,512]{1,0:T(4,128)(2,1)S(1)}, bf16[4,512]{1,0:T(4,128)(2,1)}, u32[]{:S(2)}) copy-start(bf16[4,512]{1,0:T(4,128)(2,1)} %copy-done.6) | copy-start | bytes 12292
  50.4 2.4 %copy-start.18 = (s32[4,128]{1,0:T(4,128)S(1)}, s32[4,128]{1,0:T(4,128)}, u32[]{:S(2)}) copy-start(s32[4,128]{1,0:T(4,128)} %copy-done.17) | copy-start | bytes 6148
  51.1 2.1 %copy-start.22 = (bf16[512,1]{0,1:T(2,128)(2,1)S(1)}, bf16[512,1]{0,1:T(2,128)(2,1)}, u32[]{:S(2)}) copy-start(bf16[512,1]{0,1:T(2,128)(2,1)} %get-tuple-element.33) | copy-start | bytes 3076
  51.1 2.1 %copy-start.23 = (bf16[512,1]{0,1:T(2,128)(2,1)S(1)}, bf16[512,1]{0,1:T(2,128)(2,1)}, u32[]{:S(2)}) copy-start(bf16[512,1]{0,1:T(2,128)(2,1)} %get-tuple-element.34) | copy-start | bytes 3076
  51.1 2.2 %copy-start.27 = (f32[512]{0:T(512)S(1)}, f32[512]{0:T(512)}, u32[]{:S(2)}) copy-start(f32[512]{0:T(512)} %param.31) | copy-start | bytes 6148
  51.1 2.2 %copy-start.29 = (bf16[512,2]{0,1:T(2,128)(2,1)S(1)}, bf16[512,2]{0,1:T(2,128)(2,1)}, u32[]{:S(2)}) copy-start(bf16[512,2]{0,1:T(2,128)(2,1)} %param.32) | copy-start | bytes 6148
  51.1 2.5 %copy-start.21 = (s32[2,2,128]{2,1,0:T(2,128)S(1)}, s32[2,2,128]{2,1,0:T(2,128)}, u32[]{:S(2)}) copy-start(s32[2,2,128]{2,1,0:T(2,128)} %param.33) | copy-start | bytes 6148
  51.1 2.5 %copy-start.33 = (f32[2,2,128]{2,1,0:T(2,128)S(1)}, f32[2,2,128]{2,1,0:T(2,128)}, u32[]{:S(2)}) copy-start(f32[2,2,128]{2,1,0:T(2,128)} %fusion.29) | copy-start | bytes 6148
  53.2 1.0 %copy-start.32 = (bf16[2,128,512]{2,1,0:T(8,128)(2,1)}, bf16[2,128,512]{2,1,0:T(8,128)(2,1)S(1)}, u32[]{:S(2)}) copy-start(bf16[2,128,512]{2,1,0:T(8,128)(2,1)S(1)} %get-tuple-element.48) | copy-start | bytes 786436

commit v14 on v12

--- a/solution.py
+++ b/solution.py
@@ -75,7 +75,7 @@
     z_rows = jnp.dot(row_norm, w_z, preferred_element_type=jnp.float32).astype(jnp.bfloat16)
     dt_rows = jnp.dot(row_norm, w_dt, preferred_element_type=jnp.float32)
     taps = (conv_w[:, None, :] * xbc_rows.astype(jnp.float32)[None]).reshape(KW * BASES, CONVW)
-    conv_sum = conv_bias + jnp.dot(jnp.asarray(gram_layout()), taps, precision=HIGH)
+    conv_sum = conv_bias[:, None] + jnp.dot(taps.T, jnp.asarray(gram_layout().T), precision=HIGH)
     return jax.nn.silu(conv_sum), z_rows, dt_rows
 
 
@@ -214,10 +214,10 @@
     emb_flip = jnp.dot(emb_half, flip_d, preferred_element_type=jnp.float32).astype(jnp.bfloat16)
     emb_full = jnp.concatenate([emb_half, emb_flip[1:2], emb_flip[0:1]], axis=0)
     act_tab, z_rows, dt_rows = gram_tables(emb_full, norm_gain, w_xbc, w_z, w_dt, conv_w, conv_bias)
-    x_tab = act_tab[:, :INNER].astype(jnp.bfloat16)
-    b_tab = act_tab[:, INNER : INNER + NS]
-    bc_tab = act_tab[:, INNER:]
-    x_heads = x_tab.reshape(GRAMS, HEADS, HD).transpose(1, 0, 2)
+    x_tab = act_tab[:INNER].astype(jnp.bfloat16)
+    b_tab = act_tab[INNER : INNER + NS]
+    bc_tab = act_tab[INNER:]
+    x_heads = x_tab.reshape(HEADS, HD, GRAMS)
     neg_rate = -jnp.exp(a_log)[:, None]
 
     flip_t = exchange(count)
@@ -241,10 +241,10 @@
     )
 
     oh_loc = onehot(local_gram, GRAMS)
-    x_loc = jnp.einsum("rtg,gc->rtc", oh_loc, x_tab, preferred_element_type=jnp.float32).astype(
+    x_loc = jnp.einsum("rtg,cg->rtc", oh_loc, x_tab, preferred_element_type=jnp.float32).astype(
         jnp.bfloat16
     )
-    bc_loc = jnp.einsum("rtg,gc->rtc", oh_loc, bc_tab, precision=HIGH)
+    bc_loc = jnp.einsum("rtg,cg->rtc", oh_loc, bc_tab, precision=HIGH)
     oh_tok = onehot(local_tok, BASES)
     z_loc = jnp.einsum("rtk,kc->rtc", oh_tok, z_rows, preferred_element_type=jnp.float32)
     dt_loc = jax.nn.softplus(heads_lookup(dt_rows, local_tok) + dt_bias[:, None])
@@ -300,8 +300,8 @@
             preferred_element_type=jnp.float32,
         )
         per_gram = per_gram[:, :HEADS] + per_gram[:, HEADS:]
-    b_hi, b_lo = split_bf16(per_gram[..., None] * b_tab[None, None])
-    start_state = jnp.einsum("hgp,uhgn->uhpn", x_heads, b_hi, preferred_element_type=jnp.float32)
+    b_hi, b_lo = split_bf16(per_gram[:, :, None, :] * b_tab[None, None])
+    start_state = jnp.einsum("hpg,uhng->uhpn", x_heads, b_hi, preferred_element_type=jnp.float32)
 
     y_inter = (
         jnp.einsum("utn,uhpn->uthp", c_u, start_state, precision=lax.Precision.HIGH)

time: 53.3 us -> 53.3 us (level)
  no operation moved by 1% of the time
where the time goes in v14:
time: 53.3 us; the launch traced here: 52.8 us
  matrix products  21.8 us (41%)
  local copies, waits for them, and re-layouts  9.79 us (18%)
  other arithmetic  8.79 us (16%)
  starting transfers between devices  8.3 us (16%)
  waiting for transfers between devices  2.6 us (5%)
  between operations  1.54 us (3%)
    ppermute x4, starting transfers between devices, gather_all(): lax.ppermute(held, axis, [(src, src ^ mask) for src in range(count)])  8.3 us
    dot_general x1, matrix products, local(): jnp.einsum('utn,uhpn->uthp', c_u, start_state, precision=lax.Precision.HIGH)  2.75 us
    ppermute x4, waiting for transfers between devices, gather_all(): lax.ppermute(held, axis, [(src, src ^ mask) for src in range(count)])  2.6 us
    slice x2, local copies, waits for them, and re-layouts, local(): b_tab = act_tab[INNER:INNER + NS]  2.36 us
    unnamed x101, local copies, waits for them, and re-layouts  2.25 us
    dot_general x1, matrix products, local(): jnp.einsum('rtg,cg->rtc', oh_loc, x_tab, preferred_element_type=jnp.float32)  2.12 us
    dot_general x1, matrix products, needed_per_gram(): jnp.einsum('whbs,wbsg->whg', jnp.concatenate([w_hi, w_lo], axis=1), oneho...  2.09 us
    dot_general x1, matrix products, local(): jnp.einsum('rtk,kc->rtc', oh_tok, z_rows, preferred_element_type=jnp.floa...  2.04 us
  transfers between devices with their start and end apart: 4, of which 2 were waited for; matrix products, arithmetic and copies ran while one was open for 32% of the time, Pallas kernels for 0%

profile of v14, /device:TPU:0, one launch (start us, length us, event | category | flops | bytes accessed | tf_op | source)
XLA Modules:
  0.0 52.8 jit_solution(16358732745315349039)
XLA Ops:
  0.7 1.0 %fusion.32 = s32[2,128]{1,0:T(2,128)S(1)} fusion(s32[2,128]{1,0:T(2,128)} %param.18), kind=kOutput, calls=%fused_computation.47 | convolution fusion | flops 99072 | bytes 2048 | tf_op jit(solution)/shard_map/dot_general | solution.py:224
  1.7 0.7 %pad_add_fusion.8 = s32[4,128]{1,0:T(4,128)S(1)} fusion(s32[2,128]{1,0:T(2,128)S(1)} %fusion.32, s32[2,128]{1,0:T(2,128)} %param.18), kind=kLoop, calls=%fused_computation.177 | loop fusion | flops 512 | bytes 4096 | tf_op jit(solution)/shard_map/concatenate | solution.py:227
  2.3 0.5 collective-permute-start
  2.8 0.7 %broadcast_compare_fusion.7 = (pred[4,128]{1,0:T(4,128)(4,1)S(1)}, pred[4,128]{1,0:T(4,128)(4,1)S(1)}, pred[4,128]{1,0:T(4,128)(4,1)S(1)}, pred[4,128]{1,0:T(4,128)(4,1)S(1)}) fusion(s32[2,128]{1,0:T(2,128)S(1)} %fusion.32, s32[2,128]{1,0:T(2,128)} %param.18), kind=kLoop, calls=%fused_computation.188 | loop fusion | flops 2560 | bytes 4096 | tf_op jit(solution)/shard_map/eq | solution.py:122
  3.5 0.9 %fusion.28 = bf16[2,512]{1,0:T(2,128)(2,1)S(1)} fusion(bf16[2,512]{1,0:T(2,128)(2,1)} %param.19), kind=kOutput, calls=%fused_computation.42 | convolution fusion | flops 1573888 | bytes 4096 | tf_op jit(solution)/shard_map/dot_general | solution.py:214
  4.4 0.8 %fusion.81 = (f32[4]{0:T(128)S(1)}, bf16[4,512]{1,0:T(4,128)(2,1)S(1)}) fusion(bf16[1,512]{1,0:T(2,128)(2,1)S(1)} %get-tuple-element.44, bf16[1,512]{1,0:T(2,128)(2,1)S(1)} %get-tuple-element.43, bf16[2,512]{1,0:T(2,128)(2,1)} %param.19), kind=kLoop, calls=%fused_computation.135 | loop fusion | flops 18428 | bytes 8208 | tf_op jit(solution)/shard_map/reduce_sum | solution.py:23
  5.2 1.0 %fusion.7 = f32[4,1152]{1,0:T(4,128)S(1)} fusion(bf16[512,1152]{1,0:T(8,128)(2,1)S(1)} %copy-done, bf16[4,512]{1,0:T(4,128)(2,1)S(1)} %get-tuple-element.7, f32[512]{0:T(512)} %param.20, f32[4]{0:T(128)S(1)} %add_rsqrt_fusion.2), kind=kOutput, calls=%fused_computation.12 | convolution fusion | flops 4736000 | bytes 1204240 | tf_op jit(solution)/shard_map/dot_general | solution.py:74
  6.2 0.8 %broadcast_multiply_fusion = f32[4,4,1152]{2,1,0:T(4,128)S(1)} fusion(f32[4,1152]{1,0:T(4,128)S(1)} %fusion.7, f32[4,1152]{1,0:T(4,128)} %param.24), kind=kLoop, calls=%fused_computation.106 | loop fusion | flops 18432 | bytes 110592 | tf_op jit(solution)/shard_map/mul | solution.py:77
  7.0 0.9 %fusion.110 = f32[4,16]{1,0:T(4,128)S(1)} fusion(bf16[512,16]{0,1:T(8,128)(2,1)} %param.23, bf16[4,512]{1,0:T(4,128)(2,1)S(1)} %get-tuple-element.7, f32[512]{0:T(512)} %param.20, f32[4]{0:T(128)S(1)} %add_rsqrt_fusion.2), kind=kOutput, calls=%fused_computation.210 | convolution fusion | flops 73728 | bytes 22800 | tf_op jit(solution)/shard_map/dot_general | solution.py:76
  8.0 0.7 %compare_select_fusion.2 = f32[4,16,128]{2,1,0:T(8,128)} fusion(f32[16]{0:T(128)S(1)} %copy-done.31, f32[16]{0:T(128)S(1)} %get-tuple-element.40, f32[16]{0:T(128)S(1)} %get-tuple-element.41, f32[16]{0:T(128)S(1)} %get-tuple-element.42, f32[16]{0:T(128)S(1)} %get-tuple-element.39, pred[4,128]{1,0:T(4,128)(4,1)S(1)} %get-tuple-element.37, ...), kind=kLoop, calls=%fused_computation.98 | loop fusion | flops 114688 | bytes 35136 | tf_op jit(solution)/shard_map/jit(softplus)/select_n | solution.py:250
  8.7 0.2 fusion.72
  9.0 0.6 %exponential_bitcast_fusion = f32[4,128,16]{1,2,0:T(8,128)} fusion(f32[4,16,128]{2,1,0:T(8,128)S(1)} %fusion.72), kind=kLoop, calls=%fused_computation.115 | loop fusion | bytes 65536 | tf_op jit(solution)/shard_map/exp | solution.py:308
  9.6 2.0 %fusion.36 = f32[4,128,1024]{1,2,0:T(8,128)} fusion(bf16[512,1024]{1,0:T(8,128)(2,1)S(1)} %copy-done.3, s32[4,128]{1,0:T(4,128)S(1)} %pad_add_fusion.8, bf16[4,512]{1,0:T(4,128)(2,1)S(1)} %get-tuple-element.7, f32[512]{0:T(512)S(1)} %copy-done.17, f32[4]{0:T(128)S(1)} %add_rsqrt_fusion.2), kind=kOutput, calls=%fused_computation.56 | convolution fusion | flops 8402944 | bytes 3153936 | tf_op jit(solution)/shard_map/rtk,kc->rtc/dot_general | solution.py:249
  11.9 0.6 %fusion.115 = (bf16[512,1]{0,1:T(2,128)(2,1)}, bf16[512,1]{0,1:T(2,128)(2,1)}) fusion(bf16[512,2]{0,1:T(2,128)(2,1)S(1)} %convolution_convert_fusion.5), kind=kLoop, calls=%fused_computation.212 | loop fusion | bytes 4096 | tf_op jit(solution)/shard_map/slice | solution.py:334
  12.5 0.6 %fusion.27 = f32[2,2,128]{2,1,0:T(2,128)} fusion(f32[2,2,128]{2,1,0:T(2,128)S(1)} %copy-done.37), kind=kOutput, calls=%fused_computation.39 | output fusion | flops 769 | bytes 4096 | tf_op jit(solution)/shard_map/sub | solution.py:338
  13.1 1.7 %divide_multiply_fusion = f32[1152,344]{0,1:T(8,128)S(1)} fusion(f32[16,1152]{1,0:T(8,128)S(1)} %mul.198, f32[16,344]{1,0:T(8,128)S(1)} %copy-done.44, f32[1152]{0:T(1024)S(1)} %copy-done.36), kind=kOutput, calls=%fused_computation.27 | convolution fusion | flops 78068736 | bytes 1685504 | tf_op jit(solution)/shard_map/dot_general | solution.py:78
  14.9 2.6 %collective-permute-start.1 = (s32[4,256]{1,0:T(4,128)S(1)}, s32[4,256]{1,0:T(4,128)S(1)}, u32[]{:S(2)}, u32[]{:S(2)}) collective-permute-start(s32[4,256]{1,0:T(4,128)S(1)} %pad_add_fusion.7), channel_id=1, source_target_pairs={{0,2},{1,3},{2,0},{3,1},{4,6},{5,7},{6,4},{7,5},{8,10},{9,11},{10,... | collective-permute-start | bytes 12296 | tf_op jit(solution)/shard_map/ppermute | solution.py:103
  17.5 0.6 %convert_compare_fusion = pred[128,128]{1,0:T(8,128)(4,1)} fusion(), kind=kLoop, calls=%fused_computation.102 | loop fusion | flops 49152 | bytes 16384 | tf_op jit(solution)/shard_map/gt | solution.py:267
  18.2 1.0 %collective-permute-done.1 = s32[4,256]{1,0:T(4,128)S(1)} collective-permute-done((s32[4,256]{1,0:T(4,128)S(1)}, s32[4,256]{1,0:T(4,128)S(1)}, u32[]{:S(2)}, u32[]{:S(2)}) %collective-permute-start.1) | collective-permute-done | bytes 4128 | tf_op jit(solution)/shard_map/ppermute | solution.py:103
  19.2 2.1 %collective-permute-start.2 = (s32[4,512]{1,0:T(4,128)S(1)}, s32[4,512]{1,0:T(4,128)S(1)}, u32[]{:S(2)}, u32[]{:S(2)}) collective-permute-start(s32[4,512]{1,0:T(4,128)S(1)} %pad_add_fusion.5), channel_id=1, source_target_pairs={{0,4},{1,5},{2,6},{3,7},{4,0},{5,1},{6,2},{7,3},{8,12},{9,13},{10,... | collective-permute-start | bytes 24584 | tf_op jit(solution)/shard_map/ppermute | solution.py:103
  21.3 1.6 %collective-permute-done.2 = s32[4,512]{1,0:T(4,128)S(1)} collective-permute-done((s32[4,512]{1,0:T(4,128)S(1)}, s32[4,512]{1,0:T(4,128)S(1)}, u32[]{:S(2)}, u32[]{:S(2)}) %collective-permute-start.2) | collective-permute-done | bytes 8224 | tf_op jit(solution)/shard_map/ppermute | solution.py:103
  23.0 3.1 %collective-permute-start.3 = (s32[4,1024]{1,0:T(4,128)S(1)}, s32[4,1024]{1,0:T(4,128)S(1)}, u32[]{:S(2)}, u32[]{:S(2)}) collective-permute-start(s32[4,1024]{1,0:T(4,128)S(1)} %pad_add_fusion.3), channel_id=1, source_target_pairs={{0,8},{1,9},{2,10},{3,11},{4,12},{5,13},{6,14},{7,15},{8,0},{9,1},... | collective-permute-start | bytes 49160 | tf_op jit(solution)/shard_map/ppermute | solution.py:103
  26.2 0.7 %slice.204 = f32[64,344]{0,1:T(8,128)} slice(f32[1152,344]{0,1:T(8,128)S(1)} %divide_multiply_fusion), slice={[1024:1088], [0:344]} | slice | bytes 176128 | tf_op jit(solution)/shard_map/slice | solution.py:218
  26.9 1.2 %copy.41 = bf16[1024,344]{1,0:T(8,128)(2,1)} copy(bf16[1024,344]{0,1:T(8,128)(2,1)S(1)} %slice.252) | data formatting | bytes 1409024 | tf_op jit(solution)/shard_map/slice | solution.py:217
  28.1 1.7 %copy.40 = f32[64,344]{1,0:T(8,128)} copy(f32[64,344]{0,1:T(8,128)} %slice.204) | data formatting | bytes 176128 | tf_op jit(solution)/shard_map/slice | solution.py:218
  29.8 0.7 %mul.223 = f32[16,64]{1,0:T(8,128)} reshape(f32[1024]{0:T(1024)S(1)} %copy-done.30) | data formatting | bytes 8192 | tf_op jit(solution)/shard_map/mul | solution.py:23
  30.6 0.6 %slice_bitcast_fusion.7 = (s32[1,2,16,128]{3,1,2,0:T(2,128)S(1)}, s32[1,2,16,128]{3,1,2,0:T(2,128)}, s32[2,2048]{1,0:T(2,128)S(1)}, s32[2,2048]{1,0:T(2,128)S(1)}) fusion(s32[4,2048]{1,0:T(4,128)S(1)} %select_select_fusion), kind=kLoop, calls=%fused_computation.209 | loop fusion | bytes 98304
  31.3 2.1 %convolution_convert_fusion.1 = bf16[4,128,1024]{2,1,0:T(8,128)(2,1)S(1)} fusion(s32[4,128]{1,0:T(4,128)S(1)} %pad_add_fusion.9, f32[1152,344]{0,1:T(8,128)} %copy-done.1), kind=kOutput, calls=%fused_computation.28 | convolution fusion | flops 361410560 | bytes 1755136 | tf_op jit(solution)/shard_map/rtg,cg->rtc/dot_general | solution.py:244
  33.4 1.3 %fusion.35 = f32[4,128,128]{1,2,0:T(8,128)S(1)} fusion(s32[4,128]{1,0:T(4,128)S(1)} %pad_add_fusion.9, f32[1152,344]{0,1:T(8,128)} %copy-done.1), kind=kOutput, calls=%fused_computation.53 | convolution fusion | flops 270708736 | bytes 440320 | tf_op jit(solution)/shard_map/rtg,cg->rtc/dot_general | solution.py:247
  34.9 0.5 %fusion.52 = f32[2,16,15,128]{3,1,2,0:T(8,128)S(1)} fusion(f32[16]{0:T(128)S(1)} %copy-done.32, f32[16]{0:T(128)S(1)} %copy-done.25, f32[16]{0:T(128)S(1)} %copy-done.27, f32[16]{0:T(128)S(1)} %copy-done.29, f32[16]{0:T(128)S(1)} %copy-done.23, f32[16]{0:T(128)S(1)} %copy-done.46, pred[2,15,128]{2,1,0:T(8,128)(4,1)S(1)} %get-tuple-element.22, ...), kind=kOutput, calls=%fused_computation.74 | convolution fusion | flops 95309824 | bytes 261504 | tf_op jit(solution)/shard_map/...s,st->...t/dot_general | solution.py:143
  35.9 0.3 select_reduce_fusion
  36.2 0.4 broadcast_select_fusion
  36.7 0.8 %fusion.45 = bf16[2,32,15,128]{3,1,2,0:T(8,128)(2,1)} fusion(f32[2,16,15,128]{3,1,2,0:T(8,128)S(1)} %broadcast_select_fusion.1, f32[2,16,15,128]{3,1,2,0:T(8,128)S(1)} %get-tuple-element.2), kind=kLoop, calls=%fused_computation.67 | loop fusion | flops 491520 | bytes 737280 | tf_op jit(solution)/shard_map/convert_element_type | solution.py:138
  37.5 0.7 %subtract_convert_fusion = bf16[2,32,15,128]{3,1,2,0:T(8,128)(2,1)} fusion(f32[2,16,15,128]{3,1,2,0:T(8,128)S(1)} %broadcast_select_fusion.1, f32[2,16,15,128]{3,1,2,0:T(8,128)S(1)} %get-tuple-element.2), kind=kLoop, calls=%fused_computation.66 | loop fusion | flops 614400 | bytes 737280 | tf_op jit(solution)/shard_map/convert_element_type | solution.py:139
  38.2 0.7 %copy.36 = bf16[4,128,1024]{1,2,0:T(8,128)(2,1)S(1)} copy(bf16[4,128,1024]{2,1,0:T(8,128)(2,1)S(1)} %convolution_convert_fusion.1) | data formatting | bytes 2097152 | tf_op jit(solution)/shard_map/convert_element_type | solution.py:244
  38.9 1.1 %fusion.54 = f32[4,128,128]{2,1,0:T(8,128)} fusion(f32[4,128,128]{1,2,0:T(8,128)S(1)} %fusion.35), kind=kOutput, calls=%fused_computation.78 | convolution fusion | flops 25165824 | bytes 524288 | tf_op jit(solution)/shard_map/utn,usn->uts/dot_general | solution.py:265
  40.0 0.7 %copy.60 = s32[1,2,16,128]{3,2,1,0:T(8,128)S(1)} copy(s32[1,2,16,128]{3,1,2,0:T(2,128)} %get-tuple-element.13) | data formatting | bytes 32768
  40.7 2.1 %fusion.25 = f32[2,64,344]{2,1,0:T(8,128)S(1)} fusion(s32[2,15,128]{2,1,0:T(8,128)S(1)} %fusion.78, bf16[2,32,15,128]{3,1,2,0:T(8,128)(2,1)} %subtract_convert_fusion, bf16[2,32,15,128]{3,1,2,0:T(8,128)(2,1)} %fusion.45), kind=kOutput, calls=%fused_computation.36 | convolution fusion | flops 171386880 | bytes 683008 | tf_op jit(solution)/shard_map/whbs,wbsg->whg/dot_general | solution.py:174
  43.0 1.0 %fusion.3 = f32[16,4,64,64]{3,2,0,1:T(8,128)S(1)} fusion(bf16[16,64,344,1]{2,1,0,3:T(8,128)(2,1)S(1)} %bitcast.106, f32[64,344]{1,0:T(8,128)S(1)} %copy-done.7, f32[4,16,344]{2,1,0:T(8,128)S(1)} %pad_maximum_fusion.1), kind=kOutput, calls=%fused_computation.6 | convolution fusion | flops 183173120 | bytes 1929216 | tf_op jit(solution)/shard_map/hpg,uhng->uhpn/dot_general | solution.py:304
  44.0 1.6 %fusion.8 = f32[4,16,64,128]{3,2,1,0:T(8,128)S(1)} fusion(bf16[4,128,16,64]{1,3,2,0:T(8,128)(2,1)S(1)} %bitcast.104, f32[4,16,128]{2,1,0:T(8,128)S(1)} %copy-done.11, f32[4,16,128]{2,1,0:T(8,128)S(1)} %copy-done.13, f32[4,128,128]{2,1,0:T(8,128)S(1)} %copy-done.6, pred[128,128]{1,0:T(8,128)(4,1)S(1)} %copy-done.15), kind=kOutput, calls=%fused_computation.13 | convolution fusion | flops 140509184 | bytes 3489792 | tf_op jit(solution)/shard_map/uhts,ushp->uthp/dot_general | solution.py:270
  45.7 2.8 %multiply_reduce_fusion = (f32[4,128,16]{1,2,0:T(8,128)S(1)}, f32[4,128,16,64]{1,3,2,0:T(8,128)S(1)}) fusion(f32[4,128,16,64]{1,3,2,0:T(8,128)S(1)} %bitcast.103, bf16[4,128,16,64]{1,3,2,0:T(8,128)(2,1)S(1)} %bitcast.105, f32[16]{0:T(128)S(1)} %copy-done.42, f32[4,128,16]{1,2,0:T(8,128)S(1)} %copy-done.14, f32[16,4,64,64]{3,2,0,1:T(8,128)S(1)} %fusion.3, ...), kind=kOutput, calls=%fused_computation.20 | convolution fusion | flops 207609856 | bytes 9634304 | tf_op jit(solution)/shard_map/utn,uhpn->uthp/dot_general | solution.py:307
  48.5 0.5 multiply_convert_fusion.4
  49.0 0.7 %copy-done.4 = bf16[1024,512]{1,0:T(8,128)(2,1)S(1)} copy-done((bf16[1024,512]{1,0:T(8,128)(2,1)S(1)}, bf16[1024,512]{1,0:T(8,128)(2,1)}, u32[]{:S(2)}) %copy-start.4) | copy-done | bytes 1048600
  49.7 0.7 %convolution_convert_fusion.2 = bf16[4,128,512]{2,1,0:T(8,128)(2,1)S(1)} fusion(bf16[4,128,1024]{1,2,0:T(8,128)(2,1)S(1)} %bitcast.102, bf16[1024,512]{1,0:T(8,128)(2,1)S(1)} %copy-done.4), kind=kOutput, calls=%fused_computation.30 | convolution fusion | flops 537133056 | bytes 2621440 | tf_op jit(solution)/shard_map/gre,ed->grd/dot_general | solution.py:317
  50.5 0.9 %rev.11 = bf16[2,128,512]{2,1,0:T(8,128)(2,1)S(1)} reverse(bf16[2,128,512]{2,1,0:T(8,128)(2,1)S(1)} %slice.206), dimensions={1,2} | reverse | bytes 524288 | tf_op jit(solution)/shard_map/rev | solution.py:324
  51.4 0.4 fusion.37
  51.9 0.2 fusion.48
  52.2 0.6 %multiply_reduce_fusion.1 = f32[2,128]{1,0:T(2,128)} fusion(f32[2,2,128]{2,1,0:T(2,128)S(1)} %select_reduce_fusion.1, f32[2,2,128]{2,1,0:T(2,128)S(1)} %copy-done.47), kind=kOutput, calls=%fused_computation.179 | output fusion | flops 2049 | bytes 5120 | tf_op jit(solution)/shard_map/reduce_sum | solution.py:339
  (146 shorter events, 1.6 us)
Async XLA Ops:
  0.6 4.6 %copy-start = (bf16[512,1152]{1,0:T(8,128)(2,1)S(1)}, bf16[512,1152]{1,0:T(8,128)(2,1)}, u32[]{:S(2)}) copy-start(bf16[512,1152]{1,0:T(8,128)(2,1)} %param.21) | copy-start | bytes 3538948
  0.6 9.0 %copy-start.17 = (f32[512]{0:T(512)S(1)}, f32[512]{0:T(512)}, u32[]{:S(2)}) copy-start(f32[512]{0:T(512)} %param.20) | copy-start | bytes 6148
  0.7 7.3 %copy-start.41 = (f32[16]{0:T(128)S(1)}, f32[16]{0:T(128)}, u32[]{:S(2)}) copy-start(f32[16]{0:T(128)} %param.27) | copy-start | bytes 196
  0.7 7.3 %copy-start.31 = (f32[16]{0:T(128)S(1)}, f32[16]{0:T(128)}, u32[]{:S(2)}) copy-start(f32[16]{0:T(128)} %param.26) | copy-start | bytes 196
  0.7 8.9 %copy-start.3 = (bf16[512,1024]{1,0:T(8,128)(2,1)S(1)}, bf16[512,1024]{1,0:T(8,128)(2,1)}, u32[]{:S(2)}) copy-start(bf16[512,1024]{1,0:T(8,128)(2,1)} %param.22) | copy-start | bytes 3145732
  2.3 9.3 %copy-start.18 = (s32[4,128]{1,0:T(4,128)}, s32[4,128]{1,0:T(4,128)S(1)}, u32[]{:S(2)}) copy-start(s32[4,128]{1,0:T(4,128)S(1)} %pad_add_fusion.8) | copy-start | bytes 6148
  2.3 12.6 %collective-permute-start = (s32[4,128]{1,0:T(4,128)S(1)}, s32[4,128]{1,0:T(4,128)S(1)}, u32[]{:S(2)}, u32[]{:S(2)}) collective-permute-start(s32[4,128]{1,0:T(4,128)S(1)} %pad_add_fusion.8), channel_id=1, source_target_pairs={{0,1},{1,0},{2,3},{3,2},{4,5},{5,4},{6,7},{7,6},{8,9},{9,8},{10,11... | collective-permute-start | bytes 6152 | tf_op jit(solution)/shard_map/ppermute | solution.py:103
  5.2 6.5 %copy-start.8 = (bf16[4,512]{1,0:T(4,128)(2,1)}, bf16[4,512]{1,0:T(4,128)(2,1)S(1)}, u32[]{:S(2)}) copy-start(bf16[4,512]{1,0:T(4,128)(2,1)S(1)} %get-tuple-element.7) | copy-start | bytes 12292
  6.2 5.5 %copy-start.39 = (bf16[512,2]{0,1:T(2,128)(2,1)S(1)}, bf16[512,2]{0,1:T(2,128)(2,1)}, u32[]{:S(2)}) copy-start(bf16[512,2]{0,1:T(2,128)(2,1)} %param.32) | copy-start | bytes 6148
  7.9 4.6 %copy-start.37 = (f32[2,2,128]{2,1,0:T(2,128)S(1)}, f32[2,2,128]{2,1,0:T(2,128)}, u32[]{:S(2)}) copy-start(f32[2,2,128]{2,1,0:T(2,128)} %param.34) | copy-start | bytes 6148
  7.9 5.2 %copy-start.36 = (f32[1152]{0:T(1024)S(1)}, f32[1152]{0:T(1024)}, u32[]{:S(2)}) copy-start(f32[1152]{0:T(1024)} %param.25) | copy-start | bytes 13828
  7.9 5.2 %copy-start.44 = (f32[16,344]{1,0:T(8,128)S(1)}, f32[16,344]{1,0:T(8,128)}, u32[]{:S(2)}) copy-start(f32[16,344]{1,0:T(8,128)} %constant.135.clone) | copy-start | bytes 66052
  7.9 4.5 %copy-start.22 = (f32[16]{0:T(128)}, f32[16]{0:T(128)S(1)}, u32[]{:S(2)}) copy-start(f32[16]{0:T(128)S(1)} %get-tuple-element.39) | copy-start | bytes 196
  7.9 4.5 %copy-start.24 = (f32[16]{0:T(128)}, f32[16]{0:T(128)S(1)}, u32[]{:S(2)}) copy-start(f32[16]{0:T(128)S(1)} %get-tuple-element.40) | copy-start | bytes 196
  7.9 4.5 %copy-start.26 = (f32[16]{0:T(128)}, f32[16]{0:T(128)S(1)}, u32[]{:S(2)}) copy-start(f32[16]{0:T(128)S(1)} %get-tuple-element.41) | copy-start | bytes 196
  8.0 4.5 %copy-start.28 = (f32[16]{0:T(128)}, f32[16]{0:T(128)S(1)}, u32[]{:S(2)}) copy-start(f32[16]{0:T(128)S(1)} %get-tuple-element.42) | copy-start | bytes 196
  8.0 4.5 %copy-start.45 = (f32[16]{0:T(128)}, f32[16]{0:T(128)S(1)}, u32[]{:S(2)}) copy-start(f32[16]{0:T(128)S(1)} %exponential_negate_fusion) | copy-start | bytes 196
  9.0 3.5 %copy-start.12 = (f32[4,16,128]{2,1,0:T(8,128)}, f32[4,16,128]{2,1,0:T(8,128)S(1)}, u32[]{:S(2)}) copy-start(f32[4,16,128]{2,1,0:T(8,128)S(1)} %fusion.72) | copy-start | bytes 98308
  9.0 5.8 %copy-start.20 = (pred[15]{0:T(512)(128)(4,1)}, pred[15]{0:T(512)(128)(4,1)S(1)}, u32[]{:S(2)}) copy-start(pred[15]{0:T(512)(128)(4,1)S(1)} %iota_compare_fusion.19) | copy-start | bytes 49
  13.1 1.8 %copy-start.16 = (s32[2,128]{1,0:T(2,128)S(1)}, s32[2,128]{1,0:T(2,128)}, u32[]{:S(2)}) copy-start(s32[2,128]{1,0:T(2,128)} %param.18) | copy-start | bytes 3076
  14.8 15.7 %copy-start.1 = (f32[1152,344]{0,1:T(8,128)}, f32[1152,344]{0,1:T(8,128)S(1)}, u32[]{:S(2)}) copy-start(f32[1152,344]{0,1:T(8,128)S(1)} %divide_multiply_fusion) | copy-start | bytes 4755460
  14.8 15.0 %copy-start.30 = (f32[1024]{0:T(1024)S(1)}, f32[1024]{0:T(1024)}, u32[]{:S(2)}) copy-start(f32[1024]{0:T(1024)} %param.29) | copy-start | bytes 12292
  14.9 4.2 %collective-permute-start.1 = (s32[4,256]{1,0:T(4,128)S(1)}, s32[4,256]{1,0:T(4,128)S(1)}, u32[]{:S(2)}, u32[]{:S(2)}) collective-permute-start(s32[4,256]{1,0:T(4,128)S(1)} %pad_add_fusion.7), channel_id=1, source_target_pairs={{0,2},{1,3},{2,0},{3,1},{4,6},{5,7},{6,4},{7,5},{8,10},{9,11},{10,... | collective-permute-start | bytes 12296 | tf_op jit(solution)/shard_map/ppermute | solution.py:103
  19.2 3.8 %collective-permute-start.2 = (s32[4,512]{1,0:T(4,128)S(1)}, s32[4,512]{1,0:T(4,128)S(1)}, u32[]{:S(2)}, u32[]{:S(2)}) collective-permute-start(s32[4,512]{1,0:T(4,128)S(1)} %pad_add_fusion.5), channel_id=1, source_target_pairs={{0,4},{1,5},{2,6},{3,7},{4,0},{5,1},{6,2},{7,3},{8,12},{9,13},{10,... | collective-permute-start | bytes 24584 | tf_op jit(solution)/shard_map/ppermute | solution.py:103
  23.0 7.4 %collective-permute-start.3 = (s32[4,1024]{1,0:T(4,128)S(1)}, s32[4,1024]{1,0:T(4,128)S(1)}, u32[]{:S(2)}, u32[]{:S(2)}) collective-permute-start(s32[4,1024]{1,0:T(4,128)S(1)} %pad_add_fusion.3), channel_id=1, source_target_pairs={{0,8},{1,9},{2,10},{3,11},{4,12},{5,13},{6,14},{7,15},{8,0},{9,1},... | collective-permute-start | bytes 49160 | tf_op jit(solution)/shard_map/ppermute | solution.py:103
  28.1 6.8 %copy-start.23 = (f32[16]{0:T(128)S(1)}, f32[16]{0:T(128)}, u32[]{:S(2)}) copy-start(f32[16]{0:T(128)} %copy-done.22) | copy-start | bytes 196
  28.1 6.8 %copy-start.25 = (f32[16]{0:T(128)S(1)}, f32[16]{0:T(128)}, u32[]{:S(2)}) copy-start(f32[16]{0:T(128)} %copy-done.24) | copy-start | bytes 196
  28.1 6.8 %copy-start.27 = (f32[16]{0:T(128)S(1)}, f32[16]{0:T(128)}, u32[]{:S(2)}) copy-start(f32[16]{0:T(128)} %copy-done.26) | copy-start | bytes 196
  28.1 6.8 %copy-start.29 = (f32[16]{0:T(128)S(1)}, f32[16]{0:T(128)}, u32[]{:S(2)}) copy-start(f32[16]{0:T(128)} %copy-done.28) | copy-start | bytes 196
  28.1 6.8 %copy-start.32 = (f32[16]{0:T(128)S(1)}, f32[16]{0:T(128)}, u32[]{:S(2)}) copy-start(f32[16]{0:T(128)} %param.26) | copy-start | bytes 196
  28.1 6.8 %copy-start.46 = (f32[16]{0:T(128)S(1)}, f32[16]{0:T(128)}, u32[]{:S(2)}) copy-start(f32[16]{0:T(128)} %copy-done.45) | copy-start | bytes 196
  31.3 4.9 %copy-start.21 = (pred[15]{0:T(512)(128)(4,1)S(1)}, pred[15]{0:T(512)(128)(4,1)}, u32[]{:S(2)}) copy-start(pred[15]{0:T(512)(128)(4,1)} %copy-done.20) | copy-start | bytes 49
  38.9 4.0 %copy-start.5 = (bf16[1024,344]{1,0:T(8,128)(2,1)S(1)}, bf16[1024,344]{1,0:T(8,128)(2,1)}, u32[]{:S(2)}) copy-start(bf16[1024,344]{1,0:T(8,128)(2,1)} %copy.41) | copy-start | bytes 2113540
  40.7 2.2 %copy-start.7 = (f32[64,344]{1,0:T(8,128)S(1)}, f32[64,344]{1,0:T(8,128)}, u32[]{:S(2)}) copy-start(f32[64,344]{1,0:T(8,128)} %copy.40) | copy-start | bytes 264196
  42.9 1.0 %copy-start.6 = (f32[4,128,128]{2,1,0:T(8,128)S(1)}, f32[4,128,128]{2,1,0:T(8,128)}, u32[]{:S(2)}) copy-start(f32[4,128,128]{2,1,0:T(8,128)} %fusion.54) | copy-start | bytes 786436
  44.0 1.7 %copy-start.2 = (f32[4,128,1024]{1,2,0:T(8,128)S(1)}, f32[4,128,1024]{1,2,0:T(8,128)}, u32[]{:S(2)}) copy-start(f32[4,128,1024]{1,2,0:T(8,128)} %fusion.36) | copy-start | bytes 6291460
  44.0 1.7 %copy-start.14 = (f32[4,128,16]{1,2,0:T(8,128)S(1)}, f32[4,128,16]{1,2,0:T(8,128)}, u32[]{:S(2)}) copy-start(f32[4,128,16]{1,2,0:T(8,128)} %exponential_bitcast_fusion) | copy-start | bytes 98308
  44.0 1.7 %copy-start.42 = (f32[16]{0:T(128)S(1)}, f32[16]{0:T(128)}, u32[]{:S(2)}) copy-start(f32[16]{0:T(128)} %param.28) | copy-start | bytes 196
  45.7 2.8 %copy-start.10 = (f32[16,64]{1,0:T(8,128)S(1)}, f32[16,64]{1,0:T(8,128)}, u32[]{:S(2)}) copy-start(f32[16,64]{1,0:T(8,128)} %mul.223) | copy-start | bytes 12292
  48.4 1.2 %copy-start.4 = (bf16[1024,512]{1,0:T(8,128)(2,1)S(1)}, bf16[1024,512]{1,0:T(8,128)(2,1)}, u32[]{:S(2)}) copy-start(bf16[1024,512]{1,0:T(8,128)(2,1)} %param.30) | copy-start | bytes 3145732
  49.0 2.4 %copy-start.9 = (bf16[4,512]{1,0:T(4,128)(2,1)S(1)}, bf16[4,512]{1,0:T(4,128)(2,1)}, u32[]{:S(2)}) copy-start(bf16[4,512]{1,0:T(4,128)(2,1)} %copy-done.8) | copy-start | bytes 12292
  49.0 2.4 %copy-start.19 = (s32[4,128]{1,0:T(4,128)S(1)}, s32[4,128]{1,0:T(4,128)}, u32[]{:S(2)}) copy-start(s32[4,128]{1,0:T(4,128)} %copy-done.18) | copy-start | bytes 6148
  49.7 2.1 %copy-start.34 = (bf16[512,1]{0,1:T(2,128)(2,1)S(1)}, bf16[512,1]{0,1:T(2,128)(2,1)}, u32[]{:S(2)}) copy-start(bf16[512,1]{0,1:T(2,128)(2,1)} %get-tuple-element.33) | copy-start | bytes 3076
  49.7 2.2 %copy-start.35 = (bf16[512,1]{0,1:T(2,128)(2,1)S(1)}, bf16[512,1]{0,1:T(2,128)(2,1)}, u32[]{:S(2)}) copy-start(bf16[512,1]{0,1:T(2,128)(2,1)} %get-tuple-element.34) | copy-start | bytes 3076
  49.7 2.2 %copy-start.38 = (f32[512]{0:T(512)S(1)}, f32[512]{0:T(512)}, u32[]{:S(2)}) copy-start(f32[512]{0:T(512)} %param.31) | copy-start | bytes 6148
  49.7 2.2 %copy-start.40 = (bf16[512,2]{0,1:T(2,128)(2,1)S(1)}, bf16[512,2]{0,1:T(2,128)(2,1)}, u32[]{:S(2)}) copy-start(bf16[512,2]{0,1:T(2,128)(2,1)} %param.32) | copy-start | bytes 6148
  49.7 2.5 %copy-start.33 = (s32[2,2,128]{2,1,0:T(2,128)S(1)}, s32[2,2,128]{2,1,0:T(2,128)}, u32[]{:S(2)}) copy-start(s32[2,2,128]{2,1,0:T(2,128)} %param.33) | copy-start | bytes 6148
  49.7 2.5 %copy-start.47 = (f32[2,2,128]{2,1,0:T(2,128)S(1)}, f32[2,2,128]{2,1,0:T(2,128)}, u32[]{:S(2)}) copy-start(f32[2,2,128]{2,1,0:T(2,128)} %fusion.27) | copy-start | bytes 6148
  (4 other events, 4.1 us)

commit v15 on v12

--- a/solution.py
+++ b/solution.py
@@ -241,9 +241,7 @@
     )
 
     oh_loc = onehot(local_gram, GRAMS)
-    x_loc = jnp.einsum("rtg,gc->rtc", oh_loc, x_tab, preferred_element_type=jnp.float32).astype(
-        jnp.bfloat16
-    )
+    x_loc = jnp.take(x_tab, local_gram, axis=0)
     bc_loc = jnp.einsum("rtg,gc->rtc", oh_loc, bc_tab, precision=HIGH)
     oh_tok = onehot(local_tok, BASES)
     z_loc = jnp.einsum("rtk,kc->rtc", oh_tok, z_rows, preferred_element_type=jnp.float32)

time: 53.3 us -> 61.7 us (1.16)
  local copies, waits for them, and re-layouts: 9.79 us -> 17.8 us
  other arithmetic: 8.79 us -> 10.6 us
  matrix products: 21.7 us -> 20.3 us
    gather x0 -> x3, local copies, waits for them, and re-layouts: none -> 8.4 us  [local(): x_loc = jnp.take(x_tab, local_gram, axis=0)]
    dot_general x1 -> x0, matrix products: 2.12 us -> none  [local(): jnp.einsum('rtg,gc->rtc', oh_loc, x_tab, preferred_element_type=jnp.float32)]
    dot_general x2, matrix products: 0.79 us -> 1.5 us  [block_cumsum(): return jnp.einsum('...s,st->...t', values, tri, precision=HIGH)]
    select_n x1, other arithmetic: 0.38 us -> 1.07 us  [needed_per_gram(): jnp.where(fwd_part, weight, 0.0)]
    convert_element_type x1 -> x0, local copies, waits for them, and re-layouts: 0.65 us -> none  [local(): jnp.einsum('rtg,gc->rtc', oh_loc, x_tab, preferred_element_type=jnp.float32)]
    select_n x1, other arithmetic: 0.08 us -> 0.71 us  [needed_per_gram(): jnp.where(fwd_part, 0.0, weight)]
    unnamed x101 -> x91, local copies, waits for them, and re-layouts: 2.25 us -> 2.53 us
  transfers between devices with their start and end apart: 4 -> 4, of which waited for: 2 -> 2; matrix products, arithmetic and copies ran while one was open for 32% -> 27% of each run, Pallas kernels for 0% -> 0%
where the time goes in v15:
time: 61.7 us; the launch traced here: 61.1 us
  matrix products  20.3 us (33%)
  local copies, waits for them, and re-layouts  17.8 us (29%)
  other arithmetic  10.6 us (17%)
  starting transfers between devices  8.29 us (13%)
  waiting for transfers between devices  2.6 us (4%)
  between operations  1.43 us (2%)
    gather x3, local copies, waits for them, and re-layouts, local(): x_loc = jnp.take(x_tab, local_gram, axis=0)  8.4 us
    ppermute x4, starting transfers between devices, gather_all(): lax.ppermute(held, axis, [(src, src ^ mask) for src in range(count)])  8.29 us
    dot_general x1, matrix products, local(): jnp.einsum('utn,uhpn->uthp', c_u, start_state, precision=lax.Precision.HIGH)  2.81 us
    ppermute x4, waiting for transfers between devices, gather_all(): lax.ppermute(held, axis, [(src, src ^ mask) for src in range(count)])  2.6 us
    unnamed x91, local copies, waits for them, and re-layouts  2.53 us
    slice x2, local copies, waits for them, and re-layouts, local(): b_tab = act_tab[:, INNER:INNER + NS]  2.36 us
    dot_general x1, matrix products, local(): jnp.einsum('rtk,kc->rtc', oh_tok, z_rows, preferred_element_type=jnp.floa...  2.07 us
    dot_general x1, matrix products, needed_per_gram(): jnp.einsum('whbs,wbsg->whg', jnp.concatenate([w_hi, w_lo], axis=1), oneho...  2.06 us
  transfers between devices with their start and end apart: 4, of which 2 were waited for; matrix products, arithmetic and copies ran while one was open for 27% of the time, Pallas kernels for 0%

profile of v15, /device:TPU:0, one launch (start us, length us, event | category | flops | bytes accessed | tf_op | source)
XLA Modules:
  0.0 61.1 jit_solution(1518972603410437504)
XLA Ops:
  0.7 1.0 %fusion.33 = s32[2,128]{1,0:T(2,128)S(1)} fusion(s32[2,128]{1,0:T(2,128)} %param.18), kind=kOutput, calls=%fused_computation.48 | convolution fusion | flops 99072 | bytes 2048 | tf_op jit(solution)/shard_map/dot_general | solution.py:224
  1.7 0.7 %pad_add_fusion.8 = s32[4,128]{1,0:T(4,128)S(1)} fusion(s32[2,128]{1,0:T(2,128)S(1)} %fusion.33, s32[2,128]{1,0:T(2,128)} %param.18), kind=kLoop, calls=%fused_computation.182 | loop fusion | flops 512 | bytes 4096 | tf_op jit(solution)/shard_map/concatenate | solution.py:227
  2.3 0.5 collective-permute-start
  2.8 0.7 %broadcast_compare_fusion.7 = (pred[4,128]{1,0:T(4,128)(4,1)S(1)}, pred[4,128]{1,0:T(4,128)(4,1)S(1)}, pred[4,128]{1,0:T(4,128)(4,1)S(1)}, pred[4,128]{1,0:T(4,128)(4,1)S(1)}) fusion(s32[2,128]{1,0:T(2,128)S(1)} %fusion.33, s32[2,128]{1,0:T(2,128)} %param.18), kind=kLoop, calls=%fused_computation.194 | loop fusion | flops 2560 | bytes 4096 | tf_op jit(solution)/shard_map/eq | solution.py:122
  3.5 0.9 %fusion.29 = bf16[2,512]{1,0:T(2,128)(2,1)S(1)} fusion(bf16[2,512]{1,0:T(2,128)(2,1)} %param.19), kind=kOutput, calls=%fused_computation.43 | convolution fusion | flops 1573888 | bytes 4096 | tf_op jit(solution)/shard_map/dot_general | solution.py:214
  4.4 0.8 %fusion.81 = (f32[4]{0:T(128)S(1)}, bf16[4,512]{1,0:T(4,128)(2,1)S(1)}) fusion(bf16[1,512]{1,0:T(2,128)(2,1)S(1)} %get-tuple-element.44, bf16[1,512]{1,0:T(2,128)(2,1)S(1)} %get-tuple-element.43, bf16[2,512]{1,0:T(2,128)(2,1)} %param.19), kind=kLoop, calls=%fused_computation.136 | loop fusion | flops 18428 | bytes 8208 | tf_op jit(solution)/shard_map/reduce_sum | solution.py:23
  5.2 1.0 %fusion.8 = f32[4,1152]{1,0:T(4,128)S(1)} fusion(bf16[512,1152]{1,0:T(8,128)(2,1)S(1)} %copy-done, bf16[4,512]{1,0:T(4,128)(2,1)S(1)} %get-tuple-element.7, f32[512]{0:T(512)} %param.20, f32[4]{0:T(128)S(1)} %add_rsqrt_fusion.2), kind=kOutput, calls=%fused_computation.14 | convolution fusion | flops 4736000 | bytes 1204240 | tf_op jit(solution)/shard_map/dot_general | solution.py:74
  6.2 0.8 %broadcast_multiply_fusion = f32[4,4,1152]{2,1,0:T(4,128)S(1)} fusion(f32[4,1152]{1,0:T(4,128)S(1)} %fusion.8, f32[4,1152]{1,0:T(4,128)} %param.24), kind=kLoop, calls=%fused_computation.107 | loop fusion | flops 18432 | bytes 110592 | tf_op jit(solution)/shard_map/mul | solution.py:77
  7.0 0.9 %fusion.112 = f32[4,16]{1,0:T(4,128)S(1)} fusion(bf16[512,16]{0,1:T(8,128)(2,1)} %param.23, bf16[4,512]{1,0:T(4,128)(2,1)S(1)} %get-tuple-element.7, f32[512]{0:T(512)} %param.20, f32[4]{0:T(128)S(1)} %add_rsqrt_fusion.2), kind=kOutput, calls=%fused_computation.217 | convolution fusion | flops 73728 | bytes 22800 | tf_op jit(solution)/shard_map/dot_general | solution.py:76
  8.0 0.7 %compare_select_fusion.2 = f32[4,16,128]{2,1,0:T(8,128)} fusion(f32[16]{0:T(128)S(1)} %copy-done.27, f32[16]{0:T(128)S(1)} %get-tuple-element.40, f32[16]{0:T(128)S(1)} %get-tuple-element.41, f32[16]{0:T(128)S(1)} %get-tuple-element.42, f32[16]{0:T(128)S(1)} %get-tuple-element.39, pred[4,128]{1,0:T(4,128)(4,1)S(1)} %get-tuple-element.37, ...), kind=kLoop, calls=%fused_computation.99 | loop fusion | flops 114688 | bytes 35136 | tf_op jit(solution)/shard_map/jit(softplus)/select_n | solution.py:248
  9.0 0.6 %exponential_bitcast_fusion = f32[4,128,16]{1,2,0:T(8,128)} fusion(f32[4,16,128]{2,1,0:T(8,128)S(1)} %fusion.72), kind=kLoop, calls=%fused_computation.116 | loop fusion | bytes 65536 | tf_op jit(solution)/shard_map/exp | solution.py:306
  9.6 2.1 %fusion.36 = f32[4,128,1024]{1,2,0:T(8,128)} fusion(bf16[512,1024]{1,0:T(8,128)(2,1)S(1)} %copy-done.3, s32[4,128]{1,0:T(4,128)S(1)} %pad_add_fusion.8, bf16[4,512]{1,0:T(4,128)(2,1)S(1)} %get-tuple-element.7, f32[512]{0:T(512)S(1)} %copy-done.18, f32[4]{0:T(128)S(1)} %add_rsqrt_fusion.2), kind=kOutput, calls=%fused_computation.57 | convolution fusion | flops 8402944 | bytes 3153936 | tf_op jit(solution)/shard_map/rtk,kc->rtc/dot_general | solution.py:247
  11.9 0.6 %fusion.117 = (bf16[512,1]{0,1:T(2,128)(2,1)}, bf16[512,1]{0,1:T(2,128)(2,1)}) fusion(bf16[512,2]{0,1:T(2,128)(2,1)S(1)} %convolution_convert_fusion.4), kind=kLoop, calls=%fused_computation.219 | loop fusion | bytes 4096 | tf_op jit(solution)/shard_map/slice | solution.py:332
  12.5 0.6 fusion.28
  13.1 1.6 %divide_multiply_fusion = f32[344,1152]{1,0:T(8,128)S(1)} fusion(f32[16,1152]{1,0:T(8,128)S(1)} %mul.198, f32[344,16]{1,0:T(8,128)S(1)} %copy-done.40, f32[1152]{0:T(1024)S(1)} %copy-done.32), kind=kOutput, calls=%fused_computation.29 | convolution fusion | flops 78068736 | bytes 1685504 | tf_op jit(solution)/shard_map/dot_general | solution.py:78
  14.9 2.6 %collective-permute-start.1 = (s32[4,256]{1,0:T(4,128)S(1)}, s32[4,256]{1,0:T(4,128)S(1)}, u32[]{:S(2)}, u32[]{:S(2)}) collective-permute-start(s32[4,256]{1,0:T(4,128)S(1)} %pad_add_fusion.7), channel_id=1, source_target_pairs={{0,2},{1,3},{2,0},{3,1},{4,6},{5,7},{6,4},{7,5},{8,10},{9,11},{10,... | collective-permute-start | bytes 12296 | tf_op jit(solution)/shard_map/ppermute | solution.py:103
  17.5 0.6 %convert_compare_fusion = pred[128,128]{1,0:T(8,128)(4,1)} fusion(), kind=kLoop, calls=%fused_computation.103 | loop fusion | flops 49152 | bytes 16384 | tf_op jit(solution)/shard_map/gt | solution.py:265
  18.1 1.0 %collective-permute-done.1 = s32[4,256]{1,0:T(4,128)S(1)} collective-permute-done((s32[4,256]{1,0:T(4,128)S(1)}, s32[4,256]{1,0:T(4,128)S(1)}, u32[]{:S(2)}, u32[]{:S(2)}) %collective-permute-start.1) | collective-permute-done | bytes 4128 | tf_op jit(solution)/shard_map/ppermute | solution.py:103
  19.1 2.1 %collective-permute-start.2 = (s32[4,512]{1,0:T(4,128)S(1)}, s32[4,512]{1,0:T(4,128)S(1)}, u32[]{:S(2)}, u32[]{:S(2)}) collective-permute-start(s32[4,512]{1,0:T(4,128)S(1)} %pad_add_fusion.5), channel_id=1, source_target_pairs={{0,4},{1,5},{2,6},{3,7},{4,0},{5,1},{6,2},{7,3},{8,12},{9,13},{10,... | collective-permute-start | bytes 24584 | tf_op jit(solution)/shard_map/ppermute | solution.py:103
  21.3 1.6 %collective-permute-done.2 = s32[4,512]{1,0:T(4,128)S(1)} collective-permute-done((s32[4,512]{1,0:T(4,128)S(1)}, s32[4,512]{1,0:T(4,128)S(1)}, u32[]{:S(2)}, u32[]{:S(2)}) %collective-permute-start.2) | collective-permute-done | bytes 8224 | tf_op jit(solution)/shard_map/ppermute | solution.py:103
  22.9 3.1 %collective-permute-start.3 = (s32[4,1024]{1,0:T(4,128)S(1)}, s32[4,1024]{1,0:T(4,128)S(1)}, u32[]{:S(2)}, u32[]{:S(2)}) collective-permute-start(s32[4,1024]{1,0:T(4,128)S(1)} %pad_add_fusion.3), channel_id=1, source_target_pairs={{0,8},{1,9},{2,10},{3,11},{4,12},{5,13},{6,14},{7,15},{8,0},{9,1},... | collective-permute-start | bytes 49160 | tf_op jit(solution)/shard_map/ppermute | solution.py:103
  26.2 0.7 %slice.206 = f32[344,64]{1,0:T(8,128)} slice(f32[344,1152]{1,0:T(8,128)S(1)} %divide_multiply_fusion), slice={[0:344], [1024:1088]} | slice | bytes 176128 | tf_op jit(solution)/shard_map/slice | solution.py:218
  26.8 1.2 %copy.39 = bf16[344,1024]{0,1:T(8,128)(2,1)} copy(bf16[344,1024]{1,0:T(8,128)(2,1)S(1)} %slice.254) | data formatting | bytes 1409024 | tf_op jit(solution)/shard_map/slice | solution.py:217
  28.0 1.7 %copy.38 = f32[344,64]{0,1:T(8,128)} copy(f32[344,64]{1,0:T(8,128)} %slice.206) | data formatting | bytes 176128 | tf_op jit(solution)/shard_map/slice | solution.py:218
  29.7 0.7 %mul.223 = f32[16,64]{1,0:T(8,128)} reshape(f32[1024]{0:T(1024)S(1)} %copy-done.26) | data formatting | bytes 8192 | tf_op jit(solution)/shard_map/mul | solution.py:23
  30.6 0.6 %slice_bitcast_fusion.7 = (s32[1,2,16,128]{3,1,2,0:T(2,128)S(1)}, s32[1,2,16,128]{3,1,2,0:T(2,128)}, s32[2,2048]{1,0:T(2,128)S(1)}, s32[2,2048]{1,0:T(2,128)S(1)}) fusion(s32[4,2048]{1,0:T(4,128)S(1)} %select_select_fusion), kind=kLoop, calls=%fused_computation.216 | loop fusion | bytes 98304
  31.2 0.5 compare_and_fusion
  31.8 1.2 %fusion.52 = f32[2,16,15,128]{3,1,2,0:T(8,128)S(1)} fusion(f32[16]{0:T(128)} %param.26, f32[16]{0:T(128)} %copy-done.23, f32[16]{0:T(128)} %copy-done.24, f32[16]{0:T(128)} %copy-done.25, f32[16]{0:T(128)} %copy-done.22, f32[16]{0:T(128)} %copy-done.41, pred[2,15,128]{2,1,0:T(8,128)(4,1)S(1)} %get-tuple-element.22, ...), kind=kOutput, calls=%fused_computation.75 | convolution fusion | flops 95309824 | bytes 261504 | tf_op jit(solution)/shard_map/...s,st->...t/dot_general | solution.py:143
  33.8 1.1 %broadcast_select_fusion.2 = (f32[2,16,15,128]{3,1,2,0:T(8,128)S(1)}, f32[2,16,15,128]{3,1,2,0:T(8,128)S(1)}) fusion(pred[15]{0:T(512)(128)(4,1)} %copy-done.21, f32[2,16,15]{1,2,0:T(8,128)S(1)} %copy.37, f32[16]{0:T(128)} %param.26, f32[16]{0:T(128)} %copy-done.23, pred[2,15,128]{2,1,0:T(8,128)(4,1)S(1)} %get-tuple-element.22, f32[16]{0:T(128)} %copy-done.24, ...), kind=kLoop, calls=%fused_computation.88 | loop fusion | flops 1105920 | bytes 756815 | tf_op jit(solution)/shard_map/jit(_where)/select_n | solution.py:171
  34.9 0.7 %broadcast_select_fusion.3 = f32[2,16,15,128]{3,1,2,0:T(8,128)S(1)} fusion(f32[2,16,15,128]{3,1,2,0:T(8,128)S(1)} %get-tuple-element.3, pred[15]{0:T(512)(128)(4,1)} %copy-done.21), kind=kLoop, calls=%fused_computation.90 | loop fusion | flops 61440 | bytes 491535 | tf_op jit(solution)/shard_map/jit(_where)/select_n | solution.py:171
  35.6 0.8 %fusion.46 = bf16[2,32,15,128]{3,1,2,0:T(8,128)(2,1)} fusion(f32[2,16,15,128]{3,1,2,0:T(8,128)S(1)} %broadcast_select_fusion.3, f32[2,16,15,128]{3,1,2,0:T(8,128)S(1)} %get-tuple-element.2), kind=kLoop, calls=%fused_computation.69 | loop fusion | flops 491520 | bytes 737280 | tf_op jit(solution)/shard_map/convert_element_type | solution.py:138
  36.3 0.7 %subtract_convert_fusion = bf16[2,32,15,128]{3,1,2,0:T(8,128)(2,1)} fusion(f32[2,16,15,128]{3,1,2,0:T(8,128)S(1)} %broadcast_select_fusion.3, f32[2,16,15,128]{3,1,2,0:T(8,128)S(1)} %get-tuple-element.2), kind=kLoop, calls=%fused_computation.68 | loop fusion | flops 614400 | bytes 737280 | tf_op jit(solution)/shard_map/convert_element_type | solution.py:139
  37.1 1.3 %fusion.35 = f32[4,128,128]{1,2,0:T(8,128)S(1)} fusion(s32[4,128]{1,0:T(4,128)S(1)} %pad_add_fusion.9, f32[344,1152]{1,0:T(8,128)} %copy-done.6), kind=kOutput, calls=%fused_computation.54 | convolution fusion | flops 270708736 | bytes 440320 | tf_op jit(solution)/shard_map/rtg,gc->rtc/dot_general | solution.py:245
  38.4 1.1 %fusion.54 = f32[4,128,128]{2,1,0:T(8,128)} fusion(f32[4,128,128]{1,2,0:T(8,128)S(1)} %fusion.35), kind=kOutput, calls=%fused_computation.79 | convolution fusion | flops 25165824 | bytes 524288 | tf_op jit(solution)/shard_map/utn,usn->uts/dot_general | solution.py:263
  39.5 3.0 %gather_fusion = bf16[512,1024]{1,0:T(8,128)(2,1)} fusion(bf16[344,1024]{1,0:T(8,128)(2,1)S(1)} %slice.254, s32[1024]{0:T(1024)S(1)} %pad_clamp_fusion), kind=kCustom, calls=%fused_computation | custom fusion | bytes 2099200 | tf_op jit(solution)/shard_map/jit(_take)/gather | solution.py:244
  42.5 2.9 %reshape.366 = bf16[4,128,16,64]{3,2,1,0:T(8,128)(2,1)S(1)} reshape(bf16[512,1024]{1,0:T(8,128)(2,1)} %gather_fusion) | data formatting | bytes 2097152 | tf_op jit(solution)/shard_map/jit(_take)/gather | solution.py:244
  45.5 2.5 %copy.34 = bf16[4,128,16,64]{1,3,2,0:T(8,128)(2,1)} copy(bf16[4,128,16,64]{3,2,1,0:T(8,128)(2,1)S(1)} %reshape.366) | data formatting | bytes 2097152 | tf_op jit(solution)/shard_map/jit(_take)/gather | solution.py:244
  48.0 0.8 %copy.60 = s32[1,2,16,128]{3,2,1,0:T(8,128)S(1)} copy(s32[1,2,16,128]{3,1,2,0:T(2,128)} %get-tuple-element.13) | data formatting | bytes 32768
  48.8 2.1 %fusion.26 = f32[2,64,344]{2,1,0:T(8,128)S(1)} fusion(s32[2,15,128]{2,1,0:T(8,128)S(1)} %fusion.78, bf16[2,32,15,128]{3,1,2,0:T(8,128)(2,1)} %subtract_convert_fusion, bf16[2,32,15,128]{3,1,2,0:T(8,128)(2,1)} %fusion.46), kind=kOutput, calls=%fused_computation.37 | convolution fusion | flops 171386880 | bytes 683008 | tf_op jit(solution)/shard_map/whbs,wbsg->whg/dot_general | solution.py:174
  51.0 1.0 %fusion.3 = f32[16,4,64,64]{3,2,0,1:T(8,128)S(1)} fusion(bf16[16,344,64,1]{1,2,0,3:T(8,128)(2,1)S(1)} %bitcast.111, f32[344,64]{0,1:T(8,128)S(1)} %copy-done.8, f32[4,16,344]{2,1,0:T(8,128)S(1)} %pad_maximum_fusion.1), kind=kOutput, calls=%fused_computation.7 | convolution fusion | flops 183173120 | bytes 1929216 | tf_op jit(solution)/shard_map/hgp,uhgn->uhpn/dot_general | solution.py:302
  52.2 1.6 %fusion.9 = f32[4,16,64,128]{3,2,1,0:T(8,128)S(1)} fusion(f32[4,16,128]{2,1,0:T(8,128)S(1)} %copy-done.12, f32[4,16,128]{2,1,0:T(8,128)S(1)} %copy-done.14, f32[4,128,128]{2,1,0:T(8,128)S(1)} %copy-done.7, pred[128,128]{1,0:T(8,128)(4,1)S(1)} %copy-done.16, bf16[4,128,16,64]{1,3,2,0:T(8,128)(2,1)S(1)} %copy-done.2, pred[4,128]{1,0:T(4,128)(4,1)S(1)} %copy-done.31), kind=kOutput, calls=%fused_computation.15 | convolution fusion | flops 141033472 | bytes 3490304 | tf_op jit(solution)/shard_map/uhts,ushp->uthp/dot_general | solution.py:268
  53.9 2.8 %multiply_reduce_fusion = (f32[4,128,16]{1,2,0:T(8,128)S(1)}, f32[4,128,16,64]{1,3,2,0:T(8,128)S(1)}) fusion(f32[4,128,16,64]{1,3,2,0:T(8,128)S(1)} %bitcast.110, bf16[4,128,16,64]{1,3,2,0:T(8,128)(2,1)S(1)} %copy-done.2, pred[4,128]{1,0:T(4,128)(4,1)S(1)} %copy-done.31, f32[16]{0:T(128)S(1)} %copy-done.38, f32[4,128,16]{1,2,0:T(8,128)S(1)} %copy-done.15, ...), kind=kOutput, calls=%fused_computation.22 | convolution fusion | flops 208134144 | bytes 9634816 | tf_op jit(solution)/shard_map/utn,uhpn->uthp/dot_general | solution.py:305
  56.8 0.5 multiply_convert_fusion.4
  57.3 0.7 %copy-done.4 = bf16[1024,512]{1,0:T(8,128)(2,1)S(1)} copy-done((bf16[1024,512]{1,0:T(8,128)(2,1)S(1)}, bf16[1024,512]{1,0:T(8,128)(2,1)}, u32[]{:S(2)}) %copy-start.4) | copy-done | bytes 1048600
  58.0 0.7 %convolution_convert_fusion.1 = bf16[4,128,512]{2,1,0:T(8,128)(2,1)S(1)} fusion(bf16[4,128,1024]{1,2,0:T(8,128)(2,1)S(1)} %bitcast.109, bf16[1024,512]{1,0:T(8,128)(2,1)S(1)} %copy-done.4), kind=kOutput, calls=%fused_computation.31 | convolution fusion | flops 537133056 | bytes 2621440 | tf_op jit(solution)/shard_map/gre,ed->grd/dot_general | solution.py:315
  58.8 0.9 %rev.11 = bf16[2,128,512]{2,1,0:T(8,128)(2,1)S(1)} reverse(bf16[2,128,512]{2,1,0:T(8,128)(2,1)S(1)} %slice.208), dimensions={1,2} | reverse | bytes 524288 | tf_op jit(solution)/shard_map/rev | solution.py:322
  59.7 0.4 fusion.37
  60.5 0.6 multiply_reduce_fusion.1
  (142 shorter events, 2.6 us)
Async XLA Ops:
  0.6 4.6 %copy-start = (bf16[512,1152]{1,0:T(8,128)(2,1)S(1)}, bf16[512,1152]{1,0:T(8,128)(2,1)}, u32[]{:S(2)}) copy-start(bf16[512,1152]{1,0:T(8,128)(2,1)} %param.21) | copy-start | bytes 3538948
  0.6 9.0 %copy-start.18 = (f32[512]{0:T(512)S(1)}, f32[512]{0:T(512)}, u32[]{:S(2)}) copy-start(f32[512]{0:T(512)} %param.20) | copy-start | bytes 6148
  0.7 7.3 %copy-start.37 = (f32[16]{0:T(128)S(1)}, f32[16]{0:T(128)}, u32[]{:S(2)}) copy-start(f32[16]{0:T(128)} %param.27) | copy-start | bytes 196
  0.7 7.3 %copy-start.27 = (f32[16]{0:T(128)S(1)}, f32[16]{0:T(128)}, u32[]{:S(2)}) copy-start(f32[16]{0:T(128)} %param.26) | copy-start | bytes 196
  0.7 8.9 %copy-start.3 = (bf16[512,1024]{1,0:T(8,128)(2,1)S(1)}, bf16[512,1024]{1,0:T(8,128)(2,1)}, u32[]{:S(2)}) copy-start(bf16[512,1024]{1,0:T(8,128)(2,1)} %param.22) | copy-start | bytes 3145732
  2.3 9.3 %copy-start.19 = (s32[4,128]{1,0:T(4,128)}, s32[4,128]{1,0:T(4,128)S(1)}, u32[]{:S(2)}) copy-start(s32[4,128]{1,0:T(4,128)S(1)} %pad_add_fusion.8) | copy-start | bytes 6148
  2.3 12.5 %collective-permute-start = (s32[4,128]{1,0:T(4,128)S(1)}, s32[4,128]{1,0:T(4,128)S(1)}, u32[]{:S(2)}, u32[]{:S(2)}) collective-permute-start(s32[4,128]{1,0:T(4,128)S(1)} %pad_add_fusion.8), channel_id=1, source_target_pairs={{0,1},{1,0},{2,3},{3,2},{4,5},{5,4},{6,7},{7,6},{8,9},{9,8},{10,11... | collective-permute-start | bytes 6152 | tf_op jit(solution)/shard_map/ppermute | solution.py:103
  5.2 6.5 %copy-start.9 = (bf16[4,512]{1,0:T(4,128)(2,1)}, bf16[4,512]{1,0:T(4,128)(2,1)S(1)}, u32[]{:S(2)}) copy-start(bf16[4,512]{1,0:T(4,128)(2,1)S(1)} %get-tuple-element.7) | copy-start | bytes 12292
  6.2 5.5 %copy-start.35 = (bf16[512,2]{0,1:T(2,128)(2,1)S(1)}, bf16[512,2]{0,1:T(2,128)(2,1)}, u32[]{:S(2)}) copy-start(bf16[512,2]{0,1:T(2,128)(2,1)} %param.32) | copy-start | bytes 6148
  7.9 4.6 %copy-start.33 = (f32[2,2,128]{2,1,0:T(2,128)S(1)}, f32[2,2,128]{2,1,0:T(2,128)}, u32[]{:S(2)}) copy-start(f32[2,2,128]{2,1,0:T(2,128)} %param.34) | copy-start | bytes 6148
  7.9 5.2 %copy-start.32 = (f32[1152]{0:T(1024)S(1)}, f32[1152]{0:T(1024)}, u32[]{:S(2)}) copy-start(f32[1152]{0:T(1024)} %param.25) | copy-start | bytes 13828
  7.9 5.2 %copy-start.40 = (f32[344,16]{1,0:T(8,128)S(1)}, f32[344,16]{1,0:T(8,128)}, u32[]{:S(2)}) copy-start(f32[344,16]{1,0:T(8,128)} %constant.150.clone) | copy-start | bytes 66052
  7.9 4.6 %copy-start.22 = (f32[16]{0:T(128)}, f32[16]{0:T(128)S(1)}, u32[]{:S(2)}) copy-start(f32[16]{0:T(128)S(1)} %get-tuple-element.39) | copy-start | bytes 196
  7.9 4.6 %copy-start.23 = (f32[16]{0:T(128)}, f32[16]{0:T(128)S(1)}, u32[]{:S(2)}) copy-start(f32[16]{0:T(128)S(1)} %get-tuple-element.40) | copy-start | bytes 196
  7.9 4.5 %copy-start.24 = (f32[16]{0:T(128)}, f32[16]{0:T(128)S(1)}, u32[]{:S(2)}) copy-start(f32[16]{0:T(128)S(1)} %get-tuple-element.41) | copy-start | bytes 196
  8.0 4.5 %copy-start.25 = (f32[16]{0:T(128)}, f32[16]{0:T(128)S(1)}, u32[]{:S(2)}) copy-start(f32[16]{0:T(128)S(1)} %get-tuple-element.42) | copy-start | bytes 196
  8.0 4.5 %copy-start.41 = (f32[16]{0:T(128)}, f32[16]{0:T(128)S(1)}, u32[]{:S(2)}) copy-start(f32[16]{0:T(128)S(1)} %exponential_negate_fusion) | copy-start | bytes 196
  9.0 3.6 %copy-start.13 = (f32[4,16,128]{2,1,0:T(8,128)}, f32[4,16,128]{2,1,0:T(8,128)S(1)}, u32[]{:S(2)}) copy-start(f32[4,16,128]{2,1,0:T(8,128)S(1)} %fusion.72) | copy-start | bytes 98308
  9.0 5.8 %copy-start.21 = (pred[15]{0:T(512)(128)(4,1)}, pred[15]{0:T(512)(128)(4,1)S(1)}, u32[]{:S(2)}) copy-start(pred[15]{0:T(512)(128)(4,1)S(1)} %iota_compare_fusion.18) | copy-start | bytes 49
  13.1 1.7 %copy-start.17 = (s32[2,128]{1,0:T(2,128)S(1)}, s32[2,128]{1,0:T(2,128)}, u32[]{:S(2)}) copy-start(s32[2,128]{1,0:T(2,128)} %param.18) | copy-start | bytes 3076
  14.7 15.6 %copy-start.6 = (f32[344,1152]{1,0:T(8,128)}, f32[344,1152]{1,0:T(8,128)S(1)}, u32[]{:S(2)}) copy-start(f32[344,1152]{1,0:T(8,128)S(1)} %divide_multiply_fusion) | copy-start | bytes 4755460
  14.8 14.9 %copy-start.26 = (f32[1024]{0:T(1024)S(1)}, f32[1024]{0:T(1024)}, u32[]{:S(2)}) copy-start(f32[1024]{0:T(1024)} %param.29) | copy-start | bytes 12292
  14.9 4.2 %collective-permute-start.1 = (s32[4,256]{1,0:T(4,128)S(1)}, s32[4,256]{1,0:T(4,128)S(1)}, u32[]{:S(2)}, u32[]{:S(2)}) collective-permute-start(s32[4,256]{1,0:T(4,128)S(1)} %pad_add_fusion.7), channel_id=1, source_target_pairs={{0,2},{1,3},{2,0},{3,1},{4,6},{5,7},{6,4},{7,5},{8,10},{9,11},{10,... | collective-permute-start | bytes 12296 | tf_op jit(solution)/shard_map/ppermute | solution.py:103
  19.1 3.8 %collective-permute-start.2 = (s32[4,512]{1,0:T(4,128)S(1)}, s32[4,512]{1,0:T(4,128)S(1)}, u32[]{:S(2)}, u32[]{:S(2)}) collective-permute-start(s32[4,512]{1,0:T(4,128)S(1)} %pad_add_fusion.5), channel_id=1, source_target_pairs={{0,4},{1,5},{2,6},{3,7},{4,0},{5,1},{6,2},{7,3},{8,12},{9,13},{10,... | collective-permute-start | bytes 24584 | tf_op jit(solution)/shard_map/ppermute | solution.py:103
  22.9 7.4 %collective-permute-start.3 = (s32[4,1024]{1,0:T(4,128)S(1)}, s32[4,1024]{1,0:T(4,128)S(1)}, u32[]{:S(2)}, u32[]{:S(2)}) collective-permute-start(s32[4,1024]{1,0:T(4,128)S(1)} %pad_add_fusion.3), channel_id=1, source_target_pairs={{0,8},{1,9},{2,10},{3,11},{4,12},{5,13},{6,14},{7,15},{8,0},{9,1},... | collective-permute-start | bytes 49160 | tf_op jit(solution)/shard_map/ppermute | solution.py:103
  48.0 3.0 %copy-start.5 = (bf16[344,1024]{0,1:T(8,128)(2,1)S(1)}, bf16[344,1024]{0,1:T(8,128)(2,1)}, u32[]{:S(2)}) copy-start(bf16[344,1024]{0,1:T(8,128)(2,1)} %copy.39) | copy-start | bytes 2113540
  48.0 3.0 %copy-start.8 = (f32[344,64]{0,1:T(8,128)S(1)}, f32[344,64]{0,1:T(8,128)}, u32[]{:S(2)}) copy-start(f32[344,64]{0,1:T(8,128)} %copy.38) | copy-start | bytes 264196
  50.9 1.2 %copy-start.2 = (bf16[4,128,16,64]{1,3,2,0:T(8,128)(2,1)S(1)}, bf16[4,128,16,64]{1,3,2,0:T(8,128)(2,1)}, u32[]{:S(2)}) copy-start(bf16[4,128,16,64]{1,3,2,0:T(8,128)(2,1)} %copy.34) | copy-start | bytes 3145732
  50.9 1.3 %copy-start.7 = (f32[4,128,128]{2,1,0:T(8,128)S(1)}, f32[4,128,128]{2,1,0:T(8,128)}, u32[]{:S(2)}) copy-start(f32[4,128,128]{2,1,0:T(8,128)} %fusion.54) | copy-start | bytes 786436
  51.0 1.2 %copy-start.12 = (f32[4,16,128]{2,1,0:T(8,128)S(1)}, f32[4,16,128]{2,1,0:T(8,128)}, u32[]{:S(2)}) copy-start(f32[4,16,128]{2,1,0:T(8,128)} %compare_select_fusion.2) | copy-start | bytes 98308
  51.0 1.2 %copy-start.14 = (f32[4,16,128]{2,1,0:T(8,128)S(1)}, f32[4,16,128]{2,1,0:T(8,128)}, u32[]{:S(2)}) copy-start(f32[4,16,128]{2,1,0:T(8,128)} %copy-done.13) | copy-start | bytes 98308
  51.0 1.2 %copy-start.16 = (pred[128,128]{1,0:T(8,128)(4,1)S(1)}, pred[128,128]{1,0:T(8,128)(4,1)}, u32[]{:S(2)}) copy-start(pred[128,128]{1,0:T(8,128)(4,1)} %convert_compare_fusion) | copy-start | bytes 49156
  51.0 1.2 %copy-start.31 = (pred[4,128]{1,0:T(4,128)(4,1)S(1)}, pred[4,128]{1,0:T(4,128)(4,1)}, u32[]{:S(2)}) copy-start(pred[4,128]{1,0:T(4,128)(4,1)} %compare_and_fusion) | copy-start | bytes 1540
  52.2 1.7 %copy-start.1 = (f32[4,128,1024]{1,2,0:T(8,128)S(1)}, f32[4,128,1024]{1,2,0:T(8,128)}, u32[]{:S(2)}) copy-start(f32[4,128,1024]{1,2,0:T(8,128)} %fusion.36) | copy-start | bytes 6291460
  52.2 1.7 %copy-start.15 = (f32[4,128,16]{1,2,0:T(8,128)S(1)}, f32[4,128,16]{1,2,0:T(8,128)}, u32[]{:S(2)}) copy-start(f32[4,128,16]{1,2,0:T(8,128)} %exponential_bitcast_fusion) | copy-start | bytes 98308
  52.2 1.7 %copy-start.38 = (f32[16]{0:T(128)S(1)}, f32[16]{0:T(128)}, u32[]{:S(2)}) copy-start(f32[16]{0:T(128)} %param.28) | copy-start | bytes 196
  53.9 2.9 %copy-start.11 = (f32[16,64]{1,0:T(8,128)S(1)}, f32[16,64]{1,0:T(8,128)}, u32[]{:S(2)}) copy-start(f32[16,64]{1,0:T(8,128)} %mul.223) | copy-start | bytes 12292
  56.7 1.2 %copy-start.4 = (bf16[1024,512]{1,0:T(8,128)(2,1)S(1)}, bf16[1024,512]{1,0:T(8,128)(2,1)}, u32[]{:S(2)}) copy-start(bf16[1024,512]{1,0:T(8,128)(2,1)} %param.30) | copy-start | bytes 3145732
  57.3 2.4 %copy-start.10 = (bf16[4,512]{1,0:T(4,128)(2,1)S(1)}, bf16[4,512]{1,0:T(4,128)(2,1)}, u32[]{:S(2)}) copy-start(bf16[4,512]{1,0:T(4,128)(2,1)} %copy-done.9) | copy-start | bytes 12292
  57.3 2.4 %copy-start.20 = (s32[4,128]{1,0:T(4,128)S(1)}, s32[4,128]{1,0:T(4,128)}, u32[]{:S(2)}) copy-start(s32[4,128]{1,0:T(4,128)} %copy-done.19) | copy-start | bytes 6148
  58.0 2.1 %copy-start.29 = (bf16[512,1]{0,1:T(2,128)(2,1)S(1)}, bf16[512,1]{0,1:T(2,128)(2,1)}, u32[]{:S(2)}) copy-start(bf16[512,1]{0,1:T(2,128)(2,1)} %get-tuple-element.33) | copy-start | bytes 3076
  58.0 2.1 %copy-start.30 = (bf16[512,1]{0,1:T(2,128)(2,1)S(1)}, bf16[512,1]{0,1:T(2,128)(2,1)}, u32[]{:S(2)}) copy-start(bf16[512,1]{0,1:T(2,128)(2,1)} %get-tuple-element.34) | copy-start | bytes 3076
  58.0 2.2 %copy-start.34 = (f32[512]{0:T(512)S(1)}, f32[512]{0:T(512)}, u32[]{:S(2)}) copy-start(f32[512]{0:T(512)} %param.31) | copy-start | bytes 6148
  58.0 2.2 %copy-start.36 = (bf16[512,2]{0,1:T(2,128)(2,1)S(1)}, bf16[512,2]{0,1:T(2,128)(2,1)}, u32[]{:S(2)}) copy-start(bf16[512,2]{0,1:T(2,128)(2,1)} %param.32) | copy-start | bytes 6148
  58.0 2.5 %copy-start.28 = (s32[2,2,128]{2,1,0:T(2,128)S(1)}, s32[2,2,128]{2,1,0:T(2,128)}, u32[]{:S(2)}) copy-start(s32[2,2,128]{2,1,0:T(2,128)} %param.33) | copy-start | bytes 6148
  58.0 2.5 %copy-start.42 = (f32[2,2,128]{2,1,0:T(2,128)S(1)}, f32[2,2,128]{2,1,0:T(2,128)}, u32[]{:S(2)}) copy-start(f32[2,2,128]{2,1,0:T(2,128)} %fusion.28) | copy-start | bytes 6148
  60.1 1.0 %copy-start.39 = (bf16[2,128,512]{2,1,0:T(8,128)(2,1)}, bf16[2,128,512]{2,1,0:T(8,128)(2,1)S(1)}, u32[]{:S(2)}) copy-start(bf16[2,128,512]{2,1,0:T(8,128)(2,1)S(1)} %get-tuple-element.48) | copy-start | bytes 786436

commit v16 on v12

--- a/solution.py
+++ b/solution.py
@@ -51,6 +51,10 @@
         "gshp,gsn->ghpn", x_weighted, b_blk, precision=HIGH
     )
     return (new_state, y_intra + y_inter)
+
+
+def silu(values):
+    return values * (0.5 * jnp.tanh(0.5 * values) + 0.5)
 
 
 def gram_layout():
@@ -76,7 +80,7 @@
     dt_rows = jnp.dot(row_norm, w_dt, preferred_element_type=jnp.float32)
     taps = (conv_w[:, None, :] * xbc_rows.astype(jnp.float32)[None]).reshape(KW * BASES, CONVW)
     conv_sum = conv_bias + jnp.dot(jnp.asarray(gram_layout()), taps, precision=HIGH)
-    return jax.nn.silu(conv_sum), z_rows, dt_rows
+    return silu(conv_sum), z_rows, dt_rows
 
 
 def gram_ids(ext, where_in):
@@ -309,7 +313,7 @@
     )
     y_u = y_intra + y_inter + d_skip[:, None] * x_u.astype(jnp.float32)
     z_u = per_unit(z_loc, 1).reshape(units, BLK, HEADS, HD)
-    gated_y = y_u * jax.nn.silu(z_u)
+    gated_y = y_u * silu(z_u)
     normed = rms_gain(gated_y, inner_gain.reshape(HEADS, HD)).astype(jnp.bfloat16)
     normed = jnp.moveaxis(normed.reshape(streams, nloc, BLK, INNER), 1, 1).reshape(
         streams, count, INNER

time: 53.3 us -> 69.5 us (1.30)
  local copies, waits for them, and re-layouts: 9.79 us -> 19.6 us
  other arithmetic: 8.79 us -> 12.4 us
  matrix products: 21.7 us -> 24.4 us
    slice x2, local copies, waits for them, and re-layouts: 1.26 us -> 4.6 us  [local(): x_tab = act_tab[:, :INNER].astype(jnp.bfloat16)]
    unnamed x101 -> x95, local copies, waits for them, and re-layouts: 2.25 us -> 5.03 us
    dot_general x1, matrix products: 1.6 us -> 3.69 us  [gram_tables(): jnp.dot(jnp.asarray(gram_layout()), taps, precision=HIGH)]
    rev x2, local copies, waits for them, and re-layouts: 0.02 us -> 2.03 us  [arranged(): rc = values[windows:].reshape(windows, nblk, BLK)[:, ::-1]]
    convert_element_type x1, local copies, waits for them, and re-layouts: 0.65 us -> 2.3 us  [local(): jnp.einsum('rtg,gc->rtc', oh_loc, x_tab, preferred_element_type=jnp.float32)]
    slice x2, local copies, waits for them, and re-layouts: 0.36 us -> 2 us  [needed_per_gram(): blk_total = cum[..., -1]]
    slice x2 -> x3, local copies, waits for them, and re-layouts: 2.36 us -> 0.76 us  [local(): b_tab = act_tab[:, INNER:INNER + NS]]
    select_n x1, other arithmetic: 0.38 us -> 1.39 us  [needed_per_gram(): jnp.where(fwd_part, weight, 0.0)]
  transfers between devices with their start and end apart: 4 -> 4, of which waited for: 2 -> 2; matrix products, arithmetic and copies ran while one was open for 32% -> 30% of each run, Pallas kernels for 0% -> 0%
where the time goes in v16:
time: 69.5 us; the launch traced here: 68.6 us
  matrix products  24.4 us (35%)
  local copies, waits for them, and re-layouts  19.6 us (28%)
  other arithmetic  12.4 us (18%)
  starting transfers between devices  8.29 us (12%)
  waiting for transfers between devices  2.6 us (4%)
  between operations  1.39 us (2%)
    ppermute x4, starting transfers between devices, gather_all(): lax.ppermute(held, axis, [(src, src ^ mask) for src in range(count)])  8.29 us
    unnamed x95, local copies, waits for them, and re-layouts  5.03 us
    slice x2, local copies, waits for them, and re-layouts, local(): x_tab = act_tab[:, :INNER].astype(jnp.bfloat16)  4.6 us
    dot_general x1, matrix products, gram_tables(): jnp.dot(jnp.asarray(gram_layout()), taps, precision=HIGH)  3.69 us
    dot_general x1, matrix products, local(): jnp.einsum('rtg,gc->rtc', oh_loc, x_tab, preferred_element_type=jnp.float32)  3.09 us
    dot_general x1, matrix products, local(): jnp.einsum('utn,uhpn->uthp', c_u, start_state, precision=lax.Precision.HIGH)  2.74 us
    ppermute x4, waiting for transfers between devices, gather_all(): lax.ppermute(held, axis, [(src, src ^ mask) for src in range(count)])  2.6 us
    convert_element_type x1, local copies, waits for them, and re-layouts, local(): jnp.einsum('rtg,gc->rtc', oh_loc, x_tab, preferred_element_type=jnp.float32)  2.3 us
  transfers between devices with their start and end apart: 4, of which 2 were waited for; matrix products, arithmetic and copies ran while one was open for 30% of the time, Pallas kernels for 0%

profile of v16, /device:TPU:0, one launch (start us, length us, event | category | flops | bytes accessed | tf_op | source)
XLA Modules:
  0.0 68.6 jit_solution(17446655074490394815)
XLA Ops:
  0.7 0.9 %fusion.33 = s32[2,128]{1,0:T(2,128)S(1)} fusion(s32[2,128]{1,0:T(2,128)} %param.18), kind=kOutput, calls=%fused_computation.48 | convolution fusion | flops 99072 | bytes 2048 | tf_op jit(solution)/shard_map/dot_general | solution.py:228
  1.6 0.7 %pad_add_fusion.8 = s32[4,128]{1,0:T(4,128)S(1)} fusion(s32[2,128]{1,0:T(2,128)S(1)} %fusion.33, s32[2,128]{1,0:T(2,128)} %param.18), kind=kLoop, calls=%fused_computation.178 | loop fusion | flops 512 | bytes 4096 | tf_op jit(solution)/shard_map/concatenate | solution.py:231
  2.7 0.7 %broadcast_compare_fusion.7 = (pred[4,128]{1,0:T(4,128)(4,1)S(1)}, pred[4,128]{1,0:T(4,128)(4,1)S(1)}, pred[4,128]{1,0:T(4,128)(4,1)S(1)}, pred[4,128]{1,0:T(4,128)(4,1)S(1)}) fusion(s32[2,128]{1,0:T(2,128)S(1)} %fusion.33, s32[2,128]{1,0:T(2,128)} %param.18), kind=kLoop, calls=%fused_computation.189 | loop fusion | flops 2560 | bytes 4096 | tf_op jit(solution)/shard_map/eq | solution.py:126
  3.4 0.9 %fusion.29 = bf16[2,512]{1,0:T(2,128)(2,1)S(1)} fusion(bf16[2,512]{1,0:T(2,128)(2,1)} %param.19), kind=kOutput, calls=%fused_computation.43 | convolution fusion | flops 1573888 | bytes 4096 | tf_op jit(solution)/shard_map/dot_general | solution.py:218
  4.3 0.8 %fusion.82 = (f32[4]{0:T(128)S(1)}, bf16[4,512]{1,0:T(4,128)(2,1)S(1)}) fusion(bf16[1,512]{1,0:T(2,128)(2,1)S(1)} %get-tuple-element.44, bf16[1,512]{1,0:T(2,128)(2,1)S(1)} %get-tuple-element.43, bf16[2,512]{1,0:T(2,128)(2,1)} %param.19), kind=kLoop, calls=%fused_computation.136 | loop fusion | flops 18428 | bytes 8208 | tf_op jit(solution)/shard_map/reduce_sum | solution.py:23
  5.1 1.0 %fusion.8 = f32[4,1152]{1,0:T(4,128)S(1)} fusion(bf16[512,1152]{1,0:T(8,128)(2,1)S(1)} %copy-done, bf16[4,512]{1,0:T(4,128)(2,1)S(1)} %get-tuple-element.7, f32[512]{0:T(512)} %param.20, f32[4]{0:T(128)S(1)} %add_rsqrt_fusion.2), kind=kOutput, calls=%fused_computation.13 | convolution fusion | flops 4736000 | bytes 1204240 | tf_op jit(solution)/shard_map/dot_general | solution.py:78
  6.1 0.8 %broadcast_multiply_fusion = f32[4,4,1152]{2,1,0:T(4,128)S(1)} fusion(f32[4,1152]{1,0:T(4,128)S(1)} %fusion.8, f32[4,1152]{1,0:T(4,128)} %param.24), kind=kLoop, calls=%fused_computation.107 | loop fusion | flops 18432 | bytes 110592 | tf_op jit(solution)/shard_map/mul | solution.py:81
  6.9 0.9 %fusion.111 = f32[4,16]{1,0:T(4,128)S(1)} fusion(bf16[512,16]{0,1:T(8,128)(2,1)} %param.23, bf16[4,512]{1,0:T(4,128)(2,1)S(1)} %get-tuple-element.7, f32[512]{0:T(512)} %param.20, f32[4]{0:T(128)S(1)} %add_rsqrt_fusion.2), kind=kOutput, calls=%fused_computation.211 | convolution fusion | flops 73728 | bytes 22800 | tf_op jit(solution)/shard_map/dot_general | solution.py:80
  7.9 0.7 %compare_select_fusion.2 = f32[4,16,128]{2,1,0:T(8,128)} fusion(f32[16]{0:T(128)S(1)} %copy-done.31, f32[16]{0:T(128)S(1)} %get-tuple-element.40, f32[16]{0:T(128)S(1)} %get-tuple-element.41, f32[16]{0:T(128)S(1)} %get-tuple-element.42, f32[16]{0:T(128)S(1)} %get-tuple-element.39, pred[4,128]{1,0:T(4,128)(4,1)S(1)} %get-tuple-element.37, ...), kind=kLoop, calls=%fused_computation.99 | loop fusion | flops 114688 | bytes 35136 | tf_op jit(solution)/shard_map/jit(softplus)/select_n | solution.py:254
  9.5 0.6 exponential_bitcast_fusion
  10.1 1.9 %fusion.37 = f32[4,128,1024]{1,2,0:T(8,128)S(1)} fusion(bf16[512,1024]{1,0:T(8,128)(2,1)} %param.22, s32[4,128]{1,0:T(4,128)S(1)} %pad_add_fusion.8, bf16[4,512]{1,0:T(4,128)(2,1)S(1)} %get-tuple-element.7, f32[512]{0:T(512)S(1)} %copy-done.22, f32[4]{0:T(128)S(1)} %add_rsqrt_fusion.2), kind=kOutput, calls=%fused_computation.57 | convolution fusion | flops 8402944 | bytes 3153936 | tf_op jit(solution)/shard_map/rtk,kc->rtc/dot_general | solution.py:253
  13.5 3.7 %add_multiply_fusion = f32[344,1152]{1,0:T(8,128)} fusion(f32[16,1152]{1,0:T(8,128)S(1)} %mul.208, f32[344,16]{1,0:T(8,128)} %constant.133.clone, f32[1152]{0:T(1024)S(1)} %copy-done.36), kind=kOutput, calls=%fused_computation.28 | convolution fusion | flops 78068736 | bytes 1685504 | tf_op jit(solution)/shard_map/dot_general | solution.py:82
  17.2 0.7 fusion.85
  17.9 2.6 %collective-permute-start.1 = (s32[4,256]{1,0:T(4,128)S(1)}, s32[4,256]{1,0:T(4,128)S(1)}, u32[]{:S(2)}, u32[]{:S(2)}) collective-permute-start(s32[4,256]{1,0:T(4,128)S(1)} %pad_add_fusion.7), channel_id=1, source_target_pairs={{0,2},{1,3},{2,0},{3,1},{4,6},{5,7},{6,4},{7,5},{8,10},{9,11},{10,... | collective-permute-start | bytes 12296 | tf_op jit(solution)/shard_map/ppermute | solution.py:107
  20.5 0.6 convert_compare_fusion
  21.1 1.0 %collective-permute-done.1 = s32[4,256]{1,0:T(4,128)S(1)} collective-permute-done((s32[4,256]{1,0:T(4,128)S(1)}, s32[4,256]{1,0:T(4,128)S(1)}, u32[]{:S(2)}, u32[]{:S(2)}) %collective-permute-start.1) | collective-permute-done | bytes 4128 | tf_op jit(solution)/shard_map/ppermute | solution.py:107
  22.1 2.1 %collective-permute-start.2 = (s32[4,512]{1,0:T(4,128)S(1)}, s32[4,512]{1,0:T(4,128)S(1)}, u32[]{:S(2)}, u32[]{:S(2)}) collective-permute-start(s32[4,512]{1,0:T(4,128)S(1)} %pad_add_fusion.5), channel_id=1, source_target_pairs={{0,4},{1,5},{2,6},{3,7},{4,0},{5,1},{6,2},{7,3},{8,12},{9,13},{10,... | collective-permute-start | bytes 24584 | tf_op jit(solution)/shard_map/ppermute | solution.py:107
  24.2 1.6 %collective-permute-done.2 = s32[4,512]{1,0:T(4,128)S(1)} collective-permute-done((s32[4,512]{1,0:T(4,128)S(1)}, s32[4,512]{1,0:T(4,128)S(1)}, u32[]{:S(2)}, u32[]{:S(2)}) %collective-permute-start.2) | collective-permute-done | bytes 8224 | tf_op jit(solution)/shard_map/ppermute | solution.py:107
  25.9 3.1 %collective-permute-start.3 = (s32[4,1024]{1,0:T(4,128)S(1)}, s32[4,1024]{1,0:T(4,128)S(1)}, u32[]{:S(2)}, u32[]{:S(2)}) collective-permute-start(s32[4,1024]{1,0:T(4,128)S(1)} %pad_add_fusion.3), channel_id=1, source_target_pairs={{0,8},{1,9},{2,10},{3,11},{4,12},{5,13},{6,14},{7,15},{8,0},{9,1},... | collective-permute-start | bytes 49160 | tf_op jit(solution)/shard_map/ppermute | solution.py:107
  29.0 2.3 %slice.252 = bf16[344,1024]{1,0:T(8,128)(2,1)} slice(f32[344,1152]{1,0:T(8,128)} %add_multiply_fusion), slice={[0:344], [0:1024]} | slice | bytes 1409024 | tf_op jit(solution)/shard_map/slice | solution.py:221
  31.3 2.3 %copy.39 = bf16[344,1024]{0,1:T(8,128)(2,1)} copy(bf16[344,1024]{1,0:T(8,128)(2,1)} %slice.252) | data formatting | bytes 1409024 | tf_op jit(solution)/shard_map/slice | solution.py:221
  33.6 0.8 %copy.38 = f32[344,64]{0,1:T(8,128)} copy(f32[344,64]{1,0:T(8,128)S(1)} %slice-done) | data formatting | bytes 176128 | tf_op jit(solution)/shard_map/slice | solution.py:222
  34.4 0.7 mul.237
  35.2 0.6 slice_bitcast_fusion.7
  35.9 3.1 %convolution_convert_fusion.1 = bf16[4,128,1024]{2,1,0:T(8,128)(2,1)} fusion(s32[4,128]{1,0:T(4,128)S(1)} %pad_add_fusion.9, f32[344,1152]{1,0:T(8,128)} %add_multiply_fusion), kind=kOutput, calls=%fused_computation.29 | convolution fusion | flops 361410560 | bytes 1755136 | tf_op jit(solution)/shard_map/rtg,gc->rtc/dot_general | solution.py:248
  39.4 0.6 copy.60
  40.0 1.3 %rev.9 = s32[2,16,128]{2,1,0:T(8,128)} reverse(s32[2,16,128]{2,1,0:T(8,128)} %bitcast.119), dimensions={1} | reverse | bytes 32768 | tf_op jit(solution)/shard_map/rev | solution.py:155
  41.4 0.7 %broadcast_compare_fusion.3 = (pred[2,15,128]{2,1,0:T(8,128)(4,1)S(1)}, s32[2,15,128]{2,1,0:T(8,128)S(1)}) fusion(s32[]{:T(128)S(6)} %select_n.223, s32[2,16,128]{2,1,0:T(8,128)S(1)} %bitcast.118, s32[2,16,128]{2,1,0:T(8,128)} %rev.9), kind=kLoop, calls=%fused_computation.151 | loop fusion | flops 7680 | bytes 51972 | tf_op jit(solution)/shard_map/eq | solution.py:126
  42.1 1.3 %fusion.53 = f32[2,16,15,128]{3,1,2,0:T(8,128)S(1)} fusion(f32[16]{0:T(128)} %param.26, f32[16]{0:T(128)} %copy-done.27, f32[16]{0:T(128)} %copy-done.28, f32[16]{0:T(128)} %copy-done.29, f32[16]{0:T(128)} %copy-done.26, f32[16]{0:T(128)} %copy-done.43, pred[2,15,128]{2,1,0:T(8,128)(4,1)S(1)} %get-tuple-element.22, ...), kind=kOutput, calls=%fused_computation.75 | convolution fusion | flops 95309824 | bytes 261504 | tf_op jit(solution)/shard_map/...s,st->...t/dot_general | solution.py:147
  43.5 0.7 %copy-done.4 = f32[2,16,15,128]{3,1,2,0:T(8,128)} copy-done((f32[2,16,15,128]{3,1,2,0:T(8,128)}, f32[2,16,15,128]{3,1,2,0:T(8,128)S(1)}, u32[]{:S(2)}) %copy-start.4) | copy-done | bytes 245784
  44.2 0.8 %slice.199 = f32[2,16,15,1]{3,1,2,0:T(8,128)} slice(f32[2,16,15,128]{3,1,2,0:T(8,128)S(1)} %fusion.53), slice={[0:2], [0:16], [0:15], [127:128]} | slice | bytes 3840 | tf_op jit(solution)/shard_map/slice | solution.py:165
  45.0 1.2 %copy.35 = f32[2,16,15,1]{1,0,2,3:T(2,128)S(1)} copy(f32[2,16,15,1]{3,1,2,0:T(8,128)} %slice.199) | data formatting | bytes 3840 | tf_op jit(solution)/shard_map/slice | solution.py:165
  46.2 1.0 %select_reduce_fusion = f32[2,16,15]{1,0,2:T(2,128)S(1)} fusion(pred[15,15]{1,0:T(8,128)(4,1)} %fusion.85, f32[2,16,15]{1,0,2:T(2,128)S(1)} %bitcast.116), kind=kLoop, calls=%fused_computation.77 | loop fusion | flops 13920 | bytes 4065 | tf_op jit(solution)/shard_map/reduce_sum | solution.py:170
  47.2 1.4 %broadcast_select_fusion = (f32[2,16,15,128]{3,1,2,0:T(8,128)S(1)}, f32[2,16,15,128]{3,1,2,0:T(8,128)S(1)}) fusion(pred[15]{0:T(512)(128)(4,1)} %copy-done.25, f32[2,16,15]{1,2,0:T(8,128)S(1)} %copy.37, f32[16]{0:T(128)} %param.26, f32[16]{0:T(128)} %copy-done.27, pred[2,15,128]{2,1,0:T(8,128)(4,1)} %copy-done.18, f32[16]{0:T(128)} %copy-done.28, ...), kind=kLoop, calls=%fused_computation.88 | loop fusion | flops 1105920 | bytes 756815 | tf_op jit(solution)/shard_map/jit(_where)/select_n | solution.py:175
  48.6 0.7 %broadcast_select_fusion.1 = f32[2,16,15,128]{3,1,2,0:T(8,128)S(1)} fusion(f32[2,16,15,128]{3,1,2,0:T(8,128)S(1)} %get-tuple-element.3, pred[15]{0:T(512)(128)(4,1)} %copy-done.25), kind=kLoop, calls=%fused_computation.90 | loop fusion | flops 61440 | bytes 491535 | tf_op jit(solution)/shard_map/jit(_where)/select_n | solution.py:175
  49.4 0.8 %fusion.46 = bf16[2,32,15,128]{3,1,2,0:T(8,128)(2,1)} fusion(f32[2,16,15,128]{3,1,2,0:T(8,128)S(1)} %broadcast_select_fusion.1, f32[2,16,15,128]{3,1,2,0:T(8,128)S(1)} %get-tuple-element.2), kind=kLoop, calls=%fused_computation.68 | loop fusion | flops 491520 | bytes 737280 | tf_op jit(solution)/shard_map/convert_element_type | solution.py:142
  50.1 0.7 %subtract_convert_fusion = bf16[2,32,15,128]{3,1,2,0:T(8,128)(2,1)} fusion(f32[2,16,15,128]{3,1,2,0:T(8,128)S(1)} %broadcast_select_fusion.1, f32[2,16,15,128]{3,1,2,0:T(8,128)S(1)} %get-tuple-element.2), kind=kLoop, calls=%fused_computation.67 | loop fusion | flops 614400 | bytes 737280 | tf_op jit(solution)/shard_map/convert_element_type | solution.py:143
  50.9 2.3 %copy.34 = bf16[4,128,1024]{1,2,0:T(8,128)(2,1)} copy(bf16[4,128,1024]{2,1,0:T(8,128)(2,1)} %convolution_convert_fusion.1) | data formatting | bytes 2097152 | tf_op jit(solution)/shard_map/convert_element_type | solution.py:248
  53.2 1.1 %fusion.55 = f32[4,128,128]{2,1,0:T(8,128)} fusion(f32[4,128,128]{1,2,0:T(8,128)S(1)} %fusion.36), kind=kOutput, calls=%fused_computation.79 | convolution fusion | flops 25165824 | bytes 524288 | tf_op jit(solution)/shard_map/utn,usn->uts/dot_general | solution.py:269
  54.9 0.7 %rev.10 = s32[2,16,128]{2,1,0:T(8,128)S(1)} reverse(s32[2,16,128]{2,1,0:T(8,128)} %bitcast.120), dimensions={1} | reverse | bytes 32768 | tf_op jit(solution)/shard_map/rev | solution.py:155
  55.6 0.8 %copy.57 = s32[1,2,16,128]{3,2,1,0:T(8,128)S(1)} copy(s32[1,2,16,128]{3,1,2,0:T(2,128)} %get-tuple-element.12) | data formatting | bytes 32768
  56.4 2.1 %fusion.26 = f32[2,64,344]{2,1,0:T(8,128)S(1)} fusion(s32[2,15,128]{2,1,0:T(8,128)S(1)} %fusion.79, bf16[2,32,15,128]{3,1,2,0:T(8,128)(2,1)} %subtract_convert_fusion, bf16[2,32,15,128]{3,1,2,0:T(8,128)(2,1)} %fusion.46), kind=kOutput, calls=%fused_computation.37 | convolution fusion | flops 171386880 | bytes 683008 | tf_op jit(solution)/shard_map/whbs,wbsg->whg/dot_general | solution.py:178
  58.6 1.0 %fusion.3 = f32[16,4,64,64]{3,2,0,1:T(8,128)S(1)} fusion(bf16[16,344,64,1]{1,2,0,3:T(8,128)(2,1)S(1)} %bitcast.112, f32[344,64]{0,1:T(8,128)S(1)} %copy-done.8, f32[4,16,344]{2,1,0:T(8,128)S(1)} %pad_maximum_fusion.1), kind=kOutput, calls=%fused_computation.6 | convolution fusion | flops 183173120 | bytes 1929216 | tf_op jit(solution)/shard_map/hgp,uhgn->uhpn/dot_general | solution.py:308
  59.8 1.6 %fusion.9 = f32[4,16,64,128]{3,2,1,0:T(8,128)S(1)} fusion(bf16[4,128,16,64]{1,3,2,0:T(8,128)(2,1)S(1)} %bitcast.109, f32[4,16,128]{2,1,0:T(8,128)S(1)} %copy-done.13, f32[4,16,128]{2,1,0:T(8,128)S(1)} %copy-done.15, f32[4,128,128]{2,1,0:T(8,128)S(1)} %copy-done.6, pred[128,128]{1,0:T(8,128)(4,1)S(1)} %copy-done.20), kind=kOutput, calls=%fused_computation.14 | convolution fusion | flops 140509184 | bytes 3489792 | tf_op jit(solution)/shard_map/uhts,ushp->uthp/dot_general | solution.py:274
  61.5 2.7 %multiply_reduce_fusion = (f32[4,128,16]{1,2,0:T(8,128)S(1)}, f32[4,128,16,64]{1,3,2,0:T(8,128)S(1)}) fusion(f32[4,128,16,64]{1,3,2,0:T(8,128)S(1)} %bitcast.108, bf16[4,128,16,64]{1,3,2,0:T(8,128)(2,1)S(1)} %bitcast.110, f32[16]{0:T(128)S(1)} %copy-done.35, f32[4,128,16]{1,2,0:T(8,128)S(1)} %copy-done.7, f32[16,4,64,64]{3,2,0,1:T(8,128)S(1)} %fusion.3, ...), kind=kOutput, calls=%fused_computation.21 | convolution fusion | flops 207609856 | bytes 9634304 | tf_op jit(solution)/shard_map/utn,uhpn->uthp/dot_general | solution.py:311
  64.8 0.7 copy-done.3
  65.5 0.7 %convolution_convert_fusion.2 = bf16[4,128,512]{2,1,0:T(8,128)(2,1)S(1)} fusion(bf16[4,128,1024]{1,2,0:T(8,128)(2,1)S(1)} %bitcast.111, bf16[1024,512]{1,0:T(8,128)(2,1)S(1)} %copy-done.3), kind=kOutput, calls=%fused_computation.31 | convolution fusion | flops 537133056 | bytes 2621440 | tf_op jit(solution)/shard_map/gre,ed->grd/dot_general | solution.py:321
  66.3 0.9 %rev.11 = bf16[2,128,512]{2,1,0:T(8,128)(2,1)S(1)} reverse(bf16[2,128,512]{2,1,0:T(8,128)(2,1)S(1)} %slice.206), dimensions={1,2} | reverse | bytes 524288 | tf_op jit(solution)/shard_map/rev | solution.py:328
  (141 shorter events, 6.4 us)
Async XLA Ops:
  0.6 4.5 %copy-start = (bf16[512,1152]{1,0:T(8,128)(2,1)S(1)}, bf16[512,1152]{1,0:T(8,128)(2,1)}, u32[]{:S(2)}) copy-start(bf16[512,1152]{1,0:T(8,128)(2,1)} %param.21) | copy-start | bytes 3538948
  0.6 9.5 %copy-start.22 = (f32[512]{0:T(512)S(1)}, f32[512]{0:T(512)}, u32[]{:S(2)}) copy-start(f32[512]{0:T(512)} %param.20) | copy-start | bytes 6148
  0.7 7.2 %copy-start.41 = (f32[16]{0:T(128)S(1)}, f32[16]{0:T(128)}, u32[]{:S(2)}) copy-start(f32[16]{0:T(128)} %param.27) | copy-start | bytes 196
  0.7 7.2 %copy-start.31 = (f32[16]{0:T(128)S(1)}, f32[16]{0:T(128)}, u32[]{:S(2)}) copy-start(f32[16]{0:T(128)} %param.26) | copy-start | bytes 196
  2.3 9.8 %copy-start.23 = (s32[4,128]{1,0:T(4,128)}, s32[4,128]{1,0:T(4,128)S(1)}, u32[]{:S(2)}) copy-start(s32[4,128]{1,0:T(4,128)S(1)} %pad_add_fusion.8) | copy-start | bytes 6148
  2.3 15.5 %collective-permute-start = (s32[4,128]{1,0:T(4,128)S(1)}, s32[4,128]{1,0:T(4,128)S(1)}, u32[]{:S(2)}, u32[]{:S(2)}) collective-permute-start(s32[4,128]{1,0:T(4,128)S(1)} %pad_add_fusion.8), channel_id=1, source_target_pairs={{0,1},{1,0},{2,3},{3,2},{4,5},{5,4},{6,7},{7,6},{8,9},{9,8},{10,11... | collective-permute-start | bytes 6152 | tf_op jit(solution)/shard_map/ppermute | solution.py:107
  5.1 6.9 %copy-start.10 = (bf16[4,512]{1,0:T(4,128)(2,1)}, bf16[4,512]{1,0:T(4,128)(2,1)S(1)}, u32[]{:S(2)}) copy-start(bf16[4,512]{1,0:T(4,128)(2,1)S(1)} %get-tuple-element.7) | copy-start | bytes 12292
  6.1 5.9 %copy-start.39 = (bf16[512,2]{0,1:T(2,128)(2,1)S(1)}, bf16[512,2]{0,1:T(2,128)(2,1)}, u32[]{:S(2)}) copy-start(bf16[512,2]{0,1:T(2,128)(2,1)} %param.32) | copy-start | bytes 6148
  7.8 5.0 %copy-start.37 = (f32[2,2,128]{2,1,0:T(2,128)S(1)}, f32[2,2,128]{2,1,0:T(2,128)}, u32[]{:S(2)}) copy-start(f32[2,2,128]{2,1,0:T(2,128)} %param.34) | copy-start | bytes 6148
  7.8 5.6 %copy-start.36 = (f32[1152]{0:T(1024)S(1)}, f32[1152]{0:T(1024)}, u32[]{:S(2)}) copy-start(f32[1152]{0:T(1024)} %param.25) | copy-start | bytes 13828
  7.8 2.2 %copy-start.26 = (f32[16]{0:T(128)}, f32[16]{0:T(128)S(1)}, u32[]{:S(2)}) copy-start(f32[16]{0:T(128)S(1)} %get-tuple-element.39) | copy-start | bytes 196
  7.9 5.6 %copy-start.27 = (f32[16]{0:T(128)}, f32[16]{0:T(128)S(1)}, u32[]{:S(2)}) copy-start(f32[16]{0:T(128)S(1)} %get-tuple-element.40) | copy-start | bytes 196
  7.9 5.6 %copy-start.28 = (f32[16]{0:T(128)}, f32[16]{0:T(128)S(1)}, u32[]{:S(2)}) copy-start(f32[16]{0:T(128)S(1)} %get-tuple-element.41) | copy-start | bytes 196
  7.9 5.6 %copy-start.29 = (f32[16]{0:T(128)}, f32[16]{0:T(128)S(1)}, u32[]{:S(2)}) copy-start(f32[16]{0:T(128)S(1)} %get-tuple-element.42) | copy-start | bytes 196
  7.9 5.6 %copy-start.43 = (f32[16]{0:T(128)}, f32[16]{0:T(128)S(1)}, u32[]{:S(2)}) copy-start(f32[16]{0:T(128)S(1)} %exponential_negate_fusion) | copy-start | bytes 196
  9.5 7.7 %copy-start.25 = (pred[15]{0:T(512)(128)(4,1)}, pred[15]{0:T(512)(128)(4,1)S(1)}, u32[]{:S(2)}) copy-start(pred[15]{0:T(512)(128)(4,1)S(1)} %iota_compare_fusion.19) | copy-start | bytes 49
  12.1 5.8 %copy-start.21 = (s32[2,128]{1,0:T(2,128)S(1)}, s32[2,128]{1,0:T(2,128)}, u32[]{:S(2)}) copy-start(s32[2,128]{1,0:T(2,128)} %param.18) | copy-start | bytes 3076
  17.2 16.5 %slice-start = ((f32[344,1152]{1,0:T(8,128)}), f32[344,64]{1,0:T(8,128)S(1)}, s32[]{:S(2)}) async-start(f32[344,1152]{1,0:T(8,128)} %add_multiply_fusion), calls=%async_computation | async-start | bytes 352256 | tf_op jit(solution)/shard_map/slice | solution.py:222
  17.2 17.2 %copy-start.30 = (f32[1024]{0:T(1024)S(1)}, f32[1024]{0:T(1024)}, u32[]{:S(2)}) copy-start(f32[1024]{0:T(1024)} %param.29) | copy-start | bytes 12292
  17.9 4.2 %collective-permute-start.1 = (s32[4,256]{1,0:T(4,128)S(1)}, s32[4,256]{1,0:T(4,128)S(1)}, u32[]{:S(2)}, u32[]{:S(2)}) collective-permute-start(s32[4,256]{1,0:T(4,128)S(1)} %pad_add_fusion.7), channel_id=1, source_target_pairs={{0,2},{1,3},{2,0},{3,1},{4,6},{5,7},{6,4},{7,5},{8,10},{9,11},{10,... | collective-permute-start | bytes 12296 | tf_op jit(solution)/shard_map/ppermute | solution.py:107
  22.1 3.8 %collective-permute-start.2 = (s32[4,512]{1,0:T(4,128)S(1)}, s32[4,512]{1,0:T(4,128)S(1)}, u32[]{:S(2)}, u32[]{:S(2)}) collective-permute-start(s32[4,512]{1,0:T(4,128)S(1)} %pad_add_fusion.5), channel_id=1, source_target_pairs={{0,4},{1,5},{2,6},{3,7},{4,0},{5,1},{6,2},{7,3},{8,12},{9,13},{10,... | collective-permute-start | bytes 24584 | tf_op jit(solution)/shard_map/ppermute | solution.py:107
  25.9 9.1 %collective-permute-start.3 = (s32[4,1024]{1,0:T(4,128)S(1)}, s32[4,1024]{1,0:T(4,128)S(1)}, u32[]{:S(2)}, u32[]{:S(2)}) collective-permute-start(s32[4,1024]{1,0:T(4,128)S(1)} %pad_add_fusion.3), channel_id=1, source_target_pairs={{0,8},{1,9},{2,10},{3,11},{4,12},{5,13},{6,14},{7,15},{8,0},{9,1},... | collective-permute-start | bytes 49160 | tf_op jit(solution)/shard_map/ppermute | solution.py:107
  35.0 3.9 %copy-start.2 = (f32[344,1152]{1,0:T(8,128)S(1)}, f32[344,1152]{1,0:T(8,128)}, u32[]{:S(2)}) copy-start(f32[344,1152]{1,0:T(8,128)} %add_multiply_fusion) | copy-start | bytes 4755460
  42.1 1.3 %copy-start.19 = (pred[2,15,128]{2,1,0:T(8,128)(4,1)}, pred[2,15,128]{2,1,0:T(8,128)(4,1)S(1)}, u32[]{:S(2)}) copy-start(pred[2,15,128]{2,1,0:T(8,128)(4,1)S(1)} %get-tuple-element.4) | copy-start | bytes 11524
  42.1 1.3 %copy-start.16 = (pred[2,15,128]{2,1,0:T(8,128)(4,1)}, pred[2,15,128]{2,1,0:T(8,128)(4,1)S(1)}, u32[]{:S(2)}) copy-start(pred[2,15,128]{2,1,0:T(8,128)(4,1)S(1)} %get-tuple-element.20) | copy-start | bytes 11524
  42.1 1.3 %copy-start.17 = (pred[2,15,128]{2,1,0:T(8,128)(4,1)}, pred[2,15,128]{2,1,0:T(8,128)(4,1)S(1)}, u32[]{:S(2)}) copy-start(pred[2,15,128]{2,1,0:T(8,128)(4,1)S(1)} %get-tuple-element.21) | copy-start | bytes 11524
  42.1 1.3 %copy-start.18 = (pred[2,15,128]{2,1,0:T(8,128)(4,1)}, pred[2,15,128]{2,1,0:T(8,128)(4,1)S(1)}, u32[]{:S(2)}) copy-start(pred[2,15,128]{2,1,0:T(8,128)(4,1)S(1)} %get-tuple-element.22) | copy-start | bytes 11524
  49.4 4.9 %copy-start.9 = (s32[1,2,16,128]{3,1,2,0:T(2,128)S(1)}, s32[1,2,16,128]{3,1,2,0:T(2,128)}, u32[]{:S(2)}) copy-start(s32[1,2,16,128]{3,1,2,0:T(2,128)} %get-tuple-element.13) | copy-start | bytes 49156
  55.6 2.9 %copy-start.5 = (bf16[344,1024]{0,1:T(8,128)(2,1)S(1)}, bf16[344,1024]{0,1:T(8,128)(2,1)}, u32[]{:S(2)}) copy-start(bf16[344,1024]{0,1:T(8,128)(2,1)} %copy.39) | copy-start | bytes 2113540
  55.6 3.0 %copy-start.8 = (f32[344,64]{0,1:T(8,128)S(1)}, f32[344,64]{0,1:T(8,128)}, u32[]{:S(2)}) copy-start(f32[344,64]{0,1:T(8,128)} %copy.38) | copy-start | bytes 264196
  58.5 1.2 %copy-start.1 = (bf16[4,128,1024]{1,2,0:T(8,128)(2,1)S(1)}, bf16[4,128,1024]{1,2,0:T(8,128)(2,1)}, u32[]{:S(2)}) copy-start(bf16[4,128,1024]{1,2,0:T(8,128)(2,1)} %copy.34) | copy-start | bytes 3145732
  58.6 1.3 %copy-start.6 = (f32[4,128,128]{2,1,0:T(8,128)S(1)}, f32[4,128,128]{2,1,0:T(8,128)}, u32[]{:S(2)}) copy-start(f32[4,128,128]{2,1,0:T(8,128)} %fusion.55) | copy-start | bytes 786436
  58.6 1.2 %copy-start.13 = (f32[4,16,128]{2,1,0:T(8,128)S(1)}, f32[4,16,128]{2,1,0:T(8,128)}, u32[]{:S(2)}) copy-start(f32[4,16,128]{2,1,0:T(8,128)} %compare_select_fusion.2) | copy-start | bytes 98308
  58.6 1.2 %copy-start.15 = (f32[4,16,128]{2,1,0:T(8,128)S(1)}, f32[4,16,128]{2,1,0:T(8,128)}, u32[]{:S(2)}) copy-start(f32[4,16,128]{2,1,0:T(8,128)} %copy-done.14) | copy-start | bytes 98308
  58.6 1.2 %copy-start.20 = (pred[128,128]{1,0:T(8,128)(4,1)S(1)}, pred[128,128]{1,0:T(8,128)(4,1)}, u32[]{:S(2)}) copy-start(pred[128,128]{1,0:T(8,128)(4,1)} %convert_compare_fusion) | copy-start | bytes 49156
  59.8 1.7 %copy-start.7 = (f32[4,128,16]{1,2,0:T(8,128)S(1)}, f32[4,128,16]{1,2,0:T(8,128)}, u32[]{:S(2)}) copy-start(f32[4,128,16]{1,2,0:T(8,128)} %exponential_bitcast_fusion) | copy-start | bytes 98308
  59.8 1.7 %copy-start.35 = (f32[16]{0:T(128)S(1)}, f32[16]{0:T(128)}, u32[]{:S(2)}) copy-start(f32[16]{0:T(128)} %param.28) | copy-start | bytes 196
  61.5 2.8 %copy-start.12 = (f32[16,64]{1,0:T(8,128)S(1)}, f32[16,64]{1,0:T(8,128)}, u32[]{:S(2)}) copy-start(f32[16,64]{1,0:T(8,128)} %mul.237) | copy-start | bytes 12292
  64.2 1.2 %copy-start.3 = (bf16[1024,512]{1,0:T(8,128)(2,1)S(1)}, bf16[1024,512]{1,0:T(8,128)(2,1)}, u32[]{:S(2)}) copy-start(bf16[1024,512]{1,0:T(8,128)(2,1)} %param.30) | copy-start | bytes 3145732
  64.8 2.4 %copy-start.11 = (bf16[4,512]{1,0:T(4,128)(2,1)S(1)}, bf16[4,512]{1,0:T(4,128)(2,1)}, u32[]{:S(2)}) copy-start(bf16[4,512]{1,0:T(4,128)(2,1)} %copy-done.10) | copy-start | bytes 12292
  64.8 2.4 %copy-start.24 = (s32[4,128]{1,0:T(4,128)S(1)}, s32[4,128]{1,0:T(4,128)}, u32[]{:S(2)}) copy-start(s32[4,128]{1,0:T(4,128)} %copy-done.23) | copy-start | bytes 6148
  65.5 2.2 %copy-start.33 = (bf16[512,1]{0,1:T(2,128)(2,1)S(1)}, bf16[512,1]{0,1:T(2,128)(2,1)}, u32[]{:S(2)}) copy-start(bf16[512,1]{0,1:T(2,128)(2,1)} %get-tuple-element.33) | copy-start | bytes 3076
  65.5 2.2 %copy-start.34 = (bf16[512,1]{0,1:T(2,128)(2,1)S(1)}, bf16[512,1]{0,1:T(2,128)(2,1)}, u32[]{:S(2)}) copy-start(bf16[512,1]{0,1:T(2,128)(2,1)} %get-tuple-element.34) | copy-start | bytes 3076
  65.5 2.2 %copy-start.38 = (f32[512]{0:T(512)S(1)}, f32[512]{0:T(512)}, u32[]{:S(2)}) copy-start(f32[512]{0:T(512)} %param.31) | copy-start | bytes 6148
  65.5 2.2 %copy-start.40 = (bf16[512,2]{0,1:T(2,128)(2,1)S(1)}, bf16[512,2]{0,1:T(2,128)(2,1)}, u32[]{:S(2)}) copy-start(bf16[512,2]{0,1:T(2,128)(2,1)} %param.32) | copy-start | bytes 6148
  65.5 2.5 %copy-start.32 = (s32[2,2,128]{2,1,0:T(2,128)S(1)}, s32[2,2,128]{2,1,0:T(2,128)}, u32[]{:S(2)}) copy-start(s32[2,2,128]{2,1,0:T(2,128)} %param.33) | copy-start | bytes 6148
  65.5 2.5 %copy-start.44 = (f32[2,2,128]{2,1,0:T(2,128)S(1)}, f32[2,2,128]{2,1,0:T(2,128)}, u32[]{:S(2)}) copy-start(f32[2,2,128]{2,1,0:T(2,128)} %fusion.28) | copy-start | bytes 6148
  67.6 1.0 %copy-start.42 = (bf16[2,128,512]{2,1,0:T(8,128)(2,1)}, bf16[2,128,512]{2,1,0:T(8,128)(2,1)S(1)}, u32[]{:S(2)}) copy-start(bf16[2,128,512]{2,1,0:T(8,128)(2,1)S(1)} %get-tuple-element.48) | copy-start | bytes 786436
  (2 other events, 1.3 us)
